TPU v7x, 512 devices: a whole 4x4x16 slice. The times are simulated.
512 devices in a mesh: section: 8 (over x, core), frames: 4 (over y), space: 16 (over z).
Axes of the slice: x: 4, y: 4, z: 16, core: 2. Of those that a mesh axis runs over, the one named last changes fastest.
Arguments:
- base_frames: bfloat16 [8, 32, 128, 8, 128], P(None, 'frames', 'space'), may hold values from -6 to 6
- section_noise: bfloat16 [8, 8, 32, 128, 8, 128], P('section', None, 'frames', 'space'), may hold values from -6 to 6
- noise_levels: bfloat16 [8], P('section'), may hold values from 0.29882812 to 1
- spatial_kernel: bfloat16 [8, 9, 128, 128], P('section'), may hold values from -0.15625 to 0.15625
- temporal_kernel: bfloat16 [8, 3, 128, 128], P('section'), may hold values from -0.15625 to 0.15625
- output_weight: bfloat16 [8, 128, 128], P('section'), may hold values from -0.5 to 0.5
Outputs:
- denoised: bfloat16 [8, 8, 32, 128, 8, 128], P('section', None, 'frames', 'space')
All inputs are finite; a program needn't handle non-finite values.
Results may differ from a plain program's by a relative error of at most 0.008.
Values may be sent and summed in bfloat16 or wider, within the bound.
No kernel may reach another device: no remote copies, remote signals or barrier semaphores. Data moves between devices by JAX's collectives and lax.ppermute only.
A program may use at most 64 MiB of HBM per device.

v0:
```python
import jax
import jax.numpy as jnp
from jax import lax
import functools
from jax.experimental import pallas as pl
from jax.experimental.pallas import tpu as pltpu
from jax.sharding import PartitionSpec as P
from jax.experimental import pallas as pl
from jax.experimental.pallas import tpu as pltpu


def conv_kernel(m, n, cols, xl_ref, xc_ref, xr_ref, noisy_ref, w_ref, lv_ref, out_ref):
    channels = w_ref.shape[-1]
    rows_out = (m - 2) * (n - 2) * cols
    views = (xl_ref, xc_ref, xr_ref)
    acc = jnp.zeros((rows_out, channels), jnp.float32)
    for tap in range(9):
        a, b = tap // 3, tap % 3
        v = views[b][pl.ds(1, m - 2), pl.ds(a * cols, (n - 2) * cols), :]
        v = v.reshape(rows_out, channels).astype(jnp.bfloat16)
        acc = acc + jnp.dot(v, w_ref[tap], preferred_element_type=jnp.float32)
    for t in range(3):
        v = xc_ref[pl.ds(t, m - 2), pl.ds(cols, (n - 2) * cols), :]
        v = v.reshape(rows_out, channels).astype(jnp.bfloat16)
        acc = acc + jnp.dot(v, w_ref[9 + t], preferred_element_type=jnp.float32)
    act = (acc / (1.0 + jnp.exp(-acc))).astype(jnp.bfloat16)
    est = jnp.dot(act, w_ref[12], preferred_element_type=jnp.float32)
    noisy = noisy_ref[pl.ds(1, m - 2), pl.ds(cols, (n - 2) * cols), :].reshape(rows_out, channels)
    level = lv_ref[0:1, :]
    out_ref[...] = (noisy - level * est).astype(out_ref.dtype)


def conv_call(xl, xc, xr, noisy, weights, level_row, m, n, cols):
    channels = weights.shape[-1]
    rows_out = (m - 2) * (n - 2) * cols
    flops = 2 * rows_out * channels * channels * 13
    nbytes = 4 * 4 * m * n * cols * channels + 2 * 13 * channels * channels + 2 * rows_out * channels
    return pl.pallas_call(
        functools.partial(conv_kernel, m, n, cols),
        out_shape=jax.ShapeDtypeStruct((rows_out, channels), jnp.bfloat16),
        in_specs=[pl.BlockSpec(memory_space=pltpu.VMEM)] * 6,
        out_specs=pl.BlockSpec(memory_space=pltpu.VMEM),
        cost_estimate=pl.CostEstimate(flops=flops, bytes_accessed=nbytes, transcendentals=rows_out * channels),
    )(xl, xc, xr, noisy, weights, level_row)

HALO = 4


def extend(block, width, frame_dim, row_dim):
    for axis, dim in (("frames", frame_dim), ("space", row_dim)):
        count = lax.axis_size(axis)
        forward = [(i, i + 1) for i in range(count - 1)]
        backward = [(i + 1, i) for i in range(count - 1)]
        size = block.shape[dim]
        low = lax.ppermute(lax.slice_in_dim(block, size - width, size, axis=dim), axis, forward)
        high = lax.ppermute(lax.slice_in_dim(block, 0, width, axis=dim), axis, backward)
        block = jnp.concatenate([low, block, high], axis=dim)
    return block


def inside_mask(num_frames, num_rows, width):
    frame_place = lax.axis_index("frames")
    row_place = lax.axis_index("space")
    total_frames = num_frames * lax.axis_size("frames")
    total_rows = num_rows * lax.axis_size("space")
    frames = frame_place * num_frames - width + jnp.arange(num_frames + 2 * width)
    rows = row_place * num_rows - width + jnp.arange(num_rows + 2 * width)
    frame_ok = (frames >= 0) & (frames < total_frames)
    row_ok = (rows >= 0) & (rows < total_rows)
    return (frame_ok[:, None] & row_ok[None, :])[None, :, :, None, None]


def denoise(previous, noise_part, noise_scale, weights, mask):
    noisy = previous.astype(jnp.float32) + noise_scale * noise_part.astype(jnp.float32)
    normalized = (
        noisy * lax.rsqrt(jnp.mean(noisy * noisy, axis=-1, keepdims=True) + 1e-05)
    ).astype(jnp.bfloat16)
    normalized = jnp.where(mask, normalized, jnp.zeros_like(normalized))
    num_videos, m, n, num_cols, channels = previous.shape
    padded = jnp.pad(normalized, ((0, 0), (0, 0), (0, 0), (1, 1), (0, 0)))
    flat = lambda x: x.astype(jnp.float32).reshape(m, n * num_cols, channels)
    level_row = jnp.full((8, channels), noise_scale, jnp.float32)
    outs = []
    for v in range(num_videos):
        out = conv_call(
            flat(padded[v, :, :, 0:num_cols]),
            flat(normalized[v]),
            flat(padded[v, :, :, 2 : num_cols + 2]),
            noisy[v].reshape(m, n * num_cols, channels),
            weights,
            level_row,
            m,
            n,
            num_cols,
        )
        outs.append(out.reshape(m - 2, n - 2, num_cols, channels))
    return jnp.stack(outs)


def on_device(
    base_frames, section_noise, noise_levels, spatial_kernel, temporal_kernel, output_weight
):
    place = lax.axis_index("section")
    sections = lax.axis_size("section")
    video_count, num_frames, num_rows = base_frames.shape[:3]
    per_device = video_count // sections
    halo = HALO
    noise_t = lax.all_to_all(section_noise[0], "section", 0, 0, tiled=True)
    noise_t = noise_t.reshape((sections, per_device) + noise_t.shape[1:])
    channels = spatial_kernel.shape[-1]
    level_slab = jnp.broadcast_to(
        noise_levels.reshape(1, 1, 1, 1), (1, 1, channels, channels)
    ).astype(spatial_kernel.dtype)
    packed = jnp.concatenate(
        [spatial_kernel, temporal_kernel, output_weight[:, None], level_slab], axis=1
    )
    packed = lax.all_gather(packed, "section", tiled=True)
    incoming = lax.dynamic_slice_in_dim(base_frames, place * per_device, per_device, 0)
    both = extend(jnp.concatenate([incoming[None], noise_t[:halo]], axis=0), halo, 2, 3)
    prior_ext = both[0]
    noise_parts = [both[1:]]
    for start in range(halo, sections, halo):
        noise_parts.append(extend(noise_t[start : start + halo], halo, 2, 3))
    noise_ext = jnp.concatenate(noise_parts, axis=0)
    masks = [inside_mask(num_frames, num_rows, w) for w in range(halo + 1)]
    results = []
    for k in range(sections):
        j = k % halo
        if j == 0 and k > 0:
            prior_ext = extend(prior_ext, halo, 1, 2)
        width = halo - j
        cut = halo - width
        noise_here = noise_ext[
            k, :, cut : cut + num_frames + 2 * width, cut : cut + num_rows + 2 * width
        ]
        prior_ext = denoise(
            prior_ext,
            noise_here,
            packed[k, 13, 0, 0].astype(jnp.float32),
            packed[k, 0:13],
            masks[width],
        )
        inner = width - 1
        results.append(
            prior_ext[:, inner : inner + num_frames, inner : inner + num_rows]
        )
    stacked = jnp.stack(results)
    return lax.all_to_all(stacked, "section", 0, 1, tiled=True)


def solution(mesh):
    return jax.shard_map(
        on_device,
        mesh=mesh,
        in_specs=(
            P(None, "frames", "space", None, None),
            P("section", None, "frames", "space", None, None),
            P("section"),
            P("section", None, None, None),
            P("section", None, None, None),
            P("section", None, None),
        ),
        out_specs=P("section", None, "frames", "space", None, None),
        check_vma=False,
    )
```

profile of v0, /device:TPU:96, one launch (start us, length us, event | category | flops | bytes accessed | tf_op | source)
XLA Modules:
  0.0 235.4 jit_solution(11265333984064372198)
XLA Ops:
  7.4 1.9 maximum_maximum_fusion
  9.3 4.3 %all-to-all-start = ((bf16[8,8,8,8,128]{4,3,2,1,0:T(8,128)(2,1)}), bf16[8,8,8,8,128]{4,3,2,1,0:T(8,128)(2,1)S(1)}, u32[]{:S(2)}, u32[]{:S(2)}) async-start(bf16[8,8,8,8,128]{4,3,2,1,0:T(8,128)(2,1)} %bitcast.342), calls=%async_computation | async-start | bytes 2097152 | tf_op jit(solution)/shard_map/all_to_all | solution.py:108
  14.4 15.2 %all-to-all-done = bf16[8,8,8,8,128]{4,3,2,1,0:T(8,128)(2,1)S(1)} async-done(((bf16[8,8,8,8,128]{4,3,2,1,0:T(8,128)(2,1)}), bf16[8,8,8,8,128]{4,3,2,1,0:T(8,128)(2,1)S(1)}, u32[]{:S(2)}, u32[]{:S(2)}) %all-to-all-start) | async-done | bytes 1048608 | tf_op jit(solution)/shard_map/all_to_all | solution.py:108
  30.5 3.5 %collective-permute-start.8 = (bf16[4,1,4,8,8,128]{5,4,3,2,1,0:T(8,128)(2,1)}, bf16[4,1,4,8,8,128]{5,4,3,2,1,0:T(8,128)(2,1)S(1)}, u32[]{:S(2)}, u32[]{:S(2)}) collective-permute-start(bf16[4,1,4,8,8,128]{5,4,3,2,1,0:T(8,128)(2,1)} %get-tuple-element.47), channel_id=1, source_target_pairs={{0,16},{16,32},{32,48},{1,17},{17,33},{33,49},{2,18},{18,34},{34,5... | collective-permute-start | bytes 786440 | tf_op jit(solution)/shard_map/ppermute | solution.py:55
  37.0 4.6 %collective-permute-start = (bf16[5,1,4,8,8,128]{5,4,3,2,0,1:T(8,128)(2,1)S(1)}, bf16[5,1,4,8,8,128]{5,4,3,2,0,1:T(8,128)(2,1)S(1)}, u32[]{:S(2)}, u32[]{:S(2)}) collective-permute-start(bf16[5,1,4,8,8,128]{5,4,3,2,0,1:T(8,128)(2,1)S(1)} %get-tuple-element.43), channel_id=1, source_target_pairs={{0,16},{16,32},{32,48},{1,17},{17,33},{33,49},{2,18},{18,34},{34,5... | collective-permute-start | bytes 983048 | tf_op jit(solution)/shard_map/ppermute | solution.py:55
  44.9 5.0 %collective-permute-start.10 = (bf16[4,1,16,4,8,128]{5,4,3,2,1,0:T(8,128)(2,1)}, bf16[4,1,16,4,8,128]{5,4,3,2,1,0:T(8,128)(2,1)}, u32[]{:S(2)}, u32[]{:S(2)}) collective-permute-start(bf16[4,1,16,4,8,128]{5,4,3,2,1,0:T(8,128)(2,1)} %get-tuple-element.39), channel_id=1, source_target_pairs={{0,1},{1,2},{2,3},{3,4},{4,5},{5,6},{6,7},{7,8},{8,9},{9,10},{10,1... | collective-permute-start | bytes 1572872 | tf_op jit(solution)/shard_map/ppermute | solution.py:55
  49.9 1.9 collective-permute-start.11
  52.1 1.4 fusion.89
  53.5 5.1 %collective-permute-start.2 = (bf16[5,1,16,4,8,128]{5,4,3,2,0,1:T(8,128)(2,1)}, bf16[5,1,16,4,8,128]{5,4,3,2,0,1:T(8,128)(2,1)S(1)}, u32[]{:S(2)}, u32[]{:S(2)}) collective-permute-start(bf16[5,1,16,4,8,128]{5,4,3,2,0,1:T(8,128)(2,1)} %get-tuple-element.35), channel_id=1, source_target_pairs={{0,1},{1,2},{2,3},{3,4},{4,5},{5,6},{6,7},{7,8},{8,9},{9,10},{10,1... | collective-permute-start | bytes 1966088 | tf_op jit(solution)/shard_map/ppermute | solution.py:55
  58.6 2.1 collective-permute-start.3
  60.9 1.7 collective-permute-done.10
  62.6 5.6 %collective-permute-done.11 = bf16[4,1,16,4,8,128]{5,4,3,2,1,0:T(8,128)(2,1)} collective-permute-done((bf16[4,1,16,4,8,128]{5,4,3,2,1,0:T(8,128)(2,1)}, bf16[4,1,16,4,8,128]{5,4,3,2,1,0:T(8,128)(2,1)}, u32[]{:S(2)}, u32[]{:S(2)}) %collective-permute-start.11) | collective-permute-done | bytes 524320 | tf_op jit(solution)/shard_map/ppermute | solution.py:56
  68.2 2.6 %pad_maximum_fusion.1 = bf16[4,1,16,16,8,128]{5,4,3,2,1,0:T(8,128)(2,1)} fusion(bf16[4,1,16,4,8,128]{5,4,3,2,1,0:T(8,128)(2,1)} %collective-permute-done.11, bf16[4,1,4,8,8,128]{5,4,3,2,1,0:T(8,128)(2,1)} %copy-done.12, bf16[4,1,8,8,8,128]{5,4,3,2,1,0:T(8,128)(2,1)S(1)} %get-tuple-element.41, bf16[4,1,4,8,8,128]{5,4,3,2,1,0:T(8,128)(2,1)S(1)} %copy-done.10, ...), kind=kLoop, calls=%fused_computation.1 | loop fusion | flops 4194304 | bytes 4194304 | tf_op jit(solution)/shard_map/concatenate | solution.py:57
  70.8 3.3 %collective-permute-done.2 = bf16[5,1,16,4,8,128]{5,4,3,2,0,1:T(8,128)(2,1)S(1)} collective-permute-done((bf16[5,1,16,4,8,128]{5,4,3,2,0,1:T(8,128)(2,1)}, bf16[5,1,16,4,8,128]{5,4,3,2,0,1:T(8,128)(2,1)S(1)}, u32[]{:S(2)}, u32[]{:S(2)}) %collective-permute-start.2) | collective-permute-done | bytes 655392 | tf_op jit(solution)/shard_map/ppermute | solution.py:55
  74.2 5.2 %collective-permute-done.3 = bf16[5,1,16,4,8,128]{5,4,3,2,0,1:T(8,128)(2,1)S(1)} collective-permute-done((bf16[5,1,16,4,8,128]{5,4,3,2,0,1:T(8,128)(2,1)}, bf16[5,1,16,4,8,128]{5,4,3,2,0,1:T(8,128)(2,1)S(1)}, u32[]{:S(2)}, u32[]{:S(2)}) %collective-permute-start.3) | collective-permute-done | bytes 655392 | tf_op jit(solution)/shard_map/ppermute | solution.py:56
  79.4 1.8 pad_maximum_fusion
  83.2 1.6 fusion.3
  84.9 2.4 %fusion.21 = bf16[1,16,16,8,128]{4,3,2,1,0:T(8,128)(2,1)} fusion(f32[16,16,8]{2,1,0:T(8,128)S(1)} %add_rsqrt_fusion.1, f32[]{:T(128)S(6)} %convert.32, pred[16,16]{1,0:T(8,128)(4,1)S(1)} %broadcast_and_fusion.3, bf16[5,1,16,16,8,128]{5,4,3,2,1,0:T(8,128)(2,1)} %pad_maximum_fusion), kind=kLoop, calls=%fused_computation.71 | loop fusion | flops 1835008 | bytes 1581316 | tf_op jit(solution)/shard_map/jit(_where)/select_n | solution.py:78
  88.9 3.0 %fusion.27 = (f32[16,128,128]{2,1,0:T(8,128)}, f32[16,128,128]{2,1,0:T(8,128)}) fusion(bf16[1,16,16,8,128]{4,3,2,1,0:T(8,128)(2,1)} %fusion.21), kind=kLoop, calls=%fused_computation.77 | loop fusion | flops 524288 | bytes 2621440 | tf_op jit(solution)/shard_map/convert_element_type | solution.py:81
  91.9 2.6 %fusion.19 = (f32[16,128,128]{2,1,0:T(8,128)}, f32[16,128,128]{2,1,0:T(8,128)}) fusion(f32[16,128]{1,0:T(8,128)S(1)} %copy.45, pred[16,128]{1,0:T(8,128)(4,1)S(1)} %copy.43, bf16[5,1,16,16,8,128]{5,4,3,2,1,0:T(8,128)(2,1)} %pad_maximum_fusion, f32[]{:T(128)S(6)} %convert.32), kind=kLoop, calls=%fused_computation.69 | loop fusion | flops 2097152 | bytes 3155972 | tf_op jit(solution)/shard_map/convert_element_type | solution.py:81
  94.5 1.7 slice_bitcast_fusion.2
  97.5 4.7 %shard_map.64 = bf16[1568,128]{1,0:T(8,128)(2,1)} custom-call(f32[16,128,128]{2,1,0:T(8,128)} %get-tuple-element.50.xl_ref, f32[16,128,128]{2,1,0:T(8,128)} %get-tuple-element.17.xc_ref, f32[16,128,128]{2,1,0:T(8,128)} %get-tuple-element.49.xr_ref, f32[16,128,128]{2,1,0:T(8,128)} %get-tuple-element.18.noisy_ref, ...), custom_call_target="tpu_custom_call" | custom-call | flops 667942912 | bytes 5021696 | tf_op jit(solution)/shard_map/pallas_call | solution.py:38
  104.5 1.7 convert_multiply_fusion.4
  107.5 1.3 fusion.45
  108.8 1.4 fusion.37
  111.4 4.1 %shard_map.65 = bf16[1152,128]{1,0:T(8,128)(2,1)} custom-call(f32[14,112,128]{2,1,0:T(8,128)} %get-tuple-element.54.xl_ref, f32[14,112,128]{2,1,0:T(8,128)} %get-tuple-element.15.xc_ref, f32[14,112,128]{2,1,0:T(8,128)} %get-tuple-element.53.xr_ref, f32[14,112,128]{2,1,0:T(8,128)} %get-tuple-element.16.noisy_ref, ...), custom_call_target="tpu_custom_call" | custom-call | flops 490733568 | bytes 3932160 | tf_op jit(solution)/shard_map/pallas_call | solution.py:38
  115.4 1.4 fusion.15
  123.1 3.4 %shard_map.66 = bf16[800,128]{1,0:T(8,128)(2,1)} custom-call(f32[12,96,128]{2,1,0:T(8,128)} %get-tuple-element.58.xl_ref, f32[12,96,128]{2,1,0:T(8,128)} %get-tuple-element.13.xc_ref, f32[12,96,128]{2,1,0:T(8,128)} %get-tuple-element.57.xr_ref, f32[12,96,128]{2,1,0:T(8,128)} %get-tuple-element.14.noisy_ref, bf16[13,128,128]{2,1,0:T(8,128)(2,1)} %get-tuple-element.24.w_ref, ...), custom_call_target="tpu_custom_call" | custom-call | flops 340787200 | bytes 2990080 | tf_op jit(solution)/shard_map/pallas_call | solution.py:38
  131.1 1.6 fusion.82
  136.4 2.9 %shard_map.67 = bf16[512,128]{1,0:T(8,128)(2,1)} custom-call(f32[10,80,128]{2,1,0:T(8,128)} %get-tuple-element.66.xl_ref, f32[10,80,128]{2,1,0:T(8,128)} %get-tuple-element.11.xc_ref, f32[10,80,128]{2,1,0:T(8,128)} %get-tuple-element.65.xr_ref, f32[10,80,128]{2,1,0:T(8,128)} %get-tuple-element.12.noisy_ref, bf16[13,128,128]{2,1,0:T(8,128)(2,1)} %get-tuple-element.23.w_ref, ...), custom_call_target="tpu_custom_call" | custom-call | flops 218103808 | bytes 2195456 | tf_op jit(solution)/shard_map/pallas_call | solution.py:38
  140.2 3.7 %collective-permute-start.4 = (bf16[1,4,8,8,128]{4,3,2,1,0:T(8,128)(2,1)S(1)}, bf16[1,4,8,8,128]{4,3,2,1,0:T(8,128)(2,1)S(1)}, u32[]{:S(2)}, u32[]{:S(2)}) collective-permute-start(bf16[1,4,8,8,128]{4,3,2,1,0:T(8,128)(2,1)S(1)} %get-tuple-element.67), channel_id=1, source_target_pairs={{0,16},{16,32},{32,48},{1,17},{17,33},{33,49},{2,18},{18,34},{34,5... | collective-permute-start | bytes 196616 | tf_op jit(solution)/shard_map/ppermute | solution.py:55
  143.9 1.4 collective-permute-start.5
  147.8 2.4 %collective-permute-done.5 = bf16[1,4,8,8,128]{4,3,2,1,0:T(8,128)(2,1)S(1)} collective-permute-done((bf16[1,4,8,8,128]{4,3,2,1,0:T(8,128)(2,1)S(1)}, bf16[1,4,8,8,128]{4,3,2,1,0:T(8,128)(2,1)S(1)}, u32[]{:S(2)}, u32[]{:S(2)}) %collective-permute-start.5) | collective-permute-done | bytes 65568 | tf_op jit(solution)/shard_map/ppermute | solution.py:56
  151.0 2.8 %collective-permute-start.6 = (bf16[1,16,4,8,128]{4,3,2,1,0:T(8,128)(2,1)S(1)}, bf16[1,16,4,8,128]{4,3,2,1,0:T(8,128)(2,1)S(1)}, u32[]{:S(2)}, u32[]{:S(2)}) collective-permute-start(bf16[1,16,4,8,128]{4,3,2,1,0:T(8,128)(2,1)S(1)} %get-tuple-element.61), channel_id=1, source_target_pairs={{0,1},{1,2},{2,3},{3,4},{4,5},{5,6},{6,7},{7,8},{8,9},{9,10},{10,1... | collective-permute-start | bytes 393224 | tf_op jit(solution)/shard_map/ppermute | solution.py:55
  153.8 3.3 %collective-permute-start.7 = (bf16[1,16,4,8,128]{4,3,2,1,0:T(8,128)(2,1)S(1)}, bf16[1,16,4,8,128]{4,3,2,1,0:T(8,128)(2,1)S(1)}, u32[]{:S(2)}, u32[]{:S(2)}) collective-permute-start(bf16[1,16,4,8,128]{4,3,2,1,0:T(8,128)(2,1)S(1)} %get-tuple-element.62), channel_id=1, source_target_pairs={{1,0},{2,1},{3,2},{4,3},{5,4},{6,5},{7,6},{8,7},{9,8},{10,9},{11,1... | collective-permute-start | bytes 393224 | tf_op jit(solution)/shard_map/ppermute | solution.py:56
  158.1 3.7 %collective-permute-done.7 = bf16[1,16,4,8,128]{4,3,2,1,0:T(8,128)(2,1)S(1)} collective-permute-done((bf16[1,16,4,8,128]{4,3,2,1,0:T(8,128)(2,1)S(1)}, bf16[1,16,4,8,128]{4,3,2,1,0:T(8,128)(2,1)S(1)}, u32[]{:S(2)}, u32[]{:S(2)}) %collective-permute-start.7) | collective-permute-done | bytes 131104 | tf_op jit(solution)/shard_map/ppermute | solution.py:56
  161.9 1.4 multiply_reduce_fusion
  163.5 2.5 %fusion.20 = bf16[1,16,16,8,128]{4,3,2,1,0:T(8,128)(2,1)S(1)} fusion(f32[16,16,8]{2,1,0:T(8,128)S(1)} %add_rsqrt_fusion, f32[]{:T(128)S(6)} %convert.36, pred[16,16]{1,0:T(8,128)(4,1)S(1)} %copy-done.28, bf16[4,1,16,16,8,128]{5,4,3,2,1,0:T(8,128)(2,1)} %pad_maximum_fusion.1, bf16[1,16,4,8,128]{4,3,2,1,0:T(8,128)(2,1)S(1)} %collective-permute-done.7, ...), kind=kLoop, calls=%fused_computation.70 | loop fusion | flops 2883584 | bytes 1581316 | tf_op jit(solution)/shard_map/jit(_where)/select_n | solution.py:78
  166.0 1.6 fusion.31
  167.6 1.5 fusion.23.xc_ref
  171.5 4.7 %shard_map.68 = bf16[1568,128]{1,0:T(8,128)(2,1)} custom-call(f32[16,128,128]{2,1,0:T(8,128)} %get-tuple-element.46.xl_ref, f32[16,128,128]{2,1,0:T(8,128)} %fusion.23.xc_ref, f32[16,128,128]{2,1,0:T(8,128)} %get-tuple-element.45.xr_ref, f32[16,128,128]{2,1,0:T(8,128)} %fusion.noisy_ref, bf16[13,128,128]{2,1,0:T(8,128)(2,1)} %get-tuple-element.22.w_ref, ...), custom_call_target="tpu_custom_call" | custom-call | flops 667942912 | bytes 5021696 | tf_op jit(solution)/shard_map/pallas_call | solution.py:38
  179.9 1.4 fusion.39
  182.5 4.0 %shard_map.69 = bf16[1152,128]{1,0:T(8,128)(2,1)} custom-call(f32[14,112,128]{2,1,0:T(8,128)} %get-tuple-element.52.xl_ref, f32[14,112,128]{2,1,0:T(8,128)} %get-tuple-element.9.xc_ref, f32[14,112,128]{2,1,0:T(8,128)} %get-tuple-element.51.xr_ref, f32[14,112,128]{2,1,0:T(8,128)} %get-tuple-element.10.noisy_ref, ...), custom_call_target="tpu_custom_call" | custom-call | flops 490733568 | bytes 3932160 | tf_op jit(solution)/shard_map/pallas_call | solution.py:38
  187.9 1.3 fusion.56
  193.1 3.4 %shard_map.70 = bf16[800,128]{1,0:T(8,128)(2,1)} custom-call(f32[12,96,128]{2,1,0:T(8,128)} %get-tuple-element.56.xl_ref, f32[12,96,128]{2,1,0:T(8,128)} %get-tuple-element.7.xc_ref, f32[12,96,128]{2,1,0:T(8,128)} %get-tuple-element.55.xr_ref, f32[12,96,128]{2,1,0:T(8,128)} %get-tuple-element.8.noisy_ref, bf16[13,128,128]{2,1,0:T(8,128)(2,1)} %get-tuple-element.20.w_ref, ...), custom_call_target="tpu_custom_call" | custom-call | flops 340787200 | bytes 2990080 | tf_op jit(solution)/shard_map/pallas_call | solution.py:38
  203.4 2.9 %shard_map.71 = bf16[512,128]{1,0:T(8,128)(2,1)} custom-call(f32[10,80,128]{2,1,0:T(8,128)} %get-tuple-element.64.xl_ref, f32[10,80,128]{2,1,0:T(8,128)} %get-tuple-element.5.xc_ref, f32[10,80,128]{2,1,0:T(8,128)} %get-tuple-element.63.xr_ref, f32[10,80,128]{2,1,0:T(8,128)} %get-tuple-element.6.noisy_ref, bf16[13,128,128]{2,1,0:T(8,128)(2,1)} %get-tuple-element.19.w_ref, ...), custom_call_target="tpu_custom_call" | custom-call | flops 218103808 | bytes 2195456 | tf_op jit(solution)/shard_map/pallas_call | solution.py:38
  206.3 1.7 constant_dynamic-update-slice_fusion
  208.0 19.6 %all_to_all.17 = bf16[8,1,8,8,8,128]{5,4,3,2,1,0:T(8,128)(2,1)S(1)} all-to-all(bf16[8,1,8,8,8,128]{5,4,3,2,1,0:T(8,128)(2,1)} %constant_dynamic-update-slice_fusion), channel_id=1, replica_groups=mesh['section'=8,'frames'=4,'space'=16] {'section'}, dimensions={0} | all-to-all | bytes 2097152 | tf_op jit(solution)/shard_map/all_to_all | solution.py:148
  (181 shorter events, 53.3 us)
Async XLA Ops:
  6.5 30.4 %copy-start = (bf16[8,8,8,8,128]{4,3,2,1,0:T(8,128)(2,1)S(1)}, bf16[8,8,8,8,128]{4,3,2,1,0:T(8,128)(2,1)}, u32[]{:S(2)}) copy-start(bf16[8,8,8,8,128]{4,3,2,1,0:T(8,128)(2,1)} %param.6) | copy-start | bytes 3145732
  6.5 74.7 %all-gather.2.cloned.1.call-start = ((), (), s32[]{:S(2)}) async-start(), calls=%async_computation.2 | async-start | bytes 4128768 | tf_op jit(solution)/shard_map/all_gather | solution.py:117
  9.3 20.3 %all-to-all-start = ((bf16[8,8,8,8,128]{4,3,2,1,0:T(8,128)(2,1)}), bf16[8,8,8,8,128]{4,3,2,1,0:T(8,128)(2,1)S(1)}, u32[]{:S(2)}, u32[]{:S(2)}) async-start(bf16[8,8,8,8,128]{4,3,2,1,0:T(8,128)(2,1)} %bitcast.342), calls=%async_computation | async-start | bytes 2097152 | tf_op jit(solution)/shard_map/all_to_all | solution.py:108
  13.8 0.6 copy-start.23
  14.1 92.8 %copy-start.25 = (pred[14,14]{1,0:T(8,128)(4,1)}, pred[14,14]{1,0:T(8,128)(4,1)S(1)}, u32[]{:S(2)}) copy-start(pred[14,14]{1,0:T(8,128)(4,1)S(1)} %broadcast_and_fusion.2) | copy-start | bytes 592
  30.5 12.3 %collective-permute-start.8 = (bf16[4,1,4,8,8,128]{5,4,3,2,1,0:T(8,128)(2,1)}, bf16[4,1,4,8,8,128]{5,4,3,2,1,0:T(8,128)(2,1)S(1)}, u32[]{:S(2)}, u32[]{:S(2)}) collective-permute-start(bf16[4,1,4,8,8,128]{5,4,3,2,1,0:T(8,128)(2,1)} %get-tuple-element.47), channel_id=1, source_target_pairs={{0,16},{16,32},{32,48},{1,17},{17,33},{33,49},{2,18},{18,34},{34,5... | collective-permute-start | bytes 786440 | tf_op jit(solution)/shard_map/ppermute | solution.py:55
  34.0 9.7 %collective-permute-start.9 = (bf16[4,1,4,8,8,128]{5,4,3,2,1,0:T(8,128)(2,1)}, bf16[4,1,4,8,8,128]{5,4,3,2,1,0:T(8,128)(2,1)S(1)}, u32[]{:S(2)}, u32[]{:S(2)}) collective-permute-start(bf16[4,1,4,8,8,128]{5,4,3,2,1,0:T(8,128)(2,1)} %get-tuple-element.48), channel_id=1, source_target_pairs={{16,0},{32,16},{48,32},{17,1},{33,17},{49,33},{18,2},{34,18},{50,3... | collective-permute-start | bytes 786440 | tf_op jit(solution)/shard_map/ppermute | solution.py:56
  35.4 49.5 %copy-start.27 = (pred[16,16]{1,0:T(8,128)(4,1)}, pred[16,16]{1,0:T(8,128)(4,1)S(1)}, u32[]{:S(2)}) copy-start(pred[16,16]{1,0:T(8,128)(4,1)S(1)} %broadcast_and_fusion.3) | copy-start | bytes 772
  37.0 14.9 %collective-permute-start = (bf16[5,1,4,8,8,128]{5,4,3,2,0,1:T(8,128)(2,1)S(1)}, bf16[5,1,4,8,8,128]{5,4,3,2,0,1:T(8,128)(2,1)S(1)}, u32[]{:S(2)}, u32[]{:S(2)}) collective-permute-start(bf16[5,1,4,8,8,128]{5,4,3,2,0,1:T(8,128)(2,1)S(1)} %get-tuple-element.43), channel_id=1, source_target_pairs={{0,16},{16,32},{32,48},{1,17},{17,33},{33,49},{2,18},{18,34},{34,5... | collective-permute-start | bytes 983048 | tf_op jit(solution)/shard_map/ppermute | solution.py:55
  41.5 10.3 %collective-permute-start.1 = (bf16[5,1,4,8,8,128]{5,4,3,2,0,1:T(8,128)(2,1)S(1)}, bf16[5,1,4,8,8,128]{5,4,3,2,0,1:T(8,128)(2,1)S(1)}, u32[]{:S(2)}, u32[]{:S(2)}) collective-permute-start(bf16[5,1,4,8,8,128]{5,4,3,2,0,1:T(8,128)(2,1)S(1)} %get-tuple-element.44), channel_id=1, source_target_pairs={{16,0},{32,16},{48,32},{17,1},{33,17},{49,33},{18,2},{34,18},{50,3... | collective-permute-start | bytes 983048 | tf_op jit(solution)/shard_map/ppermute | solution.py:56
  42.9 2.1 copy-start.9
  43.7 1.2 copy-start.12
  44.9 17.7 %collective-permute-start.10 = (bf16[4,1,16,4,8,128]{5,4,3,2,1,0:T(8,128)(2,1)}, bf16[4,1,16,4,8,128]{5,4,3,2,1,0:T(8,128)(2,1)}, u32[]{:S(2)}, u32[]{:S(2)}) collective-permute-start(bf16[4,1,16,4,8,128]{5,4,3,2,1,0:T(8,128)(2,1)} %get-tuple-element.39), channel_id=1, source_target_pairs={{0,1},{1,2},{2,3},{3,4},{4,5},{5,6},{6,7},{7,8},{8,9},{9,10},{10,1... | collective-permute-start | bytes 1572872 | tf_op jit(solution)/shard_map/ppermute | solution.py:55
  49.9 18.3 %collective-permute-start.11 = (bf16[4,1,16,4,8,128]{5,4,3,2,1,0:T(8,128)(2,1)}, bf16[4,1,16,4,8,128]{5,4,3,2,1,0:T(8,128)(2,1)}, u32[]{:S(2)}, u32[]{:S(2)}) collective-permute-start(bf16[4,1,16,4,8,128]{5,4,3,2,1,0:T(8,128)(2,1)} %get-tuple-element.40), channel_id=1, source_target_pairs={{1,0},{2,1},{3,2},{4,3},{5,4},{6,5},{7,6},{8,7},{9,8},{10,9},{11,1... | collective-permute-start | bytes 1572872 | tf_op jit(solution)/shard_map/ppermute | solution.py:56
  52.1 16.1 %copy-start.10 = (bf16[4,1,4,8,8,128]{5,4,3,2,1,0:T(8,128)(2,1)S(1)}, bf16[4,1,4,8,8,128]{5,4,3,2,1,0:T(8,128)(2,1)}, u32[]{:S(2)}) copy-start(bf16[4,1,4,8,8,128]{5,4,3,2,1,0:T(8,128)(2,1)} %copy-done.9) | copy-start | bytes 786436
  53.5 20.7 %collective-permute-start.2 = (bf16[5,1,16,4,8,128]{5,4,3,2,0,1:T(8,128)(2,1)}, bf16[5,1,16,4,8,128]{5,4,3,2,0,1:T(8,128)(2,1)S(1)}, u32[]{:S(2)}, u32[]{:S(2)}) collective-permute-start(bf16[5,1,16,4,8,128]{5,4,3,2,0,1:T(8,128)(2,1)} %get-tuple-element.35), channel_id=1, source_target_pairs={{0,1},{1,2},{2,3},{3,4},{4,5},{5,6},{6,7},{7,8},{8,9},{9,10},{10,1... | collective-permute-start | bytes 1966088 | tf_op jit(solution)/shard_map/ppermute | solution.py:55
  58.6 20.8 %collective-permute-start.3 = (bf16[5,1,16,4,8,128]{5,4,3,2,0,1:T(8,128)(2,1)}, bf16[5,1,16,4,8,128]{5,4,3,2,0,1:T(8,128)(2,1)S(1)}, u32[]{:S(2)}, u32[]{:S(2)}) collective-permute-start(bf16[5,1,16,4,8,128]{5,4,3,2,0,1:T(8,128)(2,1)} %get-tuple-element.36), channel_id=1, source_target_pairs={{1,0},{2,1},{3,2},{4,3},{5,4},{6,5},{7,6},{8,7},{9,8},{10,9},{11,1... | collective-permute-start | bytes 1966088 | tf_op jit(solution)/shard_map/ppermute | solution.py:56
  60.8 48.0 %copy-start.31 = (pred[14,112]{1,0:T(8,128)(4,1)}, pred[14,112]{1,0:T(8,128)(4,1)S(1)}, u32[]{:S(2)}) copy-start(pred[14,112]{1,0:T(8,128)(4,1)S(1)} %copy.47) | copy-start | bytes 4708
  60.9 31.0 %copy-start.33 = (pred[16,128]{1,0:T(8,128)(4,1)}, pred[16,128]{1,0:T(8,128)(4,1)S(1)}, u32[]{:S(2)}) copy-start(pred[16,128]{1,0:T(8,128)(4,1)S(1)} %copy.43) | copy-start | bytes 6148
  79.4 7.9 %copy-start.2 = (bf16[5,1,16,4,8,128]{5,4,3,2,0,1:T(8,128)(2,1)}, bf16[5,1,16,4,8,128]{5,4,3,2,0,1:T(8,128)(2,1)S(1)}, u32[]{:S(2)}) copy-start(bf16[5,1,16,4,8,128]{5,4,3,2,0,1:T(8,128)(2,1)S(1)} %collective-permute-done.3) | copy-start | bytes 1966084
  88.9 5.6 %copy-start.19 = (bf16[8,14,128,128]{3,2,1,0:T(8,128)(2,1)S(1)}, bf16[8,14,128,128]{3,2,1,0:T(8,128)(2,1)}, u32[]{:S(2)}) copy-start(bf16[8,14,128,128]{3,2,1,0:T(8,128)(2,1)} %all-gather.2.cloned.1.call-done) | copy-start | bytes 11010052
  104.5 1.7 copy-start.7
  111.4 6.4 %copy-start.3 = (bf16[5,1,16,4,8,128]{5,4,3,2,0,1:T(8,128)(2,1)S(1)}, bf16[5,1,16,4,8,128]{5,4,3,2,0,1:T(8,128)(2,1)}, u32[]{:S(2)}) copy-start(bf16[5,1,16,4,8,128]{5,4,3,2,0,1:T(8,128)(2,1)} %copy-done.2) | copy-start | bytes 1966084
  115.4 3.2 %copy-start.15 = (bf16[1152,128]{1,0:T(8,128)(2,1)S(1)}, bf16[1152,128]{1,0:T(8,128)(2,1)}, u32[]{:S(2)}) copy-start(bf16[1152,128]{1,0:T(8,128)(2,1)} %shard_map.65) | copy-start | bytes 884740
  117.1 1.5 copy-start.24
  117.8 1.2 copy-start.4
  118.6 2.0 copy-start.29
  120.6 5.9 %copy-start.8 = (f32[1,1,10,10,8,128]{5,4,3,2,1,0:T(8,128)S(1)}, f32[1,1,10,10,8,128]{5,4,3,2,1,0:T(8,128)}, u32[]{:S(2)}) copy-start(f32[1,1,10,10,8,128]{5,4,3,2,1,0:T(8,128)} %convert_multiply_fusion.6) | copy-start | bytes 1228804
  123.1 9.6 %copy-start.22 = (pred[10,10]{1,0:T(8,128)(4,1)S(1)}, pred[10,10]{1,0:T(8,128)(4,1)}, u32[]{:S(2)}) copy-start(pred[10,10]{1,0:T(8,128)(4,1)} %copy-done.21) | copy-start | bytes 304
  126.5 6.2 %copy-start.17 = (bf16[800,128]{1,0:T(8,128)(2,1)S(1)}, bf16[800,128]{1,0:T(8,128)(2,1)}, u32[]{:S(2)}) copy-start(bf16[800,128]{1,0:T(8,128)(2,1)} %shard_map.66) | copy-start | bytes 614404
  126.5 7.5 %copy-start.30 = (pred[10,80]{1,0:T(8,128)(4,1)S(1)}, pred[10,80]{1,0:T(8,128)(4,1)}, u32[]{:S(2)}) copy-start(pred[10,80]{1,0:T(8,128)(4,1)} %copy.51) | copy-start | bytes 2404
  134.0 11.4 %copy-start.11 = (bf16[4,1,4,8,8,128]{5,4,3,2,1,0:T(8,128)(2,1)S(1)}, bf16[4,1,4,8,8,128]{5,4,3,2,1,0:T(8,128)(2,1)}, u32[]{:S(2)}) copy-start(bf16[4,1,4,8,8,128]{5,4,3,2,1,0:T(8,128)(2,1)} %copy-done.9) | copy-start | bytes 786436
  134.0 11.4 %copy-start.13 = (bf16[4,1,4,8,8,128]{5,4,3,2,1,0:T(8,128)(2,1)S(1)}, bf16[4,1,4,8,8,128]{5,4,3,2,1,0:T(8,128)(2,1)}, u32[]{:S(2)}) copy-start(bf16[4,1,4,8,8,128]{5,4,3,2,1,0:T(8,128)(2,1)} %copy-done.12) | copy-start | bytes 786436
  140.2 7.6 %collective-permute-start.4 = (bf16[1,4,8,8,128]{4,3,2,1,0:T(8,128)(2,1)S(1)}, bf16[1,4,8,8,128]{4,3,2,1,0:T(8,128)(2,1)S(1)}, u32[]{:S(2)}, u32[]{:S(2)}) collective-permute-start(bf16[1,4,8,8,128]{4,3,2,1,0:T(8,128)(2,1)S(1)} %get-tuple-element.67), channel_id=1, source_target_pairs={{0,16},{16,32},{32,48},{1,17},{17,33},{33,49},{2,18},{18,34},{34,5... | collective-permute-start | bytes 196616 | tf_op jit(solution)/shard_map/ppermute | solution.py:55
  143.9 3.2 %copy-start.14 = (bf16[512,128]{1,0:T(8,128)(2,1)S(1)}, bf16[512,128]{1,0:T(8,128)(2,1)}, u32[]{:S(2)}) copy-start(bf16[512,128]{1,0:T(8,128)(2,1)} %shard_map.67) | copy-start | bytes 393220
  143.9 6.3 %collective-permute-start.5 = (bf16[1,4,8,8,128]{4,3,2,1,0:T(8,128)(2,1)S(1)}, bf16[1,4,8,8,128]{4,3,2,1,0:T(8,128)(2,1)S(1)}, u32[]{:S(2)}, u32[]{:S(2)}) collective-permute-start(bf16[1,4,8,8,128]{4,3,2,1,0:T(8,128)(2,1)S(1)} %get-tuple-element.68), channel_id=1, source_target_pairs={{16,0},{32,16},{48,32},{17,1},{33,17},{49,33},{18,2},{34,18},{50,3... | collective-permute-start | bytes 196616 | tf_op jit(solution)/shard_map/ppermute | solution.py:56
  151.0 7.1 %collective-permute-start.6 = (bf16[1,16,4,8,128]{4,3,2,1,0:T(8,128)(2,1)S(1)}, bf16[1,16,4,8,128]{4,3,2,1,0:T(8,128)(2,1)S(1)}, u32[]{:S(2)}, u32[]{:S(2)}) collective-permute-start(bf16[1,16,4,8,128]{4,3,2,1,0:T(8,128)(2,1)S(1)} %get-tuple-element.61), channel_id=1, source_target_pairs={{0,1},{1,2},{2,3},{3,4},{4,5},{5,6},{6,7},{7,8},{8,9},{9,10},{10,1... | collective-permute-start | bytes 393224 | tf_op jit(solution)/shard_map/ppermute | solution.py:55
  153.8 9.7 %copy-start.28 = (pred[16,16]{1,0:T(8,128)(4,1)S(1)}, pred[16,16]{1,0:T(8,128)(4,1)}, u32[]{:S(2)}) copy-start(pred[16,16]{1,0:T(8,128)(4,1)} %copy-done.27) | copy-start | bytes 772
  153.8 8.1 %collective-permute-start.7 = (bf16[1,16,4,8,128]{4,3,2,1,0:T(8,128)(2,1)S(1)}, bf16[1,16,4,8,128]{4,3,2,1,0:T(8,128)(2,1)S(1)}, u32[]{:S(2)}, u32[]{:S(2)}) collective-permute-start(bf16[1,16,4,8,128]{4,3,2,1,0:T(8,128)(2,1)S(1)} %get-tuple-element.62), channel_id=1, source_target_pairs={{1,0},{2,1},{3,2},{4,3},{5,4},{6,5},{7,6},{8,7},{9,8},{10,9},{11,1... | collective-permute-start | bytes 393224 | tf_op jit(solution)/shard_map/ppermute | solution.py:56
  163.5 4.1 %copy-start.5 = (bf16[4,1,16,16,8,128]{5,4,3,2,1,0:T(8,128)(2,1)S(1)}, bf16[4,1,16,16,8,128]{5,4,3,2,1,0:T(8,128)(2,1)}, u32[]{:S(2)}) copy-start(bf16[4,1,16,16,8,128]{5,4,3,2,1,0:T(8,128)(2,1)} %pad_maximum_fusion.1) | copy-start | bytes 6291460
  163.5 4.1 %copy-start.20 = (bf16[16,8,8,128]{3,2,1,0:T(8,128)(2,1)S(1)}, bf16[16,8,8,128]{3,2,1,0:T(8,128)(2,1)}, u32[]{:S(2)}) copy-start(bf16[16,8,8,128]{3,2,1,0:T(8,128)(2,1)} %get-tuple-element.59) | copy-start | bytes 786436
  163.5 4.1 %copy-start.34 = (pred[16,128]{1,0:T(8,128)(4,1)S(1)}, pred[16,128]{1,0:T(8,128)(4,1)}, u32[]{:S(2)}) copy-start(pred[16,128]{1,0:T(8,128)(4,1)} %copy-done.33) | copy-start | bytes 6148
  176.2 1.7 copy-start.6
  176.2 1.7 copy-start.26
  177.7 2.2 copy-start.32
  186.4 4.0 %copy-start.16 = (bf16[1152,128]{1,0:T(8,128)(2,1)S(1)}, bf16[1152,128]{1,0:T(8,128)(2,1)}, u32[]{:S(2)}) copy-start(bf16[1152,128]{1,0:T(8,128)(2,1)} %shard_map.69) | copy-start | bytes 884740
  196.5 2.8 %copy-start.18 = (bf16[800,128]{1,0:T(8,128)(2,1)S(1)}, bf16[800,128]{1,0:T(8,128)(2,1)}, u32[]{:S(2)}) copy-start(bf16[800,128]{1,0:T(8,128)(2,1)} %shard_map.70) | copy-start | bytes 614404
  206.3 22.2 %copy-start.1 = (bf16[8,8,8,8,128]{4,3,2,1,0:T(8,128)(2,1)S(1)}, bf16[8,8,8,8,128]{4,3,2,1,0:T(8,128)(2,1)}, u32[]{:S(2)}) copy-start(bf16[8,8,8,8,128]{4,3,2,1,0:T(8,128)(2,1)} %param.6) | copy-start | bytes 3145732
  (1 other events, 0.6 us)
Sparse Core Ops, SparseCore 0:
  9.5 40.9 all-gather.1
where the time goes:
time: 237 us; the launch traced here: 235 us
  other arithmetic  58.2 us (25%)
  starting transfers between devices  40.3 us (17%)
  waiting for transfers between devices  38.1 us (16%)
  Pallas kernels  30 us (13%)
  local copies, waits for them, and re-layouts  29.4 us (12%)
  between operations  19.8 us (8%)
  blocking collectives  19.6 us (8%)
    pallas_call x8, Pallas kernels, conv_call(): pl.pallas_call(functools.partial(conv_kernel, m, n, cols), out_shape=jax....  30 us
    ppermute x6, starting transfers between devices, extend(): lax.ppermute(lax.slice_in_dim(block, size - width, size, axis=dim), axis,...  24.7 us
    convert_element_type x16, other arithmetic, denoise(): flat = lambda x: x.astype(jnp.float32).reshape(m, n * num_cols, channels)  23.4 us
    all_to_all x1, blocking collectives, on_device(): return lax.all_to_all(stacked, 'section', 0, 1, tiled=True)  19.6 us
    ppermute x6, waiting for transfers between devices, extend(): lax.ppermute(lax.slice_in_dim(block, 0, width, axis=dim), axis, backward)  17.8 us
    all_to_all x1, waiting for transfers between devices, on_device(): noise_t = lax.all_to_all(section_noise[0], 'section', 0, 0, tiled=True)  15.2 us
    ppermute x6, starting transfers between devices, extend(): lax.ppermute(lax.slice_in_dim(block, 0, width, axis=dim), axis, backward)  11.3 us
    broadcast_in_dim x8, local copies, waits for them, and re-layouts, denoise(): level_row = jnp.full((8, channels), noise_scale, jnp.float32)  9.73 us
  transfers between devices with their start and end apart: 14, of which 8 were waited for; matrix products, arithmetic and copies ran while one was open for 6% of the time, Pallas kernels for 0%

commit v1 on v0

--- a/solution.py
+++ b/solution.py
@@ -5,14 +5,27 @@
 from jax.experimental import pallas as pl
 from jax.experimental.pallas import tpu as pltpu
 from jax.sharding import PartitionSpec as P
-from jax.experimental import pallas as pl
-from jax.experimental.pallas import tpu as pltpu
+
+HALO = 4
 
 
-def conv_kernel(m, n, cols, xl_ref, xc_ref, xr_ref, noisy_ref, w_ref, lv_ref, out_ref):
+def section_kernel(m, n, cols, prior_ref, noise_ref, mask_ref, w_ref, out_ref, xl, xc, xr, nz):
     channels = w_ref.shape[-1]
+    rows_in = m * n * cols
     rows_out = (m - 2) * (n - 2) * cols
-    views = (xl_ref, xc_ref, xr_ref)
+    level = w_ref[13][0:1, :].astype(jnp.float32)
+    noisy = prior_ref[...].astype(jnp.float32) + level * noise_ref[...].astype(jnp.float32)
+    mean_sq = jnp.mean(noisy * noisy, axis=-1, keepdims=True)
+    normalized = (noisy * lax.rsqrt(mean_sq + 1e-05)).astype(jnp.bfloat16).astype(jnp.float32)
+    normalized = jnp.where(mask_ref[...] > 0, normalized, 0.0)
+    col = lax.broadcasted_iota(jnp.int32, (rows_in, channels), 0) % cols
+    left = jnp.where(col == 0, 0.0, pltpu.roll(normalized, 1, 0))
+    right = jnp.where(col == cols - 1, 0.0, pltpu.roll(normalized, rows_in - 1, 0))
+    xl[...] = left.reshape(m, n * cols, channels)
+    xc[...] = normalized.reshape(m, n * cols, channels)
+    xr[...] = right.reshape(m, n * cols, channels)
+    nz[...] = noisy.reshape(m, n * cols, channels)
+    views = (xl, xc, xr)
     acc = jnp.zeros((rows_out, channels), jnp.float32)
     for tap in range(9):
         a, b = tap // 3, tap % 3
@@ -20,30 +33,33 @@
         v = v.reshape(rows_out, channels).astype(jnp.bfloat16)
         acc = acc + jnp.dot(v, w_ref[tap], preferred_element_type=jnp.float32)
     for t in range(3):
-        v = xc_ref[pl.ds(t, m - 2), pl.ds(cols, (n - 2) * cols), :]
+        v = xc[pl.ds(t, m - 2), pl.ds(cols, (n - 2) * cols), :]
         v = v.reshape(rows_out, channels).astype(jnp.bfloat16)
         acc = acc + jnp.dot(v, w_ref[9 + t], preferred_element_type=jnp.float32)
     act = (acc / (1.0 + jnp.exp(-acc))).astype(jnp.bfloat16)
     est = jnp.dot(act, w_ref[12], preferred_element_type=jnp.float32)
-    noisy = noisy_ref[pl.ds(1, m - 2), pl.ds(cols, (n - 2) * cols), :].reshape(rows_out, channels)
-    level = lv_ref[0:1, :]
-    out_ref[...] = (noisy - level * est).astype(out_ref.dtype)
+    inner = nz[pl.ds(1, m - 2), pl.ds(cols, (n - 2) * cols), :].reshape(rows_out, channels)
+    out_ref[...] = (inner - level * est).astype(out_ref.dtype)
 
 
-def conv_call(xl, xc, xr, noisy, weights, level_row, m, n, cols):
+def section_call(prior, noise, mask, weights, m, n, cols):
     channels = weights.shape[-1]
+    rows_in = m * n * cols
     rows_out = (m - 2) * (n - 2) * cols
     flops = 2 * rows_out * channels * channels * 13
-    nbytes = 4 * 4 * m * n * cols * channels + 2 * 13 * channels * channels + 2 * rows_out * channels
+    nbytes = 2 * 2 * rows_in * channels + 4 * rows_in * channels + 2 * 14 * channels * channels
+    scratch = pltpu.VMEM((m, n * cols, channels), jnp.float32)
     return pl.pallas_call(
-        functools.partial(conv_kernel, m, n, cols),
+        functools.partial(section_kernel, m, n, cols),
         out_shape=jax.ShapeDtypeStruct((rows_out, channels), jnp.bfloat16),
-        in_specs=[pl.BlockSpec(memory_space=pltpu.VMEM)] * 6,
+        in_specs=[pl.BlockSpec(memory_space=pltpu.VMEM)] * 4,
         out_specs=pl.BlockSpec(memory_space=pltpu.VMEM),
-        cost_estimate=pl.CostEstimate(flops=flops, bytes_accessed=nbytes, transcendentals=rows_out * channels),
-    )(xl, xc, xr, noisy, weights, level_row)
-
-HALO = 4
+        scratch_shapes=[scratch] * 4,
+        cost_estimate=pl.CostEstimate(
+            flops=flops, bytes_accessed=nbytes + 2 * rows_out * channels,
+            transcendentals=rows_out * channels,
+        ),
+    )(prior, noise, mask, weights)
 
 
 def extend(block, width, frame_dim, row_dim):
@@ -70,25 +86,15 @@
     return (frame_ok[:, None] & row_ok[None, :])[None, :, :, None, None]
 
 
-def denoise(previous, noise_part, noise_scale, weights, mask):
-    noisy = previous.astype(jnp.float32) + noise_scale * noise_part.astype(jnp.float32)
-    normalized = (
-        noisy * lax.rsqrt(jnp.mean(noisy * noisy, axis=-1, keepdims=True) + 1e-05)
-    ).astype(jnp.bfloat16)
-    normalized = jnp.where(mask, normalized, jnp.zeros_like(normalized))
+def denoise(previous, noise_part, weights, mask):
     num_videos, m, n, num_cols, channels = previous.shape
-    padded = jnp.pad(normalized, ((0, 0), (0, 0), (0, 0), (1, 1), (0, 0)))
-    flat = lambda x: x.astype(jnp.float32).reshape(m, n * num_cols, channels)
-    level_row = jnp.full((8, channels), noise_scale, jnp.float32)
     outs = []
     for v in range(num_videos):
-        out = conv_call(
-            flat(padded[v, :, :, 0:num_cols]),
-            flat(normalized[v]),
-            flat(padded[v, :, :, 2 : num_cols + 2]),
-            noisy[v].reshape(m, n * num_cols, channels),
+        out = section_call(
+            previous[v].reshape(-1, channels),
+            noise_part[v].reshape(-1, channels),
+            mask,
             weights,
-            level_row,
             m,
             n,
             num_cols,
@@ -122,7 +128,16 @@
     for start in range(halo, sections, halo):
         noise_parts.append(extend(noise_t[start : start + halo], halo, 2, 3))
     noise_ext = jnp.concatenate(noise_parts, axis=0)
-    masks = [inside_mask(num_frames, num_rows, w) for w in range(halo + 1)]
+    num_cols, channels = base_frames.shape[3:]
+    masks = [
+        jnp.broadcast_to(
+            inside_mask(num_frames, num_rows, w)[0],
+            (num_frames + 2 * w, num_rows + 2 * w, num_cols, channels),
+        )
+        .astype(jnp.float32)
+        .reshape(-1, channels)
+        for w in range(halo + 1)
+    ]
     results = []
     for k in range(sections):
         j = k % halo
@@ -136,8 +151,7 @@
         prior_ext = denoise(
             prior_ext,
             noise_here,
-            packed[k, 13, 0, 0].astype(jnp.float32),
-            packed[k, 0:13],
+            packed[k],
             masks[width],
         )
         inner = width - 1

time: 237 us -> 175 us (0.74)
  the two profiles are of different devices: /device:TPU:96 before, /device:TPU:408 now
where the time goes in v1:
time: 175 us; the launch traced here: 174 us
  starting transfers between devices  37.5 us (21%)
  local copies, waits for them, and re-layouts  30.9 us (18%)
  Pallas kernels  28.4 us (16%)
  waiting for transfers between devices  26.9 us (15%)
  blocking collectives  18.5 us (11%)
  other arithmetic  17.5 us (10%)
  between operations  14.5 us (8%)
    pallas_call x8, Pallas kernels, section_call(): pl.pallas_call(functools.partial(section_kernel, m, n, cols), out_shape=j...  28.4 us
    ppermute x6, starting transfers between devices, extend(): lax.ppermute(lax.slice_in_dim(block, 0, width, axis=dim), axis, backward)  23.3 us
    all_to_all x1, blocking collectives, on_device(): return lax.all_to_all(stacked, 'section', 0, 1, tiled=True)  18.5 us
    all_to_all x1, waiting for transfers between devices, on_device(): noise_t = lax.all_to_all(section_noise[0], 'section', 0, 0, tiled=True)  15.1 us
    broadcast_in_dim x12, local copies, waits for them, and re-layouts, on_device(): jnp.broadcast_to(inside_mask(num_frames, num_rows, w)[0], (num_frames + 2...  13.9 us
    ppermute x6, waiting for transfers between devices, extend(): lax.ppermute(lax.slice_in_dim(block, size - width, size, axis=dim), axis,...  11.8 us
    ppermute x6, starting transfers between devices, extend(): lax.ppermute(lax.slice_in_dim(block, size - width, size, axis=dim), axis,...  9.82 us
    slice x6, other arithmetic, on_device(): noise_ext[k, :, cut:cut + num_frames + 2 * width, cut:cut + num_rows + 2...  7.26 us
  transfers between devices with their start and end apart: 14, of which 6 were waited for; matrix products, arithmetic and copies ran while one was open for 17% of the time, Pallas kernels for 0%

profile of v1, /device:TPU:408, one launch (start us, length us, event | category | flops | bytes accessed | tf_op | source)
XLA Modules:
  0.0 174.2 jit_solution(5180237336276576693)
XLA Ops:
  7.4 1.9 %maximum_maximum_fusion = bf16[1,14,128,128]{3,2,1,0:T(8,128)(2,1)} fusion(bf16[1,1,128,128]{3,2,1,0:T(8,128)(2,1)} %bitcast.92, bf16[1,3,128,128]{3,2,1,0:T(8,128)(2,1)} %param.10, bf16[1,9,128,128]{3,2,1,0:T(8,128)(2,1)} %param.9, bf16[14]{0:T(256)(128)(2,1)S(1)} %pad.19.clone), kind=kLoop, calls=%fused_computation.17 | loop fusion | flops 688128 | bytes 884764 | tf_op jit(solution)/shard_map/concatenate | solution.py:120
  9.3 4.3 %all-to-all-start = ((bf16[8,8,8,8,128]{4,3,2,1,0:T(8,128)(2,1)}), bf16[8,8,8,8,128]{4,3,2,1,0:T(8,128)(2,1)S(1)}, u32[]{:S(2)}, u32[]{:S(2)}) async-start(bf16[8,8,8,8,128]{4,3,2,1,0:T(8,128)(2,1)} %bitcast.88), calls=%async_computation | async-start | bytes 2097152 | tf_op jit(solution)/shard_map/all_to_all | solution.py:114
  14.5 15.1 %all-to-all-done = bf16[8,8,8,8,128]{4,3,2,1,0:T(8,128)(2,1)S(1)} async-done(((bf16[8,8,8,8,128]{4,3,2,1,0:T(8,128)(2,1)}), bf16[8,8,8,8,128]{4,3,2,1,0:T(8,128)(2,1)S(1)}, u32[]{:S(2)}, u32[]{:S(2)}) %all-to-all-start) | async-done | bytes 1048608 | tf_op jit(solution)/shard_map/all_to_all | solution.py:114
  29.7 2.7 %collective-permute-start.9 = (bf16[4,1,4,8,8,128]{5,4,3,2,0,1:T(8,128)(2,1)S(1)}, bf16[4,1,4,8,8,128]{5,4,3,2,0,1:T(8,128)(2,1)S(1)}, u32[]{:S(2)}, u32[]{:S(2)}) collective-permute-start(bf16[4,1,4,8,8,128]{5,4,3,2,0,1:T(8,128)(2,1)S(1)} %get-tuple-element.24), channel_id=1, source_target_pairs={{16,0},{32,16},{48,32},{17,1},{33,17},{49,33},{18,2},{34,18},{50,3... | collective-permute-start | bytes 786440 | tf_op jit(solution)/shard_map/ppermute | solution.py:72
  32.4 1.3 collective-permute-start.8
  34.3 4.6 %collective-permute-start.1 = (bf16[5,1,4,8,8,128]{5,4,3,2,0,1:T(8,128)(2,1)S(1)}, bf16[5,1,4,8,8,128]{5,4,3,2,0,1:T(8,128)(2,1)S(1)}, u32[]{:S(2)}, u32[]{:S(2)}) collective-permute-start(bf16[5,1,4,8,8,128]{5,4,3,2,0,1:T(8,128)(2,1)S(1)} %get-tuple-element.22), channel_id=1, source_target_pairs={{16,0},{32,16},{48,32},{17,1},{33,17},{49,33},{18,2},{34,18},{50,3... | collective-permute-start | bytes 983048 | tf_op jit(solution)/shard_map/ppermute | solution.py:72
  38.9 1.3 collective-permute-start
  40.2 1.6 collective-permute-done.8
  42.0 1.1 fusion.9
  43.1 4.1 %collective-permute-start.11 = (bf16[4,1,16,4,8,128]{5,4,3,2,0,1:T(8,128)(2,1)}, bf16[4,1,16,4,8,128]{5,4,3,2,0,1:T(8,128)(2,1)}, u32[]{:S(2)}, u32[]{:S(2)}) collective-permute-start(bf16[4,1,16,4,8,128]{5,4,3,2,0,1:T(8,128)(2,1)} %get-tuple-element.18), channel_id=1, source_target_pairs={{1,0},{2,1},{3,2},{4,3},{5,4},{6,5},{7,6},{8,7},{9,8},{10,9},{11,1... | collective-permute-start | bytes 1572872 | tf_op jit(solution)/shard_map/ppermute | solution.py:72
  47.2 1.9 %collective-permute-start.10 = (bf16[4,1,16,4,8,128]{5,4,3,2,0,1:T(8,128)(2,1)}, bf16[4,1,16,4,8,128]{5,4,3,2,0,1:T(8,128)(2,1)}, u32[]{:S(2)}, u32[]{:S(2)}) collective-permute-start(bf16[4,1,16,4,8,128]{5,4,3,2,0,1:T(8,128)(2,1)} %get-tuple-element.17), channel_id=1, source_target_pairs={{0,1},{1,2},{2,3},{3,4},{4,5},{5,6},{6,7},{7,8},{8,9},{9,10},{10,1... | collective-permute-start | bytes 1572872 | tf_op jit(solution)/shard_map/ppermute | solution.py:71
  49.4 1.4 fusion.8
  50.8 5.1 %collective-permute-start.3 = (bf16[5,1,16,4,8,128]{5,4,3,2,0,1:T(8,128)(2,1)}, bf16[5,1,16,4,8,128]{5,4,3,2,0,1:T(8,128)(2,1)S(1)}, u32[]{:S(2)}, u32[]{:S(2)}) collective-permute-start(bf16[5,1,16,4,8,128]{5,4,3,2,0,1:T(8,128)(2,1)} %get-tuple-element.16), channel_id=1, source_target_pairs={{1,0},{2,1},{3,2},{4,3},{5,4},{6,5},{7,6},{8,7},{9,8},{10,9},{11,1... | collective-permute-start | bytes 1966088 | tf_op jit(solution)/shard_map/ppermute | solution.py:72
  55.9 1.9 %collective-permute-start.2 = (bf16[5,1,16,4,8,128]{5,4,3,2,0,1:T(8,128)(2,1)}, bf16[5,1,16,4,8,128]{5,4,3,2,0,1:T(8,128)(2,1)S(1)}, u32[]{:S(2)}, u32[]{:S(2)}) collective-permute-start(bf16[5,1,16,4,8,128]{5,4,3,2,0,1:T(8,128)(2,1)} %get-tuple-element.15), channel_id=1, source_target_pairs={{0,1},{1,2},{2,3},{3,4},{4,5},{5,6},{6,7},{7,8},{8,9},{9,10},{10,1... | collective-permute-start | bytes 1966088 | tf_op jit(solution)/shard_map/ppermute | solution.py:71
  59.3 1.0 broadcast_in_dim.59
  60.3 1.4 broadcast_in_dim.64
  61.7 1.6 broadcast_in_dim.65
  64.1 1.0 broadcast_in_dim.68
  65.0 1.4 broadcast_in_dim.70
  66.5 1.6 broadcast_in_dim.71
  68.0 1.7 pad_maximum_fusion.1
  70.5 1.5 pad_maximum_fusion.11
  72.0 1.7 pad_maximum_fusion.8
  73.7 1.8 %pad_maximum_fusion.5 = bf16[1,1,14,14,8,128]{5,4,3,2,0,1:T(8,128)(2,1)} fusion(bf16[4,1,16,4,8,128]{5,4,3,2,0,1:T(8,128)(2,1)} %collective-permute-done.11, bf16[4,1,16,4,8,128]{5,4,3,2,0,1:T(8,128)(2,1)} %collective-permute-done.10, bf16[4,1,4,8,8,128]{5,4,3,2,0,1:T(8,128)(2,1)S(1)} %copy-done.6, bf16[4,1,8,8,8,128]{5,4,3,2,0,1:T(8,128)(2,1)S(1)} %get-tuple-element.19, ...), kind=kLoop, calls=%fused_computation.18 | loop fusion | flops 802816 | bytes 2498560 | tf_op jit(solution)/shard_map/slice | solution.py:148
  75.4 1.2 collective-permute-done.2
  79.0 2.5 %pad_maximum_fusion = bf16[5,1,16,16,8,128]{5,4,3,2,0,1:T(8,128)(2,1)S(1)} fusion(bf16[5,1,16,4,8,128]{5,4,3,2,0,1:T(8,128)(2,1)S(1)} %collective-permute-done.3, bf16[5,1,4,8,8,128]{5,4,3,2,0,1:T(8,128)(2,1)S(1)} %copy-done.2, bf16[4,1,8,8,8,128]{5,4,3,2,0,1:T(8,128)(2,1)S(1)} %get-tuple-element.20, ...), kind=kLoop, calls=%fused_computation | loop fusion | flops 6553600 | bytes 5242880 | tf_op jit(solution)/shard_map/concatenate | solution.py:73
  81.5 1.1 fusion.7
  82.6 3.9 %slice_bitcast_fusion.2 = (bf16[14,128,128]{2,1,0:T(8,128)(2,1)}, bf16[14,128,128]{2,1,0:T(8,128)(2,1)}, bf16[14,128,128]{2,1,0:T(8,128)(2,1)}, bf16[14,128,128]...) fusion(bf16[8,14,128,128]{3,2,1,0:T(8,128)(2,1)} %all-gather.2., ...), kind=kLoop, calls=%fused_computation.9 | loop fusion | bytes 7340032 | tf_op jit(solution)/shard_map/squeeze | solution.py:154
  86.5 1.3 broadcast_in_dim.60.mask_ref
  87.8 4.4 %shard_map.64.prior_ref = bf16[1568,128]{1,0:T(8,128)(2,1)} custom-call(bf16[2048,128]{1,0:T(8,128)(2,1)} %bitcast.79, bf16[2048,128]{1,0:T(8,128)(2,1)} %bitcast.78, f32[2048,128]{1,0:T(8,128)} %broadcast_in_dim.60.mask_ref, bf16[14,128,128]{2,1,0:T(8,128)(2,1)} %get-tuple-element.12.w_ref), custom_call_target="tpu_custom_call" | custom-call | flops 667942912 | bytes 2957312 | tf_op jit(solution)/shard_map/pallas_call | solution.py:52
  93.1 1.2 broadcast_in_dim.66.mask_ref
  94.3 3.8 %shard_map.65.prior_ref = bf16[1152,128]{1,0:T(8,128)(2,1)} custom-call(bf16[1568,128]{1,0:T(8,128)(2,1)} %shard_map.64.prior_ref, bf16[1568,128]{1,0:T(8,128)(2,1)} %bitcast.83, f32[1568,128]{1,0:T(8,128)} %broadcast_in_dim.66.mask_ref, bf16[14,128,128]{2,1,0:T(8,128)(2,1)} %get-tuple-element.11.w_ref), custom_call_target="tpu_custom_call" | custom-call | flops 490733568 | bytes 2359296 | tf_op jit(solution)/shard_map/pallas_call | solution.py:52
  98.0 1.0 broadcast_in_dim.69.mask_ref
  99.1 3.2 %shard_map.66.prior_ref = bf16[800,128]{1,0:T(8,128)(2,1)} custom-call(bf16[1152,128]{1,0:T(8,128)(2,1)} %shard_map.65.prior_ref, bf16[1152,128]{1,0:T(8,128)(2,1)} %bitcast.87, f32[1152,128]{1,0:T(8,128)} %broadcast_in_dim.69.mask_ref, bf16[14,128,128]{2,1,0:T(8,128)(2,1)} %get-tuple-element.10.w_ref), custom_call_target="tpu_custom_call" | custom-call | flops 340787200 | bytes 1843200 | tf_op jit(solution)/shard_map/pallas_call | solution.py:52
  103.2 2.8 %shard_map.67 = bf16[512,128]{1,0:T(8,128)(2,1)} custom-call(bf16[800,128]{1,0:T(8,128)(2,1)} %shard_map.66.prior_ref, bf16[800,128]{1,0:T(8,128)(2,1)} %bitcast.90, f32[800,128]{1,0:T(8,128)} %broadcast_in_dim.72.mask_ref, bf16[14,128,128]{2,1,0:T(8,128)(2,1)} %get-tuple-element.9.w_ref), custom_call_target="tpu_custom_call" | custom-call | flops 218103808 | bytes 1409024 | tf_op jit(solution)/shard_map/pallas_call | solution.py:52
  107.0 3.0 %collective-permute-start.5 = (bf16[1,4,8,8,128]{4,3,2,1,0:T(8,128)(2,1)S(1)}, bf16[1,4,8,8,128]{4,3,2,1,0:T(8,128)(2,1)S(1)}, u32[]{:S(2)}, u32[]{:S(2)}) collective-permute-start(bf16[1,4,8,8,128]{4,3,2,1,0:T(8,128)(2,1)S(1)} %get-tuple-element.28), channel_id=1, source_target_pairs={{16,0},{32,16},{48,32},{17,1},{33,17},{49,33},{18,2},{34,18},{50,3... | collective-permute-start | bytes 196616 | tf_op jit(solution)/shard_map/ppermute | solution.py:72
  109.9 1.3 collective-permute-start.4
  112.2 3.9 %collective-permute-done.4 = bf16[1,4,8,8,128]{4,3,2,1,0:T(8,128)(2,1)S(1)} collective-permute-done((bf16[1,4,8,8,128]{4,3,2,1,0:T(8,128)(2,1)S(1)}, bf16[1,4,8,8,128]{4,3,2,1,0:T(8,128)(2,1)S(1)}, u32[]{:S(2)}, u32[]{:S(2)}) %collective-permute-start.4) | collective-permute-done | bytes 65568 | tf_op jit(solution)/shard_map/ppermute | solution.py:71
  116.1 0.9 pad_maximum_fusion.10
  117.1 3.9 %collective-permute-start.7 = (bf16[1,16,4,8,128]{4,3,2,1,0:T(8,128)(2,1)S(1)}, bf16[1,16,4,8,128]{4,3,2,1,0:T(8,128)(2,1)S(1)}, u32[]{:S(2)}, u32[]{:S(2)}) collective-permute-start(bf16[1,16,4,8,128]{4,3,2,1,0:T(8,128)(2,1)S(1)} %get-tuple-element.26), channel_id=1, source_target_pairs={{1,0},{2,1},{3,2},{4,3},{5,4},{6,5},{7,6},{8,7},{9,8},{10,9},{11,1... | collective-permute-start | bytes 393224 | tf_op jit(solution)/shard_map/ppermute | solution.py:72
  121.0 2.1 %collective-permute-start.6 = (bf16[1,16,4,8,128]{4,3,2,1,0:T(8,128)(2,1)S(1)}, bf16[1,16,4,8,128]{4,3,2,1,0:T(8,128)(2,1)S(1)}, u32[]{:S(2)}, u32[]{:S(2)}) collective-permute-start(bf16[1,16,4,8,128]{4,3,2,1,0:T(8,128)(2,1)S(1)} %get-tuple-element.25), channel_id=1, source_target_pairs={{0,1},{1,2},{2,3},{3,4},{4,5},{5,6},{6,7},{7,8},{8,9},{9,10},{10,1... | collective-permute-start | bytes 393224 | tf_op jit(solution)/shard_map/ppermute | solution.py:71
  124.1 5.0 %collective-permute-done.6 = bf16[1,16,4,8,128]{4,3,2,1,0:T(8,128)(2,1)S(1)} collective-permute-done((bf16[1,16,4,8,128]{4,3,2,1,0:T(8,128)(2,1)S(1)}, bf16[1,16,4,8,128]{4,3,2,1,0:T(8,128)(2,1)S(1)}, u32[]{:S(2)}, u32[]{:S(2)}) %collective-permute-start.6) | collective-permute-done | bytes 131104 | tf_op jit(solution)/shard_map/ppermute | solution.py:71
  130.0 4.4 %shard_map.68.prior_ref = bf16[1568,128]{1,0:T(8,128)(2,1)} custom-call(bf16[2048,128]{1,0:T(8,128)(2,1)} %bitcast.77, bf16[2048,128]{1,0:T(8,128)(2,1)} %bitcast.76, f32[2048,128]{1,0:T(8,128)} %broadcast_in_dim.60.mask_ref, bf16[14,128,128]{2,1,0:T(8,128)(2,1)} %get-tuple-element.8.w_ref), custom_call_target="tpu_custom_call" | custom-call | flops 667942912 | bytes 2957312 | tf_op jit(solution)/shard_map/pallas_call | solution.py:52
  135.3 3.7 %shard_map.69.prior_ref = bf16[1152,128]{1,0:T(8,128)(2,1)} custom-call(bf16[1568,128]{1,0:T(8,128)(2,1)} %shard_map.68.prior_ref, bf16[1568,128]{1,0:T(8,128)(2,1)} %bitcast.82, f32[1568,128]{1,0:T(8,128)} %broadcast_in_dim.66.mask_ref, bf16[14,128,128]{2,1,0:T(8,128)(2,1)} %get-tuple-element.7.w_ref), custom_call_target="tpu_custom_call" | custom-call | flops 490733568 | bytes 2359296 | tf_op jit(solution)/shard_map/pallas_call | solution.py:52
  140.0 3.2 %shard_map.70.prior_ref = bf16[800,128]{1,0:T(8,128)(2,1)} custom-call(bf16[1152,128]{1,0:T(8,128)(2,1)} %shard_map.69.prior_ref, bf16[1152,128]{1,0:T(8,128)(2,1)} %bitcast.86, f32[1152,128]{1,0:T(8,128)} %broadcast_in_dim.69.mask_ref, bf16[14,128,128]{2,1,0:T(8,128)(2,1)} %get-tuple-element.6.w_ref), custom_call_target="tpu_custom_call" | custom-call | flops 340787200 | bytes 1843200 | tf_op jit(solution)/shard_map/pallas_call | solution.py:52
  144.1 2.9 %shard_map.71 = bf16[512,128]{1,0:T(8,128)(2,1)} custom-call(bf16[800,128]{1,0:T(8,128)(2,1)} %shard_map.70.prior_ref, bf16[800,128]{1,0:T(8,128)(2,1)} %bitcast.89, f32[800,128]{1,0:T(8,128)} %broadcast_in_dim.72.mask_ref, bf16[14,128,128]{2,1,0:T(8,128)(2,1)} %get-tuple-element.5.w_ref), custom_call_target="tpu_custom_call" | custom-call | flops 218103808 | bytes 1409024 | tf_op jit(solution)/shard_map/pallas_call | solution.py:52
  147.8 18.5 %all_to_all.17 = bf16[8,1,8,8,8,128]{5,4,3,2,1,0:T(8,128)(2,1)S(1)} all-to-all(bf16[8,1,8,8,8,128]{5,4,3,2,1,0:T(8,128)(2,1)S(1)} %constant_dynamic-update-slice_fusion), channel_id=1, replica_groups=mesh['section'=8,'frames'=4,'space'=16] {'section'}, dimensions={0} | all-to-all | bytes 2097152 | tf_op jit(solution)/shard_map/all_to_all | solution.py:162
  166.4 1.0 copy.20
  (74 shorter events, 16.6 us)
Async XLA Ops:
  6.5 27.7 %copy-start = (bf16[8,8,8,8,128]{4,3,2,1,0:T(8,128)(2,1)S(1)}, bf16[8,8,8,8,128]{4,3,2,1,0:T(8,128)(2,1)}, u32[]{:S(2)}) copy-start(bf16[8,8,8,8,128]{4,3,2,1,0:T(8,128)(2,1)} %param.6) | copy-start | bytes 3145732
  6.5 76.0 %all-gather.2.cloned.1.call-start = ((), (), s32[]{:S(2)}) async-start(), calls=%async_computation.2 | async-start | bytes 4128768 | tf_op jit(solution)/shard_map/all_gather | solution.py:123
  9.3 20.3 %all-to-all-start = ((bf16[8,8,8,8,128]{4,3,2,1,0:T(8,128)(2,1)}), bf16[8,8,8,8,128]{4,3,2,1,0:T(8,128)(2,1)S(1)}, u32[]{:S(2)}, u32[]{:S(2)}) async-start(bf16[8,8,8,8,128]{4,3,2,1,0:T(8,128)(2,1)} %bitcast.88), calls=%async_computation | async-start | bytes 2097152 | tf_op jit(solution)/shard_map/all_to_all | solution.py:114
  29.7 10.5 %collective-permute-start.9 = (bf16[4,1,4,8,8,128]{5,4,3,2,0,1:T(8,128)(2,1)S(1)}, bf16[4,1,4,8,8,128]{5,4,3,2,0,1:T(8,128)(2,1)S(1)}, u32[]{:S(2)}, u32[]{:S(2)}) collective-permute-start(bf16[4,1,4,8,8,128]{5,4,3,2,0,1:T(8,128)(2,1)S(1)} %get-tuple-element.24), channel_id=1, source_target_pairs={{16,0},{32,16},{48,32},{17,1},{33,17},{49,33},{18,2},{34,18},{50,3... | collective-permute-start | bytes 786440 | tf_op jit(solution)/shard_map/ppermute | solution.py:72
  32.4 9.5 %collective-permute-start.8 = (bf16[4,1,4,8,8,128]{5,4,3,2,0,1:T(8,128)(2,1)S(1)}, bf16[4,1,4,8,8,128]{5,4,3,2,0,1:T(8,128)(2,1)S(1)}, u32[]{:S(2)}, u32[]{:S(2)}) collective-permute-start(bf16[4,1,4,8,8,128]{5,4,3,2,0,1:T(8,128)(2,1)S(1)} %get-tuple-element.23), channel_id=1, source_target_pairs={{0,16},{16,32},{32,48},{1,17},{17,33},{33,49},{2,18},{18,34},{34,5... | collective-permute-start | bytes 786440 | tf_op jit(solution)/shard_map/ppermute | solution.py:71
  34.3 14.8 %collective-permute-start.1 = (bf16[5,1,4,8,8,128]{5,4,3,2,0,1:T(8,128)(2,1)S(1)}, bf16[5,1,4,8,8,128]{5,4,3,2,0,1:T(8,128)(2,1)S(1)}, u32[]{:S(2)}, u32[]{:S(2)}) collective-permute-start(bf16[5,1,4,8,8,128]{5,4,3,2,0,1:T(8,128)(2,1)S(1)} %get-tuple-element.22), channel_id=1, source_target_pairs={{16,0},{32,16},{48,32},{17,1},{33,17},{49,33},{18,2},{34,18},{50,3... | collective-permute-start | bytes 983048 | tf_op jit(solution)/shard_map/ppermute | solution.py:72
  38.9 10.3 %collective-permute-start = (bf16[5,1,4,8,8,128]{5,4,3,2,0,1:T(8,128)(2,1)S(1)}, bf16[5,1,4,8,8,128]{5,4,3,2,0,1:T(8,128)(2,1)S(1)}, u32[]{:S(2)}, u32[]{:S(2)}) collective-permute-start(bf16[5,1,4,8,8,128]{5,4,3,2,0,1:T(8,128)(2,1)S(1)} %get-tuple-element.21), channel_id=1, source_target_pairs={{0,16},{16,32},{32,48},{1,17},{17,33},{33,49},{2,18},{18,34},{34,5... | collective-permute-start | bytes 983048 | tf_op jit(solution)/shard_map/ppermute | solution.py:71
  40.2 2.8 %copy-start.5 = (bf16[4,1,4,8,8,128]{5,4,3,2,0,1:T(8,128)(2,1)}, bf16[4,1,4,8,8,128]{5,4,3,2,0,1:T(8,128)(2,1)S(1)}, u32[]{:S(2)}) copy-start(bf16[4,1,4,8,8,128]{5,4,3,2,0,1:T(8,128)(2,1)S(1)} %collective-permute-done.9) | copy-start | bytes 786436
  41.8 1.2 copy-start.7
  43.1 25.0 %collective-permute-start.11 = (bf16[4,1,16,4,8,128]{5,4,3,2,0,1:T(8,128)(2,1)}, bf16[4,1,16,4,8,128]{5,4,3,2,0,1:T(8,128)(2,1)}, u32[]{:S(2)}, u32[]{:S(2)}) collective-permute-start(bf16[4,1,16,4,8,128]{5,4,3,2,0,1:T(8,128)(2,1)} %get-tuple-element.18), channel_id=1, source_target_pairs={{1,0},{2,1},{3,2},{4,3},{5,4},{6,5},{7,6},{8,7},{9,8},{10,9},{11,1... | collective-permute-start | bytes 1572872 | tf_op jit(solution)/shard_map/ppermute | solution.py:72
  47.2 10.7 %copy-start.13 = (pred[10]{0:T(512)(128)(4,1)S(1)}, pred[10]{0:T(512)(128)(4,1)}, u32[]{:S(2)}) copy-start(pred[10]{0:T(512)(128)(4,1)} %get-tuple-element.35) | copy-start | bytes 34
  47.2 10.7 %copy-start.14 = (pred[10]{0:T(512)(128)(4,1)S(1)}, pred[10]{0:T(512)(128)(4,1)}, u32[]{:S(2)}) copy-start(pred[10]{0:T(512)(128)(4,1)} %get-tuple-element.36) | copy-start | bytes 34
  47.2 20.8 %collective-permute-start.10 = (bf16[4,1,16,4,8,128]{5,4,3,2,0,1:T(8,128)(2,1)}, bf16[4,1,16,4,8,128]{5,4,3,2,0,1:T(8,128)(2,1)}, u32[]{:S(2)}, u32[]{:S(2)}) collective-permute-start(bf16[4,1,16,4,8,128]{5,4,3,2,0,1:T(8,128)(2,1)} %get-tuple-element.17), channel_id=1, source_target_pairs={{0,1},{1,2},{2,3},{3,4},{4,5},{5,6},{6,7},{7,8},{8,9},{9,10},{10,1... | collective-permute-start | bytes 1572872 | tf_op jit(solution)/shard_map/ppermute | solution.py:71
  49.2 1.7 copy-start.1
  49.2 1.6 copy-start.3
  50.8 24.6 %collective-permute-start.3 = (bf16[5,1,16,4,8,128]{5,4,3,2,0,1:T(8,128)(2,1)}, bf16[5,1,16,4,8,128]{5,4,3,2,0,1:T(8,128)(2,1)S(1)}, u32[]{:S(2)}, u32[]{:S(2)}) collective-permute-start(bf16[5,1,16,4,8,128]{5,4,3,2,0,1:T(8,128)(2,1)} %get-tuple-element.16), channel_id=1, source_target_pairs={{1,0},{2,1},{3,2},{4,3},{5,4},{6,5},{7,6},{8,7},{9,8},{10,9},{11,1... | collective-permute-start | bytes 1966088 | tf_op jit(solution)/shard_map/ppermute | solution.py:72
  55.9 20.7 %collective-permute-start.2 = (bf16[5,1,16,4,8,128]{5,4,3,2,0,1:T(8,128)(2,1)}, bf16[5,1,16,4,8,128]{5,4,3,2,0,1:T(8,128)(2,1)S(1)}, u32[]{:S(2)}, u32[]{:S(2)}) collective-permute-start(bf16[5,1,16,4,8,128]{5,4,3,2,0,1:T(8,128)(2,1)} %get-tuple-element.15), channel_id=1, source_target_pairs={{0,1},{1,2},{2,3},{3,4},{4,5},{5,6},{6,7},{7,8},{8,9},{9,10},{10,1... | collective-permute-start | bytes 1966088 | tf_op jit(solution)/shard_map/ppermute | solution.py:71
  68.0 2.5 %copy-start.6 = (bf16[4,1,4,8,8,128]{5,4,3,2,0,1:T(8,128)(2,1)S(1)}, bf16[4,1,4,8,8,128]{5,4,3,2,0,1:T(8,128)(2,1)}, u32[]{:S(2)}) copy-start(bf16[4,1,4,8,8,128]{5,4,3,2,0,1:T(8,128)(2,1)} %copy-done.5) | copy-start | bytes 786436
  68.0 2.5 %copy-start.8 = (bf16[4,1,4,8,8,128]{5,4,3,2,0,1:T(8,128)(2,1)S(1)}, bf16[4,1,4,8,8,128]{5,4,3,2,0,1:T(8,128)(2,1)}, u32[]{:S(2)}) copy-start(bf16[4,1,4,8,8,128]{5,4,3,2,0,1:T(8,128)(2,1)} %copy-done.7) | copy-start | bytes 786436
  72.0 4.7 %copy-start.2 = (bf16[5,1,4,8,8,128]{5,4,3,2,0,1:T(8,128)(2,1)S(1)}, bf16[5,1,4,8,8,128]{5,4,3,2,0,1:T(8,128)(2,1)}, u32[]{:S(2)}) copy-start(bf16[5,1,4,8,8,128]{5,4,3,2,0,1:T(8,128)(2,1)} %copy-done.1) | copy-start | bytes 983044
  72.0 4.7 %copy-start.4 = (bf16[5,1,4,8,8,128]{5,4,3,2,0,1:T(8,128)(2,1)S(1)}, bf16[5,1,4,8,8,128]{5,4,3,2,0,1:T(8,128)(2,1)}, u32[]{:S(2)}) copy-start(bf16[5,1,4,8,8,128]{5,4,3,2,0,1:T(8,128)(2,1)} %copy-done.3) | copy-start | bytes 983044
  86.5 6.6 %copy-start.11 = (f32[1568]{0:T(1024)S(1)}, f32[1568]{0:T(1024)}, u32[]{:S(2)}) copy-start(f32[1568]{0:T(1024)} %broadcast_in_dim.65) | copy-start | bytes 18820
  94.3 8.0 %copy-start.12 = (f32[800]{0:T(1024)S(1)}, f32[800]{0:T(1024)}, u32[]{:S(2)}) copy-start(f32[800]{0:T(1024)} %broadcast_in_dim.71) | copy-start | bytes 9604
  102.3 20.8 %copy-start.10 = (bf16[800,128]{1,0:T(8,128)(2,1)S(1)}, bf16[800,128]{1,0:T(8,128)(2,1)}, u32[]{:S(2)}) copy-start(bf16[800,128]{1,0:T(8,128)(2,1)} %shard_map.66.prior_ref) | copy-start | bytes 614404
  106.1 23.0 %copy-start.9 = (bf16[512,128]{1,0:T(8,128)(2,1)S(1)}, bf16[512,128]{1,0:T(8,128)(2,1)}, u32[]{:S(2)}) copy-start(bf16[512,128]{1,0:T(8,128)(2,1)} %shard_map.67) | copy-start | bytes 393220
  107.0 5.2 %collective-permute-start.5 = (bf16[1,4,8,8,128]{4,3,2,1,0:T(8,128)(2,1)S(1)}, bf16[1,4,8,8,128]{4,3,2,1,0:T(8,128)(2,1)S(1)}, u32[]{:S(2)}, u32[]{:S(2)}) collective-permute-start(bf16[1,4,8,8,128]{4,3,2,1,0:T(8,128)(2,1)S(1)} %get-tuple-element.28), channel_id=1, source_target_pairs={{16,0},{32,16},{48,32},{17,1},{33,17},{49,33},{18,2},{34,18},{50,3... | collective-permute-start | bytes 196616 | tf_op jit(solution)/shard_map/ppermute | solution.py:72
  109.9 6.2 %collective-permute-start.4 = (bf16[1,4,8,8,128]{4,3,2,1,0:T(8,128)(2,1)S(1)}, bf16[1,4,8,8,128]{4,3,2,1,0:T(8,128)(2,1)S(1)}, u32[]{:S(2)}, u32[]{:S(2)}) collective-permute-start(bf16[1,4,8,8,128]{4,3,2,1,0:T(8,128)(2,1)S(1)} %get-tuple-element.27), channel_id=1, source_target_pairs={{0,16},{16,32},{32,48},{1,17},{17,33},{33,49},{2,18},{18,34},{34,5... | collective-permute-start | bytes 196616 | tf_op jit(solution)/shard_map/ppermute | solution.py:71
  117.1 7.0 %collective-permute-start.7 = (bf16[1,16,4,8,128]{4,3,2,1,0:T(8,128)(2,1)S(1)}, bf16[1,16,4,8,128]{4,3,2,1,0:T(8,128)(2,1)S(1)}, u32[]{:S(2)}, u32[]{:S(2)}) collective-permute-start(bf16[1,16,4,8,128]{4,3,2,1,0:T(8,128)(2,1)S(1)} %get-tuple-element.26), channel_id=1, source_target_pairs={{1,0},{2,1},{3,2},{4,3},{5,4},{6,5},{7,6},{8,7},{9,8},{10,9},{11,1... | collective-permute-start | bytes 393224 | tf_op jit(solution)/shard_map/ppermute | solution.py:72
  121.0 8.1 %collective-permute-start.6 = (bf16[1,16,4,8,128]{4,3,2,1,0:T(8,128)(2,1)S(1)}, bf16[1,16,4,8,128]{4,3,2,1,0:T(8,128)(2,1)S(1)}, u32[]{:S(2)}, u32[]{:S(2)}) collective-permute-start(bf16[1,16,4,8,128]{4,3,2,1,0:T(8,128)(2,1)S(1)} %get-tuple-element.25), channel_id=1, source_target_pairs={{0,1},{1,2},{2,3},{3,4},{4,5},{5,6},{6,7},{7,8},{8,9},{9,10},{10,1... | collective-permute-start | bytes 393224 | tf_op jit(solution)/shard_map/ppermute | solution.py:71
Sparse Core Ops, SparseCore 0:
  9.5 37.4 all-gather.1

commit v2 on v1

--- a/solution.py
+++ b/solution.py
@@ -9,7 +9,10 @@
 HALO = 4
 
 
-def section_kernel(m, n, cols, prior_ref, noise_ref, mask_ref, w_ref, out_ref, xl, xc, xr, nz):
+def section_kernel(
+    m, n, cols, inner, num_frames, num_rows,
+    prior_ref, noise_ref, fm_ref, rm_ref, w_ref, out_ref, crop_ref, xl, xc, xr, nz,
+):
     channels = w_ref.shape[-1]
     rows_in = m * n * cols
     rows_out = (m - 2) * (n - 2) * cols
@@ -17,7 +20,9 @@
     noisy = prior_ref[...].astype(jnp.float32) + level * noise_ref[...].astype(jnp.float32)
     mean_sq = jnp.mean(noisy * noisy, axis=-1, keepdims=True)
     normalized = (noisy * lax.rsqrt(mean_sq + 1e-05)).astype(jnp.bfloat16).astype(jnp.float32)
-    normalized = jnp.where(mask_ref[...] > 0, normalized, 0.0)
+    mask = fm_ref[...][:, 0:1, :] * rm_ref[...][None, :, :]
+    normalized = jnp.where(mask > 0, normalized.reshape(m, n * cols, channels), 0.0)
+    normalized = normalized.reshape(rows_in, channels)
     col = lax.broadcasted_iota(jnp.int32, (rows_in, channels), 0) % cols
     left = jnp.where(col == 0, 0.0, pltpu.roll(normalized, 1, 0))
     right = jnp.where(col == cols - 1, 0.0, pltpu.roll(normalized, rows_in - 1, 0))
@@ -38,28 +43,40 @@
         acc = acc + jnp.dot(v, w_ref[9 + t], preferred_element_type=jnp.float32)
     act = (acc / (1.0 + jnp.exp(-acc))).astype(jnp.bfloat16)
     est = jnp.dot(act, w_ref[12], preferred_element_type=jnp.float32)
-    inner = nz[pl.ds(1, m - 2), pl.ds(cols, (n - 2) * cols), :].reshape(rows_out, channels)
-    out_ref[...] = (inner - level * est).astype(out_ref.dtype)
+    center = nz[pl.ds(1, m - 2), pl.ds(cols, (n - 2) * cols), :].reshape(rows_out, channels)
+    result = center - level * est
+    out_ref[...] = result.astype(out_ref.dtype)
+    nz[pl.ds(0, m - 2), pl.ds(0, (n - 2) * cols), :] = result.reshape(m - 2, (n - 2) * cols, channels)
+    crop = nz[pl.ds(inner, num_frames), pl.ds(inner * cols, num_rows * cols), :]
+    crop_ref[...] = crop.reshape(num_frames * num_rows * cols, channels).astype(crop_ref.dtype)
 
 
-def section_call(prior, noise, mask, weights, m, n, cols):
+def section_call(prior, noise, frame_mask, row_mask, weights, m, n, cols, num_frames, num_rows):
     channels = weights.shape[-1]
     rows_in = m * n * cols
     rows_out = (m - 2) * (n - 2) * cols
+    rows_crop = num_frames * num_rows * cols
+    inner = (m - 2 - num_frames) // 2
     flops = 2 * rows_out * channels * channels * 13
-    nbytes = 2 * 2 * rows_in * channels + 4 * rows_in * channels + 2 * 14 * channels * channels
+    nbytes = 2 * 2 * rows_in * channels + 2 * 14 * channels * channels
+    nbytes += 2 * (rows_out + rows_crop) * channels
     scratch = pltpu.VMEM((m, n * cols, channels), jnp.float32)
     return pl.pallas_call(
-        functools.partial(section_kernel, m, n, cols),
-        out_shape=jax.ShapeDtypeStruct((rows_out, channels), jnp.bfloat16),
-        in_specs=[pl.BlockSpec(memory_space=pltpu.VMEM)] * 4,
-        out_specs=pl.BlockSpec(memory_space=pltpu.VMEM),
+        functools.partial(section_kernel, m, n, cols, inner, num_frames, num_rows),
+        out_shape=(
+            jax.ShapeDtypeStruct((rows_out, channels), jnp.bfloat16),
+            jax.ShapeDtypeStruct((rows_crop, channels), jnp.bfloat16),
+        ),
+        in_specs=[pl.BlockSpec(memory_space=pltpu.VMEM)] * 5,
+        out_specs=(
+            pl.BlockSpec(memory_space=pltpu.VMEM),
+            pl.BlockSpec(memory_space=pltpu.VMEM),
+        ),
         scratch_shapes=[scratch] * 4,
         cost_estimate=pl.CostEstimate(
-            flops=flops, bytes_accessed=nbytes + 2 * rows_out * channels,
-            transcendentals=rows_out * channels,
+            flops=flops, bytes_accessed=nbytes, transcendentals=rows_out * channels
         ),
-    )(prior, noise, mask, weights)
+    )(prior, noise, frame_mask, row_mask, weights)
 
 
 def extend(block, width, frame_dim, row_dim):
@@ -74,33 +91,42 @@
     return block
 
 
-def inside_mask(num_frames, num_rows, width):
+def inside_masks(num_frames, num_rows, num_cols, channels, width):
     frame_place = lax.axis_index("frames")
     row_place = lax.axis_index("space")
     total_frames = num_frames * lax.axis_size("frames")
     total_rows = num_rows * lax.axis_size("space")
     frames = frame_place * num_frames - width + jnp.arange(num_frames + 2 * width)
     rows = row_place * num_rows - width + jnp.arange(num_rows + 2 * width)
-    frame_ok = (frames >= 0) & (frames < total_frames)
-    row_ok = (rows >= 0) & (rows < total_rows)
-    return (frame_ok[:, None] & row_ok[None, :])[None, :, :, None, None]
+    frame_ok = ((frames >= 0) & (frames < total_frames)).astype(jnp.float32)
+    row_ok = ((rows >= 0) & (rows < total_rows)).astype(jnp.float32)
+    frame_mask = jnp.broadcast_to(frame_ok[:, None, None], (num_frames + 2 * width, 8, channels))
+    row_mask = jnp.broadcast_to(
+        row_ok[:, None, None], (num_rows + 2 * width, num_cols, channels)
+    ).reshape(-1, channels)
+    return frame_mask, row_mask
 
 
-def denoise(previous, noise_part, weights, mask):
+def denoise(previous, noise_part, weights, masks, num_frames, num_rows):
     num_videos, m, n, num_cols, channels = previous.shape
     outs = []
+    crops = []
     for v in range(num_videos):
-        out = section_call(
+        out, crop = section_call(
             previous[v].reshape(-1, channels),
             noise_part[v].reshape(-1, channels),
-            mask,
+            masks[0],
+            masks[1],
             weights,
             m,
             n,
             num_cols,
+            num_frames,
+            num_rows,
         )
         outs.append(out.reshape(m - 2, n - 2, num_cols, channels))
-    return jnp.stack(outs)
+        crops.append(crop)
+    return jnp.stack(outs), jnp.stack(crops)
 
 
 def on_device(
@@ -130,13 +156,7 @@
     noise_ext = jnp.concatenate(noise_parts, axis=0)
     num_cols, channels = base_frames.shape[3:]
     masks = [
-        jnp.broadcast_to(
-            inside_mask(num_frames, num_rows, w)[0],
-            (num_frames + 2 * w, num_rows + 2 * w, num_cols, channels),
-        )
-        .astype(jnp.float32)
-        .reshape(-1, channels)
-        for w in range(halo + 1)
+        inside_masks(num_frames, num_rows, num_cols, channels, w) for w in range(halo + 1)
     ]
     results = []
     for k in range(sections):
@@ -148,17 +168,13 @@
         noise_here = noise_ext[
             k, :, cut : cut + num_frames + 2 * width, cut : cut + num_rows + 2 * width
         ]
-        prior_ext = denoise(
-            prior_ext,
-            noise_here,
-            packed[k],
-            masks[width],
+        prior_ext, crop = denoise(
+            prior_ext, noise_here, packed[k], masks[width], num_frames, num_rows
         )
-        inner = width - 1
-        results.append(
-            prior_ext[:, inner : inner + num_frames, inner : inner + num_rows]
-        )
-    stacked = jnp.stack(results)
+        results.append(crop)
+    stacked = jnp.stack(results).reshape(
+        (sections, per_device, num_frames, num_rows, num_cols, channels)
+    )
     return lax.all_to_all(stacked, "section", 0, 1, tiled=True)
 
 

time: 175 us -> 174 us (level)
  the two profiles are of different devices: /device:TPU:408 before, /device:TPU:96 now
where the time goes in v2:
time: 174 us; the launch traced here: 173 us
  waiting for transfers between devices  43.3 us (25%)
  starting transfers between devices  39.7 us (23%)
  Pallas kernels  27.4 us (16%)
  blocking collectives  18.5 us (11%)
  local copies, waits for them, and re-layouts  18.2 us (10%)
  between operations  14.5 us (8%)
  other arithmetic  11.6 us (7%)
    pallas_call x8, Pallas kernels, section_call(): pl.pallas_call(functools.partial(section_kernel, m, n, cols, inner, num_f...  27.4 us
    ppermute x6, starting transfers between devices, extend(): lax.ppermute(lax.slice_in_dim(block, size - width, size, axis=dim), axis,...  24.4 us
    ppermute x6, waiting for transfers between devices, extend(): lax.ppermute(lax.slice_in_dim(block, 0, width, axis=dim), axis, backward)  21 us
    all_to_all x1, blocking collectives, on_device(): return lax.all_to_all(stacked, 'section', 0, 1, tiled=True)  18.5 us
    all_to_all x1, waiting for transfers between devices, on_device(): noise_t = lax.all_to_all(section_noise[0], 'section', 0, 0, tiled=True)  15.9 us
    ppermute x6, starting transfers between devices, extend(): lax.ppermute(lax.slice_in_dim(block, 0, width, axis=dim), axis, backward)  10.9 us
    ppermute x6, waiting for transfers between devices, extend(): lax.ppermute(lax.slice_in_dim(block, size - width, size, axis=dim), axis,...  6.38 us
    concatenate x6, other arithmetic, extend(): block = jnp.concatenate([low, block, high], axis=dim)  4.84 us
  transfers between devices with their start and end apart: 14, of which 11 were waited for; matrix products, arithmetic and copies ran while one was open for 6% of the time, Pallas kernels for 0%

profile of v2, /device:TPU:96, one launch (start us, length us, event | category | flops | bytes accessed | tf_op | source)
XLA Modules:
  0.0 173.2 jit_solution(7443621796814363627)
XLA Ops:
  7.4 1.9 %maximum_maximum_fusion = bf16[1,14,128,128]{3,2,1,0:T(8,128)(2,1)} fusion(bf16[1,1,128,128]{3,2,1,0:T(8,128)(2,1)} %bitcast.68, bf16[1,3,128,128]{3,2,1,0:T(8,128)(2,1)} %param.10, bf16[1,9,128,128]{3,2,1,0:T(8,128)(2,1)} %param.9, bf16[14]{0:T(256)(128)(2,1)S(1)} %pad.19.clone), kind=kLoop, calls=%fused_computation.17 | loop fusion | flops 688128 | bytes 884764 | tf_op jit(solution)/shard_map/concatenate | solution.py:146
  9.3 4.3 %all-to-all-start = ((bf16[8,8,8,8,128]{4,3,2,1,0:T(8,128)(2,1)}), bf16[8,8,8,8,128]{4,3,2,1,0:T(8,128)(2,1)S(1)}, u32[]{:S(2)}, u32[]{:S(2)}) async-start(bf16[8,8,8,8,128]{4,3,2,1,0:T(8,128)(2,1)} %bitcast.49), calls=%async_computation | async-start | bytes 2097152 | tf_op jit(solution)/shard_map/all_to_all | solution.py:140
  13.7 15.9 %all-to-all-done = bf16[8,8,8,8,128]{4,3,2,1,0:T(8,128)(2,1)S(1)} async-done(((bf16[8,8,8,8,128]{4,3,2,1,0:T(8,128)(2,1)}), bf16[8,8,8,8,128]{4,3,2,1,0:T(8,128)(2,1)S(1)}, u32[]{:S(2)}, u32[]{:S(2)}) %all-to-all-start) | async-done | bytes 1048608 | tf_op jit(solution)/shard_map/all_to_all | solution.py:140
  29.7 3.5 %collective-permute-start.8 = (bf16[4,1,4,8,8,128]{5,4,3,2,0,1:T(8,128)(2,1)S(1)}, bf16[4,1,4,8,8,128]{5,4,3,2,0,1:T(8,128)(2,1)S(1)}, u32[]{:S(2)}, u32[]{:S(2)}) collective-permute-start(bf16[4,1,4,8,8,128]{5,4,3,2,0,1:T(8,128)(2,1)S(1)} %get-tuple-element.53), channel_id=1, source_target_pairs={{0,16},{16,32},{32,48},{1,17},{17,33},{33,49},{2,18},{18,34},{34,5... | collective-permute-start | bytes 786440 | tf_op jit(solution)/shard_map/ppermute | solution.py:88
  33.2 1.3 collective-permute-start.9
  35.3 4.6 %collective-permute-start = (bf16[5,1,4,8,8,128]{5,4,3,2,0,1:T(8,128)(2,1)S(1)}, bf16[5,1,4,8,8,128]{5,4,3,2,0,1:T(8,128)(2,1)S(1)}, u32[]{:S(2)}, u32[]{:S(2)}) collective-permute-start(bf16[5,1,4,8,8,128]{5,4,3,2,0,1:T(8,128)(2,1)S(1)} %get-tuple-element.51), channel_id=1, source_target_pairs={{0,16},{16,32},{32,48},{1,17},{17,33},{33,49},{2,18},{18,34},{34,5... | collective-permute-start | bytes 983048 | tf_op jit(solution)/shard_map/ppermute | solution.py:88
  39.9 1.3 collective-permute-start.1
  41.2 1.5 collective-permute-done.9
  42.9 5.0 %collective-permute-start.10 = (bf16[4,1,16,4,8,128]{5,4,3,2,0,1:T(8,128)(2,1)S(1)}, bf16[4,1,16,4,8,128]{5,4,3,2,0,1:T(8,128)(2,1)S(1)}, u32[]{:S(2)}, u32[]{:S(2)}) collective-permute-start(bf16[4,1,16,4,8,128]{5,4,3,2,0,1:T(8,128)(2,1)S(1)} %get-tuple-element.47), channel_id=1, source_target_pairs={{0,1},{1,2},{2,3},{3,4},{4,5},{5,6},{6,7},{7,8},{8,9},{9,10},{10,1... | collective-permute-start | bytes 1572872 | tf_op jit(solution)/shard_map/ppermute | solution.py:88
  47.9 1.9 %collective-permute-start.11 = (bf16[4,1,16,4,8,128]{5,4,3,2,0,1:T(8,128)(2,1)S(1)}, bf16[4,1,16,4,8,128]{5,4,3,2,0,1:T(8,128)(2,1)S(1)}, u32[]{:S(2)}, u32[]{:S(2)}) collective-permute-start(bf16[4,1,16,4,8,128]{5,4,3,2,0,1:T(8,128)(2,1)S(1)} %get-tuple-element.48), channel_id=1, source_target_pairs={{1,0},{2,1},{3,2},{4,3},{5,4},{6,5},{7,6},{8,7},{9,8},{10,9},{11,1... | collective-permute-start | bytes 1572872 | tf_op jit(solution)/shard_map/ppermute | solution.py:89
  50.6 5.0 %collective-permute-start.2 = (bf16[5,1,16,4,8,128]{5,4,3,2,0,1:T(8,128)(2,1)S(1)}, bf16[5,1,16,4,8,128]{5,4,3,2,0,1:T(8,128)(2,1)S(1)}, u32[]{:S(2)}, u32[]{:S(2)}) collective-permute-start(bf16[5,1,16,4,8,128]{5,4,3,2,0,1:T(8,128)(2,1)S(1)} %get-tuple-element.45), channel_id=1, source_target_pairs={{0,1},{1,2},{2,3},{3,4},{4,5},{5,6},{6,7},{7,8},{8,9},{9,10},{10,1... | collective-permute-start | bytes 1966088 | tf_op jit(solution)/shard_map/ppermute | solution.py:88
  55.7 1.9 %collective-permute-start.3 = (bf16[5,1,16,4,8,128]{5,4,3,2,0,1:T(8,128)(2,1)S(1)}, bf16[5,1,16,4,8,128]{5,4,3,2,0,1:T(8,128)(2,1)S(1)}, u32[]{:S(2)}, u32[]{:S(2)}) collective-permute-start(bf16[5,1,16,4,8,128]{5,4,3,2,0,1:T(8,128)(2,1)S(1)} %get-tuple-element.46), channel_id=1, source_target_pairs={{1,0},{2,1},{3,2},{4,3},{5,4},{6,5},{7,6},{8,7},{9,8},{10,9},{11,1... | collective-permute-start | bytes 1966088 | tf_op jit(solution)/shard_map/ppermute | solution.py:89
  57.6 2.7 %collective-permute-done.10 = bf16[4,1,16,4,8,128]{5,4,3,2,0,1:T(8,128)(2,1)S(1)} collective-permute-done((bf16[4,1,16,4,8,128]{5,4,3,2,0,1:T(8,128)(2,1)S(1)}, bf16[4,1,16,4,8,128]{5,4,3,2,0,1:T(8,128)(2,1)S(1)}, u32[]{:S(2)}, u32[]{:S(2)}) %collective-permute-start.10) | collective-permute-done | bytes 524320 | tf_op jit(solution)/shard_map/ppermute | solution.py:88
  60.3 5.6 %collective-permute-done.11 = bf16[4,1,16,4,8,128]{5,4,3,2,0,1:T(8,128)(2,1)S(1)} collective-permute-done((bf16[4,1,16,4,8,128]{5,4,3,2,0,1:T(8,128)(2,1)S(1)}, bf16[4,1,16,4,8,128]{5,4,3,2,0,1:T(8,128)(2,1)S(1)}, u32[]{:S(2)}, u32[]{:S(2)}) %collective-permute-start.11) | collective-permute-done | bytes 524320 | tf_op jit(solution)/shard_map/ppermute | solution.py:89
  66.2 0.8 slice.157
  67.8 0.8 pad_maximum_fusion.8
  68.5 0.9 pad_maximum_fusion.5
  69.4 2.4 %collective-permute-done.2 = bf16[5,1,16,4,8,128]{5,4,3,2,0,1:T(8,128)(2,1)S(1)} collective-permute-done((bf16[5,1,16,4,8,128]{5,4,3,2,0,1:T(8,128)(2,1)S(1)}, bf16[5,1,16,4,8,128]{5,4,3,2,0,1:T(8,128)(2,1)S(1)}, u32[]{:S(2)}, u32[]{:S(2)}) %collective-permute-start.2) | collective-permute-done | bytes 655392 | tf_op jit(solution)/shard_map/ppermute | solution.py:88
  71.8 5.3 %collective-permute-done.3 = bf16[5,1,16,4,8,128]{5,4,3,2,0,1:T(8,128)(2,1)S(1)} collective-permute-done((bf16[5,1,16,4,8,128]{5,4,3,2,0,1:T(8,128)(2,1)S(1)}, bf16[5,1,16,4,8,128]{5,4,3,2,0,1:T(8,128)(2,1)S(1)}, u32[]{:S(2)}, u32[]{:S(2)}) %collective-permute-start.3) | collective-permute-done | bytes 655392 | tf_op jit(solution)/shard_map/ppermute | solution.py:89
  77.9 0.8 pad_maximum_fusion.9
  78.7 0.8 pad_maximum_fusion.6
  79.5 2.5 %pad_maximum_fusion = bf16[5,1,16,16,8,128]{5,4,3,2,0,1:T(8,128)(2,1)S(1)} fusion(bf16[5,1,16,4,8,128]{5,4,3,2,0,1:T(8,128)(2,1)S(1)} %collective-permute-done.3, bf16[5,1,4,8,8,128]{5,4,3,2,0,1:T(8,128)(2,1)S(1)} %collective-permute-done.1, bf16[4,1,8,8,8,128]{5,4,3,2,0,1:T(8,128)(2,1)S(1)} %get-tuple-element.50, ...), kind=kLoop, calls=%fused_computation | loop fusion | flops 6553600 | bytes 5242880 | tf_op jit(solution)/shard_map/concatenate | solution.py:90
  82.0 1.0 fusion.1
  83.0 3.9 %slice_bitcast_fusion.2 = (bf16[14,128,128]{2,1,0:T(8,128)(2,1)}, bf16[14,128,128]{2,1,0:T(8,128)(2,1)}, bf16[14,128,128]{2,1,0:T(8,128)(2,1)}, bf16[14,128,128]...) fusion(bf16[8,14,128,128]{3,2,1,0:T(8,128)(2,1)} %all-gather.2., ...), kind=kLoop, calls=%fused_computation.9 | loop fusion | bytes 7340032 | tf_op jit(solution)/shard_map/squeeze | solution.py:172
  88.3 4.1 %shard_map.64 = (bf16[1568,128]{1,0:T(8,128)(2,1)}, bf16[512,128]{1,0:T(8,128)(2,1)}) custom-call(bf16[2048,128]{1,0:T(8,128)(2,1)} %bitcast.55, bf16[2048,128]{1,0:T(8,128)(2,1)} %bitcast.54, f32[16,8,128]{2,1,0:T(8,128)} %broadcast_in_dim.78.fm_ref, f32[128,128]{1,0:T(8,128)} %broadcast_in_dim.81.rm_ref, bf16[14,128,128]{2,1,0:T(8,128)(2,1)} %get-tuple-element.42.w_ref), custom_call_target="tpu_custom_call" | custom-call | flops 667942912 | bytes 2039808 | tf_op jit(solution)/shard_map/pallas_call | solution.py:64
  93.8 3.6 %shard_map.65 = (bf16[1152,128]{1,0:T(8,128)(2,1)}, bf16[512,128]{1,0:T(8,128)(2,1)}) custom-call(bf16[1568,128]{1,0:T(8,128)(2,1)} %get-tuple-element.21.prior_ref, bf16[1568,128]{1,0:T(8,128)(2,1)} %bitcast.57, f32[14,8,128]{2,1,0:T(8,128)} %broadcast_in_dim.85.fm_ref, f32[112,128]{1,0:T(8,128)} %broadcast_in_dim.88.rm_ref, ...), custom_call_target="tpu_custom_call" | custom-call | flops 490733568 | bytes 1687552 | tf_op jit(solution)/shard_map/pallas_call | solution.py:64
  98.8 3.1 %shard_map.66 = (bf16[800,128]{1,0:T(8,128)(2,1)}, bf16[512,128]{1,0:T(8,128)(2,1)}) custom-call(bf16[1152,128]{1,0:T(8,128)(2,1)} %get-tuple-element.23.prior_ref, bf16[1152,128]{1,0:T(8,128)(2,1)} %bitcast.59, f32[12,8,128]{2,1,0:T(8,128)} %broadcast_in_dim.89.fm_ref, f32[96,128]{1,0:T(8,128)} %broadcast_in_dim.92.rm_ref, ...), custom_call_target="tpu_custom_call" | custom-call | flops 340787200 | bytes 1384448 | tf_op jit(solution)/shard_map/pallas_call | solution.py:64
  103.4 2.8 %shard_map.67 = (bf16[512,128]{1,0:T(8,128)(2,1)}, bf16[512,128]{1,0:T(8,128)(2,1)}) custom-call(bf16[800,128]{1,0:T(8,128)(2,1)} %get-tuple-element.25.prior_ref, bf16[800,128]{1,0:T(8,128)(2,1)} %bitcast.51, f32[10,8,128]{2,1,0:T(8,128)} %broadcast_in_dim.93.fm_ref, f32[80,128]{1,0:T(8,128)} %broadcast_in_dim.96.rm_ref, ...), custom_call_target="tpu_custom_call" | custom-call | flops 218103808 | bytes 1130496 | tf_op jit(solution)/shard_map/pallas_call | solution.py:64
  106.2 0.9 fusion.6
  107.1 3.5 %collective-permute-start.4 = (bf16[1,4,8,8,128]{4,3,2,1,0:T(8,128)(2,1)S(1)}, bf16[1,4,8,8,128]{4,3,2,1,0:T(8,128)(2,1)S(1)}, u32[]{:S(2)}, u32[]{:S(2)}) collective-permute-start(bf16[1,4,8,8,128]{4,3,2,1,0:T(8,128)(2,1)S(1)} %get-tuple-element.57), channel_id=1, source_target_pairs={{0,16},{16,32},{32,48},{1,17},{17,33},{33,49},{2,18},{18,34},{34,5... | collective-permute-start | bytes 196616 | tf_op jit(solution)/shard_map/ppermute | solution.py:88
  110.6 1.3 collective-permute-start.5
  112.5 4.3 %collective-permute-done.5 = bf16[1,4,8,8,128]{4,3,2,1,0:T(8,128)(2,1)S(1)} collective-permute-done((bf16[1,4,8,8,128]{4,3,2,1,0:T(8,128)(2,1)S(1)}, bf16[1,4,8,8,128]{4,3,2,1,0:T(8,128)(2,1)S(1)}, u32[]{:S(2)}, u32[]{:S(2)}) %collective-permute-start.5) | collective-permute-done | bytes 65568 | tf_op jit(solution)/shard_map/ppermute | solution.py:89
  116.7 0.9 pad_maximum_fusion.10
  117.7 2.8 %collective-permute-start.6 = (bf16[1,16,4,8,128]{4,3,2,1,0:T(8,128)(2,1)S(1)}, bf16[1,16,4,8,128]{4,3,2,1,0:T(8,128)(2,1)S(1)}, u32[]{:S(2)}, u32[]{:S(2)}) collective-permute-start(bf16[1,16,4,8,128]{4,3,2,1,0:T(8,128)(2,1)S(1)} %get-tuple-element.55), channel_id=1, source_target_pairs={{0,1},{1,2},{2,3},{3,4},{4,5},{5,6},{6,7},{7,8},{8,9},{9,10},{10,1... | collective-permute-start | bytes 393224 | tf_op jit(solution)/shard_map/ppermute | solution.py:88
  120.5 3.2 %collective-permute-start.7 = (bf16[1,16,4,8,128]{4,3,2,1,0:T(8,128)(2,1)S(1)}, bf16[1,16,4,8,128]{4,3,2,1,0:T(8,128)(2,1)S(1)}, u32[]{:S(2)}, u32[]{:S(2)}) collective-permute-start(bf16[1,16,4,8,128]{4,3,2,1,0:T(8,128)(2,1)S(1)} %get-tuple-element.56), channel_id=1, source_target_pairs={{1,0},{2,1},{3,2},{4,3},{5,4},{6,5},{7,6},{8,7},{9,8},{10,9},{11,1... | collective-permute-start | bytes 393224 | tf_op jit(solution)/shard_map/ppermute | solution.py:89
  123.8 0.7 collective-permute-done.6
  124.6 4.0 %collective-permute-done.7 = bf16[1,16,4,8,128]{4,3,2,1,0:T(8,128)(2,1)S(1)} collective-permute-done((bf16[1,16,4,8,128]{4,3,2,1,0:T(8,128)(2,1)S(1)}, bf16[1,16,4,8,128]{4,3,2,1,0:T(8,128)(2,1)S(1)}, u32[]{:S(2)}, u32[]{:S(2)}) %collective-permute-start.7) | collective-permute-done | bytes 131104 | tf_op jit(solution)/shard_map/ppermute | solution.py:89
  128.6 0.9 pad_maximum_fusion.4
  129.5 4.2 %shard_map.68 = (bf16[1568,128]{1,0:T(8,128)(2,1)}, bf16[512,128]{1,0:T(8,128)(2,1)}) custom-call(bf16[2048,128]{1,0:T(8,128)(2,1)} %bitcast.53, bf16[2048,128]{1,0:T(8,128)(2,1)} %bitcast.52, f32[16,8,128]{2,1,0:T(8,128)} %broadcast_in_dim.78.fm_ref, f32[128,128]{1,0:T(8,128)} %broadcast_in_dim.81.rm_ref, bf16[14,128,128]{2,1,0:T(8,128)(2,1)} %get-tuple-element.38.w_ref), custom_call_target="tpu_custom_call" | custom-call | flops 667942912 | bytes 2039808 | tf_op jit(solution)/shard_map/pallas_call | solution.py:64
  133.6 0.9 constant_dynamic-update-slice_fusion.3
  134.6 3.6 %shard_map.69 = (bf16[1152,128]{1,0:T(8,128)(2,1)}, bf16[512,128]{1,0:T(8,128)(2,1)}) custom-call(bf16[1568,128]{1,0:T(8,128)(2,1)} %get-tuple-element.29.prior_ref, bf16[1568,128]{1,0:T(8,128)(2,1)} %bitcast.56, f32[14,8,128]{2,1,0:T(8,128)} %broadcast_in_dim.85.fm_ref, f32[112,128]{1,0:T(8,128)} %broadcast_in_dim.88.rm_ref, ...), custom_call_target="tpu_custom_call" | custom-call | flops 490733568 | bytes 1687552 | tf_op jit(solution)/shard_map/pallas_call | solution.py:64
  138.1 0.9 constant_dynamic-update-slice_fusion.2
  139.1 3.1 %shard_map.70 = (bf16[800,128]{1,0:T(8,128)(2,1)}, bf16[512,128]{1,0:T(8,128)(2,1)}) custom-call(bf16[1152,128]{1,0:T(8,128)(2,1)} %get-tuple-element.31.prior_ref, bf16[1152,128]{1,0:T(8,128)(2,1)} %bitcast.58, f32[12,8,128]{2,1,0:T(8,128)} %broadcast_in_dim.89.fm_ref, f32[96,128]{1,0:T(8,128)} %broadcast_in_dim.92.rm_ref, ...), custom_call_target="tpu_custom_call" | custom-call | flops 340787200 | bytes 1384448 | tf_op jit(solution)/shard_map/pallas_call | solution.py:64
  142.2 0.9 constant_dynamic-update-slice_fusion.1
  143.1 2.8 %shard_map.71 = (bf16[512,128]{1,0:T(8,128)(2,1)}, bf16[512,128]{1,0:T(8,128)(2,1)}) custom-call(bf16[800,128]{1,0:T(8,128)(2,1)} %get-tuple-element.33.prior_ref, bf16[800,128]{1,0:T(8,128)(2,1)} %bitcast.50, f32[10,8,128]{2,1,0:T(8,128)} %broadcast_in_dim.93.fm_ref, f32[80,128]{1,0:T(8,128)} %broadcast_in_dim.96.rm_ref, ...), custom_call_target="tpu_custom_call" | custom-call | flops 218103808 | bytes 1130496 | tf_op jit(solution)/shard_map/pallas_call | solution.py:64
  145.9 0.9 constant_dynamic-update-slice_fusion
  146.9 18.5 %all_to_all.17 = bf16[8,1,8,8,8,128]{5,4,3,2,1,0:T(8,128)(2,1)S(1)} all-to-all(bf16[8,1,8,8,8,128]{5,4,3,2,1,0:T(8,128)(2,1)S(1)} %constant_dynamic-update-slice_fusion), channel_id=1, replica_groups=mesh['section'=8,'frames'=4,'space'=16] {'section'}, dimensions={0} | all-to-all | bytes 2097152 | tf_op jit(solution)/shard_map/all_to_all | solution.py:178
  165.4 1.0 copy.32
  (60 shorter events, 9.9 us)
Async XLA Ops:
  6.5 28.7 %copy-start = (bf16[8,8,8,8,128]{4,3,2,1,0:T(8,128)(2,1)S(1)}, bf16[8,8,8,8,128]{4,3,2,1,0:T(8,128)(2,1)}, u32[]{:S(2)}) copy-start(bf16[8,8,8,8,128]{4,3,2,1,0:T(8,128)(2,1)} %param.6) | copy-start | bytes 3145732
  6.5 76.5 %all-gather.2.cloned.1.call-start = ((), (), s32[]{:S(2)}) async-start(), calls=%async_computation.2 | async-start | bytes 4128768 | tf_op jit(solution)/shard_map/all_gather | solution.py:149
  9.3 20.3 %all-to-all-start = ((bf16[8,8,8,8,128]{4,3,2,1,0:T(8,128)(2,1)}), bf16[8,8,8,8,128]{4,3,2,1,0:T(8,128)(2,1)S(1)}, u32[]{:S(2)}, u32[]{:S(2)}) async-start(bf16[8,8,8,8,128]{4,3,2,1,0:T(8,128)(2,1)} %bitcast.49), calls=%async_computation | async-start | bytes 2097152 | tf_op jit(solution)/shard_map/all_to_all | solution.py:140
  29.7 11.4 %collective-permute-start.8 = (bf16[4,1,4,8,8,128]{5,4,3,2,0,1:T(8,128)(2,1)S(1)}, bf16[4,1,4,8,8,128]{5,4,3,2,0,1:T(8,128)(2,1)S(1)}, u32[]{:S(2)}, u32[]{:S(2)}) collective-permute-start(bf16[4,1,4,8,8,128]{5,4,3,2,0,1:T(8,128)(2,1)S(1)} %get-tuple-element.53), channel_id=1, source_target_pairs={{0,16},{16,32},{32,48},{1,17},{17,33},{33,49},{2,18},{18,34},{34,5... | collective-permute-start | bytes 786440 | tf_op jit(solution)/shard_map/ppermute | solution.py:88
  33.2 9.5 %collective-permute-start.9 = (bf16[4,1,4,8,8,128]{5,4,3,2,0,1:T(8,128)(2,1)S(1)}, bf16[4,1,4,8,8,128]{5,4,3,2,0,1:T(8,128)(2,1)S(1)}, u32[]{:S(2)}, u32[]{:S(2)}) collective-permute-start(bf16[4,1,4,8,8,128]{5,4,3,2,0,1:T(8,128)(2,1)S(1)} %get-tuple-element.54), channel_id=1, source_target_pairs={{16,0},{32,16},{48,32},{17,1},{33,17},{49,33},{18,2},{34,18},{50,3... | collective-permute-start | bytes 786440 | tf_op jit(solution)/shard_map/ppermute | solution.py:89
  35.3 14.6 %collective-permute-start = (bf16[5,1,4,8,8,128]{5,4,3,2,0,1:T(8,128)(2,1)S(1)}, bf16[5,1,4,8,8,128]{5,4,3,2,0,1:T(8,128)(2,1)S(1)}, u32[]{:S(2)}, u32[]{:S(2)}) collective-permute-start(bf16[5,1,4,8,8,128]{5,4,3,2,0,1:T(8,128)(2,1)S(1)} %get-tuple-element.51), channel_id=1, source_target_pairs={{0,16},{16,32},{32,48},{1,17},{17,33},{33,49},{2,18},{18,34},{34,5... | collective-permute-start | bytes 983048 | tf_op jit(solution)/shard_map/ppermute | solution.py:88
  39.9 10.3 %collective-permute-start.1 = (bf16[5,1,4,8,8,128]{5,4,3,2,0,1:T(8,128)(2,1)S(1)}, bf16[5,1,4,8,8,128]{5,4,3,2,0,1:T(8,128)(2,1)S(1)}, u32[]{:S(2)}, u32[]{:S(2)}) collective-permute-start(bf16[5,1,4,8,8,128]{5,4,3,2,0,1:T(8,128)(2,1)S(1)} %get-tuple-element.52), channel_id=1, source_target_pairs={{16,0},{32,16},{48,32},{17,1},{33,17},{49,33},{18,2},{34,18},{50,3... | collective-permute-start | bytes 983048 | tf_op jit(solution)/shard_map/ppermute | solution.py:89
  42.9 17.4 %collective-permute-start.10 = (bf16[4,1,16,4,8,128]{5,4,3,2,0,1:T(8,128)(2,1)S(1)}, bf16[4,1,16,4,8,128]{5,4,3,2,0,1:T(8,128)(2,1)S(1)}, u32[]{:S(2)}, u32[]{:S(2)}) collective-permute-start(bf16[4,1,16,4,8,128]{5,4,3,2,0,1:T(8,128)(2,1)S(1)} %get-tuple-element.47), channel_id=1, source_target_pairs={{0,1},{1,2},{2,3},{3,4},{4,5},{5,6},{6,7},{7,8},{8,9},{9,10},{10,1... | collective-permute-start | bytes 1572872 | tf_op jit(solution)/shard_map/ppermute | solution.py:88
  47.9 18.0 %collective-permute-start.11 = (bf16[4,1,16,4,8,128]{5,4,3,2,0,1:T(8,128)(2,1)S(1)}, bf16[4,1,16,4,8,128]{5,4,3,2,0,1:T(8,128)(2,1)S(1)}, u32[]{:S(2)}, u32[]{:S(2)}) collective-permute-start(bf16[4,1,16,4,8,128]{5,4,3,2,0,1:T(8,128)(2,1)S(1)} %get-tuple-element.48), channel_id=1, source_target_pairs={{1,0},{2,1},{3,2},{4,3},{5,4},{6,5},{7,6},{8,7},{9,8},{10,9},{11,1... | collective-permute-start | bytes 1572872 | tf_op jit(solution)/shard_map/ppermute | solution.py:89
  50.6 21.2 %collective-permute-start.2 = (bf16[5,1,16,4,8,128]{5,4,3,2,0,1:T(8,128)(2,1)S(1)}, bf16[5,1,16,4,8,128]{5,4,3,2,0,1:T(8,128)(2,1)S(1)}, u32[]{:S(2)}, u32[]{:S(2)}) collective-permute-start(bf16[5,1,16,4,8,128]{5,4,3,2,0,1:T(8,128)(2,1)S(1)} %get-tuple-element.45), channel_id=1, source_target_pairs={{0,1},{1,2},{2,3},{3,4},{4,5},{5,6},{6,7},{7,8},{8,9},{9,10},{10,1... | collective-permute-start | bytes 1966088 | tf_op jit(solution)/shard_map/ppermute | solution.py:88
  55.7 21.5 %collective-permute-start.3 = (bf16[5,1,16,4,8,128]{5,4,3,2,0,1:T(8,128)(2,1)S(1)}, bf16[5,1,16,4,8,128]{5,4,3,2,0,1:T(8,128)(2,1)S(1)}, u32[]{:S(2)}, u32[]{:S(2)}) collective-permute-start(bf16[5,1,16,4,8,128]{5,4,3,2,0,1:T(8,128)(2,1)S(1)} %get-tuple-element.46), channel_id=1, source_target_pairs={{1,0},{2,1},{3,2},{4,3},{5,4},{6,5},{7,6},{8,7},{9,8},{10,9},{11,1... | collective-permute-start | bytes 1966088 | tf_op jit(solution)/shard_map/ppermute | solution.py:89
  93.8 18.1 %copy-start.4 = (bf16[512,128]{1,0:T(8,128)(2,1)S(1)}, bf16[512,128]{1,0:T(8,128)(2,1)}, u32[]{:S(2)}) copy-start(bf16[512,128]{1,0:T(8,128)(2,1)} %get-tuple-element.20) | copy-start | bytes 393220
  97.5 14.5 %copy-start.5 = (bf16[512,128]{1,0:T(8,128)(2,1)S(1)}, bf16[512,128]{1,0:T(8,128)(2,1)}, u32[]{:S(2)}) copy-start(bf16[512,128]{1,0:T(8,128)(2,1)} %get-tuple-element.22) | copy-start | bytes 393220
  102.0 21.8 %copy-start.2 = (bf16[512,128]{1,0:T(8,128)(2,1)S(1)}, bf16[512,128]{1,0:T(8,128)(2,1)}, u32[]{:S(2)}) copy-start(bf16[512,128]{1,0:T(8,128)(2,1)} %get-tuple-element.24) | copy-start | bytes 393220
  106.2 17.6 %copy-start.3 = (bf16[512,128]{1,0:T(8,128)(2,1)S(1)}, bf16[512,128]{1,0:T(8,128)(2,1)}, u32[]{:S(2)}) copy-start(bf16[512,128]{1,0:T(8,128)(2,1)} %get-tuple-element.26) | copy-start | bytes 393220
  106.2 22.4 %copy-start.1 = (bf16[512,128]{1,0:T(8,128)(2,1)S(1)}, bf16[512,128]{1,0:T(8,128)(2,1)}, u32[]{:S(2)}) copy-start(bf16[512,128]{1,0:T(8,128)(2,1)} %get-tuple-element.27) | copy-start | bytes 393220
  107.1 5.4 %collective-permute-start.4 = (bf16[1,4,8,8,128]{4,3,2,1,0:T(8,128)(2,1)S(1)}, bf16[1,4,8,8,128]{4,3,2,1,0:T(8,128)(2,1)S(1)}, u32[]{:S(2)}, u32[]{:S(2)}) collective-permute-start(bf16[1,4,8,8,128]{4,3,2,1,0:T(8,128)(2,1)S(1)} %get-tuple-element.57), channel_id=1, source_target_pairs={{0,16},{16,32},{32,48},{1,17},{17,33},{33,49},{2,18},{18,34},{34,5... | collective-permute-start | bytes 196616 | tf_op jit(solution)/shard_map/ppermute | solution.py:88
  110.6 6.2 %collective-permute-start.5 = (bf16[1,4,8,8,128]{4,3,2,1,0:T(8,128)(2,1)S(1)}, bf16[1,4,8,8,128]{4,3,2,1,0:T(8,128)(2,1)S(1)}, u32[]{:S(2)}, u32[]{:S(2)}) collective-permute-start(bf16[1,4,8,8,128]{4,3,2,1,0:T(8,128)(2,1)S(1)} %get-tuple-element.58), channel_id=1, source_target_pairs={{16,0},{32,16},{48,32},{17,1},{33,17},{49,33},{18,2},{34,18},{50,3... | collective-permute-start | bytes 196616 | tf_op jit(solution)/shard_map/ppermute | solution.py:89
  117.7 6.9 %collective-permute-start.6 = (bf16[1,16,4,8,128]{4,3,2,1,0:T(8,128)(2,1)S(1)}, bf16[1,16,4,8,128]{4,3,2,1,0:T(8,128)(2,1)S(1)}, u32[]{:S(2)}, u32[]{:S(2)}) collective-permute-start(bf16[1,16,4,8,128]{4,3,2,1,0:T(8,128)(2,1)S(1)} %get-tuple-element.55), channel_id=1, source_target_pairs={{0,1},{1,2},{2,3},{3,4},{4,5},{5,6},{6,7},{7,8},{8,9},{9,10},{10,1... | collective-permute-start | bytes 393224 | tf_op jit(solution)/shard_map/ppermute | solution.py:88
  120.5 8.1 %collective-permute-start.7 = (bf16[1,16,4,8,128]{4,3,2,1,0:T(8,128)(2,1)S(1)}, bf16[1,16,4,8,128]{4,3,2,1,0:T(8,128)(2,1)S(1)}, u32[]{:S(2)}, u32[]{:S(2)}) collective-permute-start(bf16[1,16,4,8,128]{4,3,2,1,0:T(8,128)(2,1)S(1)} %get-tuple-element.56), channel_id=1, source_target_pairs={{1,0},{2,1},{3,2},{4,3},{5,4},{6,5},{7,6},{8,7},{9,8},{10,9},{11,1... | collective-permute-start | bytes 393224 | tf_op jit(solution)/shard_map/ppermute | solution.py:89
Sparse Core Ops, SparseCore 0:
  9.5 40.9 all-gather.1

commit v3 on v2

--- a/solution.py
+++ b/solution.py
@@ -10,18 +10,25 @@
 
 
 def section_kernel(
-    m, n, cols, inner, num_frames, num_rows,
-    prior_ref, noise_ref, fm_ref, rm_ref, w_ref, out_ref, crop_ref, xl, xc, xr, nz,
+    m, n, cols, inner, num_frames, num_rows, total_frames, total_rows, k,
+    offs_ref, lv_ref, prior_ref, noise_ref, w_hbm, out_ref, crop_ref, w_ref, sem, xl, xc, xr, nz,
 ):
+    weight_copy = pltpu.make_async_copy(w_hbm.at[k], w_ref, sem)
+    weight_copy.start()
     channels = w_ref.shape[-1]
     rows_in = m * n * cols
     rows_out = (m - 2) * (n - 2) * cols
-    level = w_ref[13][0:1, :].astype(jnp.float32)
+    width = (m - num_frames) // 2
+    level = lv_ref[k]
     noisy = prior_ref[...].astype(jnp.float32) + level * noise_ref[...].astype(jnp.float32)
     mean_sq = jnp.mean(noisy * noisy, axis=-1, keepdims=True)
     normalized = (noisy * lax.rsqrt(mean_sq + 1e-05)).astype(jnp.bfloat16).astype(jnp.float32)
-    mask = fm_ref[...][:, 0:1, :] * rm_ref[...][None, :, :]
-    normalized = jnp.where(mask > 0, normalized.reshape(m, n * cols, channels), 0.0)
+    shape4 = (m, n, cols, channels)
+    frame_at = offs_ref[0] - width + lax.broadcasted_iota(jnp.int32, shape4, 0)
+    row_at = offs_ref[1] - width + lax.broadcasted_iota(jnp.int32, shape4, 1)
+    inside = (frame_at >= 0) & (frame_at < total_frames) & (row_at >= 0) & (row_at < total_rows)
+    inside = inside.reshape(m, n * cols, channels)
+    normalized = jnp.where(inside, normalized.reshape(m, n * cols, channels), 0.0)
     normalized = normalized.reshape(rows_in, channels)
     col = lax.broadcasted_iota(jnp.int32, (rows_in, channels), 0) % cols
     left = jnp.where(col == 0, 0.0, pltpu.roll(normalized, 1, 0))
@@ -30,6 +37,7 @@
     xc[...] = normalized.reshape(m, n * cols, channels)
     xr[...] = right.reshape(m, n * cols, channels)
     nz[...] = noisy.reshape(m, n * cols, channels)
+    weight_copy.wait()
     views = (xl, xc, xr)
     acc = jnp.zeros((rows_out, channels), jnp.float32)
     for tap in range(9):
@@ -51,32 +59,37 @@
     crop_ref[...] = crop.reshape(num_frames * num_rows * cols, channels).astype(crop_ref.dtype)
 
 
-def section_call(prior, noise, frame_mask, row_mask, weights, m, n, cols, num_frames, num_rows):
-    channels = weights.shape[-1]
+def section_call(offs, levels, prior, noise, packed, k, m, n, cols, num_frames, num_rows, totals):
+    channels = packed.shape[-1]
     rows_in = m * n * cols
     rows_out = (m - 2) * (n - 2) * cols
     rows_crop = num_frames * num_rows * cols
     inner = (m - 2 - num_frames) // 2
     flops = 2 * rows_out * channels * channels * 13
-    nbytes = 2 * 2 * rows_in * channels + 2 * 14 * channels * channels
+    nbytes = 2 * 2 * rows_in * channels + 2 * 13 * channels * channels
     nbytes += 2 * (rows_out + rows_crop) * channels
     scratch = pltpu.VMEM((m, n * cols, channels), jnp.float32)
+    smem = pl.BlockSpec(memory_space=pltpu.SMEM)
+    vmem = pl.BlockSpec(memory_space=pltpu.VMEM)
     return pl.pallas_call(
-        functools.partial(section_kernel, m, n, cols, inner, num_frames, num_rows),
+        functools.partial(
+            section_kernel, m, n, cols, inner, num_frames, num_rows, totals[0], totals[1], k
+        ),
         out_shape=(
             jax.ShapeDtypeStruct((rows_out, channels), jnp.bfloat16),
             jax.ShapeDtypeStruct((rows_crop, channels), jnp.bfloat16),
         ),
-        in_specs=[pl.BlockSpec(memory_space=pltpu.VMEM)] * 5,
-        out_specs=(
-            pl.BlockSpec(memory_space=pltpu.VMEM),
-            pl.BlockSpec(memory_space=pltpu.VMEM),
-        ),
-        scratch_shapes=[scratch] * 4,
+        in_specs=[smem, smem, vmem, vmem, pl.BlockSpec(memory_space=pl.ANY)],
+        out_specs=(vmem, vmem),
+        scratch_shapes=[
+            pltpu.VMEM(packed.shape[1:], packed.dtype),
+            pltpu.SemaphoreType.DMA(()),
+        ]
+        + [scratch] * 4,
         cost_estimate=pl.CostEstimate(
             flops=flops, bytes_accessed=nbytes, transcendentals=rows_out * channels
         ),
-    )(prior, noise, frame_mask, row_mask, weights)
+    )(offs, levels, prior, noise, packed)
 
 
 def extend(block, width, frame_dim, row_dim):
@@ -91,38 +104,24 @@
     return block
 
 
-def inside_masks(num_frames, num_rows, num_cols, channels, width):
-    frame_place = lax.axis_index("frames")
-    row_place = lax.axis_index("space")
-    total_frames = num_frames * lax.axis_size("frames")
-    total_rows = num_rows * lax.axis_size("space")
-    frames = frame_place * num_frames - width + jnp.arange(num_frames + 2 * width)
-    rows = row_place * num_rows - width + jnp.arange(num_rows + 2 * width)
-    frame_ok = ((frames >= 0) & (frames < total_frames)).astype(jnp.float32)
-    row_ok = ((rows >= 0) & (rows < total_rows)).astype(jnp.float32)
-    frame_mask = jnp.broadcast_to(frame_ok[:, None, None], (num_frames + 2 * width, 8, channels))
-    row_mask = jnp.broadcast_to(
-        row_ok[:, None, None], (num_rows + 2 * width, num_cols, channels)
-    ).reshape(-1, channels)
-    return frame_mask, row_mask
-
-
-def denoise(previous, noise_part, weights, masks, num_frames, num_rows):
+def denoise(offs, levels, previous, noise_part, packed, k, num_frames, num_rows, totals):
     num_videos, m, n, num_cols, channels = previous.shape
     outs = []
     crops = []
     for v in range(num_videos):
         out, crop = section_call(
+            offs,
+            levels,
             previous[v].reshape(-1, channels),
             noise_part[v].reshape(-1, channels),
-            masks[0],
-            masks[1],
-            weights,
+            packed,
+            k,
             m,
             n,
             num_cols,
             num_frames,
             num_rows,
+            totals,
         )
         outs.append(out.reshape(m - 2, n - 2, num_cols, channels))
         crops.append(crop)
@@ -148,30 +147,33 @@
     )
     packed = lax.all_gather(packed, "section", tiled=True)
     incoming = lax.dynamic_slice_in_dim(base_frames, place * per_device, per_device, 0)
+    levels = packed[:, 13, 0, 0].astype(jnp.float32)
+    offs = jnp.stack(
+        [lax.axis_index("frames") * num_frames, lax.axis_index("space") * num_rows]
+    ).astype(jnp.int32)
+    totals = (num_frames * lax.axis_size("frames"), num_rows * lax.axis_size("space"))
     both = extend(jnp.concatenate([incoming[None], noise_t[:halo]], axis=0), halo, 2, 3)
     prior_ext = both[0]
-    noise_parts = [both[1:]]
-    for start in range(halo, sections, halo):
-        noise_parts.append(extend(noise_t[start : start + halo], halo, 2, 3))
-    noise_ext = jnp.concatenate(noise_parts, axis=0)
-    num_cols, channels = base_frames.shape[3:]
-    masks = [
-        inside_masks(num_frames, num_rows, num_cols, channels, w) for w in range(halo + 1)
-    ]
+    noise_round = both[1:]
     results = []
     for k in range(sections):
         j = k % halo
         if j == 0 and k > 0:
             prior_ext = extend(prior_ext, halo, 1, 2)
+            noise_round = noise_next
         width = halo - j
         cut = halo - width
-        noise_here = noise_ext[
-            k, :, cut : cut + num_frames + 2 * width, cut : cut + num_rows + 2 * width
+        noise_here = noise_round[
+            j, :, cut : cut + num_frames + 2 * width, cut : cut + num_rows + 2 * width
         ]
         prior_ext, crop = denoise(
-            prior_ext, noise_here, packed[k], masks[width], num_frames, num_rows
+            offs, levels, prior_ext, noise_here, packed, k, num_frames, num_rows, totals
         )
         results.append(crop)
+        if j == 0 and k + halo < sections:
+            later, _ = lax.optimization_barrier((noise_t[k + halo : k + 2 * halo], crop))
+            noise_next = extend(later, halo, 2, 3)
+    num_cols, channels = base_frames.shape[3:]
     stacked = jnp.stack(results).reshape(
         (sections, per_device, num_frames, num_rows, num_cols, channels)
     )

time: 174 us -> 171 us (0.983)
  blocking collectives: 18.5 us -> 38.9 us
  waiting for transfers between devices: 43.3 us -> 27.1 us
  local copies, waits for them, and re-layouts: 18.2 us -> 8.14 us
  Pallas kernels: 27.4 us -> 32.4 us
  starting transfers between devices: 39.7 us -> 35.4 us
  other arithmetic: 11.6 us -> 13.5 us
    all_to_all x0 -> x1, blocking collectives: none -> 20.4 us  [on_device(): noise_t = lax.all_to_all(section_noise[0], 'section', 0, 0, tiled=True)]
    all_to_all x1 -> x0, waiting for transfers between devices: 15.9 us -> none  [on_device(): noise_t = lax.all_to_all(section_noise[0], 'section', 0, 0, tiled=True)]
    broadcast_in_dim x16 -> x0, local copies, waits for them, and re-layouts: 6.21 us -> none  [the longest x12 3.42 us: inside_masks(): jnp.broadcast_to(row_ok[:, None, None], (num_rows + 2 * width, num_cols,...]
    pallas_call x8, Pallas kernels: 27.4 us -> 32.4 us  [section_call(): pl.pallas_call(functools.partial(section_kernel, m, n, cols, inner, num_f...]
    all_to_all x1 -> x0, starting transfers between devices: 4.31 us -> none  [on_device(): noise_t = lax.all_to_all(section_noise[0], 'section', 0, 0, tiled=True)]
    squeeze x1 -> x0, local copies, waits for them, and re-layouts: 3.88 us -> none  [on_device(): packed[k]]
  transfers between devices with their start and end apart: 14 -> 13, of which waited for: 11 -> 9; matrix products, arithmetic and copies ran while one was open for 6% -> 6% of each run, Pallas kernels for 0% -> 0%
where the time goes in v3:
time: 171 us; the launch traced here: 170 us
  blocking collectives  38.9 us (23%)
  starting transfers between devices  35.4 us (21%)
  Pallas kernels  32.4 us (19%)
  waiting for transfers between devices  27.1 us (16%)
  between operations  14.5 us (8%)
  other arithmetic  13.5 us (8%)
  local copies, waits for them, and re-layouts  8.14 us (5%)
    pallas_call x8, Pallas kernels, section_call(): pl.pallas_call(functools.partial(section_kernel, m, n, cols, inner, num_f...  32.4 us
    ppermute x6, starting transfers between devices, extend(): lax.ppermute(lax.slice_in_dim(block, size - width, size, axis=dim), axis,...  24.5 us
    ppermute x6, waiting for transfers between devices, extend(): lax.ppermute(lax.slice_in_dim(block, 0, width, axis=dim), axis, backward)  21.4 us
    all_to_all x1, blocking collectives, on_device(): noise_t = lax.all_to_all(section_noise[0], 'section', 0, 0, tiled=True)  20.4 us
    all_to_all x1, blocking collectives, on_device(): return lax.all_to_all(stacked, 'section', 0, 1, tiled=True)  18.5 us
    ppermute x6, starting transfers between devices, extend(): lax.ppermute(lax.slice_in_dim(block, 0, width, axis=dim), axis, backward)  10.9 us
    ppermute x6, waiting for transfers between devices, extend(): lax.ppermute(lax.slice_in_dim(block, size - width, size, axis=dim), axis,...  5.68 us
    concatenate x6, other arithmetic, extend(): block = jnp.concatenate([low, block, high], axis=dim)  4.85 us
  transfers between devices with their start and end apart: 13, of which 9 were waited for; matrix products, arithmetic and copies ran while one was open for 6% of the time, Pallas kernels for 0%

profile of v3, /device:TPU:96, one launch (start us, length us, event | category | flops | bytes accessed | tf_op | source)
XLA Modules:
  0.0 170.0 jit_solution(10606350196363893740)
XLA Ops:
  7.4 1.9 %maximum_maximum_fusion = bf16[1,14,128,128]{3,2,1,0:T(8,128)(2,1)} fusion(bf16[1,1,128,128]{3,2,1,0:T(8,128)(2,1)} %bitcast.54, bf16[1,3,128,128]{3,2,1,0:T(8,128)(2,1)} %param.10, bf16[1,9,128,128]{3,2,1,0:T(8,128)(2,1)} %param.9, bf16[14]{0:T(256)(128)(2,1)S(1)} %pad.31.clone), kind=kLoop, calls=%fused_computation.9 | loop fusion | flops 688128 | bytes 884764 | tf_op jit(solution)/shard_map/concatenate | solution.py:145
  9.3 20.4 %all_to_all.17 = bf16[8,8,8,8,128]{4,3,2,1,0:T(8,128)(2,1)S(1)} all-to-all(bf16[8,8,8,8,128]{4,3,2,1,0:T(8,128)(2,1)} %bitcast.43), channel_id=1, replica_groups=mesh['section'=8,'frames'=4,'space'=16] {'section'}, dimensions={0} | all-to-all | bytes 2097152 | tf_op jit(solution)/shard_map/all_to_all | solution.py:139
  29.8 3.5 %collective-permute-start.8 = (bf16[4,1,4,8,8,128]{5,4,3,2,0,1:T(8,128)(2,1)S(1)}, bf16[4,1,4,8,8,128]{5,4,3,2,0,1:T(8,128)(2,1)S(1)}, u32[]{:S(2)}, u32[]{:S(2)}) collective-permute-start(bf16[4,1,4,8,8,128]{5,4,3,2,0,1:T(8,128)(2,1)S(1)} %get-tuple-element.45), channel_id=1, source_target_pairs={{0,16},{16,32},{32,48},{1,17},{17,33},{33,49},{2,18},{18,34},{34,5... | collective-permute-start | bytes 786440 | tf_op jit(solution)/shard_map/ppermute | solution.py:101
  33.3 1.3 collective-permute-start.9
  34.8 4.6 %collective-permute-start = (bf16[5,1,4,8,8,128]{5,4,3,2,0,1:T(8,128)(2,1)S(1)}, bf16[5,1,4,8,8,128]{5,4,3,2,0,1:T(8,128)(2,1)S(1)}, u32[]{:S(2)}, u32[]{:S(2)}) collective-permute-start(bf16[5,1,4,8,8,128]{5,4,3,2,0,1:T(8,128)(2,1)S(1)} %get-tuple-element.43), channel_id=1, source_target_pairs={{0,16},{16,32},{32,48},{1,17},{17,33},{33,49},{2,18},{18,34},{34,5... | collective-permute-start | bytes 983048 | tf_op jit(solution)/shard_map/ppermute | solution.py:101
  39.3 1.3 collective-permute-start.1
  40.6 2.1 %collective-permute-done.9 = bf16[4,1,4,8,8,128]{5,4,3,2,0,1:T(8,128)(2,1)S(1)} collective-permute-done((bf16[4,1,4,8,8,128]{5,4,3,2,0,1:T(8,128)(2,1)S(1)}, bf16[4,1,4,8,8,128]{5,4,3,2,0,1:T(8,128)(2,1)S(1)}, u32[]{:S(2)}, u32[]{:S(2)}) %collective-permute-start.9) | collective-permute-done | bytes 262176 | tf_op jit(solution)/shard_map/ppermute | solution.py:102
  43.0 5.0 %collective-permute-start.10 = (bf16[4,1,16,4,8,128]{5,4,3,2,0,1:T(8,128)(2,1)S(1)}, bf16[4,1,16,4,8,128]{5,4,3,2,0,1:T(8,128)(2,1)S(1)}, u32[]{:S(2)}, u32[]{:S(2)}) collective-permute-start(bf16[4,1,16,4,8,128]{5,4,3,2,0,1:T(8,128)(2,1)S(1)} %get-tuple-element.39), channel_id=1, source_target_pairs={{0,1},{1,2},{2,3},{3,4},{4,5},{5,6},{6,7},{7,8},{8,9},{9,10},{10,1... | collective-permute-start | bytes 1572872 | tf_op jit(solution)/shard_map/ppermute | solution.py:101
  48.0 1.9 %collective-permute-start.11 = (bf16[4,1,16,4,8,128]{5,4,3,2,0,1:T(8,128)(2,1)S(1)}, bf16[4,1,16,4,8,128]{5,4,3,2,0,1:T(8,128)(2,1)S(1)}, u32[]{:S(2)}, u32[]{:S(2)}) collective-permute-start(bf16[4,1,16,4,8,128]{5,4,3,2,0,1:T(8,128)(2,1)S(1)} %get-tuple-element.40), channel_id=1, source_target_pairs={{1,0},{2,1},{3,2},{4,3},{5,4},{6,5},{7,6},{8,7},{9,8},{10,9},{11,1... | collective-permute-start | bytes 1572872 | tf_op jit(solution)/shard_map/ppermute | solution.py:102
  50.4 5.1 %collective-permute-start.2 = (bf16[5,1,16,4,8,128]{5,4,3,2,0,1:T(8,128)(2,1)S(1)}, bf16[5,1,16,4,8,128]{5,4,3,2,0,1:T(8,128)(2,1)S(1)}, u32[]{:S(2)}, u32[]{:S(2)}) collective-permute-start(bf16[5,1,16,4,8,128]{5,4,3,2,0,1:T(8,128)(2,1)S(1)} %get-tuple-element.37), channel_id=1, source_target_pairs={{0,1},{1,2},{2,3},{3,4},{4,5},{5,6},{6,7},{7,8},{8,9},{9,10},{10,1... | collective-permute-start | bytes 1966088 | tf_op jit(solution)/shard_map/ppermute | solution.py:101
  55.6 1.9 %collective-permute-start.3 = (bf16[5,1,16,4,8,128]{5,4,3,2,0,1:T(8,128)(2,1)S(1)}, bf16[5,1,16,4,8,128]{5,4,3,2,0,1:T(8,128)(2,1)S(1)}, u32[]{:S(2)}, u32[]{:S(2)}) collective-permute-start(bf16[5,1,16,4,8,128]{5,4,3,2,0,1:T(8,128)(2,1)S(1)} %get-tuple-element.38), channel_id=1, source_target_pairs={{1,0},{2,1},{3,2},{4,3},{5,4},{6,5},{7,6},{8,7},{9,8},{10,9},{11,1... | collective-permute-start | bytes 1966088 | tf_op jit(solution)/shard_map/ppermute | solution.py:102
  58.1 2.2 %collective-permute-done.10 = bf16[4,1,16,4,8,128]{5,4,3,2,0,1:T(8,128)(2,1)S(1)} collective-permute-done((bf16[4,1,16,4,8,128]{5,4,3,2,0,1:T(8,128)(2,1)S(1)}, bf16[4,1,16,4,8,128]{5,4,3,2,0,1:T(8,128)(2,1)S(1)}, u32[]{:S(2)}, u32[]{:S(2)}) %collective-permute-start.10) | collective-permute-done | bytes 524320 | tf_op jit(solution)/shard_map/ppermute | solution.py:101
  60.4 5.6 %collective-permute-done.11 = bf16[4,1,16,4,8,128]{5,4,3,2,0,1:T(8,128)(2,1)S(1)} collective-permute-done((bf16[4,1,16,4,8,128]{5,4,3,2,0,1:T(8,128)(2,1)S(1)}, bf16[4,1,16,4,8,128]{5,4,3,2,0,1:T(8,128)(2,1)S(1)}, u32[]{:S(2)}, u32[]{:S(2)}) %collective-permute-start.11) | collective-permute-done | bytes 524320 | tf_op jit(solution)/shard_map/ppermute | solution.py:102
  66.3 0.8 slice.126
  67.1 0.7 pad_maximum_fusion.11
  67.8 0.8 pad_maximum_fusion.8
  68.6 0.8 pad_maximum_fusion.5
  69.4 2.2 %collective-permute-done.2 = bf16[5,1,16,4,8,128]{5,4,3,2,0,1:T(8,128)(2,1)S(1)} collective-permute-done((bf16[5,1,16,4,8,128]{5,4,3,2,0,1:T(8,128)(2,1)S(1)}, bf16[5,1,16,4,8,128]{5,4,3,2,0,1:T(8,128)(2,1)S(1)}, u32[]{:S(2)}, u32[]{:S(2)}) %collective-permute-start.2) | collective-permute-done | bytes 655392 | tf_op jit(solution)/shard_map/ppermute | solution.py:101
  71.6 5.3 %collective-permute-done.3 = bf16[5,1,16,4,8,128]{5,4,3,2,0,1:T(8,128)(2,1)S(1)} collective-permute-done((bf16[5,1,16,4,8,128]{5,4,3,2,0,1:T(8,128)(2,1)S(1)}, bf16[5,1,16,4,8,128]{5,4,3,2,0,1:T(8,128)(2,1)S(1)}, u32[]{:S(2)}, u32[]{:S(2)}) %collective-permute-start.3) | collective-permute-done | bytes 655392 | tf_op jit(solution)/shard_map/ppermute | solution.py:102
  77.7 0.8 pad_maximum_fusion.9
  78.5 0.8 pad_maximum_fusion.6
  79.3 2.5 %pad_maximum_fusion = bf16[5,1,16,16,8,128]{5,4,3,2,0,1:T(8,128)(2,1)S(1)} fusion(bf16[5,1,16,4,8,128]{5,4,3,2,0,1:T(8,128)(2,1)S(1)} %collective-permute-done.3, bf16[5,1,4,8,8,128]{5,4,3,2,0,1:T(8,128)(2,1)S(1)} %collective-permute-done.1, bf16[4,1,8,8,8,128]{5,4,3,2,0,1:T(8,128)(2,1)S(1)} %get-tuple-element.42, ...), kind=kLoop, calls=%fused_computation | loop fusion | flops 6553600 | bytes 5242880 | tf_op jit(solution)/shard_map/concatenate | solution.py:103
  81.8 1.1 fusion.2
  82.8 1.4 fusion.1.lv_ref
  84.2 4.7 %shard_map.64 = (bf16[1568,128]{1,0:T(8,128)(2,1)}, bf16[512,128]{1,0:T(8,128)(2,1)}) custom-call(s32[2]{0:T(128)} %pad_add_fusion.offs_ref, f32[8]{0:T(128)} %fusion.1.lv_ref, bf16[2048,128]{1,0:T(8,128)(2,1)} %bitcast.35, bf16[2048,128]{1,0:T(8,128)(2,1)} %bitcast.34, bf16[8,14,128,128]{3,2,1,0:T(8,128)(2,1)} %all-gather.2.cloned.1.call-done.w_hbm), custom_call_target="tpu_custom_call" | custom-call | flops 667942912 | bytes 2007040 | tf_op jit(solution)/shard_map/pallas_call | solution.py:74
  88.9 4.2 %shard_map.65 = (bf16[1152,128]{1,0:T(8,128)(2,1)}, bf16[512,128]{1,0:T(8,128)(2,1)}) custom-call(s32[2]{0:T(128)} %pad_add_fusion.offs_ref, f32[8]{0:T(128)} %fusion.1.lv_ref, bf16[1568,128]{1,0:T(8,128)(2,1)} %get-tuple-element.21.prior_ref, bf16[1568,128]{1,0:T(8,128)(2,1)} %bitcast.37, bf16[8,14,128,128]{3,2,1,0:T(8,128)(2,1)} %all-gather.2.cloned.1.call-done.w_hbm), custom_call_target="tpu_custom_call" | custom-call | flops 490733568 | bytes 1654784 | tf_op jit(solution)/shard_map/pallas_call | solution.py:74
  93.1 3.8 %shard_map.66 = (bf16[800,128]{1,0:T(8,128)(2,1)}, bf16[512,128]{1,0:T(8,128)(2,1)}) custom-call(s32[2]{0:T(128)} %pad_add_fusion.offs_ref, f32[8]{0:T(128)} %fusion.1.lv_ref, bf16[1152,128]{1,0:T(8,128)(2,1)} %get-tuple-element.23.prior_ref, bf16[1152,128]{1,0:T(8,128)(2,1)} %bitcast.39, bf16[8,14,128,128]{3,2,1,0:T(8,128)(2,1)} %all-gather.2.cloned.1.call-done.w_hbm), custom_call_target="tpu_custom_call" | custom-call | flops 340787200 | bytes 1351680 | tf_op jit(solution)/shard_map/pallas_call | solution.py:74
  96.9 3.6 %shard_map.67 = (bf16[512,128]{1,0:T(8,128)(2,1)}, bf16[512,128]{1,0:T(8,128)(2,1)}) custom-call(s32[2]{0:T(128)} %pad_add_fusion.offs_ref, f32[8]{0:T(128)} %fusion.1.lv_ref, bf16[800,128]{1,0:T(8,128)(2,1)} %get-tuple-element.25.prior_ref, bf16[800,128]{1,0:T(8,128)(2,1)} %bitcast.45, bf16[8,14,128,128]{3,2,1,0:T(8,128)(2,1)} %all-gather.2.cloned.1.call-done.w_hbm), custom_call_target="tpu_custom_call" | custom-call | flops 218103808 | bytes 1097728 | tf_op jit(solution)/shard_map/pallas_call | solution.py:74
  100.5 0.9 fusion.7
  101.4 3.5 %collective-permute-start.4 = (bf16[1,4,8,8,128]{4,3,2,1,0:T(8,128)(2,1)S(1)}, bf16[1,4,8,8,128]{4,3,2,1,0:T(8,128)(2,1)S(1)}, u32[]{:S(2)}, u32[]{:S(2)}) collective-permute-start(bf16[1,4,8,8,128]{4,3,2,1,0:T(8,128)(2,1)S(1)} %get-tuple-element.49), channel_id=1, source_target_pairs={{0,16},{16,32},{32,48},{1,17},{17,33},{33,49},{2,18},{18,34},{34,5... | collective-permute-start | bytes 196616 | tf_op jit(solution)/shard_map/ppermute | solution.py:101
  104.9 1.3 collective-permute-start.5
  106.8 4.3 %collective-permute-done.5 = bf16[1,4,8,8,128]{4,3,2,1,0:T(8,128)(2,1)S(1)} collective-permute-done((bf16[1,4,8,8,128]{4,3,2,1,0:T(8,128)(2,1)S(1)}, bf16[1,4,8,8,128]{4,3,2,1,0:T(8,128)(2,1)S(1)}, u32[]{:S(2)}, u32[]{:S(2)}) %collective-permute-start.5) | collective-permute-done | bytes 65568 | tf_op jit(solution)/shard_map/ppermute | solution.py:102
  111.0 0.9 pad_maximum_fusion.10
  112.0 2.8 %collective-permute-start.6 = (bf16[1,16,4,8,128]{4,3,2,1,0:T(8,128)(2,1)S(1)}, bf16[1,16,4,8,128]{4,3,2,1,0:T(8,128)(2,1)S(1)}, u32[]{:S(2)}, u32[]{:S(2)}) collective-permute-start(bf16[1,16,4,8,128]{4,3,2,1,0:T(8,128)(2,1)S(1)} %get-tuple-element.47), channel_id=1, source_target_pairs={{0,1},{1,2},{2,3},{3,4},{4,5},{5,6},{6,7},{7,8},{8,9},{9,10},{10,1... | collective-permute-start | bytes 393224 | tf_op jit(solution)/shard_map/ppermute | solution.py:101
  114.8 3.2 %collective-permute-start.7 = (bf16[1,16,4,8,128]{4,3,2,1,0:T(8,128)(2,1)S(1)}, bf16[1,16,4,8,128]{4,3,2,1,0:T(8,128)(2,1)S(1)}, u32[]{:S(2)}, u32[]{:S(2)}) collective-permute-start(bf16[1,16,4,8,128]{4,3,2,1,0:T(8,128)(2,1)S(1)} %get-tuple-element.48), channel_id=1, source_target_pairs={{1,0},{2,1},{3,2},{4,3},{5,4},{6,5},{7,6},{8,7},{9,8},{10,9},{11,1... | collective-permute-start | bytes 393224 | tf_op jit(solution)/shard_map/ppermute | solution.py:102
  118.1 0.7 collective-permute-done.6
  118.9 4.0 %collective-permute-done.7 = bf16[1,16,4,8,128]{4,3,2,1,0:T(8,128)(2,1)S(1)} collective-permute-done((bf16[1,16,4,8,128]{4,3,2,1,0:T(8,128)(2,1)S(1)}, bf16[1,16,4,8,128]{4,3,2,1,0:T(8,128)(2,1)S(1)}, u32[]{:S(2)}, u32[]{:S(2)}) %collective-permute-start.7) | collective-permute-done | bytes 131104 | tf_op jit(solution)/shard_map/ppermute | solution.py:102
  122.9 0.9 pad_maximum_fusion.4
  123.8 4.7 %shard_map.68 = (bf16[1568,128]{1,0:T(8,128)(2,1)}, bf16[512,128]{1,0:T(8,128)(2,1)}) custom-call(s32[2]{0:T(128)} %pad_add_fusion.offs_ref, f32[8]{0:T(128)} %fusion.1.lv_ref, bf16[2048,128]{1,0:T(8,128)(2,1)} %bitcast.33, bf16[2048,128]{1,0:T(8,128)(2,1)} %bitcast.32, bf16[8,14,128,128]{3,2,1,0:T(8,128)(2,1)} %all-gather.2.cloned.1.call-done.w_hbm), custom_call_target="tpu_custom_call" | custom-call | flops 667942912 | bytes 2007040 | tf_op jit(solution)/shard_map/pallas_call | solution.py:74
  128.5 0.9 constant_dynamic-update-slice_fusion.3
  129.4 4.2 %shard_map.69 = (bf16[1152,128]{1,0:T(8,128)(2,1)}, bf16[512,128]{1,0:T(8,128)(2,1)}) custom-call(s32[2]{0:T(128)} %pad_add_fusion.offs_ref, f32[8]{0:T(128)} %fusion.1.lv_ref, bf16[1568,128]{1,0:T(8,128)(2,1)} %get-tuple-element.29.prior_ref, bf16[1568,128]{1,0:T(8,128)(2,1)} %bitcast.36, bf16[8,14,128,128]{3,2,1,0:T(8,128)(2,1)} %all-gather.2.cloned.1.call-done.w_hbm), custom_call_target="tpu_custom_call" | custom-call | flops 490733568 | bytes 1654784 | tf_op jit(solution)/shard_map/pallas_call | solution.py:74
  133.6 0.9 constant_dynamic-update-slice_fusion.2
  134.5 3.8 %shard_map.70 = (bf16[800,128]{1,0:T(8,128)(2,1)}, bf16[512,128]{1,0:T(8,128)(2,1)}) custom-call(s32[2]{0:T(128)} %pad_add_fusion.offs_ref, f32[8]{0:T(128)} %fusion.1.lv_ref, bf16[1152,128]{1,0:T(8,128)(2,1)} %get-tuple-element.31.prior_ref, bf16[1152,128]{1,0:T(8,128)(2,1)} %bitcast.38, bf16[8,14,128,128]{3,2,1,0:T(8,128)(2,1)} %all-gather.2.cloned.1.call-done.w_hbm), custom_call_target="tpu_custom_call" | custom-call | flops 340787200 | bytes 1351680 | tf_op jit(solution)/shard_map/pallas_call | solution.py:74
  138.3 0.9 constant_dynamic-update-slice_fusion.1
  139.2 3.5 %shard_map.71 = (bf16[512,128]{1,0:T(8,128)(2,1)}, bf16[512,128]{1,0:T(8,128)(2,1)}) custom-call(s32[2]{0:T(128)} %pad_add_fusion.offs_ref, f32[8]{0:T(128)} %fusion.1.lv_ref, bf16[800,128]{1,0:T(8,128)(2,1)} %get-tuple-element.33.prior_ref, bf16[800,128]{1,0:T(8,128)(2,1)} %bitcast.44, bf16[8,14,128,128]{3,2,1,0:T(8,128)(2,1)} %all-gather.2.cloned.1.call-done.w_hbm), custom_call_target="tpu_custom_call" | custom-call | flops 218103808 | bytes 1097728 | tf_op jit(solution)/shard_map/pallas_call | solution.py:74
  142.7 0.9 constant_dynamic-update-slice_fusion
  143.7 18.5 %all_to_all.18 = bf16[8,1,8,8,8,128]{5,4,3,2,1,0:T(8,128)(2,1)S(1)} all-to-all(bf16[8,1,8,8,8,128]{5,4,3,2,1,0:T(8,128)(2,1)S(1)} %constant_dynamic-update-slice_fusion), channel_id=1, replica_groups=mesh['section'=8,'frames'=4,'space'=16] {'section'}, dimensions={0} | all-to-all | bytes 2097152 | tf_op jit(solution)/shard_map/all_to_all | solution.py:180
  162.2 1.0 copy.32
  (36 shorter events, 3.2 us)
Async XLA Ops:
  6.5 28.1 %copy-start = (bf16[8,8,8,8,128]{4,3,2,1,0:T(8,128)(2,1)S(1)}, bf16[8,8,8,8,128]{4,3,2,1,0:T(8,128)(2,1)}, u32[]{:S(2)}) copy-start(bf16[8,8,8,8,128]{4,3,2,1,0:T(8,128)(2,1)} %param.6) | copy-start | bytes 3145732
  6.5 76.3 %all-gather.2.cloned.1.call-start = ((), (), s32[]{:S(2)}) async-start(), calls=%async_computation.2 | async-start | bytes 4128768 | tf_op jit(solution)/shard_map/all_gather | solution.py:148
  29.8 10.8 %collective-permute-start.8 = (bf16[4,1,4,8,8,128]{5,4,3,2,0,1:T(8,128)(2,1)S(1)}, bf16[4,1,4,8,8,128]{5,4,3,2,0,1:T(8,128)(2,1)S(1)}, u32[]{:S(2)}, u32[]{:S(2)}) collective-permute-start(bf16[4,1,4,8,8,128]{5,4,3,2,0,1:T(8,128)(2,1)S(1)} %get-tuple-element.45), channel_id=1, source_target_pairs={{0,16},{16,32},{32,48},{1,17},{17,33},{33,49},{2,18},{18,34},{34,5... | collective-permute-start | bytes 786440 | tf_op jit(solution)/shard_map/ppermute | solution.py:101
  33.3 9.4 %collective-permute-start.9 = (bf16[4,1,4,8,8,128]{5,4,3,2,0,1:T(8,128)(2,1)S(1)}, bf16[4,1,4,8,8,128]{5,4,3,2,0,1:T(8,128)(2,1)S(1)}, u32[]{:S(2)}, u32[]{:S(2)}) collective-permute-start(bf16[4,1,4,8,8,128]{5,4,3,2,0,1:T(8,128)(2,1)S(1)} %get-tuple-element.46), channel_id=1, source_target_pairs={{16,0},{32,16},{48,32},{17,1},{33,17},{49,33},{18,2},{34,18},{50,3... | collective-permute-start | bytes 786440 | tf_op jit(solution)/shard_map/ppermute | solution.py:102
  34.8 15.2 %collective-permute-start = (bf16[5,1,4,8,8,128]{5,4,3,2,0,1:T(8,128)(2,1)S(1)}, bf16[5,1,4,8,8,128]{5,4,3,2,0,1:T(8,128)(2,1)S(1)}, u32[]{:S(2)}, u32[]{:S(2)}) collective-permute-start(bf16[5,1,4,8,8,128]{5,4,3,2,0,1:T(8,128)(2,1)S(1)} %get-tuple-element.43), channel_id=1, source_target_pairs={{0,16},{16,32},{32,48},{1,17},{17,33},{33,49},{2,18},{18,34},{34,5... | collective-permute-start | bytes 983048 | tf_op jit(solution)/shard_map/ppermute | solution.py:101
  39.3 10.6 %collective-permute-start.1 = (bf16[5,1,4,8,8,128]{5,4,3,2,0,1:T(8,128)(2,1)S(1)}, bf16[5,1,4,8,8,128]{5,4,3,2,0,1:T(8,128)(2,1)S(1)}, u32[]{:S(2)}, u32[]{:S(2)}) collective-permute-start(bf16[5,1,4,8,8,128]{5,4,3,2,0,1:T(8,128)(2,1)S(1)} %get-tuple-element.44), channel_id=1, source_target_pairs={{16,0},{32,16},{48,32},{17,1},{33,17},{49,33},{18,2},{34,18},{50,3... | collective-permute-start | bytes 983048 | tf_op jit(solution)/shard_map/ppermute | solution.py:102
  43.0 17.4 %collective-permute-start.10 = (bf16[4,1,16,4,8,128]{5,4,3,2,0,1:T(8,128)(2,1)S(1)}, bf16[4,1,16,4,8,128]{5,4,3,2,0,1:T(8,128)(2,1)S(1)}, u32[]{:S(2)}, u32[]{:S(2)}) collective-permute-start(bf16[4,1,16,4,8,128]{5,4,3,2,0,1:T(8,128)(2,1)S(1)} %get-tuple-element.39), channel_id=1, source_target_pairs={{0,1},{1,2},{2,3},{3,4},{4,5},{5,6},{6,7},{7,8},{8,9},{9,10},{10,1... | collective-permute-start | bytes 1572872 | tf_op jit(solution)/shard_map/ppermute | solution.py:101
  48.0 18.0 %collective-permute-start.11 = (bf16[4,1,16,4,8,128]{5,4,3,2,0,1:T(8,128)(2,1)S(1)}, bf16[4,1,16,4,8,128]{5,4,3,2,0,1:T(8,128)(2,1)S(1)}, u32[]{:S(2)}, u32[]{:S(2)}) collective-permute-start(bf16[4,1,16,4,8,128]{5,4,3,2,0,1:T(8,128)(2,1)S(1)} %get-tuple-element.40), channel_id=1, source_target_pairs={{1,0},{2,1},{3,2},{4,3},{5,4},{6,5},{7,6},{8,7},{9,8},{10,9},{11,1... | collective-permute-start | bytes 1572872 | tf_op jit(solution)/shard_map/ppermute | solution.py:102
  50.4 21.2 %collective-permute-start.2 = (bf16[5,1,16,4,8,128]{5,4,3,2,0,1:T(8,128)(2,1)S(1)}, bf16[5,1,16,4,8,128]{5,4,3,2,0,1:T(8,128)(2,1)S(1)}, u32[]{:S(2)}, u32[]{:S(2)}) collective-permute-start(bf16[5,1,16,4,8,128]{5,4,3,2,0,1:T(8,128)(2,1)S(1)} %get-tuple-element.37), channel_id=1, source_target_pairs={{0,1},{1,2},{2,3},{3,4},{4,5},{5,6},{6,7},{7,8},{8,9},{9,10},{10,1... | collective-permute-start | bytes 1966088 | tf_op jit(solution)/shard_map/ppermute | solution.py:101
  55.6 21.4 %collective-permute-start.3 = (bf16[5,1,16,4,8,128]{5,4,3,2,0,1:T(8,128)(2,1)S(1)}, bf16[5,1,16,4,8,128]{5,4,3,2,0,1:T(8,128)(2,1)S(1)}, u32[]{:S(2)}, u32[]{:S(2)}) collective-permute-start(bf16[5,1,16,4,8,128]{5,4,3,2,0,1:T(8,128)(2,1)S(1)} %get-tuple-element.38), channel_id=1, source_target_pairs={{1,0},{2,1},{3,2},{4,3},{5,4},{6,5},{7,6},{8,7},{9,8},{10,9},{11,1... | collective-permute-start | bytes 1966088 | tf_op jit(solution)/shard_map/ppermute | solution.py:102
  96.9 9.3 %copy-start.4 = (bf16[512,128]{1,0:T(8,128)(2,1)S(1)}, bf16[512,128]{1,0:T(8,128)(2,1)}, u32[]{:S(2)}) copy-start(bf16[512,128]{1,0:T(8,128)(2,1)} %get-tuple-element.20) | copy-start | bytes 393220
  96.9 9.3 %copy-start.5 = (bf16[512,128]{1,0:T(8,128)(2,1)S(1)}, bf16[512,128]{1,0:T(8,128)(2,1)}, u32[]{:S(2)}) copy-start(bf16[512,128]{1,0:T(8,128)(2,1)} %get-tuple-element.22) | copy-start | bytes 393220
  96.9 21.2 %copy-start.2 = (bf16[512,128]{1,0:T(8,128)(2,1)S(1)}, bf16[512,128]{1,0:T(8,128)(2,1)}, u32[]{:S(2)}) copy-start(bf16[512,128]{1,0:T(8,128)(2,1)} %get-tuple-element.24) | copy-start | bytes 393220
  100.5 17.6 %copy-start.3 = (bf16[512,128]{1,0:T(8,128)(2,1)S(1)}, bf16[512,128]{1,0:T(8,128)(2,1)}, u32[]{:S(2)}) copy-start(bf16[512,128]{1,0:T(8,128)(2,1)} %get-tuple-element.26) | copy-start | bytes 393220
  100.5 22.4 %copy-start.1 = (bf16[512,128]{1,0:T(8,128)(2,1)S(1)}, bf16[512,128]{1,0:T(8,128)(2,1)}, u32[]{:S(2)}) copy-start(bf16[512,128]{1,0:T(8,128)(2,1)} %get-tuple-element.27) | copy-start | bytes 393220
  101.4 5.4 %collective-permute-start.4 = (bf16[1,4,8,8,128]{4,3,2,1,0:T(8,128)(2,1)S(1)}, bf16[1,4,8,8,128]{4,3,2,1,0:T(8,128)(2,1)S(1)}, u32[]{:S(2)}, u32[]{:S(2)}) collective-permute-start(bf16[1,4,8,8,128]{4,3,2,1,0:T(8,128)(2,1)S(1)} %get-tuple-element.49), channel_id=1, source_target_pairs={{0,16},{16,32},{32,48},{1,17},{17,33},{33,49},{2,18},{18,34},{34,5... | collective-permute-start | bytes 196616 | tf_op jit(solution)/shard_map/ppermute | solution.py:101
  104.9 6.2 %collective-permute-start.5 = (bf16[1,4,8,8,128]{4,3,2,1,0:T(8,128)(2,1)S(1)}, bf16[1,4,8,8,128]{4,3,2,1,0:T(8,128)(2,1)S(1)}, u32[]{:S(2)}, u32[]{:S(2)}) collective-permute-start(bf16[1,4,8,8,128]{4,3,2,1,0:T(8,128)(2,1)S(1)} %get-tuple-element.50), channel_id=1, source_target_pairs={{16,0},{32,16},{48,32},{17,1},{33,17},{49,33},{18,2},{34,18},{50,3... | collective-permute-start | bytes 196616 | tf_op jit(solution)/shard_map/ppermute | solution.py:102
  112.0 6.9 %collective-permute-start.6 = (bf16[1,16,4,8,128]{4,3,2,1,0:T(8,128)(2,1)S(1)}, bf16[1,16,4,8,128]{4,3,2,1,0:T(8,128)(2,1)S(1)}, u32[]{:S(2)}, u32[]{:S(2)}) collective-permute-start(bf16[1,16,4,8,128]{4,3,2,1,0:T(8,128)(2,1)S(1)} %get-tuple-element.47), channel_id=1, source_target_pairs={{0,1},{1,2},{2,3},{3,4},{4,5},{5,6},{6,7},{7,8},{8,9},{9,10},{10,1... | collective-permute-start | bytes 393224 | tf_op jit(solution)/shard_map/ppermute | solution.py:101
  114.8 8.1 %collective-permute-start.7 = (bf16[1,16,4,8,128]{4,3,2,1,0:T(8,128)(2,1)S(1)}, bf16[1,16,4,8,128]{4,3,2,1,0:T(8,128)(2,1)S(1)}, u32[]{:S(2)}, u32[]{:S(2)}) collective-permute-start(bf16[1,16,4,8,128]{4,3,2,1,0:T(8,128)(2,1)S(1)} %get-tuple-element.48), channel_id=1, source_target_pairs={{1,0},{2,1},{3,2},{4,3},{5,4},{6,5},{7,6},{8,7},{9,8},{10,9},{11,1... | collective-permute-start | bytes 393224 | tf_op jit(solution)/shard_map/ppermute | solution.py:102
Sparse Core Ops, SparseCore 0:
  9.5 40.9 all-gather.1

commit v4 on v3

--- a/solution.py
+++ b/solution.py
@@ -104,6 +104,33 @@
     return block
 
 
+def extend_each(items, widths):
+    for axis, dim in (("frames", 1), ("space", 2)):
+        count = lax.axis_size(axis)
+        forward = [(i, i + 1) for i in range(count - 1)]
+        backward = [(i + 1, i) for i in range(count - 1)]
+        lows, highs, sizes = [], [], []
+        for item, width in zip(items, widths):
+            size = item.shape[dim]
+            low = lax.slice_in_dim(item, size - width, size, axis=dim)
+            high = lax.slice_in_dim(item, 0, width, axis=dim)
+            sizes.append(low.shape)
+            lows.append(low.reshape((low.shape[0], -1) + low.shape[3:]))
+            highs.append(high.reshape((high.shape[0], -1) + high.shape[3:]))
+        got_low = lax.ppermute(jnp.concatenate(lows, axis=1), axis, forward)
+        got_high = lax.ppermute(jnp.concatenate(highs, axis=1), axis, backward)
+        grown = []
+        offset = 0
+        for item, shape in zip(items, sizes):
+            length = shape[1] * shape[2]
+            low = got_low[:, offset : offset + length].reshape(shape)
+            high = got_high[:, offset : offset + length].reshape(shape)
+            offset += length
+            grown.append(jnp.concatenate([low, item, high], axis=dim))
+        items = grown
+    return items
+
+
 def denoise(offs, levels, previous, noise_part, packed, k, num_frames, num_rows, totals):
     num_videos, m, n, num_cols, channels = previous.shape
     outs = []
@@ -152,27 +179,18 @@
         [lax.axis_index("frames") * num_frames, lax.axis_index("space") * num_rows]
     ).astype(jnp.int32)
     totals = (num_frames * lax.axis_size("frames"), num_rows * lax.axis_size("space"))
-    both = extend(jnp.concatenate([incoming[None], noise_t[:halo]], axis=0), halo, 2, 3)
-    prior_ext = both[0]
-    noise_round = both[1:]
+    widths = [halo - k % halo for k in range(sections)]
+    grown = extend_each([incoming] + [noise_t[k] for k in range(sections)], [halo] + widths)
+    prior_ext = grown[0]
+    noise_ext = grown[1:]
     results = []
     for k in range(sections):
-        j = k % halo
-        if j == 0 and k > 0:
+        if k % halo == 0 and k > 0:
             prior_ext = extend(prior_ext, halo, 1, 2)
-            noise_round = noise_next
-        width = halo - j
-        cut = halo - width
-        noise_here = noise_round[
-            j, :, cut : cut + num_frames + 2 * width, cut : cut + num_rows + 2 * width
-        ]
         prior_ext, crop = denoise(
-            offs, levels, prior_ext, noise_here, packed, k, num_frames, num_rows, totals
+            offs, levels, prior_ext, noise_ext[k], packed, k, num_frames, num_rows, totals
         )
         results.append(crop)
-        if j == 0 and k + halo < sections:
-            later, _ = lax.optimization_barrier((noise_t[k + halo : k + 2 * halo], crop))
-            noise_next = extend(later, halo, 2, 3)
     num_cols, channels = base_frames.shape[3:]
     stacked = jnp.stack(results).reshape(
         (sections, per_device, num_frames, num_rows, num_cols, channels)

time: 171 us -> 181 us (1.058)
  waiting for transfers between devices: 27.1 us -> 50 us
  blocking collectives: 38.9 us -> 18.5 us
  local copies, waits for them, and re-layouts: 8.14 us -> 24.2 us
  starting transfers between devices: 35.4 us -> 27 us
    ppermute x0 -> x4, waiting for transfers between devices: none -> 27.7 us  [the longest x2 16.3 us: extend_each(): got_low = lax.ppermute(jnp.concatenate(lows, axis=1), axis, forward)]
    all_to_all x1 -> x0, blocking collectives: 20.4 us -> none  [on_device(): noise_t = lax.all_to_all(section_noise[0], 'section', 0, 0, tiled=True)]
    ppermute x6 -> x2, starting transfers between devices: 24.5 us -> 6.26 us  [extend(): lax.ppermute(lax.slice_in_dim(block, size - width, size, axis=dim), axis,...]
    unnamed x20 -> x48, local copies, waits for them, and re-layouts: 3.84 us -> 18.8 us
    all_to_all x0 -> x1, waiting for transfers between devices: none -> 13.7 us  [on_device(): noise_t = lax.all_to_all(section_noise[0], 'section', 0, 0, tiled=True)]
    ppermute x6 -> x2, waiting for transfers between devices: 21.4 us -> 8.14 us  [extend(): lax.ppermute(lax.slice_in_dim(block, 0, width, axis=dim), axis, backward)]
    ppermute x0 -> x4, starting transfers between devices: none -> 11.7 us  [the longest x2 8.52 us: extend_each(): got_low = lax.ppermute(jnp.concatenate(lows, axis=1), axis, forward)]
    concatenate x1 -> x13, other arithmetic: 0.06 us -> 7.26 us  [the longest x12 6.65 us: extend_each(): grown.append(jnp.concatenate([low, item, high], axis=dim))]
  transfers between devices with their start and end apart: 13 -> 10, of which waited for: 9 -> 8; matrix products, arithmetic and copies ran while one was open for 6% -> 13% of each run, Pallas kernels for 0% -> 0%
where the time goes in v4:
time: 181 us; the launch traced here: 180 us
  waiting for transfers between devices  50 us (28%)
  Pallas kernels  32.4 us (18%)
  starting transfers between devices  27 us (15%)
  local copies, waits for them, and re-layouts  24.2 us (13%)
  blocking collectives  18.5 us (10%)
  between operations  14.5 us (8%)
  other arithmetic  13.6 us (8%)
    pallas_call x8, Pallas kernels, section_call(): pl.pallas_call(functools.partial(section_kernel, m, n, cols, inner, num_f...  32.4 us
    unnamed x48, local copies, waits for them, and re-layouts  18.8 us
    all_to_all x1, blocking collectives, on_device(): return lax.all_to_all(stacked, 'section', 0, 1, tiled=True)  18.5 us
    ppermute x2, waiting for transfers between devices, extend_each(): got_low = lax.ppermute(jnp.concatenate(lows, axis=1), axis, forward)  16.3 us
    all_to_all x1, waiting for transfers between devices, on_device(): noise_t = lax.all_to_all(section_noise[0], 'section', 0, 0, tiled=True)  13.7 us
    ppermute x2, waiting for transfers between devices, extend_each(): got_high = lax.ppermute(jnp.concatenate(highs, axis=1), axis, backward)  11.4 us
    ppermute x2, starting transfers between devices, extend_each(): got_low = lax.ppermute(jnp.concatenate(lows, axis=1), axis, forward)  8.52 us
    ppermute x2, waiting for transfers between devices, extend(): lax.ppermute(lax.slice_in_dim(block, 0, width, axis=dim), axis, backward)  8.14 us
  transfers between devices with their start and end apart: 10, of which 8 were waited for; matrix products, arithmetic and copies ran while one was open for 13% of the time, Pallas kernels for 0%

profile of v4, /device:TPU:96, one launch (start us, length us, event | category | flops | bytes accessed | tf_op | source)
XLA Modules:
  0.0 180.2 jit_solution(2685515910209879429)
XLA Ops:
  6.5 4.4 %all-to-all-start = ((bf16[8,8,8,8,128]{4,3,2,1,0:T(8,128)(2,1)}), bf16[8,8,8,8,128]{4,3,2,1,0:T(8,128)(2,1)S(1)}, u32[]{:S(2)}, u32[]{:S(2)}) async-start(bf16[8,8,8,8,128]{4,3,2,1,0:T(8,128)(2,1)} %bitcast.147), calls=%async_computation | async-start | bytes 2097152 | tf_op jit(solution)/shard_map/all_to_all | solution.py:166
  11.8 0.9 constant_dynamic-slice_fusion.1
  13.3 13.7 %all-to-all-done = bf16[8,8,8,8,128]{4,3,2,1,0:T(8,128)(2,1)S(1)} async-done(((bf16[8,8,8,8,128]{4,3,2,1,0:T(8,128)(2,1)}), bf16[8,8,8,8,128]{4,3,2,1,0:T(8,128)(2,1)S(1)}, u32[]{:S(2)}, u32[]{:S(2)}) %all-to-all-start) | async-done | bytes 1048608 | tf_op jit(solution)/shard_map/all_to_all | solution.py:166
  32.1 3.5 %collective-permute-start = (bf16[1,192,8,128]{3,2,1,0:T(8,128)(2,1)S(1)}, bf16[1,192,8,128]{3,2,1,0:T(8,128)(2,1)S(1)}, u32[]{:S(2)}, u32[]{:S(2)}) collective-permute-start(bf16[1,192,8,128]{3,2,1,0:T(8,128)(2,1)S(1)} %get-tuple-element.43), channel_id=1, source_target_pairs={{0,16},{16,32},{32,48},{1,17},{17,33},{33,49},{2,18},{18,34},{34,5... | collective-permute-start | bytes 1179656 | tf_op jit(solution)/shard_map/ppermute | solution.py:120
  35.6 0.9 maximum_maximum_fusion
  36.5 0.9 constant_dynamic-slice_fusion.2
  37.4 1.3 collective-permute-start.1
  38.8 4.9 %collective-permute-done = bf16[1,192,8,128]{3,2,1,0:T(8,128)(2,1)S(1)} collective-permute-done((bf16[1,192,8,128]{3,2,1,0:T(8,128)(2,1)S(1)}, bf16[1,192,8,128]{3,2,1,0:T(8,128)(2,1)S(1)}, u32[]{:S(2)}, u32[]{:S(2)}) %collective-permute-start) | collective-permute-done | bytes 393248 | tf_op jit(solution)/shard_map/ppermute | solution.py:120
  43.7 6.2 %collective-permute-done.1 = bf16[1,192,8,128]{3,2,1,0:T(8,128)(2,1)S(1)} collective-permute-done((bf16[1,192,8,128]{3,2,1,0:T(8,128)(2,1)}, bf16[1,192,8,128]{3,2,1,0:T(8,128)(2,1)S(1)}, u32[]{:S(2)}, u32[]{:S(2)}) %collective-permute-start.1) | collective-permute-done | bytes 393248 | tf_op jit(solution)/shard_map/ppermute | solution.py:121
  56.0 0.7 constant_dynamic-update-slice_fusion.30
  60.5 5.0 %collective-permute-start.2 = (bf16[1,344,8,128]{3,2,1,0:T(8,128)(2,1)}, bf16[1,344,8,128]{3,2,1,0:T(8,128)(2,1)S(1)}, u32[]{:S(2)}, u32[]{:S(2)}) collective-permute-start(bf16[1,344,8,128]{3,2,1,0:T(8,128)(2,1)} %get-tuple-element.113), channel_id=1, source_target_pairs={{0,1},{1,2},{2,3},{3,4},{4,5},{5,6},{6,7},{7,8},{8,9},{9,10},{10,1... | collective-permute-start | bytes 2113544 | tf_op jit(solution)/shard_map/ppermute | solution.py:120
  65.6 1.9 %collective-permute-start.3 = (bf16[1,344,8,128]{3,2,1,0:T(8,128)(2,1)}, bf16[1,344,8,128]{3,2,1,0:T(8,128)(2,1)S(1)}, u32[]{:S(2)}, u32[]{:S(2)}) collective-permute-start(bf16[1,344,8,128]{3,2,1,0:T(8,128)(2,1)} %get-tuple-element.114), channel_id=1, source_target_pairs={{1,0},{2,1},{3,2},{4,3},{5,4},{6,5},{7,6},{8,7},{9,8},{10,9},{11,1... | collective-permute-start | bytes 2113544 | tf_op jit(solution)/shard_map/ppermute | solution.py:121
  68.2 11.4 %collective-permute-done.2 = bf16[1,344,8,128]{3,2,1,0:T(8,128)(2,1)S(1)} collective-permute-done((bf16[1,344,8,128]{3,2,1,0:T(8,128)(2,1)}, bf16[1,344,8,128]{3,2,1,0:T(8,128)(2,1)S(1)}, u32[]{:S(2)}, u32[]{:S(2)}) %collective-permute-start.2) | collective-permute-done | bytes 704544 | tf_op jit(solution)/shard_map/ppermute | solution.py:120
  79.5 5.2 %collective-permute-done.3 = bf16[1,344,8,128]{3,2,1,0:T(8,128)(2,1)S(1)} collective-permute-done((bf16[1,344,8,128]{3,2,1,0:T(8,128)(2,1)}, bf16[1,344,8,128]{3,2,1,0:T(8,128)(2,1)S(1)}, u32[]{:S(2)}, u32[]{:S(2)}) %collective-permute-start.3) | collective-permute-done | bytes 704544 | tf_op jit(solution)/shard_map/ppermute | solution.py:121
  84.8 0.7 copy.36
  85.5 0.7 pad_maximum_fusion.13
  86.2 0.8 pad_maximum_fusion.7
  87.0 0.8 pad_maximum_fusion.6
  87.8 0.8 pad_maximum_fusion.5
  88.6 0.8 pad_maximum_fusion.4
  89.5 0.9 pad_maximum_fusion.3
  90.4 0.9 pad_maximum_fusion.1
  91.3 0.9 pad_maximum_fusion
  92.1 1.4 fusion.2.lv_ref
  93.5 4.7 %shard_map.64 = (bf16[1568,128]{1,0:T(8,128)(2,1)}, bf16[512,128]{1,0:T(8,128)(2,1)}) custom-call(s32[2]{0:T(128)} %pad_add_fusion.offs_ref, f32[8]{0:T(128)} %fusion.2.lv_ref, bf16[2048,128]{1,0:T(8,128)(2,1)} %bitcast.138, bf16[2048,128]{1,0:T(8,128)(2,1)} %bitcast.137, bf16[8,14,128,128]{3,2,1,0:T(8,128)(2,1)} %all-gather.2.cloned.1.call-done.w_hbm), custom_call_target="tpu_custom_call" | custom-call | flops 667942912 | bytes 2007040 | tf_op jit(solution)/shard_map/pallas_call | solution.py:74
  98.2 4.2 %shard_map.65 = (bf16[1152,128]{1,0:T(8,128)(2,1)}, bf16[512,128]{1,0:T(8,128)(2,1)}) custom-call(s32[2]{0:T(128)} %pad_add_fusion.offs_ref, f32[8]{0:T(128)} %fusion.2.lv_ref, bf16[1568,128]{1,0:T(8,128)(2,1)} %get-tuple-element.21.prior_ref, bf16[1568,128]{1,0:T(8,128)(2,1)} %bitcast.141, bf16[8,14,128,128]{3,2,1,0:T(8,128)(2,1)} %all-gather.2.cloned.1.call-done.w_hbm), custom_call_target="tpu_custom_call" | custom-call | flops 490733568 | bytes 1654784 | tf_op jit(solution)/shard_map/pallas_call | solution.py:74
  102.4 3.9 %shard_map.66 = (bf16[800,128]{1,0:T(8,128)(2,1)}, bf16[512,128]{1,0:T(8,128)(2,1)}) custom-call(s32[2]{0:T(128)} %pad_add_fusion.offs_ref, f32[8]{0:T(128)} %fusion.2.lv_ref, bf16[1152,128]{1,0:T(8,128)(2,1)} %get-tuple-element.23.prior_ref, bf16[1152,128]{1,0:T(8,128)(2,1)} %bitcast.143, bf16[8,14,128,128]{3,2,1,0:T(8,128)(2,1)} %all-gather.2.cloned.1.call-done.w_hbm), custom_call_target="tpu_custom_call" | custom-call | flops 340787200 | bytes 1351680 | tf_op jit(solution)/shard_map/pallas_call | solution.py:74
  106.3 3.5 %shard_map.67 = (bf16[512,128]{1,0:T(8,128)(2,1)}, bf16[512,128]{1,0:T(8,128)(2,1)}) custom-call(s32[2]{0:T(128)} %pad_add_fusion.offs_ref, f32[8]{0:T(128)} %fusion.2.lv_ref, bf16[800,128]{1,0:T(8,128)(2,1)} %get-tuple-element.25.prior_ref, bf16[800,128]{1,0:T(8,128)(2,1)} %bitcast.149, bf16[8,14,128,128]{3,2,1,0:T(8,128)(2,1)} %all-gather.2.cloned.1.call-done.w_hbm), custom_call_target="tpu_custom_call" | custom-call | flops 218103808 | bytes 1097728 | tf_op jit(solution)/shard_map/pallas_call | solution.py:74
  109.8 0.9 fusion.23
  110.7 3.5 %collective-permute-start.4 = (bf16[1,4,8,8,128]{4,3,2,1,0:T(8,128)(2,1)S(1)}, bf16[1,4,8,8,128]{4,3,2,1,0:T(8,128)(2,1)S(1)}, u32[]{:S(2)}, u32[]{:S(2)}) collective-permute-start(bf16[1,4,8,8,128]{4,3,2,1,0:T(8,128)(2,1)S(1)} %get-tuple-element.117), channel_id=1, source_target_pairs={{0,16},{16,32},{32,48},{1,17},{17,33},{33,49},{2,18},{18,34},{34,5... | collective-permute-start | bytes 196616 | tf_op jit(solution)/shard_map/ppermute | solution.py:101
  114.2 1.3 collective-permute-start.5
  116.1 4.3 %collective-permute-done.5 = bf16[1,4,8,8,128]{4,3,2,1,0:T(8,128)(2,1)S(1)} collective-permute-done((bf16[1,4,8,8,128]{4,3,2,1,0:T(8,128)(2,1)S(1)}, bf16[1,4,8,8,128]{4,3,2,1,0:T(8,128)(2,1)S(1)}, u32[]{:S(2)}, u32[]{:S(2)}) %collective-permute-start.5) | collective-permute-done | bytes 65568 | tf_op jit(solution)/shard_map/ppermute | solution.py:102
  120.4 0.9 pad_maximum_fusion.11
  121.3 2.8 %collective-permute-start.6 = (bf16[1,16,4,8,128]{4,3,2,1,0:T(8,128)(2,1)S(1)}, bf16[1,16,4,8,128]{4,3,2,1,0:T(8,128)(2,1)S(1)}, u32[]{:S(2)}, u32[]{:S(2)}) collective-permute-start(bf16[1,16,4,8,128]{4,3,2,1,0:T(8,128)(2,1)S(1)} %get-tuple-element.97), channel_id=1, source_target_pairs={{0,1},{1,2},{2,3},{3,4},{4,5},{5,6},{6,7},{7,8},{8,9},{9,10},{10,1... | collective-permute-start | bytes 393224 | tf_op jit(solution)/shard_map/ppermute | solution.py:101
  124.1 3.2 %collective-permute-start.7 = (bf16[1,16,4,8,128]{4,3,2,1,0:T(8,128)(2,1)S(1)}, bf16[1,16,4,8,128]{4,3,2,1,0:T(8,128)(2,1)S(1)}, u32[]{:S(2)}, u32[]{:S(2)}) collective-permute-start(bf16[1,16,4,8,128]{4,3,2,1,0:T(8,128)(2,1)S(1)} %get-tuple-element.98), channel_id=1, source_target_pairs={{1,0},{2,1},{3,2},{4,3},{5,4},{6,5},{7,6},{8,7},{9,8},{10,9},{11,1... | collective-permute-start | bytes 393224 | tf_op jit(solution)/shard_map/ppermute | solution.py:102
  127.4 0.9 constant_dynamic-update-slice_fusion.40
  128.3 3.9 %collective-permute-done.7 = bf16[1,16,4,8,128]{4,3,2,1,0:T(8,128)(2,1)S(1)} collective-permute-done((bf16[1,16,4,8,128]{4,3,2,1,0:T(8,128)(2,1)S(1)}, bf16[1,16,4,8,128]{4,3,2,1,0:T(8,128)(2,1)S(1)}, u32[]{:S(2)}, u32[]{:S(2)}) %collective-permute-start.7) | collective-permute-done | bytes 131104 | tf_op jit(solution)/shard_map/ppermute | solution.py:102
  132.2 1.8 pad_maximum_fusion.2
  134.0 4.7 %shard_map.68 = (bf16[1568,128]{1,0:T(8,128)(2,1)}, bf16[512,128]{1,0:T(8,128)(2,1)}) custom-call(s32[2]{0:T(128)} %pad_add_fusion.offs_ref, f32[8]{0:T(128)} %fusion.2.lv_ref, bf16[2048,128]{1,0:T(8,128)(2,1)} %bitcast.139, bf16[2048,128]{1,0:T(8,128)(2,1)} %bitcast.136, bf16[8,14,128,128]{3,2,1,0:T(8,128)(2,1)} %all-gather.2.cloned.1.call-done.w_hbm), custom_call_target="tpu_custom_call" | custom-call | flops 667942912 | bytes 2007040 | tf_op jit(solution)/shard_map/pallas_call | solution.py:74
  138.6 0.9 constant_dynamic-update-slice_fusion.39
  139.6 4.2 %shard_map.69 = (bf16[1152,128]{1,0:T(8,128)(2,1)}, bf16[512,128]{1,0:T(8,128)(2,1)}) custom-call(s32[2]{0:T(128)} %pad_add_fusion.offs_ref, f32[8]{0:T(128)} %fusion.2.lv_ref, bf16[1568,128]{1,0:T(8,128)(2,1)} %get-tuple-element.29.prior_ref, bf16[1568,128]{1,0:T(8,128)(2,1)} %bitcast.140, bf16[8,14,128,128]{3,2,1,0:T(8,128)(2,1)} %all-gather.2.cloned.1.call-done.w_hbm), custom_call_target="tpu_custom_call" | custom-call | flops 490733568 | bytes 1654784 | tf_op jit(solution)/shard_map/pallas_call | solution.py:74
  143.8 0.9 constant_dynamic-update-slice_fusion.38
  144.7 3.8 %shard_map.70 = (bf16[800,128]{1,0:T(8,128)(2,1)}, bf16[512,128]{1,0:T(8,128)(2,1)}) custom-call(s32[2]{0:T(128)} %pad_add_fusion.offs_ref, f32[8]{0:T(128)} %fusion.2.lv_ref, bf16[1152,128]{1,0:T(8,128)(2,1)} %get-tuple-element.31.prior_ref, bf16[1152,128]{1,0:T(8,128)(2,1)} %bitcast.142, bf16[8,14,128,128]{3,2,1,0:T(8,128)(2,1)} %all-gather.2.cloned.1.call-done.w_hbm), custom_call_target="tpu_custom_call" | custom-call | flops 340787200 | bytes 1351680 | tf_op jit(solution)/shard_map/pallas_call | solution.py:74
  148.5 0.9 constant_dynamic-update-slice_fusion.37
  149.4 3.5 %shard_map.71 = (bf16[512,128]{1,0:T(8,128)(2,1)}, bf16[512,128]{1,0:T(8,128)(2,1)}) custom-call(s32[2]{0:T(128)} %pad_add_fusion.offs_ref, f32[8]{0:T(128)} %fusion.2.lv_ref, bf16[800,128]{1,0:T(8,128)(2,1)} %get-tuple-element.33.prior_ref, bf16[800,128]{1,0:T(8,128)(2,1)} %bitcast.148, bf16[8,14,128,128]{3,2,1,0:T(8,128)(2,1)} %all-gather.2.cloned.1.call-done.w_hbm), custom_call_target="tpu_custom_call" | custom-call | flops 218103808 | bytes 1097728 | tf_op jit(solution)/shard_map/pallas_call | solution.py:74
  152.9 0.9 constant_dynamic-update-slice_fusion.36
  153.9 18.5 %all_to_all.17 = bf16[8,1,8,8,8,128]{5,4,3,2,1,0:T(8,128)(2,1)S(1)} all-to-all(bf16[8,1,8,8,8,128]{5,4,3,2,1,0:T(8,128)(2,1)S(1)} %constant_dynamic-update-slice_fusion.36), channel_id=1, replica_groups=mesh['section'=8,'frames'=4,'space'=16] {'section'}, dimensions={0} | all-to-all | bytes 2097152 | tf_op jit(solution)/shard_map/all_to_all | solution.py:198
  172.4 1.0 copy.86
  (84 shorter events, 17.2 us)
Async XLA Ops:
  6.5 29.0 %copy-start.5 = (bf16[1,128,128]{2,1,0:T(8,128)(2,1)S(1)}, bf16[1,128,128]{2,1,0:T(8,128)(2,1)}, u32[]{:S(2)}) copy-start(bf16[1,128,128]{2,1,0:T(8,128)(2,1)} %param.11) | copy-start | bytes 98308
  6.5 29.0 %copy-start.4 = (bf16[1,3,128,128]{3,2,1,0:T(8,128)(2,1)S(1)}, bf16[1,3,128,128]{3,2,1,0:T(8,128)(2,1)}, u32[]{:S(2)}) copy-start(bf16[1,3,128,128]{3,2,1,0:T(8,128)(2,1)} %param.10) | copy-start | bytes 294916
  6.5 29.0 %copy-start = (bf16[1,9,128,128]{3,2,1,0:T(8,128)(2,1)S(1)}, bf16[1,9,128,128]{3,2,1,0:T(8,128)(2,1)}, u32[]{:S(2)}) copy-start(bf16[1,9,128,128]{3,2,1,0:T(8,128)(2,1)} %param.9) | copy-start | bytes 884740
  6.5 20.4 %all-to-all-start = ((bf16[8,8,8,8,128]{4,3,2,1,0:T(8,128)(2,1)}), bf16[8,8,8,8,128]{4,3,2,1,0:T(8,128)(2,1)S(1)}, u32[]{:S(2)}, u32[]{:S(2)}) async-start(bf16[8,8,8,8,128]{4,3,2,1,0:T(8,128)(2,1)} %bitcast.147), calls=%async_computation | async-start | bytes 2097152 | tf_op jit(solution)/shard_map/all_to_all | solution.py:166
  11.0 81.2 %all-gather.2.cloned.1.call-start = ((), (), s32[]{:S(2)}) async-start(), calls=%async_computation.2 | async-start | bytes 4128768 | tf_op jit(solution)/shard_map/all_gather | solution.py:175
  32.1 11.6 %collective-permute-start = (bf16[1,192,8,128]{3,2,1,0:T(8,128)(2,1)S(1)}, bf16[1,192,8,128]{3,2,1,0:T(8,128)(2,1)S(1)}, u32[]{:S(2)}, u32[]{:S(2)}) collective-permute-start(bf16[1,192,8,128]{3,2,1,0:T(8,128)(2,1)S(1)} %get-tuple-element.43), channel_id=1, source_target_pairs={{0,16},{16,32},{32,48},{1,17},{17,33},{33,49},{2,18},{18,34},{34,5... | collective-permute-start | bytes 1179656 | tf_op jit(solution)/shard_map/ppermute | solution.py:120
  37.4 12.5 %collective-permute-start.1 = (bf16[1,192,8,128]{3,2,1,0:T(8,128)(2,1)}, bf16[1,192,8,128]{3,2,1,0:T(8,128)(2,1)S(1)}, u32[]{:S(2)}, u32[]{:S(2)}) collective-permute-start(bf16[1,192,8,128]{3,2,1,0:T(8,128)(2,1)} %get-tuple-element.44), channel_id=1, source_target_pairs={{16,0},{32,16},{48,32},{17,1},{33,17},{49,33},{18,2},{34,18},{50,3... | collective-permute-start | bytes 1179656 | tf_op jit(solution)/shard_map/ppermute | solution.py:121
  60.5 19.0 %collective-permute-start.2 = (bf16[1,344,8,128]{3,2,1,0:T(8,128)(2,1)}, bf16[1,344,8,128]{3,2,1,0:T(8,128)(2,1)S(1)}, u32[]{:S(2)}, u32[]{:S(2)}) collective-permute-start(bf16[1,344,8,128]{3,2,1,0:T(8,128)(2,1)} %get-tuple-element.113), channel_id=1, source_target_pairs={{0,1},{1,2},{2,3},{3,4},{4,5},{5,6},{6,7},{7,8},{8,9},{9,10},{10,1... | collective-permute-start | bytes 2113544 | tf_op jit(solution)/shard_map/ppermute | solution.py:120
  65.6 19.2 %collective-permute-start.3 = (bf16[1,344,8,128]{3,2,1,0:T(8,128)(2,1)}, bf16[1,344,8,128]{3,2,1,0:T(8,128)(2,1)S(1)}, u32[]{:S(2)}, u32[]{:S(2)}) collective-permute-start(bf16[1,344,8,128]{3,2,1,0:T(8,128)(2,1)} %get-tuple-element.114), channel_id=1, source_target_pairs={{1,0},{2,1},{3,2},{4,3},{5,4},{6,5},{7,6},{8,7},{9,8},{10,9},{11,1... | collective-permute-start | bytes 2113544 | tf_op jit(solution)/shard_map/ppermute | solution.py:121
  102.4 13.1 %copy-start.2 = (bf16[512,128]{1,0:T(8,128)(2,1)S(1)}, bf16[512,128]{1,0:T(8,128)(2,1)}, u32[]{:S(2)}) copy-start(bf16[512,128]{1,0:T(8,128)(2,1)} %get-tuple-element.20) | copy-start | bytes 393220
  102.4 13.1 %copy-start.3 = (bf16[512,128]{1,0:T(8,128)(2,1)S(1)}, bf16[512,128]{1,0:T(8,128)(2,1)}, u32[]{:S(2)}) copy-start(bf16[512,128]{1,0:T(8,128)(2,1)} %get-tuple-element.22) | copy-start | bytes 393220
  106.3 21.1 %copy-start.1 = (bf16[512,128]{1,0:T(8,128)(2,1)S(1)}, bf16[512,128]{1,0:T(8,128)(2,1)}, u32[]{:S(2)}) copy-start(bf16[512,128]{1,0:T(8,128)(2,1)} %get-tuple-element.24) | copy-start | bytes 393220
  110.7 5.4 %collective-permute-start.4 = (bf16[1,4,8,8,128]{4,3,2,1,0:T(8,128)(2,1)S(1)}, bf16[1,4,8,8,128]{4,3,2,1,0:T(8,128)(2,1)S(1)}, u32[]{:S(2)}, u32[]{:S(2)}) collective-permute-start(bf16[1,4,8,8,128]{4,3,2,1,0:T(8,128)(2,1)S(1)} %get-tuple-element.117), channel_id=1, source_target_pairs={{0,16},{16,32},{32,48},{1,17},{17,33},{33,49},{2,18},{18,34},{34,5... | collective-permute-start | bytes 196616 | tf_op jit(solution)/shard_map/ppermute | solution.py:101
  114.2 6.2 %collective-permute-start.5 = (bf16[1,4,8,8,128]{4,3,2,1,0:T(8,128)(2,1)S(1)}, bf16[1,4,8,8,128]{4,3,2,1,0:T(8,128)(2,1)S(1)}, u32[]{:S(2)}, u32[]{:S(2)}) collective-permute-start(bf16[1,4,8,8,128]{4,3,2,1,0:T(8,128)(2,1)S(1)} %get-tuple-element.118), channel_id=1, source_target_pairs={{16,0},{32,16},{48,32},{17,1},{33,17},{49,33},{18,2},{34,18},{50,3... | collective-permute-start | bytes 196616 | tf_op jit(solution)/shard_map/ppermute | solution.py:102
  121.3 7.0 %collective-permute-start.6 = (bf16[1,16,4,8,128]{4,3,2,1,0:T(8,128)(2,1)S(1)}, bf16[1,16,4,8,128]{4,3,2,1,0:T(8,128)(2,1)S(1)}, u32[]{:S(2)}, u32[]{:S(2)}) collective-permute-start(bf16[1,16,4,8,128]{4,3,2,1,0:T(8,128)(2,1)S(1)} %get-tuple-element.97), channel_id=1, source_target_pairs={{0,1},{1,2},{2,3},{3,4},{4,5},{5,6},{6,7},{7,8},{8,9},{9,10},{10,1... | collective-permute-start | bytes 393224 | tf_op jit(solution)/shard_map/ppermute | solution.py:101
  124.1 8.1 %collective-permute-start.7 = (bf16[1,16,4,8,128]{4,3,2,1,0:T(8,128)(2,1)S(1)}, bf16[1,16,4,8,128]{4,3,2,1,0:T(8,128)(2,1)S(1)}, u32[]{:S(2)}, u32[]{:S(2)}) collective-permute-start(bf16[1,16,4,8,128]{4,3,2,1,0:T(8,128)(2,1)S(1)} %get-tuple-element.98), channel_id=1, source_target_pairs={{1,0},{2,1},{3,2},{4,3},{5,4},{6,5},{7,6},{8,7},{9,8},{10,9},{11,1... | collective-permute-start | bytes 393224 | tf_op jit(solution)/shard_map/ppermute | solution.py:102
Sparse Core Ops, SparseCore 0:
  36.6 38.7 all-gather.1

commit v5 on v3

--- a/solution.py
+++ b/solution.py
@@ -11,7 +11,7 @@
 
 def section_kernel(
     m, n, cols, inner, num_frames, num_rows, total_frames, total_rows, k,
-    offs_ref, lv_ref, prior_ref, noise_ref, w_hbm, out_ref, crop_ref, w_ref, sem, xl, xc, xr, nz,
+    offs_ref, prior_ref, noise_ref, w_hbm, out_ref, crop_ref, w_ref, sem, xs, nz,
 ):
     weight_copy = pltpu.make_async_copy(w_hbm.at[k], w_ref, sem)
     weight_copy.start()
@@ -19,8 +19,11 @@
     rows_in = m * n * cols
     rows_out = (m - 2) * (n - 2) * cols
     width = (m - num_frames) // 2
-    level = lv_ref[k]
-    noisy = prior_ref[...].astype(jnp.float32) + level * noise_ref[...].astype(jnp.float32)
+    prior = prior_ref[...].astype(jnp.float32)
+    noise = noise_ref[...].astype(jnp.float32)
+    weight_copy.wait()
+    level = w_ref[13][0:1, :].astype(jnp.float32)
+    noisy = prior + level * noise
     mean_sq = jnp.mean(noisy * noisy, axis=-1, keepdims=True)
     normalized = (noisy * lax.rsqrt(mean_sq + 1e-05)).astype(jnp.bfloat16).astype(jnp.float32)
     shape4 = (m, n, cols, channels)
@@ -33,22 +36,25 @@
     col = lax.broadcasted_iota(jnp.int32, (rows_in, channels), 0) % cols
     left = jnp.where(col == 0, 0.0, pltpu.roll(normalized, 1, 0))
     right = jnp.where(col == cols - 1, 0.0, pltpu.roll(normalized, rows_in - 1, 0))
-    xl[...] = left.reshape(m, n * cols, channels)
-    xc[...] = normalized.reshape(m, n * cols, channels)
-    xr[...] = right.reshape(m, n * cols, channels)
+    xs[:, :, 0:channels] = left.reshape(m, n * cols, channels)
+    xs[:, :, channels : 2 * channels] = normalized.reshape(m, n * cols, channels)
+    xs[:, :, 2 * channels : 3 * channels] = right.reshape(m, n * cols, channels)
     nz[...] = noisy.reshape(m, n * cols, channels)
-    weight_copy.wait()
-    views = (xl, xc, xr)
     acc = jnp.zeros((rows_out, channels), jnp.float32)
-    for tap in range(9):
-        a, b = tap // 3, tap % 3
-        v = views[b][pl.ds(1, m - 2), pl.ds(a * cols, (n - 2) * cols), :]
-        v = v.reshape(rows_out, channels).astype(jnp.bfloat16)
-        acc = acc + jnp.dot(v, w_ref[tap], preferred_element_type=jnp.float32)
-    for t in range(3):
-        v = xc[pl.ds(t, m - 2), pl.ds(cols, (n - 2) * cols), :]
-        v = v.reshape(rows_out, channels).astype(jnp.bfloat16)
-        acc = acc + jnp.dot(v, w_ref[9 + t], preferred_element_type=jnp.float32)
+    for a in range(3):
+        v = xs[pl.ds(1, m - 2), pl.ds(a * cols, (n - 2) * cols), :]
+        v = v.reshape(rows_out, 3 * channels).astype(jnp.bfloat16)
+        w = w_ref[pl.ds(3 * a, 3)].reshape(3 * channels, channels)
+        acc = acc + jnp.dot(v, w, preferred_element_type=jnp.float32)
+    frame_views = [
+        xs[pl.ds(t, m - 2), pl.ds(cols, (n - 2) * cols), pl.ds(channels, channels)].reshape(
+            rows_out, channels
+        )
+        for t in range(3)
+    ]
+    v = jnp.concatenate(frame_views, axis=1).astype(jnp.bfloat16)
+    w = w_ref[pl.ds(9, 3)].reshape(3 * channels, channels)
+    acc = acc + jnp.dot(v, w, preferred_element_type=jnp.float32)
     act = (acc / (1.0 + jnp.exp(-acc))).astype(jnp.bfloat16)
     est = jnp.dot(act, w_ref[12], preferred_element_type=jnp.float32)
     center = nz[pl.ds(1, m - 2), pl.ds(cols, (n - 2) * cols), :].reshape(rows_out, channels)
@@ -59,7 +65,7 @@
     crop_ref[...] = crop.reshape(num_frames * num_rows * cols, channels).astype(crop_ref.dtype)
 
 
-def section_call(offs, levels, prior, noise, packed, k, m, n, cols, num_frames, num_rows, totals):
+def section_call(offs, prior, noise, packed, k, m, n, cols, num_frames, num_rows, totals):
     channels = packed.shape[-1]
     rows_in = m * n * cols
     rows_out = (m - 2) * (n - 2) * cols
@@ -79,17 +85,17 @@
             jax.ShapeDtypeStruct((rows_out, channels), jnp.bfloat16),
             jax.ShapeDtypeStruct((rows_crop, channels), jnp.bfloat16),
         ),
-        in_specs=[smem, smem, vmem, vmem, pl.BlockSpec(memory_space=pl.ANY)],
+        in_specs=[smem, vmem, vmem, pl.BlockSpec(memory_space=pl.ANY)],
         out_specs=(vmem, vmem),
         scratch_shapes=[
             pltpu.VMEM(packed.shape[1:], packed.dtype),
             pltpu.SemaphoreType.DMA(()),
         ]
-        + [scratch] * 4,
+        + [pltpu.VMEM((m, n * cols, 3 * channels), jnp.float32), scratch],
         cost_estimate=pl.CostEstimate(
             flops=flops, bytes_accessed=nbytes, transcendentals=rows_out * channels
         ),
-    )(offs, levels, prior, noise, packed)
+    )(offs, prior, noise, packed)
 
 
 def extend(block, width, frame_dim, row_dim):
@@ -104,14 +110,13 @@
     return block
 
 
-def denoise(offs, levels, previous, noise_part, packed, k, num_frames, num_rows, totals):
+def denoise(offs, previous, noise_part, packed, k, num_frames, num_rows, totals):
     num_videos, m, n, num_cols, channels = previous.shape
     outs = []
     crops = []
     for v in range(num_videos):
         out, crop = section_call(
             offs,
-            levels,
             previous[v].reshape(-1, channels),
             noise_part[v].reshape(-1, channels),
             packed,
@@ -147,7 +152,6 @@
     )
     packed = lax.all_gather(packed, "section", tiled=True)
     incoming = lax.dynamic_slice_in_dim(base_frames, place * per_device, per_device, 0)
-    levels = packed[:, 13, 0, 0].astype(jnp.float32)
     offs = jnp.stack(
         [lax.axis_index("frames") * num_frames, lax.axis_index("space") * num_rows]
     ).astype(jnp.int32)
@@ -167,7 +171,7 @@
             j, :, cut : cut + num_frames + 2 * width, cut : cut + num_rows + 2 * width
         ]
         prior_ext, crop = denoise(
-            offs, levels, prior_ext, noise_here, packed, k, num_frames, num_rows, totals
+            offs, prior_ext, noise_here, packed, k, num_frames, num_rows, totals
         )
         results.append(crop)
         if j == 0 and k + halo < sections:

time: 171 us -> 172 us (level)
  Pallas kernels: 32.4 us -> 35.1 us
    pallas_call x8, Pallas kernels: 32.4 us -> 35.1 us  [section_call(): pl.pallas_call(functools.partial(section_kernel, m, n, cols, inner, num_f...]
where the time goes in v5:
time: 172 us; the launch traced here: 171 us
  blocking collectives  38.9 us (23%)
  starting transfers between devices  35.4 us (21%)
  Pallas kernels  35.1 us (20%)
  waiting for transfers between devices  27.1 us (16%)
  between operations  14.5 us (8%)
  other arithmetic  12.1 us (7%)
  local copies, waits for them, and re-layouts  8.16 us (5%)
    pallas_call x8, Pallas kernels, section_call(): pl.pallas_call(functools.partial(section_kernel, m, n, cols, inner, num_f...  35.1 us
    ppermute x6, starting transfers between devices, extend(): lax.ppermute(lax.slice_in_dim(block, size - width, size, axis=dim), axis,...  24.5 us
    ppermute x6, waiting for transfers between devices, extend(): lax.ppermute(lax.slice_in_dim(block, 0, width, axis=dim), axis, backward)  21.4 us
    all_to_all x1, blocking collectives, on_device(): noise_t = lax.all_to_all(section_noise[0], 'section', 0, 0, tiled=True)  20.4 us
    all_to_all x1, blocking collectives, on_device(): return lax.all_to_all(stacked, 'section', 0, 1, tiled=True)  18.5 us
    ppermute x6, starting transfers between devices, extend(): lax.ppermute(lax.slice_in_dim(block, 0, width, axis=dim), axis, backward)  10.9 us
    ppermute x6, waiting for transfers between devices, extend(): lax.ppermute(lax.slice_in_dim(block, size - width, size, axis=dim), axis,...  5.68 us
    concatenate x6, other arithmetic, extend(): block = jnp.concatenate([low, block, high], axis=dim)  4.85 us
  transfers between devices with their start and end apart: 13, of which 9 were waited for; matrix products, arithmetic and copies ran while one was open for 6% of the time, Pallas kernels for 0%

profile of v5, /device:TPU:96, one launch (start us, length us, event | category | flops | bytes accessed | tf_op | source)
XLA Modules:
  0.0 171.3 jit_solution(1403942503917852339)
XLA Ops:
  7.4 1.9 %maximum_maximum_fusion = bf16[1,14,128,128]{3,2,1,0:T(8,128)(2,1)} fusion(bf16[1,1,128,128]{3,2,1,0:T(8,128)(2,1)} %bitcast.54, bf16[1,3,128,128]{3,2,1,0:T(8,128)(2,1)} %param.10, bf16[1,9,128,128]{3,2,1,0:T(8,128)(2,1)} %param.9, bf16[14]{0:T(256)(128)(2,1)S(1)} %pad.19.clone), kind=kLoop, calls=%fused_computation.9 | loop fusion | flops 688128 | bytes 884764 | tf_op jit(solution)/shard_map/concatenate | solution.py:150
  9.3 20.4 %all_to_all.17 = bf16[8,8,8,8,128]{4,3,2,1,0:T(8,128)(2,1)S(1)} all-to-all(bf16[8,8,8,8,128]{4,3,2,1,0:T(8,128)(2,1)} %bitcast.43), channel_id=1, replica_groups=mesh['section'=8,'frames'=4,'space'=16] {'section'}, dimensions={0} | all-to-all | bytes 2097152 | tf_op jit(solution)/shard_map/all_to_all | solution.py:144
  29.8 3.5 %collective-permute-start.8 = (bf16[4,1,4,8,8,128]{5,4,3,2,0,1:T(8,128)(2,1)S(1)}, bf16[4,1,4,8,8,128]{5,4,3,2,0,1:T(8,128)(2,1)S(1)}, u32[]{:S(2)}, u32[]{:S(2)}) collective-permute-start(bf16[4,1,4,8,8,128]{5,4,3,2,0,1:T(8,128)(2,1)S(1)} %get-tuple-element.45), channel_id=1, source_target_pairs={{0,16},{16,32},{32,48},{1,17},{17,33},{33,49},{2,18},{18,34},{34,5... | collective-permute-start | bytes 786440 | tf_op jit(solution)/shard_map/ppermute | solution.py:107
  33.3 1.3 collective-permute-start.9
  34.7 4.6 %collective-permute-start = (bf16[5,1,4,8,8,128]{5,4,3,2,0,1:T(8,128)(2,1)S(1)}, bf16[5,1,4,8,8,128]{5,4,3,2,0,1:T(8,128)(2,1)S(1)}, u32[]{:S(2)}, u32[]{:S(2)}) collective-permute-start(bf16[5,1,4,8,8,128]{5,4,3,2,0,1:T(8,128)(2,1)S(1)} %get-tuple-element.43), channel_id=1, source_target_pairs={{0,16},{16,32},{32,48},{1,17},{17,33},{33,49},{2,18},{18,34},{34,5... | collective-permute-start | bytes 983048 | tf_op jit(solution)/shard_map/ppermute | solution.py:107
  39.3 1.3 collective-permute-start.1
  40.6 2.1 %collective-permute-done.9 = bf16[4,1,4,8,8,128]{5,4,3,2,0,1:T(8,128)(2,1)S(1)} collective-permute-done((bf16[4,1,4,8,8,128]{5,4,3,2,0,1:T(8,128)(2,1)S(1)}, bf16[4,1,4,8,8,128]{5,4,3,2,0,1:T(8,128)(2,1)S(1)}, u32[]{:S(2)}, u32[]{:S(2)}) %collective-permute-start.9) | collective-permute-done | bytes 262176 | tf_op jit(solution)/shard_map/ppermute | solution.py:108
  42.9 5.0 %collective-permute-start.10 = (bf16[4,1,16,4,8,128]{5,4,3,2,0,1:T(8,128)(2,1)S(1)}, bf16[4,1,16,4,8,128]{5,4,3,2,0,1:T(8,128)(2,1)S(1)}, u32[]{:S(2)}, u32[]{:S(2)}) collective-permute-start(bf16[4,1,16,4,8,128]{5,4,3,2,0,1:T(8,128)(2,1)S(1)} %get-tuple-element.39), channel_id=1, source_target_pairs={{0,1},{1,2},{2,3},{3,4},{4,5},{5,6},{6,7},{7,8},{8,9},{9,10},{10,1... | collective-permute-start | bytes 1572872 | tf_op jit(solution)/shard_map/ppermute | solution.py:107
  48.0 1.9 %collective-permute-start.11 = (bf16[4,1,16,4,8,128]{5,4,3,2,0,1:T(8,128)(2,1)S(1)}, bf16[4,1,16,4,8,128]{5,4,3,2,0,1:T(8,128)(2,1)S(1)}, u32[]{:S(2)}, u32[]{:S(2)}) collective-permute-start(bf16[4,1,16,4,8,128]{5,4,3,2,0,1:T(8,128)(2,1)S(1)} %get-tuple-element.40), channel_id=1, source_target_pairs={{1,0},{2,1},{3,2},{4,3},{5,4},{6,5},{7,6},{8,7},{9,8},{10,9},{11,1... | collective-permute-start | bytes 1572872 | tf_op jit(solution)/shard_map/ppermute | solution.py:108
  50.4 5.1 %collective-permute-start.2 = (bf16[5,1,16,4,8,128]{5,4,3,2,0,1:T(8,128)(2,1)S(1)}, bf16[5,1,16,4,8,128]{5,4,3,2,0,1:T(8,128)(2,1)S(1)}, u32[]{:S(2)}, u32[]{:S(2)}) collective-permute-start(bf16[5,1,16,4,8,128]{5,4,3,2,0,1:T(8,128)(2,1)S(1)} %get-tuple-element.37), channel_id=1, source_target_pairs={{0,1},{1,2},{2,3},{3,4},{4,5},{5,6},{6,7},{7,8},{8,9},{9,10},{10,1... | collective-permute-start | bytes 1966088 | tf_op jit(solution)/shard_map/ppermute | solution.py:107
  55.5 1.9 %collective-permute-start.3 = (bf16[5,1,16,4,8,128]{5,4,3,2,0,1:T(8,128)(2,1)S(1)}, bf16[5,1,16,4,8,128]{5,4,3,2,0,1:T(8,128)(2,1)S(1)}, u32[]{:S(2)}, u32[]{:S(2)}) collective-permute-start(bf16[5,1,16,4,8,128]{5,4,3,2,0,1:T(8,128)(2,1)S(1)} %get-tuple-element.38), channel_id=1, source_target_pairs={{1,0},{2,1},{3,2},{4,3},{5,4},{6,5},{7,6},{8,7},{9,8},{10,9},{11,1... | collective-permute-start | bytes 1966088 | tf_op jit(solution)/shard_map/ppermute | solution.py:108
  58.1 2.3 %collective-permute-done.10 = bf16[4,1,16,4,8,128]{5,4,3,2,0,1:T(8,128)(2,1)S(1)} collective-permute-done((bf16[4,1,16,4,8,128]{5,4,3,2,0,1:T(8,128)(2,1)S(1)}, bf16[4,1,16,4,8,128]{5,4,3,2,0,1:T(8,128)(2,1)S(1)}, u32[]{:S(2)}, u32[]{:S(2)}) %collective-permute-start.10) | collective-permute-done | bytes 524320 | tf_op jit(solution)/shard_map/ppermute | solution.py:107
  60.4 5.6 %collective-permute-done.11 = bf16[4,1,16,4,8,128]{5,4,3,2,0,1:T(8,128)(2,1)S(1)} collective-permute-done((bf16[4,1,16,4,8,128]{5,4,3,2,0,1:T(8,128)(2,1)S(1)}, bf16[4,1,16,4,8,128]{5,4,3,2,0,1:T(8,128)(2,1)S(1)}, u32[]{:S(2)}, u32[]{:S(2)}) %collective-permute-start.11) | collective-permute-done | bytes 524320 | tf_op jit(solution)/shard_map/ppermute | solution.py:108
  66.3 0.9 slice.121
  67.1 0.7 pad_maximum_fusion.11
  67.9 0.8 pad_maximum_fusion.8
  68.6 0.8 pad_maximum_fusion.5
  69.5 2.1 %collective-permute-done.2 = bf16[5,1,16,4,8,128]{5,4,3,2,0,1:T(8,128)(2,1)S(1)} collective-permute-done((bf16[5,1,16,4,8,128]{5,4,3,2,0,1:T(8,128)(2,1)S(1)}, bf16[5,1,16,4,8,128]{5,4,3,2,0,1:T(8,128)(2,1)S(1)}, u32[]{:S(2)}, u32[]{:S(2)}) %collective-permute-start.2) | collective-permute-done | bytes 655392 | tf_op jit(solution)/shard_map/ppermute | solution.py:107
  71.6 5.3 %collective-permute-done.3 = bf16[5,1,16,4,8,128]{5,4,3,2,0,1:T(8,128)(2,1)S(1)} collective-permute-done((bf16[5,1,16,4,8,128]{5,4,3,2,0,1:T(8,128)(2,1)S(1)}, bf16[5,1,16,4,8,128]{5,4,3,2,0,1:T(8,128)(2,1)S(1)}, u32[]{:S(2)}, u32[]{:S(2)}) %collective-permute-start.3) | collective-permute-done | bytes 655392 | tf_op jit(solution)/shard_map/ppermute | solution.py:108
  76.9 0.7 pad_maximum_fusion.12
  77.7 0.8 pad_maximum_fusion.9
  78.4 0.8 pad_maximum_fusion.6
  79.2 2.5 %pad_maximum_fusion = bf16[5,1,16,16,8,128]{5,4,3,2,0,1:T(8,128)(2,1)S(1)} fusion(bf16[5,1,16,4,8,128]{5,4,3,2,0,1:T(8,128)(2,1)S(1)} %collective-permute-done.3, bf16[5,1,4,8,8,128]{5,4,3,2,0,1:T(8,128)(2,1)S(1)} %collective-permute-done.1, bf16[4,1,8,8,8,128]{5,4,3,2,0,1:T(8,128)(2,1)S(1)} %get-tuple-element.42, ...), kind=kLoop, calls=%fused_computation | loop fusion | flops 6553600 | bytes 5242880 | tf_op jit(solution)/shard_map/concatenate | solution.py:109
  81.7 1.1 fusion.1
  82.8 5.2 %shard_map.64 = (bf16[1568,128]{1,0:T(8,128)(2,1)}, bf16[512,128]{1,0:T(8,128)(2,1)}) custom-call(s32[2]{0:T(128)} %pad_add_fusion.offs_ref, bf16[2048,128]{1,0:T(8,128)(2,1)} %bitcast.35, bf16[2048,128]{1,0:T(8,128)(2,1)} %bitcast.34, bf16[8,14,128,128]{3,2,1,0:T(8,128)(2,1)} %all-gather.2.cloned.1.call-done.w_hbm), custom_call_target="tpu_custom_call" | custom-call | flops 667942912 | bytes 2007040 | tf_op jit(solution)/shard_map/pallas_call | solution.py:80
  88.0 4.5 %shard_map.65 = (bf16[1152,128]{1,0:T(8,128)(2,1)}, bf16[512,128]{1,0:T(8,128)(2,1)}) custom-call(s32[2]{0:T(128)} %pad_add_fusion.offs_ref, bf16[1568,128]{1,0:T(8,128)(2,1)} %get-tuple-element.21.prior_ref, bf16[1568,128]{1,0:T(8,128)(2,1)} %bitcast.37, bf16[8,14,128,128]{3,2,1,0:T(8,128)(2,1)} %all-gather.2.cloned.1.call-done.w_hbm), custom_call_target="tpu_custom_call" | custom-call | flops 490733568 | bytes 1654784 | tf_op jit(solution)/shard_map/pallas_call | solution.py:80
  92.6 4.0 %shard_map.66 = (bf16[800,128]{1,0:T(8,128)(2,1)}, bf16[512,128]{1,0:T(8,128)(2,1)}) custom-call(s32[2]{0:T(128)} %pad_add_fusion.offs_ref, bf16[1152,128]{1,0:T(8,128)(2,1)} %get-tuple-element.23.prior_ref, bf16[1152,128]{1,0:T(8,128)(2,1)} %bitcast.39, bf16[8,14,128,128]{3,2,1,0:T(8,128)(2,1)} %all-gather.2.cloned.1.call-done.w_hbm), custom_call_target="tpu_custom_call" | custom-call | flops 340787200 | bytes 1351680 | tf_op jit(solution)/shard_map/pallas_call | solution.py:80
  96.6 3.7 %shard_map.67 = (bf16[512,128]{1,0:T(8,128)(2,1)}, bf16[512,128]{1,0:T(8,128)(2,1)}) custom-call(s32[2]{0:T(128)} %pad_add_fusion.offs_ref, bf16[800,128]{1,0:T(8,128)(2,1)} %get-tuple-element.25.prior_ref, bf16[800,128]{1,0:T(8,128)(2,1)} %bitcast.45, bf16[8,14,128,128]{3,2,1,0:T(8,128)(2,1)} %all-gather.2.cloned.1.call-done.w_hbm), custom_call_target="tpu_custom_call" | custom-call | flops 218103808 | bytes 1097728 | tf_op jit(solution)/shard_map/pallas_call | solution.py:80
  100.4 0.9 fusion.6
  101.3 3.5 %collective-permute-start.4 = (bf16[1,4,8,8,128]{4,3,2,1,0:T(8,128)(2,1)S(1)}, bf16[1,4,8,8,128]{4,3,2,1,0:T(8,128)(2,1)S(1)}, u32[]{:S(2)}, u32[]{:S(2)}) collective-permute-start(bf16[1,4,8,8,128]{4,3,2,1,0:T(8,128)(2,1)S(1)} %get-tuple-element.49), channel_id=1, source_target_pairs={{0,16},{16,32},{32,48},{1,17},{17,33},{33,49},{2,18},{18,34},{34,5... | collective-permute-start | bytes 196616 | tf_op jit(solution)/shard_map/ppermute | solution.py:107
  104.8 1.3 collective-permute-start.5
  106.7 4.3 %collective-permute-done.5 = bf16[1,4,8,8,128]{4,3,2,1,0:T(8,128)(2,1)S(1)} collective-permute-done((bf16[1,4,8,8,128]{4,3,2,1,0:T(8,128)(2,1)S(1)}, bf16[1,4,8,8,128]{4,3,2,1,0:T(8,128)(2,1)S(1)}, u32[]{:S(2)}, u32[]{:S(2)}) %collective-permute-start.5) | collective-permute-done | bytes 65568 | tf_op jit(solution)/shard_map/ppermute | solution.py:108
  110.9 0.9 pad_maximum_fusion.10
  111.9 2.8 %collective-permute-start.6 = (bf16[1,16,4,8,128]{4,3,2,1,0:T(8,128)(2,1)S(1)}, bf16[1,16,4,8,128]{4,3,2,1,0:T(8,128)(2,1)S(1)}, u32[]{:S(2)}, u32[]{:S(2)}) collective-permute-start(bf16[1,16,4,8,128]{4,3,2,1,0:T(8,128)(2,1)S(1)} %get-tuple-element.47), channel_id=1, source_target_pairs={{0,1},{1,2},{2,3},{3,4},{4,5},{5,6},{6,7},{7,8},{8,9},{9,10},{10,1... | collective-permute-start | bytes 393224 | tf_op jit(solution)/shard_map/ppermute | solution.py:107
  114.7 3.2 %collective-permute-start.7 = (bf16[1,16,4,8,128]{4,3,2,1,0:T(8,128)(2,1)S(1)}, bf16[1,16,4,8,128]{4,3,2,1,0:T(8,128)(2,1)S(1)}, u32[]{:S(2)}, u32[]{:S(2)}) collective-permute-start(bf16[1,16,4,8,128]{4,3,2,1,0:T(8,128)(2,1)S(1)} %get-tuple-element.48), channel_id=1, source_target_pairs={{1,0},{2,1},{3,2},{4,3},{5,4},{6,5},{7,6},{8,7},{9,8},{10,9},{11,1... | collective-permute-start | bytes 393224 | tf_op jit(solution)/shard_map/ppermute | solution.py:108
  118.0 0.7 collective-permute-done.6
  118.8 4.0 %collective-permute-done.7 = bf16[1,16,4,8,128]{4,3,2,1,0:T(8,128)(2,1)S(1)} collective-permute-done((bf16[1,16,4,8,128]{4,3,2,1,0:T(8,128)(2,1)S(1)}, bf16[1,16,4,8,128]{4,3,2,1,0:T(8,128)(2,1)S(1)}, u32[]{:S(2)}, u32[]{:S(2)}) %collective-permute-start.7) | collective-permute-done | bytes 131104 | tf_op jit(solution)/shard_map/ppermute | solution.py:108
  122.8 0.9 pad_maximum_fusion.4
  123.7 5.3 %shard_map.68 = (bf16[1568,128]{1,0:T(8,128)(2,1)}, bf16[512,128]{1,0:T(8,128)(2,1)}) custom-call(s32[2]{0:T(128)} %pad_add_fusion.offs_ref, bf16[2048,128]{1,0:T(8,128)(2,1)} %bitcast.33, bf16[2048,128]{1,0:T(8,128)(2,1)} %bitcast.32, bf16[8,14,128,128]{3,2,1,0:T(8,128)(2,1)} %all-gather.2.cloned.1.call-done.w_hbm), custom_call_target="tpu_custom_call" | custom-call | flops 667942912 | bytes 2007040 | tf_op jit(solution)/shard_map/pallas_call | solution.py:80
  128.9 0.9 constant_dynamic-update-slice_fusion.3
  129.9 4.5 %shard_map.69 = (bf16[1152,128]{1,0:T(8,128)(2,1)}, bf16[512,128]{1,0:T(8,128)(2,1)}) custom-call(s32[2]{0:T(128)} %pad_add_fusion.offs_ref, bf16[1568,128]{1,0:T(8,128)(2,1)} %get-tuple-element.29.prior_ref, bf16[1568,128]{1,0:T(8,128)(2,1)} %bitcast.36, bf16[8,14,128,128]{3,2,1,0:T(8,128)(2,1)} %all-gather.2.cloned.1.call-done.w_hbm), custom_call_target="tpu_custom_call" | custom-call | flops 490733568 | bytes 1654784 | tf_op jit(solution)/shard_map/pallas_call | solution.py:80
  134.4 0.9 constant_dynamic-update-slice_fusion.2
  135.3 4.1 %shard_map.70 = (bf16[800,128]{1,0:T(8,128)(2,1)}, bf16[512,128]{1,0:T(8,128)(2,1)}) custom-call(s32[2]{0:T(128)} %pad_add_fusion.offs_ref, bf16[1152,128]{1,0:T(8,128)(2,1)} %get-tuple-element.31.prior_ref, bf16[1152,128]{1,0:T(8,128)(2,1)} %bitcast.38, bf16[8,14,128,128]{3,2,1,0:T(8,128)(2,1)} %all-gather.2.cloned.1.call-done.w_hbm), custom_call_target="tpu_custom_call" | custom-call | flops 340787200 | bytes 1351680 | tf_op jit(solution)/shard_map/pallas_call | solution.py:80
  139.4 0.9 constant_dynamic-update-slice_fusion.1
  140.3 3.7 %shard_map.71 = (bf16[512,128]{1,0:T(8,128)(2,1)}, bf16[512,128]{1,0:T(8,128)(2,1)}) custom-call(s32[2]{0:T(128)} %pad_add_fusion.offs_ref, bf16[800,128]{1,0:T(8,128)(2,1)} %get-tuple-element.33.prior_ref, bf16[800,128]{1,0:T(8,128)(2,1)} %bitcast.44, bf16[8,14,128,128]{3,2,1,0:T(8,128)(2,1)} %all-gather.2.cloned.1.call-done.w_hbm), custom_call_target="tpu_custom_call" | custom-call | flops 218103808 | bytes 1097728 | tf_op jit(solution)/shard_map/pallas_call | solution.py:80
  144.0 0.9 constant_dynamic-update-slice_fusion
  144.9 18.5 %all_to_all.18 = bf16[8,1,8,8,8,128]{5,4,3,2,1,0:T(8,128)(2,1)S(1)} all-to-all(bf16[8,1,8,8,8,128]{5,4,3,2,1,0:T(8,128)(2,1)S(1)} %constant_dynamic-update-slice_fusion), channel_id=1, replica_groups=mesh['section'=8,'frames'=4,'space'=16] {'section'}, dimensions={0} | all-to-all | bytes 2097152 | tf_op jit(solution)/shard_map/all_to_all | solution.py:184
  163.5 1.0 copy.24
  (35 shorter events, 2.5 us)
Async XLA Ops:
  6.5 28.1 %copy-start = (bf16[8,8,8,8,128]{4,3,2,1,0:T(8,128)(2,1)S(1)}, bf16[8,8,8,8,128]{4,3,2,1,0:T(8,128)(2,1)}, u32[]{:S(2)}) copy-start(bf16[8,8,8,8,128]{4,3,2,1,0:T(8,128)(2,1)} %param.6) | copy-start | bytes 3145732
  6.5 76.2 %all-gather.2.cloned.1.call-start = ((), (), s32[]{:S(2)}) async-start(), calls=%async_computation.2 | async-start | bytes 4128768 | tf_op jit(solution)/shard_map/all_gather | solution.py:153
  29.8 10.8 %collective-permute-start.8 = (bf16[4,1,4,8,8,128]{5,4,3,2,0,1:T(8,128)(2,1)S(1)}, bf16[4,1,4,8,8,128]{5,4,3,2,0,1:T(8,128)(2,1)S(1)}, u32[]{:S(2)}, u32[]{:S(2)}) collective-permute-start(bf16[4,1,4,8,8,128]{5,4,3,2,0,1:T(8,128)(2,1)S(1)} %get-tuple-element.45), channel_id=1, source_target_pairs={{0,16},{16,32},{32,48},{1,17},{17,33},{33,49},{2,18},{18,34},{34,5... | collective-permute-start | bytes 786440 | tf_op jit(solution)/shard_map/ppermute | solution.py:107
  33.3 9.4 %collective-permute-start.9 = (bf16[4,1,4,8,8,128]{5,4,3,2,0,1:T(8,128)(2,1)S(1)}, bf16[4,1,4,8,8,128]{5,4,3,2,0,1:T(8,128)(2,1)S(1)}, u32[]{:S(2)}, u32[]{:S(2)}) collective-permute-start(bf16[4,1,4,8,8,128]{5,4,3,2,0,1:T(8,128)(2,1)S(1)} %get-tuple-element.46), channel_id=1, source_target_pairs={{16,0},{32,16},{48,32},{17,1},{33,17},{49,33},{18,2},{34,18},{50,3... | collective-permute-start | bytes 786440 | tf_op jit(solution)/shard_map/ppermute | solution.py:108
  34.7 15.2 %collective-permute-start = (bf16[5,1,4,8,8,128]{5,4,3,2,0,1:T(8,128)(2,1)S(1)}, bf16[5,1,4,8,8,128]{5,4,3,2,0,1:T(8,128)(2,1)S(1)}, u32[]{:S(2)}, u32[]{:S(2)}) collective-permute-start(bf16[5,1,4,8,8,128]{5,4,3,2,0,1:T(8,128)(2,1)S(1)} %get-tuple-element.43), channel_id=1, source_target_pairs={{0,16},{16,32},{32,48},{1,17},{17,33},{33,49},{2,18},{18,34},{34,5... | collective-permute-start | bytes 983048 | tf_op jit(solution)/shard_map/ppermute | solution.py:107
  39.3 10.6 %collective-permute-start.1 = (bf16[5,1,4,8,8,128]{5,4,3,2,0,1:T(8,128)(2,1)S(1)}, bf16[5,1,4,8,8,128]{5,4,3,2,0,1:T(8,128)(2,1)S(1)}, u32[]{:S(2)}, u32[]{:S(2)}) collective-permute-start(bf16[5,1,4,8,8,128]{5,4,3,2,0,1:T(8,128)(2,1)S(1)} %get-tuple-element.44), channel_id=1, source_target_pairs={{16,0},{32,16},{48,32},{17,1},{33,17},{49,33},{18,2},{34,18},{50,3... | collective-permute-start | bytes 983048 | tf_op jit(solution)/shard_map/ppermute | solution.py:108
  42.9 17.4 %collective-permute-start.10 = (bf16[4,1,16,4,8,128]{5,4,3,2,0,1:T(8,128)(2,1)S(1)}, bf16[4,1,16,4,8,128]{5,4,3,2,0,1:T(8,128)(2,1)S(1)}, u32[]{:S(2)}, u32[]{:S(2)}) collective-permute-start(bf16[4,1,16,4,8,128]{5,4,3,2,0,1:T(8,128)(2,1)S(1)} %get-tuple-element.39), channel_id=1, source_target_pairs={{0,1},{1,2},{2,3},{3,4},{4,5},{5,6},{6,7},{7,8},{8,9},{9,10},{10,1... | collective-permute-start | bytes 1572872 | tf_op jit(solution)/shard_map/ppermute | solution.py:107
  48.0 18.0 %collective-permute-start.11 = (bf16[4,1,16,4,8,128]{5,4,3,2,0,1:T(8,128)(2,1)S(1)}, bf16[4,1,16,4,8,128]{5,4,3,2,0,1:T(8,128)(2,1)S(1)}, u32[]{:S(2)}, u32[]{:S(2)}) collective-permute-start(bf16[4,1,16,4,8,128]{5,4,3,2,0,1:T(8,128)(2,1)S(1)} %get-tuple-element.40), channel_id=1, source_target_pairs={{1,0},{2,1},{3,2},{4,3},{5,4},{6,5},{7,6},{8,7},{9,8},{10,9},{11,1... | collective-permute-start | bytes 1572872 | tf_op jit(solution)/shard_map/ppermute | solution.py:108
  50.4 21.2 %collective-permute-start.2 = (bf16[5,1,16,4,8,128]{5,4,3,2,0,1:T(8,128)(2,1)S(1)}, bf16[5,1,16,4,8,128]{5,4,3,2,0,1:T(8,128)(2,1)S(1)}, u32[]{:S(2)}, u32[]{:S(2)}) collective-permute-start(bf16[5,1,16,4,8,128]{5,4,3,2,0,1:T(8,128)(2,1)S(1)} %get-tuple-element.37), channel_id=1, source_target_pairs={{0,1},{1,2},{2,3},{3,4},{4,5},{5,6},{6,7},{7,8},{8,9},{9,10},{10,1... | collective-permute-start | bytes 1966088 | tf_op jit(solution)/shard_map/ppermute | solution.py:107
  55.5 21.4 %collective-permute-start.3 = (bf16[5,1,16,4,8,128]{5,4,3,2,0,1:T(8,128)(2,1)S(1)}, bf16[5,1,16,4,8,128]{5,4,3,2,0,1:T(8,128)(2,1)S(1)}, u32[]{:S(2)}, u32[]{:S(2)}) collective-permute-start(bf16[5,1,16,4,8,128]{5,4,3,2,0,1:T(8,128)(2,1)S(1)} %get-tuple-element.38), channel_id=1, source_target_pairs={{1,0},{2,1},{3,2},{4,3},{5,4},{6,5},{7,6},{8,7},{9,8},{10,9},{11,1... | collective-permute-start | bytes 1966088 | tf_op jit(solution)/shard_map/ppermute | solution.py:108
  96.6 9.5 %copy-start.4 = (bf16[512,128]{1,0:T(8,128)(2,1)S(1)}, bf16[512,128]{1,0:T(8,128)(2,1)}, u32[]{:S(2)}) copy-start(bf16[512,128]{1,0:T(8,128)(2,1)} %get-tuple-element.20) | copy-start | bytes 393220
  96.6 9.5 %copy-start.5 = (bf16[512,128]{1,0:T(8,128)(2,1)S(1)}, bf16[512,128]{1,0:T(8,128)(2,1)}, u32[]{:S(2)}) copy-start(bf16[512,128]{1,0:T(8,128)(2,1)} %get-tuple-element.22) | copy-start | bytes 393220
  96.6 21.3 %copy-start.2 = (bf16[512,128]{1,0:T(8,128)(2,1)S(1)}, bf16[512,128]{1,0:T(8,128)(2,1)}, u32[]{:S(2)}) copy-start(bf16[512,128]{1,0:T(8,128)(2,1)} %get-tuple-element.24) | copy-start | bytes 393220
  100.4 17.6 %copy-start.3 = (bf16[512,128]{1,0:T(8,128)(2,1)S(1)}, bf16[512,128]{1,0:T(8,128)(2,1)}, u32[]{:S(2)}) copy-start(bf16[512,128]{1,0:T(8,128)(2,1)} %get-tuple-element.26) | copy-start | bytes 393220
  100.4 22.4 %copy-start.1 = (bf16[512,128]{1,0:T(8,128)(2,1)S(1)}, bf16[512,128]{1,0:T(8,128)(2,1)}, u32[]{:S(2)}) copy-start(bf16[512,128]{1,0:T(8,128)(2,1)} %get-tuple-element.27) | copy-start | bytes 393220
  101.3 5.4 %collective-permute-start.4 = (bf16[1,4,8,8,128]{4,3,2,1,0:T(8,128)(2,1)S(1)}, bf16[1,4,8,8,128]{4,3,2,1,0:T(8,128)(2,1)S(1)}, u32[]{:S(2)}, u32[]{:S(2)}) collective-permute-start(bf16[1,4,8,8,128]{4,3,2,1,0:T(8,128)(2,1)S(1)} %get-tuple-element.49), channel_id=1, source_target_pairs={{0,16},{16,32},{32,48},{1,17},{17,33},{33,49},{2,18},{18,34},{34,5... | collective-permute-start | bytes 196616 | tf_op jit(solution)/shard_map/ppermute | solution.py:107
  104.8 6.2 %collective-permute-start.5 = (bf16[1,4,8,8,128]{4,3,2,1,0:T(8,128)(2,1)S(1)}, bf16[1,4,8,8,128]{4,3,2,1,0:T(8,128)(2,1)S(1)}, u32[]{:S(2)}, u32[]{:S(2)}) collective-permute-start(bf16[1,4,8,8,128]{4,3,2,1,0:T(8,128)(2,1)S(1)} %get-tuple-element.50), channel_id=1, source_target_pairs={{16,0},{32,16},{48,32},{17,1},{33,17},{49,33},{18,2},{34,18},{50,3... | collective-permute-start | bytes 196616 | tf_op jit(solution)/shard_map/ppermute | solution.py:108
  111.9 6.9 %collective-permute-start.6 = (bf16[1,16,4,8,128]{4,3,2,1,0:T(8,128)(2,1)S(1)}, bf16[1,16,4,8,128]{4,3,2,1,0:T(8,128)(2,1)S(1)}, u32[]{:S(2)}, u32[]{:S(2)}) collective-permute-start(bf16[1,16,4,8,128]{4,3,2,1,0:T(8,128)(2,1)S(1)} %get-tuple-element.47), channel_id=1, source_target_pairs={{0,1},{1,2},{2,3},{3,4},{4,5},{5,6},{6,7},{7,8},{8,9},{9,10},{10,1... | collective-permute-start | bytes 393224 | tf_op jit(solution)/shard_map/ppermute | solution.py:107
  114.7 8.1 %collective-permute-start.7 = (bf16[1,16,4,8,128]{4,3,2,1,0:T(8,128)(2,1)S(1)}, bf16[1,16,4,8,128]{4,3,2,1,0:T(8,128)(2,1)S(1)}, u32[]{:S(2)}, u32[]{:S(2)}) collective-permute-start(bf16[1,16,4,8,128]{4,3,2,1,0:T(8,128)(2,1)S(1)} %get-tuple-element.48), channel_id=1, source_target_pairs={{1,0},{2,1},{3,2},{4,3},{5,4},{6,5},{7,6},{8,7},{9,8},{10,9},{11,1... | collective-permute-start | bytes 393224 | tf_op jit(solution)/shard_map/ppermute | solution.py:108
Sparse Core Ops, SparseCore 0:
  9.5 40.9 all-gather.1

commit v6 on v5

--- a/solution.py
+++ b/solution.py
@@ -99,15 +99,44 @@
 
 
 def extend(block, width, frame_dim, row_dim):
-    for axis, dim in (("frames", frame_dim), ("space", row_dim)):
-        count = lax.axis_size(axis)
-        forward = [(i, i + 1) for i in range(count - 1)]
-        backward = [(i + 1, i) for i in range(count - 1)]
-        size = block.shape[dim]
-        low = lax.ppermute(lax.slice_in_dim(block, size - width, size, axis=dim), axis, forward)
-        high = lax.ppermute(lax.slice_in_dim(block, 0, width, axis=dim), axis, backward)
-        block = jnp.concatenate([low, block, high], axis=dim)
-    return block
+    frames_count = lax.axis_size("frames")
+    space_count = lax.axis_size("space")
+    num_frames = block.shape[frame_dim]
+    num_rows = block.shape[row_dim]
+
+    def cut(x, f0, f1, r0, r1):
+        x = lax.slice_in_dim(x, f0, f1, axis=frame_dim)
+        return lax.slice_in_dim(x, r0, r1, axis=row_dim)
+
+    def send(piece, df, dr):
+        if dr == 0:
+            pairs = [(i, i + df) for i in range(frames_count) if 0 <= i + df < frames_count]
+            return lax.ppermute(piece, "frames", pairs)
+        if df == 0:
+            pairs = [(i, i + dr) for i in range(space_count) if 0 <= i + dr < space_count]
+            return lax.ppermute(piece, "space", pairs)
+        pairs = []
+        for f in range(frames_count):
+            for r in range(space_count):
+                if 0 <= f + df < frames_count and 0 <= r + dr < space_count:
+                    pairs.append((f * space_count + r, (f + df) * space_count + r + dr))
+        return lax.ppermute(piece, ("frames", "space"), pairs)
+
+    w = width
+    lo_f, hi_f = (num_frames - w, num_frames), (0, w)
+    lo_r, hi_r = (num_rows - w, num_rows), (0, w)
+    all_f, all_r = (0, num_frames), (0, num_rows)
+    grid = {}
+    for sf, (src_f, df) in enumerate(((lo_f, 1), (all_f, 0), (hi_f, -1))):
+        for sr, (src_r, dr) in enumerate(((lo_r, 1), (all_r, 0), (hi_r, -1))):
+            if df == 0 and dr == 0:
+                grid[sf, sr] = block
+            else:
+                grid[sf, sr] = send(cut(block, *src_f, *src_r), df, dr)
+    bands = [
+        jnp.concatenate([grid[sf, 0], grid[sf, 1], grid[sf, 2]], axis=row_dim) for sf in range(3)
+    ]
+    return jnp.concatenate(bands, axis=frame_dim)
 
 
 def denoise(offs, previous, noise_part, packed, k, num_frames, num_rows, totals):

time: 172 us -> 209 us (1.22)
  the two profiles are of different devices: /device:TPU:96 before, /device:TPU:144 now
where the time goes in v6:
time: 209 us; the launch traced here: 207 us
  starting transfers between devices  85.8 us (41%)
  Pallas kernels  35.1 us (17%)
  waiting for transfers between devices  26.9 us (13%)
  blocking collectives  18.5 us (9%)
  other arithmetic  15.9 us (8%)
  between operations  14.7 us (7%)
  local copies, waits for them, and re-layouts  10.4 us (5%)
    ppermute x12, starting transfers between devices, send(): return lax.ppermute(piece, ('frames', 'space'), pairs)  42.8 us
    pallas_call x8, Pallas kernels, section_call(): pl.pallas_call(functools.partial(section_kernel, m, n, cols, inner, num_f...  35.1 us
    ppermute x6, starting transfers between devices, send(): return lax.ppermute(piece, 'space', pairs)  21.2 us
    all_to_all x1, blocking collectives, on_device(): return lax.all_to_all(stacked, 'section', 0, 1, tiled=True)  18.5 us
    ppermute x6, starting transfers between devices, send(): return lax.ppermute(piece, 'frames', pairs)  17.5 us
    all_to_all x1, waiting for transfers between devices, on_device(): noise_t = lax.all_to_all(section_noise[0], 'section', 0, 0, tiled=True)  15.4 us
    ppermute x12, waiting for transfers between devices, send(): return lax.ppermute(piece, ('frames', 'space'), pairs)  11.5 us
    concatenate x3, other arithmetic, extend(): return jnp.concatenate(bands, axis=frame_dim)  8.64 us
  transfers between devices with their start and end apart: 26, of which 4 were waited for; matrix products, arithmetic and copies ran while one was open for 7% of the time, Pallas kernels for 0%

profile of v6, /device:TPU:144, one launch (start us, length us, event | category | flops | bytes accessed | tf_op | source)
XLA Modules:
  0.0 207.3 jit_solution(15288054275899813438)
XLA Ops:
  7.4 1.9 maximum_maximum_fusion.3
  9.3 4.3 %all-to-all-start = ((bf16[8,8,8,8,128]{4,3,2,1,0:T(8,128)(2,1)}), bf16[8,8,8,8,128]{4,3,2,1,0:T(8,128)(2,1)S(1)}, u32[]{:S(2)}, u32[]{:S(2)}) async-start(bf16[8,8,8,8,128]{4,3,2,1,0:T(8,128)(2,1)} %bitcast.44), calls=%async_computation | async-start | bytes 2097152 | tf_op jit(solution)/shard_map/all_to_all | solution.py:173
  14.2 15.4 %all-to-all-done = bf16[8,8,8,8,128]{4,3,2,1,0:T(8,128)(2,1)S(1)} async-done(((bf16[8,8,8,8,128]{4,3,2,1,0:T(8,128)(2,1)}), bf16[8,8,8,8,128]{4,3,2,1,0:T(8,128)(2,1)S(1)}, u32[]{:S(2)}, u32[]{:S(2)}) %all-to-all-start) | async-done | bytes 1048608 | tf_op jit(solution)/shard_map/all_to_all | solution.py:173
  29.7 4.5 %collective-permute-start.16 = (bf16[4,1,4,4,8,128]{5,4,3,2,0,1:T(8,128)(2,1)S(1)}, bf16[4,1,4,4,8,128]{5,4,3,2,0,1:T(8,128)(2,1)S(1)}, u32[]{:S(2)}, u32[]{:S(2)}) collective-permute-start(bf16[4,1,4,4,8,128]{5,4,3,2,0,1:T(8,128)(2,1)S(1)} %get-tuple-element.47), channel_id=1, source_target_pairs={{0,17},{1,18},{2,19},{3,20},{4,21},{5,22},{6,23},{7,24},{8,25},{9,... | collective-permute-start | bytes 393224 | tf_op jit(solution)/shard_map/ppermute | solution.py:123
  34.3 1.9 collective-permute-start.18
  36.2 4.8 %collective-permute-start.21 = (bf16[4,1,4,4,8,128]{5,4,3,2,0,1:T(8,128)(2,1)S(1)}, bf16[4,1,4,4,8,128]{5,4,3,2,0,1:T(8,128)(2,1)S(1)}, u32[]{:S(2)}, u32[]{:S(2)}) collective-permute-start(bf16[4,1,4,4,8,128]{5,4,3,2,0,1:T(8,128)(2,1)S(1)} %get-tuple-element.49), channel_id=1, source_target_pairs={{16,1},{17,2},{18,3},{19,4},{20,5},{21,6},{22,7},{23,8},{24,9},{25... | collective-permute-start | bytes 393224 | tf_op jit(solution)/shard_map/ppermute | solution.py:123
  41.1 2.4 %collective-permute-start.17 = (bf16[4,1,4,8,8,128]{5,4,3,2,0,1:T(8,128)(2,1)S(1)}, bf16[4,1,4,8,8,128]{5,4,3,2,0,1:T(8,128)(2,1)S(1)}, u32[]{:S(2)}, u32[]{:S(2)}) collective-permute-start(bf16[4,1,4,8,8,128]{5,4,3,2,0,1:T(8,128)(2,1)S(1)} %get-tuple-element.51), channel_id=1, source_target_pairs={{0,16},{16,32},{32,48},{1,17},{17,33},{33,49},{2,18},{18,34},{34,5... | collective-permute-start | bytes 786440 | tf_op jit(solution)/shard_map/ppermute | solution.py:114
  43.5 3.8 %collective-permute-start.19 = (bf16[4,1,8,4,8,128]{5,4,3,2,0,1:T(8,128)(2,1)S(1)}, bf16[4,1,8,4,8,128]{5,4,3,2,0,1:T(8,128)(2,1)S(1)}, u32[]{:S(2)}, u32[]{:S(2)}) collective-permute-start(bf16[4,1,8,4,8,128]{5,4,3,2,0,1:T(8,128)(2,1)S(1)} %get-tuple-element.53), channel_id=1, source_target_pairs={{0,1},{1,2},{2,3},{3,4},{4,5},{5,6},{6,7},{7,8},{8,9},{9,10},{10,1... | collective-permute-start | bytes 786440 | tf_op jit(solution)/shard_map/ppermute | solution.py:117
  47.4 3.2 %collective-permute-start.20 = (bf16[4,1,8,4,8,128]{5,4,3,2,0,1:T(8,128)(2,1)S(1)}, bf16[4,1,8,4,8,128]{5,4,3,2,0,1:T(8,128)(2,1)S(1)}, u32[]{:S(2)}, u32[]{:S(2)}) collective-permute-start(bf16[4,1,8,4,8,128]{5,4,3,2,0,1:T(8,128)(2,1)S(1)} %get-tuple-element.54), channel_id=1, source_target_pairs={{1,0},{2,1},{3,2},{4,3},{5,4},{6,5},{7,6},{8,7},{9,8},{10,9},{11,1... | collective-permute-start | bytes 786440 | tf_op jit(solution)/shard_map/ppermute | solution.py:117
  50.6 3.5 %collective-permute-start.22 = (bf16[4,1,4,8,8,128]{5,4,3,2,0,1:T(8,128)(2,1)S(1)}, bf16[4,1,4,8,8,128]{5,4,3,2,0,1:T(8,128)(2,1)S(1)}, u32[]{:S(2)}, u32[]{:S(2)}) collective-permute-start(bf16[4,1,4,8,8,128]{5,4,3,2,0,1:T(8,128)(2,1)S(1)} %get-tuple-element.52), channel_id=1, source_target_pairs={{16,0},{32,16},{48,32},{17,1},{33,17},{49,33},{18,2},{34,18},{50,3... | collective-permute-start | bytes 786440 | tf_op jit(solution)/shard_map/ppermute | solution.py:114
  54.2 3.4 %collective-permute-start.23 = (bf16[4,1,4,4,8,128]{5,4,3,2,0,1:T(8,128)(2,1)S(1)}, bf16[4,1,4,4,8,128]{5,4,3,2,0,1:T(8,128)(2,1)S(1)}, u32[]{:S(2)}, u32[]{:S(2)}) collective-permute-start(bf16[4,1,4,4,8,128]{5,4,3,2,0,1:T(8,128)(2,1)S(1)} %get-tuple-element.48), channel_id=1, source_target_pairs={{17,0},{18,1},{19,2},{20,3},{21,4},{22,5},{23,6},{24,7},{25,8},{26... | collective-permute-start | bytes 393224 | tf_op jit(solution)/shard_map/ppermute | solution.py:123
  57.7 4.2 %collective-permute-done.23 = bf16[4,1,4,4,8,128]{5,4,3,2,0,1:T(8,128)(2,1)S(1)} collective-permute-done((bf16[4,1,4,4,8,128]{5,4,3,2,0,1:T(8,128)(2,1)S(1)}, bf16[4,1,4,4,8,128]{5,4,3,2,0,1:T(8,128)(2,1)S(1)}, u32[]{:S(2)}, u32[]{:S(2)}) %collective-permute-start.23) | collective-permute-done | bytes 131104 | tf_op jit(solution)/shard_map/ppermute | solution.py:123
  61.9 1.9 collective-permute-start
  63.8 1.9 collective-permute-start.2
  65.8 7.7 %collective-permute-start.5 = (bf16[5,1,4,4,8,128]{5,4,3,2,0,1:T(8,128)(2,1)S(1)}, bf16[5,1,4,4,8,128]{5,4,3,2,0,1:T(8,128)(2,1)S(1)}, u32[]{:S(2)}, u32[]{:S(2)}) collective-permute-start(bf16[5,1,4,4,8,128]{5,4,3,2,0,1:T(8,128)(2,1)S(1)} %get-tuple-element.41), channel_id=1, source_target_pairs={{16,1},{17,2},{18,3},{19,4},{20,5},{21,6},{22,7},{23,8},{24,9},{25... | collective-permute-start | bytes 491528 | tf_op jit(solution)/shard_map/ppermute | solution.py:123
  73.5 1.9 collective-permute-start.1
  75.5 5.1 %collective-permute-start.3 = (bf16[5,1,8,4,8,128]{5,4,3,2,0,1:T(8,128)(2,1)S(1)}, bf16[5,1,8,4,8,128]{5,4,3,2,0,1:T(8,128)(2,1)S(1)}, u32[]{:S(2)}, u32[]{:S(2)}) collective-permute-start(bf16[5,1,8,4,8,128]{5,4,3,2,0,1:T(8,128)(2,1)S(1)} %get-tuple-element.45), channel_id=1, source_target_pairs={{0,1},{1,2},{2,3},{3,4},{4,5},{5,6},{6,7},{7,8},{8,9},{9,10},{10,1... | collective-permute-start | bytes 983048 | tf_op jit(solution)/shard_map/ppermute | solution.py:117
  81.0 1.9 collective-permute-start.4
  82.9 3.9 %collective-permute-start.6 = (bf16[5,1,4,8,8,128]{5,4,3,2,0,1:T(8,128)(2,1)S(1)}, bf16[5,1,4,8,8,128]{5,4,3,2,0,1:T(8,128)(2,1)S(1)}, u32[]{:S(2)}, u32[]{:S(2)}) collective-permute-start(bf16[5,1,4,8,8,128]{5,4,3,2,0,1:T(8,128)(2,1)S(1)} %get-tuple-element.44), channel_id=1, source_target_pairs={{16,0},{32,16},{48,32},{17,1},{33,17},{49,33},{18,2},{34,18},{50,3... | collective-permute-start | bytes 983048 | tf_op jit(solution)/shard_map/ppermute | solution.py:114
  87.6 3.3 %collective-permute-start.7 = (bf16[5,1,4,4,8,128]{5,4,3,2,0,1:T(8,128)(2,1)S(1)}, bf16[5,1,4,4,8,128]{5,4,3,2,0,1:T(8,128)(2,1)S(1)}, u32[]{:S(2)}, u32[]{:S(2)}) collective-permute-start(bf16[5,1,4,4,8,128]{5,4,3,2,0,1:T(8,128)(2,1)S(1)} %get-tuple-element.42), channel_id=1, source_target_pairs={{17,0},{18,1},{19,2},{20,3},{21,4},{22,5},{23,6},{24,7},{25,8},{26... | collective-permute-start | bytes 491528 | tf_op jit(solution)/shard_map/ppermute | solution.py:123
  93.3 2.4 %collective-permute-done.7 = bf16[5,1,4,4,8,128]{5,4,3,2,0,1:T(8,128)(2,1)S(1)} collective-permute-done((bf16[5,1,4,4,8,128]{5,4,3,2,0,1:T(8,128)(2,1)S(1)}, bf16[5,1,4,4,8,128]{5,4,3,2,0,1:T(8,128)(2,1)S(1)}, u32[]{:S(2)}, u32[]{:S(2)}) %collective-permute-start.7) | collective-permute-done | bytes 163872 | tf_op jit(solution)/shard_map/ppermute | solution.py:123
  98.0 6.6 %maximum_maximum_fusion = bf16[5,1,16,16,8,128]{5,4,3,2,0,1:T(8,128)(2,1)S(1)} fusion(bf16[5,1,4,4,8,128]{5,4,3,2,0,1:T(8,128)(2,1)S(1)} %collective-permute-done.7, bf16[5,1,4,8,8,128]{5,4,3,2,0,1:T(8,128)(2,1)S(1)} %collective-permute-done.6, bf16[5,1,4,4,8,128]{5,4,3,2,0,1:T(8,128)(2,1)S(1)} %collective-permute-done.5, ...), kind=kLoop, calls=%fused_computation | loop fusion | flops 11796480 | bytes 5242880 | tf_op jit(solution)/shard_map/concatenate | solution.py:139
  104.6 1.1 fusion.7
  105.7 5.3 %shard_map.64 = (bf16[1568,128]{1,0:T(8,128)(2,1)}, bf16[512,128]{1,0:T(8,128)(2,1)}) custom-call(s32[2]{0:T(128)} %pad_add_fusion.offs_ref, bf16[2048,128]{1,0:T(8,128)(2,1)} %bitcast.35, bf16[2048,128]{1,0:T(8,128)(2,1)} %bitcast.34, bf16[8,14,128,128]{3,2,1,0:T(8,128)(2,1)} %all-gather.2.cloned.1.call-done.w_hbm), custom_call_target="tpu_custom_call" | custom-call | flops 667942912 | bytes 2007040 | tf_op jit(solution)/shard_map/pallas_call | solution.py:80
  111.0 4.5 %shard_map.65 = (bf16[1152,128]{1,0:T(8,128)(2,1)}, bf16[512,128]{1,0:T(8,128)(2,1)}) custom-call(s32[2]{0:T(128)} %pad_add_fusion.offs_ref, bf16[1568,128]{1,0:T(8,128)(2,1)} %get-tuple-element.21.prior_ref, bf16[1568,128]{1,0:T(8,128)(2,1)} %bitcast.41, bf16[8,14,128,128]{3,2,1,0:T(8,128)(2,1)} %all-gather.2.cloned.1.call-done.w_hbm), custom_call_target="tpu_custom_call" | custom-call | flops 490733568 | bytes 1654784 | tf_op jit(solution)/shard_map/pallas_call | solution.py:80
  115.5 4.0 %shard_map.66 = (bf16[800,128]{1,0:T(8,128)(2,1)}, bf16[512,128]{1,0:T(8,128)(2,1)}) custom-call(s32[2]{0:T(128)} %pad_add_fusion.offs_ref, bf16[1152,128]{1,0:T(8,128)(2,1)} %get-tuple-element.23.prior_ref, bf16[1152,128]{1,0:T(8,128)(2,1)} %bitcast.43, bf16[8,14,128,128]{3,2,1,0:T(8,128)(2,1)} %all-gather.2.cloned.1.call-done.w_hbm), custom_call_target="tpu_custom_call" | custom-call | flops 340787200 | bytes 1351680 | tf_op jit(solution)/shard_map/pallas_call | solution.py:80
  119.6 3.7 %shard_map.67 = (bf16[512,128]{1,0:T(8,128)(2,1)}, bf16[512,128]{1,0:T(8,128)(2,1)}) custom-call(s32[2]{0:T(128)} %pad_add_fusion.offs_ref, bf16[800,128]{1,0:T(8,128)(2,1)} %get-tuple-element.25.prior_ref, bf16[800,128]{1,0:T(8,128)(2,1)} %bitcast.46, bf16[8,14,128,128]{3,2,1,0:T(8,128)(2,1)} %all-gather.2.cloned.1.call-done.w_hbm), custom_call_target="tpu_custom_call" | custom-call | flops 218103808 | bytes 1097728 | tf_op jit(solution)/shard_map/pallas_call | solution.py:80
  125.9 3.9 %collective-permute-start.11 = (bf16[1,8,4,8,128]{4,3,2,1,0:T(8,128)(2,1)S(1)}, bf16[1,8,4,8,128]{4,3,2,1,0:T(8,128)(2,1)S(1)}, u32[]{:S(2)}, u32[]{:S(2)}) collective-permute-start(bf16[1,8,4,8,128]{4,3,2,1,0:T(8,128)(2,1)S(1)} %get-tuple-element.61), channel_id=1, source_target_pairs={{0,1},{1,2},{2,3},{3,4},{4,5},{5,6},{6,7},{7,8},{8,9},{9,10},{10,1... | collective-permute-start | bytes 196616 | tf_op jit(solution)/shard_map/ppermute | solution.py:117
  129.9 3.1 %collective-permute-start.12 = (bf16[1,8,4,8,128]{4,3,2,1,0:T(8,128)(2,1)S(1)}, bf16[1,8,4,8,128]{4,3,2,1,0:T(8,128)(2,1)S(1)}, u32[]{:S(2)}, u32[]{:S(2)}) collective-permute-start(bf16[1,8,4,8,128]{4,3,2,1,0:T(8,128)(2,1)S(1)} %get-tuple-element.62), channel_id=1, source_target_pairs={{1,0},{2,1},{3,2},{4,3},{5,4},{6,5},{7,6},{8,7},{9,8},{10,9},{11,1... | collective-permute-start | bytes 196616 | tf_op jit(solution)/shard_map/ppermute | solution.py:117
  133.0 1.9 collective-permute-start.10
  134.9 4.8 %collective-permute-start.13 = (bf16[1,4,4,8,128]{4,3,2,1,0:T(8,128)(2,1)S(1)}, bf16[1,4,4,8,128]{4,3,2,1,0:T(8,128)(2,1)S(1)}, u32[]{:S(2)}, u32[]{:S(2)}) collective-permute-start(bf16[1,4,4,8,128]{4,3,2,1,0:T(8,128)(2,1)S(1)} %get-tuple-element.57), channel_id=1, source_target_pairs={{16,1},{17,2},{18,3},{19,4},{20,5},{21,6},{22,7},{23,8},{24,9},{25... | collective-permute-start | bytes 98312 | tf_op jit(solution)/shard_map/ppermute | solution.py:123
  139.7 4.3 %collective-permute-start.15 = (bf16[1,4,4,8,128]{4,3,2,1,0:T(8,128)(2,1)S(1)}, bf16[1,4,4,8,128]{4,3,2,1,0:T(8,128)(2,1)S(1)}, u32[]{:S(2)}, u32[]{:S(2)}) collective-permute-start(bf16[1,4,4,8,128]{4,3,2,1,0:T(8,128)(2,1)S(1)} %get-tuple-element.56), channel_id=1, source_target_pairs={{17,0},{18,1},{19,2},{20,3},{21,4},{22,5},{23,6},{24,7},{25,8},{26... | collective-permute-start | bytes 98312 | tf_op jit(solution)/shard_map/ppermute | solution.py:123
  144.2 1.9 collective-permute-start.14
  146.1 3.9 %collective-permute-start.9 = (bf16[1,4,8,8,128]{4,3,2,1,0:T(8,128)(2,1)S(1)}, bf16[1,4,8,8,128]{4,3,2,1,0:T(8,128)(2,1)S(1)}, u32[]{:S(2)}, u32[]{:S(2)}) collective-permute-start(bf16[1,4,8,8,128]{4,3,2,1,0:T(8,128)(2,1)S(1)} %get-tuple-element.59), channel_id=1, source_target_pairs={{0,16},{16,32},{32,48},{1,17},{17,33},{33,49},{2,18},{18,34},{34,5... | collective-permute-start | bytes 196616 | tf_op jit(solution)/shard_map/ppermute | solution.py:114
  150.1 2.1 %collective-permute-start.8 = (bf16[1,4,4,8,128]{4,3,2,1,0:T(8,128)(2,1)S(1)}, bf16[1,4,4,8,128]{4,3,2,1,0:T(8,128)(2,1)S(1)}, u32[]{:S(2)}, u32[]{:S(2)}) collective-permute-start(bf16[1,4,4,8,128]{4,3,2,1,0:T(8,128)(2,1)S(1)} %get-tuple-element.55), channel_id=1, source_target_pairs={{0,17},{1,18},{2,19},{3,20},{4,21},{5,22},{6,23},{7,24},{8,25},{9,... | collective-permute-start | bytes 98312 | tf_op jit(solution)/shard_map/ppermute | solution.py:123
  152.2 0.9 constant_dynamic-update-slice_fusion.4
  153.2 4.8 %collective-permute-done.8 = bf16[1,4,4,8,128]{4,3,2,1,0:T(8,128)(2,1)S(1)} collective-permute-done((bf16[1,4,4,8,128]{4,3,2,1,0:T(8,128)(2,1)S(1)}, bf16[1,4,4,8,128]{4,3,2,1,0:T(8,128)(2,1)S(1)}, u32[]{:S(2)}, u32[]{:S(2)}) %collective-permute-start.8) | collective-permute-done | bytes 32800 | tf_op jit(solution)/shard_map/ppermute | solution.py:123
  158.0 1.8 maximum_maximum_fusion.2
  159.8 5.2 %shard_map.68 = (bf16[1568,128]{1,0:T(8,128)(2,1)}, bf16[512,128]{1,0:T(8,128)(2,1)}) custom-call(s32[2]{0:T(128)} %pad_add_fusion.offs_ref, bf16[2048,128]{1,0:T(8,128)(2,1)} %bitcast.33, bf16[2048,128]{1,0:T(8,128)(2,1)} %bitcast.32, bf16[8,14,128,128]{3,2,1,0:T(8,128)(2,1)} %all-gather.2.cloned.1.call-done.w_hbm), custom_call_target="tpu_custom_call" | custom-call | flops 667942912 | bytes 2007040 | tf_op jit(solution)/shard_map/pallas_call | solution.py:80
  165.0 0.9 constant_dynamic-update-slice_fusion.3
  165.9 4.5 %shard_map.69 = (bf16[1152,128]{1,0:T(8,128)(2,1)}, bf16[512,128]{1,0:T(8,128)(2,1)}) custom-call(s32[2]{0:T(128)} %pad_add_fusion.offs_ref, bf16[1568,128]{1,0:T(8,128)(2,1)} %get-tuple-element.29.prior_ref, bf16[1568,128]{1,0:T(8,128)(2,1)} %bitcast.40, bf16[8,14,128,128]{3,2,1,0:T(8,128)(2,1)} %all-gather.2.cloned.1.call-done.w_hbm), custom_call_target="tpu_custom_call" | custom-call | flops 490733568 | bytes 1654784 | tf_op jit(solution)/shard_map/pallas_call | solution.py:80
  170.5 0.9 constant_dynamic-update-slice_fusion.2
  171.4 4.0 %shard_map.70 = (bf16[800,128]{1,0:T(8,128)(2,1)}, bf16[512,128]{1,0:T(8,128)(2,1)}) custom-call(s32[2]{0:T(128)} %pad_add_fusion.offs_ref, bf16[1152,128]{1,0:T(8,128)(2,1)} %get-tuple-element.31.prior_ref, bf16[1152,128]{1,0:T(8,128)(2,1)} %bitcast.42, bf16[8,14,128,128]{3,2,1,0:T(8,128)(2,1)} %all-gather.2.cloned.1.call-done.w_hbm), custom_call_target="tpu_custom_call" | custom-call | flops 340787200 | bytes 1351680 | tf_op jit(solution)/shard_map/pallas_call | solution.py:80
  175.5 0.9 constant_dynamic-update-slice_fusion.1
  176.4 3.7 %shard_map.71 = (bf16[512,128]{1,0:T(8,128)(2,1)}, bf16[512,128]{1,0:T(8,128)(2,1)}) custom-call(s32[2]{0:T(128)} %pad_add_fusion.offs_ref, bf16[800,128]{1,0:T(8,128)(2,1)} %get-tuple-element.33.prior_ref, bf16[800,128]{1,0:T(8,128)(2,1)} %bitcast.45, bf16[8,14,128,128]{3,2,1,0:T(8,128)(2,1)} %all-gather.2.cloned.1.call-done.w_hbm), custom_call_target="tpu_custom_call" | custom-call | flops 218103808 | bytes 1097728 | tf_op jit(solution)/shard_map/pallas_call | solution.py:80
  180.1 0.9 constant_dynamic-update-slice_fusion
  181.0 18.5 %all_to_all.17 = bf16[8,1,8,8,8,128]{5,4,3,2,1,0:T(8,128)(2,1)S(1)} all-to-all(bf16[8,1,8,8,8,128]{5,4,3,2,1,0:T(8,128)(2,1)S(1)} %constant_dynamic-update-slice_fusion), channel_id=1, replica_groups=mesh['section'=8,'frames'=4,'space'=16] {'section'}, dimensions={0} | all-to-all | bytes 2097152 | tf_op jit(solution)/shard_map/all_to_all | solution.py:213
  199.5 1.0 copy.24
  (56 shorter events, 9.5 us)
Async XLA Ops:
  6.5 7.7 %copy-start = (bf16[8,8,8,8,128]{4,3,2,1,0:T(8,128)(2,1)S(1)}, bf16[8,8,8,8,128]{4,3,2,1,0:T(8,128)(2,1)}, u32[]{:S(2)}) copy-start(bf16[8,8,8,8,128]{4,3,2,1,0:T(8,128)(2,1)} %param.6) | copy-start | bytes 3145732
  6.5 99.1 %all-gather.2.cloned.1.call-start = ((), (), s32[]{:S(2)}) async-start(), calls=%async_computation.2 | async-start | bytes 4128768 | tf_op jit(solution)/shard_map/all_gather | solution.py:182
  9.3 20.3 %all-to-all-start = ((bf16[8,8,8,8,128]{4,3,2,1,0:T(8,128)(2,1)}), bf16[8,8,8,8,128]{4,3,2,1,0:T(8,128)(2,1)S(1)}, u32[]{:S(2)}, u32[]{:S(2)}) async-start(bf16[8,8,8,8,128]{4,3,2,1,0:T(8,128)(2,1)} %bitcast.44), calls=%async_computation | async-start | bytes 2097152 | tf_op jit(solution)/shard_map/all_to_all | solution.py:173
  29.7 17.6 %collective-permute-start.16 = (bf16[4,1,4,4,8,128]{5,4,3,2,0,1:T(8,128)(2,1)S(1)}, bf16[4,1,4,4,8,128]{5,4,3,2,0,1:T(8,128)(2,1)S(1)}, u32[]{:S(2)}, u32[]{:S(2)}) collective-permute-start(bf16[4,1,4,4,8,128]{5,4,3,2,0,1:T(8,128)(2,1)S(1)} %get-tuple-element.47), channel_id=1, source_target_pairs={{0,17},{1,18},{2,19},{3,20},{4,21},{5,22},{6,23},{7,24},{8,25},{9,... | collective-permute-start | bytes 393224 | tf_op jit(solution)/shard_map/ppermute | solution.py:123
  34.3 16.3 %collective-permute-start.18 = (bf16[4,1,4,4,8,128]{5,4,3,2,0,1:T(8,128)(2,1)S(1)}, bf16[4,1,4,4,8,128]{5,4,3,2,0,1:T(8,128)(2,1)S(1)}, u32[]{:S(2)}, u32[]{:S(2)}) collective-permute-start(bf16[4,1,4,4,8,128]{5,4,3,2,0,1:T(8,128)(2,1)S(1)} %get-tuple-element.50), channel_id=1, source_target_pairs={{1,16},{2,17},{3,18},{4,19},{5,20},{6,21},{7,22},{8,23},{9,24},{10... | collective-permute-start | bytes 393224 | tf_op jit(solution)/shard_map/ppermute | solution.py:123
  36.2 17.9 %collective-permute-start.21 = (bf16[4,1,4,4,8,128]{5,4,3,2,0,1:T(8,128)(2,1)S(1)}, bf16[4,1,4,4,8,128]{5,4,3,2,0,1:T(8,128)(2,1)S(1)}, u32[]{:S(2)}, u32[]{:S(2)}) collective-permute-start(bf16[4,1,4,4,8,128]{5,4,3,2,0,1:T(8,128)(2,1)S(1)} %get-tuple-element.49), channel_id=1, source_target_pairs={{16,1},{17,2},{18,3},{19,4},{20,5},{21,6},{22,7},{23,8},{24,9},{25... | collective-permute-start | bytes 393224 | tf_op jit(solution)/shard_map/ppermute | solution.py:123
  41.1 22.7 %collective-permute-start.17 = (bf16[4,1,4,8,8,128]{5,4,3,2,0,1:T(8,128)(2,1)S(1)}, bf16[4,1,4,8,8,128]{5,4,3,2,0,1:T(8,128)(2,1)S(1)}, u32[]{:S(2)}, u32[]{:S(2)}) collective-permute-start(bf16[4,1,4,8,8,128]{5,4,3,2,0,1:T(8,128)(2,1)S(1)} %get-tuple-element.51), channel_id=1, source_target_pairs={{0,16},{16,32},{32,48},{1,17},{17,33},{33,49},{2,18},{18,34},{34,5... | collective-permute-start | bytes 786440 | tf_op jit(solution)/shard_map/ppermute | solution.py:114
  43.5 22.3 %collective-permute-start.19 = (bf16[4,1,8,4,8,128]{5,4,3,2,0,1:T(8,128)(2,1)S(1)}, bf16[4,1,8,4,8,128]{5,4,3,2,0,1:T(8,128)(2,1)S(1)}, u32[]{:S(2)}, u32[]{:S(2)}) collective-permute-start(bf16[4,1,8,4,8,128]{5,4,3,2,0,1:T(8,128)(2,1)S(1)} %get-tuple-element.53), channel_id=1, source_target_pairs={{0,1},{1,2},{2,3},{3,4},{4,5},{5,6},{6,7},{7,8},{8,9},{9,10},{10,1... | collective-permute-start | bytes 786440 | tf_op jit(solution)/shard_map/ppermute | solution.py:117
  47.4 26.2 %collective-permute-start.20 = (bf16[4,1,8,4,8,128]{5,4,3,2,0,1:T(8,128)(2,1)S(1)}, bf16[4,1,8,4,8,128]{5,4,3,2,0,1:T(8,128)(2,1)S(1)}, u32[]{:S(2)}, u32[]{:S(2)}) collective-permute-start(bf16[4,1,8,4,8,128]{5,4,3,2,0,1:T(8,128)(2,1)S(1)} %get-tuple-element.54), channel_id=1, source_target_pairs={{1,0},{2,1},{3,2},{4,3},{5,4},{6,5},{7,6},{8,7},{9,8},{10,9},{11,1... | collective-permute-start | bytes 786440 | tf_op jit(solution)/shard_map/ppermute | solution.py:117
  50.6 24.9 %collective-permute-start.22 = (bf16[4,1,4,8,8,128]{5,4,3,2,0,1:T(8,128)(2,1)S(1)}, bf16[4,1,4,8,8,128]{5,4,3,2,0,1:T(8,128)(2,1)S(1)}, u32[]{:S(2)}, u32[]{:S(2)}) collective-permute-start(bf16[4,1,4,8,8,128]{5,4,3,2,0,1:T(8,128)(2,1)S(1)} %get-tuple-element.52), channel_id=1, source_target_pairs={{16,0},{32,16},{48,32},{17,1},{33,17},{49,33},{18,2},{34,18},{50,3... | collective-permute-start | bytes 786440 | tf_op jit(solution)/shard_map/ppermute | solution.py:114
  54.2 7.8 %collective-permute-start.23 = (bf16[4,1,4,4,8,128]{5,4,3,2,0,1:T(8,128)(2,1)S(1)}, bf16[4,1,4,4,8,128]{5,4,3,2,0,1:T(8,128)(2,1)S(1)}, u32[]{:S(2)}, u32[]{:S(2)}) collective-permute-start(bf16[4,1,4,4,8,128]{5,4,3,2,0,1:T(8,128)(2,1)S(1)} %get-tuple-element.48), channel_id=1, source_target_pairs={{17,0},{18,1},{19,2},{20,3},{21,4},{22,5},{23,6},{24,7},{25,8},{26... | collective-permute-start | bytes 393224 | tf_op jit(solution)/shard_map/ppermute | solution.py:123
  61.9 19.0 %collective-permute-start = (bf16[5,1,4,4,8,128]{5,4,3,2,0,1:T(8,128)(2,1)S(1)}, bf16[5,1,4,4,8,128]{5,4,3,2,0,1:T(8,128)(2,1)S(1)}, u32[]{:S(2)}, u32[]{:S(2)}) collective-permute-start(bf16[5,1,4,4,8,128]{5,4,3,2,0,1:T(8,128)(2,1)S(1)} %get-tuple-element.39), channel_id=1, source_target_pairs={{0,17},{1,18},{2,19},{3,20},{4,21},{5,22},{6,23},{7,24},{8,25},{9,... | collective-permute-start | bytes 491528 | tf_op jit(solution)/shard_map/ppermute | solution.py:123
  63.8 19.0 %collective-permute-start.2 = (bf16[5,1,4,4,8,128]{5,4,3,2,0,1:T(8,128)(2,1)S(1)}, bf16[5,1,4,4,8,128]{5,4,3,2,0,1:T(8,128)(2,1)S(1)}, u32[]{:S(2)}, u32[]{:S(2)}) collective-permute-start(bf16[5,1,4,4,8,128]{5,4,3,2,0,1:T(8,128)(2,1)S(1)} %get-tuple-element.40), channel_id=1, source_target_pairs={{1,16},{2,17},{3,18},{4,19},{5,20},{6,21},{7,22},{8,23},{9,24},{10... | collective-permute-start | bytes 491528 | tf_op jit(solution)/shard_map/ppermute | solution.py:123
  65.8 21.8 %collective-permute-start.5 = (bf16[5,1,4,4,8,128]{5,4,3,2,0,1:T(8,128)(2,1)S(1)}, bf16[5,1,4,4,8,128]{5,4,3,2,0,1:T(8,128)(2,1)S(1)}, u32[]{:S(2)}, u32[]{:S(2)}) collective-permute-start(bf16[5,1,4,4,8,128]{5,4,3,2,0,1:T(8,128)(2,1)S(1)} %get-tuple-element.41), channel_id=1, source_target_pairs={{16,1},{17,2},{18,3},{19,4},{20,5},{21,6},{22,7},{23,8},{24,9},{25... | collective-permute-start | bytes 491528 | tf_op jit(solution)/shard_map/ppermute | solution.py:123
  73.5 22.2 %collective-permute-start.1 = (bf16[5,1,4,8,8,128]{5,4,3,2,0,1:T(8,128)(2,1)S(1)}, bf16[5,1,4,8,8,128]{5,4,3,2,0,1:T(8,128)(2,1)S(1)}, u32[]{:S(2)}, u32[]{:S(2)}) collective-permute-start(bf16[5,1,4,8,8,128]{5,4,3,2,0,1:T(8,128)(2,1)S(1)} %get-tuple-element.43), channel_id=1, source_target_pairs={{0,16},{16,32},{32,48},{1,17},{17,33},{33,49},{2,18},{18,34},{34,5... | collective-permute-start | bytes 983048 | tf_op jit(solution)/shard_map/ppermute | solution.py:114
  75.5 20.2 %collective-permute-start.3 = (bf16[5,1,8,4,8,128]{5,4,3,2,0,1:T(8,128)(2,1)S(1)}, bf16[5,1,8,4,8,128]{5,4,3,2,0,1:T(8,128)(2,1)S(1)}, u32[]{:S(2)}, u32[]{:S(2)}) collective-permute-start(bf16[5,1,8,4,8,128]{5,4,3,2,0,1:T(8,128)(2,1)S(1)} %get-tuple-element.45), channel_id=1, source_target_pairs={{0,1},{1,2},{2,3},{3,4},{4,5},{5,6},{6,7},{7,8},{8,9},{9,10},{10,1... | collective-permute-start | bytes 983048 | tf_op jit(solution)/shard_map/ppermute | solution.py:117
  81.0 14.7 %collective-permute-start.4 = (bf16[5,1,8,4,8,128]{5,4,3,2,0,1:T(8,128)(2,1)S(1)}, bf16[5,1,8,4,8,128]{5,4,3,2,0,1:T(8,128)(2,1)S(1)}, u32[]{:S(2)}, u32[]{:S(2)}) collective-permute-start(bf16[5,1,8,4,8,128]{5,4,3,2,0,1:T(8,128)(2,1)S(1)} %get-tuple-element.46), channel_id=1, source_target_pairs={{1,0},{2,1},{3,2},{4,3},{5,4},{6,5},{7,6},{8,7},{9,8},{10,9},{11,1... | collective-permute-start | bytes 983048 | tf_op jit(solution)/shard_map/ppermute | solution.py:117
  82.9 12.8 %collective-permute-start.6 = (bf16[5,1,4,8,8,128]{5,4,3,2,0,1:T(8,128)(2,1)S(1)}, bf16[5,1,4,8,8,128]{5,4,3,2,0,1:T(8,128)(2,1)S(1)}, u32[]{:S(2)}, u32[]{:S(2)}) collective-permute-start(bf16[5,1,4,8,8,128]{5,4,3,2,0,1:T(8,128)(2,1)S(1)} %get-tuple-element.44), channel_id=1, source_target_pairs={{16,0},{32,16},{48,32},{17,1},{33,17},{49,33},{18,2},{34,18},{50,3... | collective-permute-start | bytes 983048 | tf_op jit(solution)/shard_map/ppermute | solution.py:114
  87.6 8.1 %collective-permute-start.7 = (bf16[5,1,4,4,8,128]{5,4,3,2,0,1:T(8,128)(2,1)S(1)}, bf16[5,1,4,4,8,128]{5,4,3,2,0,1:T(8,128)(2,1)S(1)}, u32[]{:S(2)}, u32[]{:S(2)}) collective-permute-start(bf16[5,1,4,4,8,128]{5,4,3,2,0,1:T(8,128)(2,1)S(1)} %get-tuple-element.42), channel_id=1, source_target_pairs={{17,0},{18,1},{19,2},{20,3},{21,4},{22,5},{23,6},{24,7},{25,8},{26... | collective-permute-start | bytes 491528 | tf_op jit(solution)/shard_map/ppermute | solution.py:123
  119.6 24.5 %copy-start.1 = (bf16[512,128]{1,0:T(8,128)(2,1)S(1)}, bf16[512,128]{1,0:T(8,128)(2,1)}, u32[]{:S(2)}) copy-start(bf16[512,128]{1,0:T(8,128)(2,1)} %get-tuple-element.20) | copy-start | bytes 393220
  119.6 24.5 %copy-start.2 = (bf16[512,128]{1,0:T(8,128)(2,1)S(1)}, bf16[512,128]{1,0:T(8,128)(2,1)}, u32[]{:S(2)}) copy-start(bf16[512,128]{1,0:T(8,128)(2,1)} %get-tuple-element.22) | copy-start | bytes 393220
  119.6 24.6 %copy-start.3 = (bf16[512,128]{1,0:T(8,128)(2,1)S(1)}, bf16[512,128]{1,0:T(8,128)(2,1)}, u32[]{:S(2)}) copy-start(bf16[512,128]{1,0:T(8,128)(2,1)} %get-tuple-element.24) | copy-start | bytes 393220
  125.9 32.1 %collective-permute-start.11 = (bf16[1,8,4,8,128]{4,3,2,1,0:T(8,128)(2,1)S(1)}, bf16[1,8,4,8,128]{4,3,2,1,0:T(8,128)(2,1)S(1)}, u32[]{:S(2)}, u32[]{:S(2)}) collective-permute-start(bf16[1,8,4,8,128]{4,3,2,1,0:T(8,128)(2,1)S(1)} %get-tuple-element.61), channel_id=1, source_target_pairs={{0,1},{1,2},{2,3},{3,4},{4,5},{5,6},{6,7},{7,8},{8,9},{9,10},{10,1... | collective-permute-start | bytes 196616 | tf_op jit(solution)/shard_map/ppermute | solution.py:117
  129.9 28.1 %collective-permute-start.12 = (bf16[1,8,4,8,128]{4,3,2,1,0:T(8,128)(2,1)S(1)}, bf16[1,8,4,8,128]{4,3,2,1,0:T(8,128)(2,1)S(1)}, u32[]{:S(2)}, u32[]{:S(2)}) collective-permute-start(bf16[1,8,4,8,128]{4,3,2,1,0:T(8,128)(2,1)S(1)} %get-tuple-element.62), channel_id=1, source_target_pairs={{1,0},{2,1},{3,2},{4,3},{5,4},{6,5},{7,6},{8,7},{9,8},{10,9},{11,1... | collective-permute-start | bytes 196616 | tf_op jit(solution)/shard_map/ppermute | solution.py:117
  133.0 11.2 %collective-permute-start.10 = (bf16[1,4,4,8,128]{4,3,2,1,0:T(8,128)(2,1)S(1)}, bf16[1,4,4,8,128]{4,3,2,1,0:T(8,128)(2,1)S(1)}, u32[]{:S(2)}, u32[]{:S(2)}) collective-permute-start(bf16[1,4,4,8,128]{4,3,2,1,0:T(8,128)(2,1)S(1)} %get-tuple-element.58), channel_id=1, source_target_pairs={{1,16},{2,17},{3,18},{4,19},{5,20},{6,21},{7,22},{8,23},{9,24},{10... | collective-permute-start | bytes 98312 | tf_op jit(solution)/shard_map/ppermute | solution.py:123
  134.9 11.2 %collective-permute-start.13 = (bf16[1,4,4,8,128]{4,3,2,1,0:T(8,128)(2,1)S(1)}, bf16[1,4,4,8,128]{4,3,2,1,0:T(8,128)(2,1)S(1)}, u32[]{:S(2)}, u32[]{:S(2)}) collective-permute-start(bf16[1,4,4,8,128]{4,3,2,1,0:T(8,128)(2,1)S(1)} %get-tuple-element.57), channel_id=1, source_target_pairs={{16,1},{17,2},{18,3},{19,4},{20,5},{21,6},{22,7},{23,8},{24,9},{25... | collective-permute-start | bytes 98312 | tf_op jit(solution)/shard_map/ppermute | solution.py:123
  139.7 10.3 %collective-permute-start.15 = (bf16[1,4,4,8,128]{4,3,2,1,0:T(8,128)(2,1)S(1)}, bf16[1,4,4,8,128]{4,3,2,1,0:T(8,128)(2,1)S(1)}, u32[]{:S(2)}, u32[]{:S(2)}) collective-permute-start(bf16[1,4,4,8,128]{4,3,2,1,0:T(8,128)(2,1)S(1)} %get-tuple-element.56), channel_id=1, source_target_pairs={{17,0},{18,1},{19,2},{20,3},{21,4},{22,5},{23,6},{24,7},{25,8},{26... | collective-permute-start | bytes 98312 | tf_op jit(solution)/shard_map/ppermute | solution.py:123
  144.2 13.8 %collective-permute-start.14 = (bf16[1,4,8,8,128]{4,3,2,1,0:T(8,128)(2,1)S(1)}, bf16[1,4,8,8,128]{4,3,2,1,0:T(8,128)(2,1)S(1)}, u32[]{:S(2)}, u32[]{:S(2)}) collective-permute-start(bf16[1,4,8,8,128]{4,3,2,1,0:T(8,128)(2,1)S(1)} %get-tuple-element.60), channel_id=1, source_target_pairs={{16,0},{32,16},{48,32},{17,1},{33,17},{49,33},{18,2},{34,18},{50,3... | collective-permute-start | bytes 196616 | tf_op jit(solution)/shard_map/ppermute | solution.py:114
  146.1 11.9 %collective-permute-start.9 = (bf16[1,4,8,8,128]{4,3,2,1,0:T(8,128)(2,1)S(1)}, bf16[1,4,8,8,128]{4,3,2,1,0:T(8,128)(2,1)S(1)}, u32[]{:S(2)}, u32[]{:S(2)}) collective-permute-start(bf16[1,4,8,8,128]{4,3,2,1,0:T(8,128)(2,1)S(1)} %get-tuple-element.59), channel_id=1, source_target_pairs={{0,16},{16,32},{32,48},{1,17},{17,33},{33,49},{2,18},{18,34},{34,5... | collective-permute-start | bytes 196616 | tf_op jit(solution)/shard_map/ppermute | solution.py:114
  150.1 7.9 %collective-permute-start.8 = (bf16[1,4,4,8,128]{4,3,2,1,0:T(8,128)(2,1)S(1)}, bf16[1,4,4,8,128]{4,3,2,1,0:T(8,128)(2,1)S(1)}, u32[]{:S(2)}, u32[]{:S(2)}) collective-permute-start(bf16[1,4,4,8,128]{4,3,2,1,0:T(8,128)(2,1)S(1)} %get-tuple-element.55), channel_id=1, source_target_pairs={{0,17},{1,18},{2,19},{3,20},{4,21},{5,22},{6,23},{7,24},{8,25},{9,... | collective-permute-start | bytes 98312 | tf_op jit(solution)/shard_map/ppermute | solution.py:123
Sparse Core Ops, SparseCore 0:
  9.5 40.4 all-gather.1

commit v7 on v3

--- a/solution.py
+++ b/solution.py
@@ -152,27 +152,23 @@
         [lax.axis_index("frames") * num_frames, lax.axis_index("space") * num_rows]
     ).astype(jnp.int32)
     totals = (num_frames * lax.axis_size("frames"), num_rows * lax.axis_size("space"))
-    both = extend(jnp.concatenate([incoming[None], noise_t[:halo]], axis=0), halo, 2, 3)
+    both = extend(jnp.concatenate([incoming[None], noise_t], axis=0), halo, 2, 3)
     prior_ext = both[0]
-    noise_round = both[1:]
+    noise_all = both[1:]
     results = []
     for k in range(sections):
         j = k % halo
         if j == 0 and k > 0:
             prior_ext = extend(prior_ext, halo, 1, 2)
-            noise_round = noise_next
         width = halo - j
         cut = halo - width
-        noise_here = noise_round[
-            j, :, cut : cut + num_frames + 2 * width, cut : cut + num_rows + 2 * width
+        noise_here = noise_all[
+            k, :, cut : cut + num_frames + 2 * width, cut : cut + num_rows + 2 * width
         ]
         prior_ext, crop = denoise(
             offs, levels, prior_ext, noise_here, packed, k, num_frames, num_rows, totals
         )
         results.append(crop)
-        if j == 0 and k + halo < sections:
-            later, _ = lax.optimization_barrier((noise_t[k + halo : k + 2 * halo], crop))
-            noise_next = extend(later, halo, 2, 3)
     num_cols, channels = base_frames.shape[3:]
     stacked = jnp.stack(results).reshape(
         (sections, per_device, num_frames, num_rows, num_cols, channels)

time: 171 us -> 186 us (1.088)
  waiting for transfers between devices: 27.1 us -> 66.7 us
  blocking collectives: 38.9 us -> 18.5 us
  starting transfers between devices: 35.4 us -> 26.8 us
  other arithmetic: 13.5 us -> 16.5 us
    ppermute x6 -> x4, waiting for transfers between devices: 5.68 us -> 33.2 us  [extend(): lax.ppermute(lax.slice_in_dim(block, size - width, size, axis=dim), axis,...]
    all_to_all x1 -> x0, blocking collectives: 20.4 us -> none  [on_device(): noise_t = lax.all_to_all(section_noise[0], 'section', 0, 0, tiled=True)]
    all_to_all x0 -> x1, waiting for transfers between devices: none -> 15.9 us  [on_device(): noise_t = lax.all_to_all(section_noise[0], 'section', 0, 0, tiled=True)]
    ppermute x6 -> x4, starting transfers between devices: 24.5 us -> 14.7 us  [extend(): lax.ppermute(lax.slice_in_dim(block, size - width, size, axis=dim), axis,...]
    all_to_all x0 -> x1, starting transfers between devices: none -> 4.31 us  [on_device(): noise_t = lax.all_to_all(section_noise[0], 'section', 0, 0, tiled=True)]
    ppermute x6 -> x4, waiting for transfers between devices: 21.4 us -> 17.5 us  [extend(): lax.ppermute(lax.slice_in_dim(block, 0, width, axis=dim), axis, backward)]
    ppermute x6 -> x4, starting transfers between devices: 10.9 us -> 7.84 us  [extend(): lax.ppermute(lax.slice_in_dim(block, 0, width, axis=dim), axis, backward)]
    slice x6 -> x4, other arithmetic: 4.65 us -> 7.19 us  [on_device(): noise_all[k, :, cut:cut + num_frames + 2 * width, cut:cut + num_rows + 2...]
  transfers between devices with their start and end apart: 13 -> 10, of which waited for: 9 -> 8; matrix products, arithmetic and copies ran while one was open for 6% -> 8% of each run, Pallas kernels for 0% -> 0%
where the time goes in v7:
time: 186 us; the launch traced here: 185 us
  waiting for transfers between devices  66.7 us (36%)
  Pallas kernels  32.4 us (17%)
  starting transfers between devices  26.8 us (14%)
  blocking collectives  18.5 us (10%)
  other arithmetic  16.5 us (9%)
  between operations  14.4 us (8%)
  local copies, waits for them, and re-layouts  9.85 us (5%)
    ppermute x4, waiting for transfers between devices, extend(): lax.ppermute(lax.slice_in_dim(block, size - width, size, axis=dim), axis,...  33.2 us
    pallas_call x8, Pallas kernels, section_call(): pl.pallas_call(functools.partial(section_kernel, m, n, cols, inner, num_f...  32.4 us
    all_to_all x1, blocking collectives, on_device(): return lax.all_to_all(stacked, 'section', 0, 1, tiled=True)  18.5 us
    ppermute x4, waiting for transfers between devices, extend(): lax.ppermute(lax.slice_in_dim(block, 0, width, axis=dim), axis, backward)  17.5 us
    all_to_all x1, waiting for transfers between devices, on_device(): noise_t = lax.all_to_all(section_noise[0], 'section', 0, 0, tiled=True)  15.9 us
    ppermute x4, starting transfers between devices, extend(): lax.ppermute(lax.slice_in_dim(block, size - width, size, axis=dim), axis,...  14.7 us
    ppermute x4, starting transfers between devices, extend(): lax.ppermute(lax.slice_in_dim(block, 0, width, axis=dim), axis, backward)  7.84 us
    slice x4, other arithmetic, on_device(): noise_all[k, :, cut:cut + num_frames + 2 * width, cut:cut + num_rows + 2...  7.19 us
  transfers between devices with their start and end apart: 10, of which 8 were waited for; matrix products, arithmetic and copies ran while one was open for 8% of the time, Pallas kernels for 0%

profile of v7, /device:TPU:96, one launch (start us, length us, event | category | flops | bytes accessed | tf_op | source)
XLA Modules:
  0.0 185.1 jit_solution(11825214308314282502)
XLA Ops:
  7.3 0.1 pad.23.clone
  7.4 2.0 %maximum_maximum_fusion = bf16[1,14,128,128]{3,2,1,0:T(8,128)(2,1)} fusion(bf16[1,1,128,128]{3,2,1,0:T(8,128)(2,1)} %bitcast.58, bf16[1,3,128,128]{3,2,1,0:T(8,128)(2,1)} %param.10, bf16[1,9,128,128]{3,2,1,0:T(8,128)(2,1)} %param.9, bf16[14]{0:T(256)(128)(2,1)S(1)} %pad.23.clone), kind=kLoop, calls=%fused_computation.8 | loop fusion | flops 688128 | bytes 884764 | tf_op jit(solution)/shard_map/concatenate | solution.py:145
  9.3 4.3 %all-to-all-start = ((bf16[8,8,8,8,128]{4,3,2,1,0:T(8,128)(2,1)}), bf16[8,8,8,8,128]{4,3,2,1,0:T(8,128)(2,1)S(1)}, u32[]{:S(2)}, u32[]{:S(2)}) async-start(bf16[8,8,8,8,128]{4,3,2,1,0:T(8,128)(2,1)} %bitcast.47), calls=%async_computation | async-start | bytes 2097152 | tf_op jit(solution)/shard_map/all_to_all | solution.py:139
  13.7 15.9 %all-to-all-done = bf16[8,8,8,8,128]{4,3,2,1,0:T(8,128)(2,1)S(1)} async-done(((bf16[8,8,8,8,128]{4,3,2,1,0:T(8,128)(2,1)}), bf16[8,8,8,8,128]{4,3,2,1,0:T(8,128)(2,1)S(1)}, u32[]{:S(2)}, u32[]{:S(2)}) %all-to-all-start) | async-done | bytes 1048608 | tf_op jit(solution)/shard_map/all_to_all | solution.py:139
  29.6 0.1 fusion
  29.7 3.5 %collective-permute-start = (bf16[9,1,4,8,8,128]{5,4,3,2,0,1:T(8,128)(2,1)S(1)}, bf16[9,1,4,8,8,128]{5,4,3,2,0,1:T(8,128)(2,1)S(1)}, u32[]{:S(2)}, u32[]{:S(2)}) collective-permute-start(bf16[9,1,4,8,8,128]{5,4,3,2,0,1:T(8,128)(2,1)S(1)} %get-tuple-element.45), channel_id=1, source_target_pairs={{0,16},{16,32},{32,48},{1,17},{17,33},{33,49},{2,18},{18,34},{34,5... | collective-permute-start | bytes 1769480 | tf_op jit(solution)/shard_map/ppermute | solution.py:101
  33.3 1.3 collective-permute-start.1
  34.6 11.0 %collective-permute-done = bf16[9,1,4,8,8,128]{5,4,3,2,0,1:T(8,128)(2,1)S(1)} collective-permute-done((bf16[9,1,4,8,8,128]{5,4,3,2,0,1:T(8,128)(2,1)S(1)}, bf16[9,1,4,8,8,128]{5,4,3,2,0,1:T(8,128)(2,1)S(1)}, u32[]{:S(2)}, u32[]{:S(2)}) %collective-permute-start) | collective-permute-done | bytes 589856 | tf_op jit(solution)/shard_map/ppermute | solution.py:101
  45.6 4.1 %collective-permute-done.1 = bf16[9,1,4,8,8,128]{5,4,3,2,0,1:T(8,128)(2,1)S(1)} collective-permute-done((bf16[9,1,4,8,8,128]{5,4,3,2,0,1:T(8,128)(2,1)S(1)}, bf16[9,1,4,8,8,128]{5,4,3,2,0,1:T(8,128)(2,1)S(1)}, u32[]{:S(2)}, u32[]{:S(2)}) %collective-permute-start.1) | collective-permute-done | bytes 589856 | tf_op jit(solution)/shard_map/ppermute | solution.py:102
  49.7 0.3 pad_maximum_fusion.1
  50.0 2.1 %fusion.3 = (bf16[9,1,16,4,8,128]{5,4,3,2,0,1:T(8,128)(2,1)}, bf16[9,1,16,4,8,128]{5,4,3,2,0,1:T(8,128)(2,1)}) fusion(bf16[9,1,16,8,8,128]{5,4,3,2,0,1:T(8,128)(2,1)S(1)} %pad_maximum_fusion.1), kind=kLoop, calls=%fused_computation.29 | loop fusion | bytes 4718592 | tf_op jit(solution)/shard_map/slice | solution.py:101
  52.1 5.0 %collective-permute-start.2 = (bf16[9,1,16,4,8,128]{5,4,3,2,0,1:T(8,128)(2,1)}, bf16[9,1,16,4,8,128]{5,4,3,2,0,1:T(8,128)(2,1)S(1)}, u32[]{:S(2)}, u32[]{:S(2)}) collective-permute-start(bf16[9,1,16,4,8,128]{5,4,3,2,0,1:T(8,128)(2,1)} %get-tuple-element.43), channel_id=1, source_target_pairs={{0,1},{1,2},{2,3},{3,4},{4,5},{5,6},{6,7},{7,8},{8,9},{9,10},{10,1... | collective-permute-start | bytes 3538952 | tf_op jit(solution)/shard_map/ppermute | solution.py:101
  57.1 1.9 %collective-permute-start.3 = (bf16[9,1,16,4,8,128]{5,4,3,2,0,1:T(8,128)(2,1)}, bf16[9,1,16,4,8,128]{5,4,3,2,0,1:T(8,128)(2,1)}, u32[]{:S(2)}, u32[]{:S(2)}) collective-permute-start(bf16[9,1,16,4,8,128]{5,4,3,2,0,1:T(8,128)(2,1)} %get-tuple-element.44), channel_id=1, source_target_pairs={{1,0},{2,1},{3,2},{4,3},{5,4},{6,5},{7,6},{8,7},{9,8},{10,9},{11,1... | collective-permute-start | bytes 3538952 | tf_op jit(solution)/shard_map/ppermute | solution.py:102
  59.1 0.7 pad_add_fusion.offs_ref
  59.7 21.6 %collective-permute-done.2 = bf16[9,1,16,4,8,128]{5,4,3,2,0,1:T(8,128)(2,1)S(1)} collective-permute-done((bf16[9,1,16,4,8,128]{5,4,3,2,0,1:T(8,128)(2,1)}, bf16[9,1,16,4,8,128]{5,4,3,2,0,1:T(8,128)(2,1)S(1)}, u32[]{:S(2)}, u32[]{:S(2)}) %collective-permute-start.2) | collective-permute-done | bytes 1179680 | tf_op jit(solution)/shard_map/ppermute | solution.py:101
  81.4 5.3 %collective-permute-done.3 = bf16[9,1,16,4,8,128]{5,4,3,2,0,1:T(8,128)(2,1)} collective-permute-done((bf16[9,1,16,4,8,128]{5,4,3,2,0,1:T(8,128)(2,1)}, bf16[9,1,16,4,8,128]{5,4,3,2,0,1:T(8,128)(2,1)}, u32[]{:S(2)}, u32[]{:S(2)}) %collective-permute-start.3) | collective-permute-done | bytes 1179680 | tf_op jit(solution)/shard_map/ppermute | solution.py:102
  86.7 1.6 pad_maximum_fusion.10
  88.4 1.8 pad_maximum_fusion.3
  90.2 1.8 pad_maximum_fusion.7
  91.9 2.0 %pad_maximum_fusion.5 = (bf16[1,1,14,14,8,128]{5,4,3,2,0,1:T(8,128)(2,1)}, bf16[1,1,14,14,8,128]{5,4,3,2,0,1:T(8,128)(2,1)}) fusion(bf16[9,1,16,4,8,128]{5,4,3,2,0,1:T(8,128)(2,1)} %collective-permute-done.3, bf16[9,1,16,4,8,128]{5,4,3,2,0,1:T(8,128)(2,1)S(1)} %collective-permute-done.2, bf16[9,1,4,8,8,128]{5,4,3,2,0,1:T(8,128)(2,1)S(1)} %copy-done.4, ...), kind=kLoop, calls=%fused_computation.9 | loop fusion | flops 2007040 | bytes 5521408 | tf_op jit(solution)/shard_map/slice | solution.py:165
  93.9 3.1 %pad_maximum_fusion = bf16[9,1,16,16,8,128]{5,4,3,2,0,1:T(8,128)(2,1)S(1)} fusion(bf16[9,1,16,4,8,128]{5,4,3,2,0,1:T(8,128)(2,1)} %collective-permute-done.3, bf16[9,1,4,8,8,128]{5,4,3,2,0,1:T(8,128)(2,1)S(1)} %copy-done.4, bf16[8,1,8,8,8,128]{5,4,3,2,0,1:T(8,128)(2,1)S(1)} %bitcast.34, bf16[1,1,8,8,8,128]{5,4,3,2,0,1:T(8,128)(2,1)S(1)} %dynamic-slice_bitcast_fusion, ...), kind=kLoop, calls=%fused_computation | loop fusion | flops 11796480 | bytes 9437184 | tf_op jit(solution)/shard_map/concatenate | solution.py:103
  97.0 1.1 fusion.2
  98.1 1.4 fusion.1.lv_ref
  99.5 4.7 %shard_map.64 = (bf16[1568,128]{1,0:T(8,128)(2,1)}, bf16[512,128]{1,0:T(8,128)(2,1)}) custom-call(s32[2]{0:T(128)} %pad_add_fusion.offs_ref, f32[8]{0:T(128)} %fusion.1.lv_ref, bf16[2048,128]{1,0:T(8,128)(2,1)} %bitcast.39, bf16[2048,128]{1,0:T(8,128)(2,1)} %bitcast.38, bf16[8,14,128,128]{3,2,1,0:T(8,128)(2,1)} %all-gather.2.cloned.1.call-done.w_hbm), custom_call_target="tpu_custom_call" | custom-call | flops 667942912 | bytes 2007040 | tf_op jit(solution)/shard_map/pallas_call | solution.py:74
  104.1 4.2 %shard_map.65 = (bf16[1152,128]{1,0:T(8,128)(2,1)}, bf16[512,128]{1,0:T(8,128)(2,1)}) custom-call(s32[2]{0:T(128)} %pad_add_fusion.offs_ref, f32[8]{0:T(128)} %fusion.1.lv_ref, bf16[1568,128]{1,0:T(8,128)(2,1)} %get-tuple-element.21.prior_ref, bf16[1568,128]{1,0:T(8,128)(2,1)} %bitcast.41, bf16[8,14,128,128]{3,2,1,0:T(8,128)(2,1)} %all-gather.2.cloned.1.call-done.w_hbm), custom_call_target="tpu_custom_call" | custom-call | flops 490733568 | bytes 1654784 | tf_op jit(solution)/shard_map/pallas_call | solution.py:74
  108.3 3.8 %shard_map.66 = (bf16[800,128]{1,0:T(8,128)(2,1)}, bf16[512,128]{1,0:T(8,128)(2,1)}) custom-call(s32[2]{0:T(128)} %pad_add_fusion.offs_ref, f32[8]{0:T(128)} %fusion.1.lv_ref, bf16[1152,128]{1,0:T(8,128)(2,1)} %get-tuple-element.23.prior_ref, bf16[1152,128]{1,0:T(8,128)(2,1)} %bitcast.43, bf16[8,14,128,128]{3,2,1,0:T(8,128)(2,1)} %all-gather.2.cloned.1.call-done.w_hbm), custom_call_target="tpu_custom_call" | custom-call | flops 340787200 | bytes 1351680 | tf_op jit(solution)/shard_map/pallas_call | solution.py:74
  112.2 3.5 %shard_map.67 = (bf16[512,128]{1,0:T(8,128)(2,1)}, bf16[512,128]{1,0:T(8,128)(2,1)}) custom-call(s32[2]{0:T(128)} %pad_add_fusion.offs_ref, f32[8]{0:T(128)} %fusion.1.lv_ref, bf16[800,128]{1,0:T(8,128)(2,1)} %get-tuple-element.25.prior_ref, bf16[800,128]{1,0:T(8,128)(2,1)} %bitcast.49, bf16[8,14,128,128]{3,2,1,0:T(8,128)(2,1)} %all-gather.2.cloned.1.call-done.w_hbm), custom_call_target="tpu_custom_call" | custom-call | flops 218103808 | bytes 1097728 | tf_op jit(solution)/shard_map/pallas_call | solution.py:74
  115.7 0.9 fusion.5
  116.7 3.5 %collective-permute-start.4 = (bf16[1,4,8,8,128]{4,3,2,1,0:T(8,128)(2,1)S(1)}, bf16[1,4,8,8,128]{4,3,2,1,0:T(8,128)(2,1)S(1)}, u32[]{:S(2)}, u32[]{:S(2)}) collective-permute-start(bf16[1,4,8,8,128]{4,3,2,1,0:T(8,128)(2,1)S(1)} %get-tuple-element.49), channel_id=1, source_target_pairs={{0,16},{16,32},{32,48},{1,17},{17,33},{33,49},{2,18},{18,34},{34,5... | collective-permute-start | bytes 196616 | tf_op jit(solution)/shard_map/ppermute | solution.py:101
  120.1 1.3 collective-permute-start.5
  121.5 0.5 collective-permute-done.4
  122.0 4.3 %collective-permute-done.5 = bf16[1,4,8,8,128]{4,3,2,1,0:T(8,128)(2,1)S(1)} collective-permute-done((bf16[1,4,8,8,128]{4,3,2,1,0:T(8,128)(2,1)S(1)}, bf16[1,4,8,8,128]{4,3,2,1,0:T(8,128)(2,1)S(1)}, u32[]{:S(2)}, u32[]{:S(2)}) %collective-permute-start.5) | collective-permute-done | bytes 65568 | tf_op jit(solution)/shard_map/ppermute | solution.py:102
  126.3 0.9 pad_maximum_fusion.9
  127.3 2.7 %collective-permute-start.6 = (bf16[1,16,4,8,128]{4,3,2,1,0:T(8,128)(2,1)S(1)}, bf16[1,16,4,8,128]{4,3,2,1,0:T(8,128)(2,1)S(1)}, u32[]{:S(2)}, u32[]{:S(2)}) collective-permute-start(bf16[1,16,4,8,128]{4,3,2,1,0:T(8,128)(2,1)S(1)} %get-tuple-element.47), channel_id=1, source_target_pairs={{0,1},{1,2},{2,3},{3,4},{4,5},{5,6},{6,7},{7,8},{8,9},{9,10},{10,1... | collective-permute-start | bytes 393224 | tf_op jit(solution)/shard_map/ppermute | solution.py:101
  130.0 3.3 %collective-permute-start.7 = (bf16[1,16,4,8,128]{4,3,2,1,0:T(8,128)(2,1)S(1)}, bf16[1,16,4,8,128]{4,3,2,1,0:T(8,128)(2,1)S(1)}, u32[]{:S(2)}, u32[]{:S(2)}) collective-permute-start(bf16[1,16,4,8,128]{4,3,2,1,0:T(8,128)(2,1)S(1)} %get-tuple-element.48), channel_id=1, source_target_pairs={{1,0},{2,1},{3,2},{4,3},{5,4},{6,5},{7,6},{8,7},{9,8},{10,9},{11,1... | collective-permute-start | bytes 393224 | tf_op jit(solution)/shard_map/ppermute | solution.py:102
  133.3 0.9 constant_dynamic-update-slice_fusion.4
  134.3 3.8 %collective-permute-done.7 = bf16[1,16,4,8,128]{4,3,2,1,0:T(8,128)(2,1)S(1)} collective-permute-done((bf16[1,16,4,8,128]{4,3,2,1,0:T(8,128)(2,1)S(1)}, bf16[1,16,4,8,128]{4,3,2,1,0:T(8,128)(2,1)S(1)}, u32[]{:S(2)}, u32[]{:S(2)}) %collective-permute-start.7) | collective-permute-done | bytes 131104 | tf_op jit(solution)/shard_map/ppermute | solution.py:102
  138.0 0.9 pad_maximum_fusion.4
  138.9 4.7 %shard_map.68 = (bf16[1568,128]{1,0:T(8,128)(2,1)}, bf16[512,128]{1,0:T(8,128)(2,1)}) custom-call(s32[2]{0:T(128)} %pad_add_fusion.offs_ref, f32[8]{0:T(128)} %fusion.1.lv_ref, bf16[2048,128]{1,0:T(8,128)(2,1)} %bitcast.37, bf16[2048,128]{1,0:T(8,128)(2,1)} %bitcast.36, bf16[8,14,128,128]{3,2,1,0:T(8,128)(2,1)} %all-gather.2.cloned.1.call-done.w_hbm), custom_call_target="tpu_custom_call" | custom-call | flops 667942912 | bytes 2007040 | tf_op jit(solution)/shard_map/pallas_call | solution.py:74
  143.6 0.9 constant_dynamic-update-slice_fusion.3
  144.5 4.2 %shard_map.69 = (bf16[1152,128]{1,0:T(8,128)(2,1)}, bf16[512,128]{1,0:T(8,128)(2,1)}) custom-call(s32[2]{0:T(128)} %pad_add_fusion.offs_ref, f32[8]{0:T(128)} %fusion.1.lv_ref, bf16[1568,128]{1,0:T(8,128)(2,1)} %get-tuple-element.29.prior_ref, bf16[1568,128]{1,0:T(8,128)(2,1)} %bitcast.40, bf16[8,14,128,128]{3,2,1,0:T(8,128)(2,1)} %all-gather.2.cloned.1.call-done.w_hbm), custom_call_target="tpu_custom_call" | custom-call | flops 490733568 | bytes 1654784 | tf_op jit(solution)/shard_map/pallas_call | solution.py:74
  148.7 0.9 constant_dynamic-update-slice_fusion.2
  149.6 3.8 %shard_map.70 = (bf16[800,128]{1,0:T(8,128)(2,1)}, bf16[512,128]{1,0:T(8,128)(2,1)}) custom-call(s32[2]{0:T(128)} %pad_add_fusion.offs_ref, f32[8]{0:T(128)} %fusion.1.lv_ref, bf16[1152,128]{1,0:T(8,128)(2,1)} %get-tuple-element.31.prior_ref, bf16[1152,128]{1,0:T(8,128)(2,1)} %bitcast.42, bf16[8,14,128,128]{3,2,1,0:T(8,128)(2,1)} %all-gather.2.cloned.1.call-done.w_hbm), custom_call_target="tpu_custom_call" | custom-call | flops 340787200 | bytes 1351680 | tf_op jit(solution)/shard_map/pallas_call | solution.py:74
  153.4 0.9 constant_dynamic-update-slice_fusion.1
  154.3 3.5 %shard_map.71 = (bf16[512,128]{1,0:T(8,128)(2,1)}, bf16[512,128]{1,0:T(8,128)(2,1)}) custom-call(s32[2]{0:T(128)} %pad_add_fusion.offs_ref, f32[8]{0:T(128)} %fusion.1.lv_ref, bf16[800,128]{1,0:T(8,128)(2,1)} %get-tuple-element.33.prior_ref, bf16[800,128]{1,0:T(8,128)(2,1)} %bitcast.48, bf16[8,14,128,128]{3,2,1,0:T(8,128)(2,1)} %all-gather.2.cloned.1.call-done.w_hbm), custom_call_target="tpu_custom_call" | custom-call | flops 218103808 | bytes 1097728 | tf_op jit(solution)/shard_map/pallas_call | solution.py:74
  157.8 0.9 constant_dynamic-update-slice_fusion
  158.8 18.5 %all_to_all.17 = bf16[8,1,8,8,8,128]{5,4,3,2,1,0:T(8,128)(2,1)S(1)} all-to-all(bf16[8,1,8,8,8,128]{5,4,3,2,1,0:T(8,128)(2,1)S(1)} %constant_dynamic-update-slice_fusion), channel_id=1, replica_groups=mesh['section'=8,'frames'=4,'space'=16] {'section'}, dimensions={0} | all-to-all | bytes 2097152 | tf_op jit(solution)/shard_map/all_to_all | solution.py:176
  177.3 1.0 copy.32
  (27 shorter events, 0.1 us)
Async XLA Ops:
  6.5 7.1 %copy-start = (bf16[8,8,8,8,128]{4,3,2,1,0:T(8,128)(2,1)S(1)}, bf16[8,8,8,8,128]{4,3,2,1,0:T(8,128)(2,1)}, u32[]{:S(2)}) copy-start(bf16[8,8,8,8,128]{4,3,2,1,0:T(8,128)(2,1)} %param.6) | copy-start | bytes 3145732
  6.5 91.5 %all-gather.2.cloned.1.call-start = ((), (), s32[]{:S(2)}) async-start(), calls=%async_computation.2 | async-start | bytes 4128768 | tf_op jit(solution)/shard_map/all_gather | solution.py:148
  9.3 20.3 %all-to-all-start = ((bf16[8,8,8,8,128]{4,3,2,1,0:T(8,128)(2,1)}), bf16[8,8,8,8,128]{4,3,2,1,0:T(8,128)(2,1)S(1)}, u32[]{:S(2)}, u32[]{:S(2)}) async-start(bf16[8,8,8,8,128]{4,3,2,1,0:T(8,128)(2,1)} %bitcast.47), calls=%async_computation | async-start | bytes 2097152 | tf_op jit(solution)/shard_map/all_to_all | solution.py:139
  29.7 15.9 %collective-permute-start = (bf16[9,1,4,8,8,128]{5,4,3,2,0,1:T(8,128)(2,1)S(1)}, bf16[9,1,4,8,8,128]{5,4,3,2,0,1:T(8,128)(2,1)S(1)}, u32[]{:S(2)}, u32[]{:S(2)}) collective-permute-start(bf16[9,1,4,8,8,128]{5,4,3,2,0,1:T(8,128)(2,1)S(1)} %get-tuple-element.45), channel_id=1, source_target_pairs={{0,16},{16,32},{32,48},{1,17},{17,33},{33,49},{2,18},{18,34},{34,5... | collective-permute-start | bytes 1769480 | tf_op jit(solution)/shard_map/ppermute | solution.py:101
  33.3 16.5 %collective-permute-start.1 = (bf16[9,1,4,8,8,128]{5,4,3,2,0,1:T(8,128)(2,1)S(1)}, bf16[9,1,4,8,8,128]{5,4,3,2,0,1:T(8,128)(2,1)S(1)}, u32[]{:S(2)}, u32[]{:S(2)}) collective-permute-start(bf16[9,1,4,8,8,128]{5,4,3,2,0,1:T(8,128)(2,1)S(1)} %get-tuple-element.46), channel_id=1, source_target_pairs={{16,0},{32,16},{48,32},{17,1},{33,17},{49,33},{18,2},{34,18},{50,3... | collective-permute-start | bytes 1769480 | tf_op jit(solution)/shard_map/ppermute | solution.py:102
  45.6 6.5 %copy-start.1 = (bf16[9,1,4,8,8,128]{5,4,3,2,0,1:T(8,128)(2,1)}, bf16[9,1,4,8,8,128]{5,4,3,2,0,1:T(8,128)(2,1)S(1)}, u32[]{:S(2)}) copy-start(bf16[9,1,4,8,8,128]{5,4,3,2,0,1:T(8,128)(2,1)S(1)} %collective-permute-done) | copy-start | bytes 1769476
  49.7 2.4 %copy-start.3 = (bf16[9,1,4,8,8,128]{5,4,3,2,0,1:T(8,128)(2,1)}, bf16[9,1,4,8,8,128]{5,4,3,2,0,1:T(8,128)(2,1)S(1)}, u32[]{:S(2)}) copy-start(bf16[9,1,4,8,8,128]{5,4,3,2,0,1:T(8,128)(2,1)S(1)} %collective-permute-done.1) | copy-start | bytes 1769476
  52.1 29.3 %collective-permute-start.2 = (bf16[9,1,16,4,8,128]{5,4,3,2,0,1:T(8,128)(2,1)}, bf16[9,1,16,4,8,128]{5,4,3,2,0,1:T(8,128)(2,1)S(1)}, u32[]{:S(2)}, u32[]{:S(2)}) collective-permute-start(bf16[9,1,16,4,8,128]{5,4,3,2,0,1:T(8,128)(2,1)} %get-tuple-element.43), channel_id=1, source_target_pairs={{0,1},{1,2},{2,3},{3,4},{4,5},{5,6},{6,7},{7,8},{8,9},{9,10},{10,1... | collective-permute-start | bytes 3538952 | tf_op jit(solution)/shard_map/ppermute | solution.py:101
  57.1 29.6 %collective-permute-start.3 = (bf16[9,1,16,4,8,128]{5,4,3,2,0,1:T(8,128)(2,1)}, bf16[9,1,16,4,8,128]{5,4,3,2,0,1:T(8,128)(2,1)}, u32[]{:S(2)}, u32[]{:S(2)}) collective-permute-start(bf16[9,1,16,4,8,128]{5,4,3,2,0,1:T(8,128)(2,1)} %get-tuple-element.44), channel_id=1, source_target_pairs={{1,0},{2,1},{3,2},{4,3},{5,4},{6,5},{7,6},{8,7},{9,8},{10,9},{11,1... | collective-permute-start | bytes 3538952 | tf_op jit(solution)/shard_map/ppermute | solution.py:102
  59.7 28.6 %copy-start.2 = (bf16[9,1,4,8,8,128]{5,4,3,2,0,1:T(8,128)(2,1)S(1)}, bf16[9,1,4,8,8,128]{5,4,3,2,0,1:T(8,128)(2,1)}, u32[]{:S(2)}) copy-start(bf16[9,1,4,8,8,128]{5,4,3,2,0,1:T(8,128)(2,1)} %copy-done.1) | copy-start | bytes 1769476
  59.7 28.6 %copy-start.4 = (bf16[9,1,4,8,8,128]{5,4,3,2,0,1:T(8,128)(2,1)S(1)}, bf16[9,1,4,8,8,128]{5,4,3,2,0,1:T(8,128)(2,1)}, u32[]{:S(2)}) copy-start(bf16[9,1,4,8,8,128]{5,4,3,2,0,1:T(8,128)(2,1)} %copy-done.3) | copy-start | bytes 1769476
  112.2 9.3 %copy-start.7 = (bf16[512,128]{1,0:T(8,128)(2,1)S(1)}, bf16[512,128]{1,0:T(8,128)(2,1)}, u32[]{:S(2)}) copy-start(bf16[512,128]{1,0:T(8,128)(2,1)} %get-tuple-element.20) | copy-start | bytes 393220
  112.2 9.3 %copy-start.8 = (bf16[512,128]{1,0:T(8,128)(2,1)S(1)}, bf16[512,128]{1,0:T(8,128)(2,1)}, u32[]{:S(2)}) copy-start(bf16[512,128]{1,0:T(8,128)(2,1)} %get-tuple-element.22) | copy-start | bytes 393220
  112.2 21.1 %copy-start.6 = (bf16[512,128]{1,0:T(8,128)(2,1)S(1)}, bf16[512,128]{1,0:T(8,128)(2,1)}, u32[]{:S(2)}) copy-start(bf16[512,128]{1,0:T(8,128)(2,1)} %get-tuple-element.24) | copy-start | bytes 393220
  115.7 22.3 %copy-start.5 = (bf16[512,128]{1,0:T(8,128)(2,1)S(1)}, bf16[512,128]{1,0:T(8,128)(2,1)}, u32[]{:S(2)}) copy-start(bf16[512,128]{1,0:T(8,128)(2,1)} %get-tuple-element.27) | copy-start | bytes 393220
  116.7 5.3 %collective-permute-start.4 = (bf16[1,4,8,8,128]{4,3,2,1,0:T(8,128)(2,1)S(1)}, bf16[1,4,8,8,128]{4,3,2,1,0:T(8,128)(2,1)S(1)}, u32[]{:S(2)}, u32[]{:S(2)}) collective-permute-start(bf16[1,4,8,8,128]{4,3,2,1,0:T(8,128)(2,1)S(1)} %get-tuple-element.49), channel_id=1, source_target_pairs={{0,16},{16,32},{32,48},{1,17},{17,33},{33,49},{2,18},{18,34},{34,5... | collective-permute-start | bytes 196616 | tf_op jit(solution)/shard_map/ppermute | solution.py:101
  120.1 6.2 %collective-permute-start.5 = (bf16[1,4,8,8,128]{4,3,2,1,0:T(8,128)(2,1)S(1)}, bf16[1,4,8,8,128]{4,3,2,1,0:T(8,128)(2,1)S(1)}, u32[]{:S(2)}, u32[]{:S(2)}) collective-permute-start(bf16[1,4,8,8,128]{4,3,2,1,0:T(8,128)(2,1)S(1)} %get-tuple-element.50), channel_id=1, source_target_pairs={{16,0},{32,16},{48,32},{17,1},{33,17},{49,33},{18,2},{34,18},{50,3... | collective-permute-start | bytes 196616 | tf_op jit(solution)/shard_map/ppermute | solution.py:102
  127.3 7.0 %collective-permute-start.6 = (bf16[1,16,4,8,128]{4,3,2,1,0:T(8,128)(2,1)S(1)}, bf16[1,16,4,8,128]{4,3,2,1,0:T(8,128)(2,1)S(1)}, u32[]{:S(2)}, u32[]{:S(2)}) collective-permute-start(bf16[1,16,4,8,128]{4,3,2,1,0:T(8,128)(2,1)S(1)} %get-tuple-element.47), channel_id=1, source_target_pairs={{0,1},{1,2},{2,3},{3,4},{4,5},{5,6},{6,7},{7,8},{8,9},{9,10},{10,1... | collective-permute-start | bytes 393224 | tf_op jit(solution)/shard_map/ppermute | solution.py:101
  130.0 8.1 %collective-permute-start.7 = (bf16[1,16,4,8,128]{4,3,2,1,0:T(8,128)(2,1)S(1)}, bf16[1,16,4,8,128]{4,3,2,1,0:T(8,128)(2,1)S(1)}, u32[]{:S(2)}, u32[]{:S(2)}) collective-permute-start(bf16[1,16,4,8,128]{4,3,2,1,0:T(8,128)(2,1)S(1)} %get-tuple-element.48), channel_id=1, source_target_pairs={{1,0},{2,1},{3,2},{4,3},{5,4},{6,5},{7,6},{8,7},{9,8},{10,9},{11,1... | collective-permute-start | bytes 393224 | tf_op jit(solution)/shard_map/ppermute | solution.py:102
Sparse Core Ops, SparseCore 0:
  9.5 40.9 all-gather.1

commit v8 on v3

--- a/solution.py
+++ b/solution.py
@@ -10,17 +10,24 @@
 
 
 def section_kernel(
-    m, n, cols, inner, num_frames, num_rows, total_frames, total_rows, k,
-    offs_ref, lv_ref, prior_ref, noise_ref, w_hbm, out_ref, crop_ref, w_ref, sem, xl, xc, xr, nz,
+    m, n, cols, inner, num_frames, num_rows, total_frames, total_rows, k, j, cut,
+    offs_ref, lv_ref, prior_ref, noise_hbm, w_hbm, out_ref, crop_ref,
+    w_ref, sem, noise_raw, noise_sem, noise_wide, xl, xc, xr, nz,
 ):
     weight_copy = pltpu.make_async_copy(w_hbm.at[k], w_ref, sem)
     weight_copy.start()
+    noise_copy = pltpu.make_async_copy(noise_hbm.at[j], noise_raw, noise_sem)
+    noise_copy.start()
+    noise_copy.wait()
+    noise_wide[...] = noise_raw[...].astype(jnp.float32)
+    noise = noise_wide[pl.ds(cut, m), pl.ds(cut * cols, n * cols), :]
     channels = w_ref.shape[-1]
     rows_in = m * n * cols
     rows_out = (m - 2) * (n - 2) * cols
     width = (m - num_frames) // 2
     level = lv_ref[k]
-    noisy = prior_ref[...].astype(jnp.float32) + level * noise_ref[...].astype(jnp.float32)
+    noise = noise.reshape(m * n * cols, w_ref.shape[-1])
+    noisy = prior_ref[...].astype(jnp.float32) + level * noise
     mean_sq = jnp.mean(noisy * noisy, axis=-1, keepdims=True)
     normalized = (noisy * lax.rsqrt(mean_sq + 1e-05)).astype(jnp.bfloat16).astype(jnp.float32)
     shape4 = (m, n, cols, channels)
@@ -59,7 +66,7 @@
     crop_ref[...] = crop.reshape(num_frames * num_rows * cols, channels).astype(crop_ref.dtype)
 
 
-def section_call(offs, levels, prior, noise, packed, k, m, n, cols, num_frames, num_rows, totals):
+def section_call(offs, levels, prior, noise, packed, k, j, m, n, cols, num_frames, num_rows, totals):
     channels = packed.shape[-1]
     rows_in = m * n * cols
     rows_out = (m - 2) * (n - 2) * cols
@@ -73,17 +80,21 @@
     vmem = pl.BlockSpec(memory_space=pltpu.VMEM)
     return pl.pallas_call(
         functools.partial(
-            section_kernel, m, n, cols, inner, num_frames, num_rows, totals[0], totals[1], k
+            section_kernel, m, n, cols, inner, num_frames, num_rows, totals[0], totals[1], k, j,
+            (noise.shape[1] - m) // 2,
         ),
         out_shape=(
             jax.ShapeDtypeStruct((rows_out, channels), jnp.bfloat16),
             jax.ShapeDtypeStruct((rows_crop, channels), jnp.bfloat16),
         ),
-        in_specs=[smem, smem, vmem, vmem, pl.BlockSpec(memory_space=pl.ANY)],
+        in_specs=[smem, smem, vmem, pl.BlockSpec(memory_space=pl.ANY), pl.BlockSpec(memory_space=pl.ANY)],
         out_specs=(vmem, vmem),
         scratch_shapes=[
             pltpu.VMEM(packed.shape[1:], packed.dtype),
             pltpu.SemaphoreType.DMA(()),
+            pltpu.VMEM(noise.shape[1:], noise.dtype),
+            pltpu.SemaphoreType.DMA(()),
+            pltpu.VMEM(noise.shape[1:], jnp.float32),
         ]
         + [scratch] * 4,
         cost_estimate=pl.CostEstimate(
@@ -104,7 +115,7 @@
     return block
 
 
-def denoise(offs, levels, previous, noise_part, packed, k, num_frames, num_rows, totals):
+def denoise(offs, levels, previous, noise_round, j, packed, k, num_frames, num_rows, totals):
     num_videos, m, n, num_cols, channels = previous.shape
     outs = []
     crops = []
@@ -113,9 +124,10 @@
             offs,
             levels,
             previous[v].reshape(-1, channels),
-            noise_part[v].reshape(-1, channels),
+            noise_round,
             packed,
             k,
+            j,
             m,
             n,
             num_cols,
@@ -126,6 +138,11 @@
         outs.append(out.reshape(m - 2, n - 2, num_cols, channels))
         crops.append(crop)
     return jnp.stack(outs), jnp.stack(crops)
+
+
+def flat_noise(noise):
+    groups, _, big_m, big_n, cols, channels = noise.shape
+    return noise.reshape(groups, big_m, big_n * cols, channels)
 
 
 def on_device(
@@ -154,7 +171,7 @@
     totals = (num_frames * lax.axis_size("frames"), num_rows * lax.axis_size("space"))
     both = extend(jnp.concatenate([incoming[None], noise_t[:halo]], axis=0), halo, 2, 3)
     prior_ext = both[0]
-    noise_round = both[1:]
+    noise_round = flat_noise(both[1:])
     results = []
     for k in range(sections):
         j = k % halo
@@ -163,16 +180,13 @@
             noise_round = noise_next
         width = halo - j
         cut = halo - width
-        noise_here = noise_round[
-            j, :, cut : cut + num_frames + 2 * width, cut : cut + num_rows + 2 * width
-        ]
         prior_ext, crop = denoise(
-            offs, levels, prior_ext, noise_here, packed, k, num_frames, num_rows, totals
+            offs, levels, prior_ext, noise_round, j, packed, k, num_frames, num_rows, totals
         )
         results.append(crop)
         if j == 0 and k + halo < sections:
             later, _ = lax.optimization_barrier((noise_t[k + halo : k + 2 * halo], crop))
-            noise_next = extend(later, halo, 2, 3)
+            noise_next = flat_noise(extend(later, halo, 2, 3))
     num_cols, channels = base_frames.shape[3:]
     stacked = jnp.stack(results).reshape(
         (sections, per_device, num_frames, num_rows, num_cols, channels)

time: 171 us -> 176 us (1.029)
  Pallas kernels: 32.4 us -> 36.9 us
    reshape x0 -> x2, other arithmetic: none -> 5.18 us  [flat_noise(): return noise.reshape(groups, big_m, big_n * cols, channels)]
    pallas_call x8, Pallas kernels: 32.4 us -> 36.9 us  [section_call(): pl.pallas_call(functools.partial(section_kernel, m, n, cols, inner, num_f...]
    slice x5, local copies, waits for them, and re-layouts: 1.32 us -> 4.25 us  [extend(): lax.slice_in_dim(block, size - width, size, axis=dim)]
    slice x6 -> x1, other arithmetic: 4.65 us -> 1.77 us  [on_device(): prior_ext = both[0]]
    concatenate x6 -> x4, other arithmetic: 4.85 us -> 2.09 us  [extend(): block = jnp.concatenate([low, block, high], axis=dim)]
    slice x2 -> x0, local copies, waits for them, and re-layouts: 1.89 us -> none  [on_device(): noise_round[j, :, cut:cut + num_frames + 2 * width, cut:cut + num_rows +...]
    unnamed x20 -> x24, local copies, waits for them, and re-layouts: 3.84 us -> 3.85 us
where the time goes in v8:
time: 176 us; the launch traced here: 175 us
  blocking collectives  38.9 us (22%)
  Pallas kernels  36.9 us (21%)
  starting transfers between devices  35.4 us (20%)
  waiting for transfers between devices  27.4 us (16%)
  between operations  14.5 us (8%)
  other arithmetic  13 us (7%)
  local copies, waits for them, and re-layouts  9.18 us (5%)
    pallas_call x8, Pallas kernels, section_call(): pl.pallas_call(functools.partial(section_kernel, m, n, cols, inner, num_f...  36.9 us
    ppermute x6, starting transfers between devices, extend(): lax.ppermute(lax.slice_in_dim(block, size - width, size, axis=dim), axis,...  24.5 us
    ppermute x6, waiting for transfers between devices, extend(): lax.ppermute(lax.slice_in_dim(block, 0, width, axis=dim), axis, backward)  21.6 us
    all_to_all x1, blocking collectives, on_device(): noise_t = lax.all_to_all(section_noise[0], 'section', 0, 0, tiled=True)  20.4 us
    all_to_all x1, blocking collectives, on_device(): return lax.all_to_all(stacked, 'section', 0, 1, tiled=True)  18.5 us
    ppermute x6, starting transfers between devices, extend(): lax.ppermute(lax.slice_in_dim(block, 0, width, axis=dim), axis, backward)  10.9 us
    ppermute x6, waiting for transfers between devices, extend(): lax.ppermute(lax.slice_in_dim(block, size - width, size, axis=dim), axis,...  5.8 us
    reshape x2, other arithmetic, flat_noise(): return noise.reshape(groups, big_m, big_n * cols, channels)  5.18 us
  transfers between devices with their start and end apart: 13, of which 9 were waited for; matrix products, arithmetic and copies ran while one was open for 6% of the time, Pallas kernels for 0%

profile of v8, /device:TPU:96, one launch (start us, length us, event | category | flops | bytes accessed | tf_op | source)
XLA Modules:
  0.0 175.3 jit_solution(11419616636045599466)
XLA Ops:
  7.4 1.9 %maximum_maximum_fusion = bf16[1,14,128,128]{3,2,1,0:T(8,128)(2,1)} fusion(bf16[1,1,128,128]{3,2,1,0:T(8,128)(2,1)} %bitcast.42, bf16[1,3,128,128]{3,2,1,0:T(8,128)(2,1)} %param.10, bf16[1,9,128,128]{3,2,1,0:T(8,128)(2,1)} %param.9, bf16[14]{0:T(256)(128)(2,1)S(1)} %pad.31.clone), kind=kLoop, calls=%fused_computation.15 | loop fusion | flops 688128 | bytes 884764 | tf_op jit(solution)/shard_map/concatenate | solution.py:162
  9.3 20.4 %all_to_all.17 = bf16[8,8,8,8,128]{4,3,2,1,0:T(8,128)(2,1)S(1)} all-to-all(bf16[8,8,8,8,128]{4,3,2,1,0:T(8,128)(2,1)} %bitcast.33), channel_id=1, replica_groups=mesh['section'=8,'frames'=4,'space'=16] {'section'}, dimensions={0} | all-to-all | bytes 2097152 | tf_op jit(solution)/shard_map/all_to_all | solution.py:156
  29.8 0.9 fusion.5
  30.7 3.5 %collective-permute-start.8 = (bf16[4,1,4,8,8,128]{5,4,3,2,0,1:T(8,128)(2,1)}, bf16[4,1,4,8,8,128]{5,4,3,2,0,1:T(8,128)(2,1)S(1)}, u32[]{:S(2)}, u32[]{:S(2)}) collective-permute-start(bf16[4,1,4,8,8,128]{5,4,3,2,0,1:T(8,128)(2,1)} %get-tuple-element.43), channel_id=1, source_target_pairs={{0,16},{16,32},{32,48},{1,17},{17,33},{33,49},{2,18},{18,34},{34,5... | collective-permute-start | bytes 786440 | tf_op jit(solution)/shard_map/ppermute | solution.py:112
  34.2 1.3 collective-permute-start.9
  35.6 4.6 %collective-permute-start = (bf16[5,1,4,8,8,128]{5,4,3,2,0,1:T(8,128)(2,1)S(1)}, bf16[5,1,4,8,8,128]{5,4,3,2,0,1:T(8,128)(2,1)S(1)}, u32[]{:S(2)}, u32[]{:S(2)}) collective-permute-start(bf16[5,1,4,8,8,128]{5,4,3,2,0,1:T(8,128)(2,1)S(1)} %get-tuple-element.41), channel_id=1, source_target_pairs={{0,16},{16,32},{32,48},{1,17},{17,33},{33,49},{2,18},{18,34},{34,5... | collective-permute-start | bytes 983048 | tf_op jit(solution)/shard_map/ppermute | solution.py:112
  40.2 1.3 collective-permute-start.1
  41.5 2.5 %collective-permute-done.9 = bf16[4,1,4,8,8,128]{5,4,3,2,0,1:T(8,128)(2,1)S(1)} collective-permute-done((bf16[4,1,4,8,8,128]{5,4,3,2,0,1:T(8,128)(2,1)}, bf16[4,1,4,8,8,128]{5,4,3,2,0,1:T(8,128)(2,1)S(1)}, u32[]{:S(2)}, u32[]{:S(2)}) %collective-permute-start.9) | collective-permute-done | bytes 262176 | tf_op jit(solution)/shard_map/ppermute | solution.py:113
  44.1 1.1 fusion.4
  45.2 5.0 %collective-permute-start.10 = (bf16[4,1,16,4,8,128]{5,4,3,2,0,1:T(8,128)(2,1)}, bf16[4,1,16,4,8,128]{5,4,3,2,0,1:T(8,128)(2,1)}, u32[]{:S(2)}, u32[]{:S(2)}) collective-permute-start(bf16[4,1,16,4,8,128]{5,4,3,2,0,1:T(8,128)(2,1)} %get-tuple-element.37), channel_id=1, source_target_pairs={{0,1},{1,2},{2,3},{3,4},{4,5},{5,6},{6,7},{7,8},{8,9},{9,10},{10,1... | collective-permute-start | bytes 1572872 | tf_op jit(solution)/shard_map/ppermute | solution.py:112
  50.3 1.9 %collective-permute-start.11 = (bf16[4,1,16,4,8,128]{5,4,3,2,0,1:T(8,128)(2,1)}, bf16[4,1,16,4,8,128]{5,4,3,2,0,1:T(8,128)(2,1)}, u32[]{:S(2)}, u32[]{:S(2)}) collective-permute-start(bf16[4,1,16,4,8,128]{5,4,3,2,0,1:T(8,128)(2,1)} %get-tuple-element.38), channel_id=1, source_target_pairs={{1,0},{2,1},{3,2},{4,3},{5,4},{6,5},{7,6},{8,7},{9,8},{10,9},{11,1... | collective-permute-start | bytes 1572872 | tf_op jit(solution)/shard_map/ppermute | solution.py:113
  52.4 1.4 fusion.3
  53.7 5.1 %collective-permute-start.2 = (bf16[5,1,16,4,8,128]{5,4,3,2,0,1:T(8,128)(2,1)}, bf16[5,1,16,4,8,128]{5,4,3,2,0,1:T(8,128)(2,1)S(1)}, u32[]{:S(2)}, u32[]{:S(2)}) collective-permute-start(bf16[5,1,16,4,8,128]{5,4,3,2,0,1:T(8,128)(2,1)} %get-tuple-element.35), channel_id=1, source_target_pairs={{0,1},{1,2},{2,3},{3,4},{4,5},{5,6},{6,7},{7,8},{8,9},{9,10},{10,1... | collective-permute-start | bytes 1966088 | tf_op jit(solution)/shard_map/ppermute | solution.py:112
  58.9 1.9 %collective-permute-start.3 = (bf16[5,1,16,4,8,128]{5,4,3,2,0,1:T(8,128)(2,1)}, bf16[5,1,16,4,8,128]{5,4,3,2,0,1:T(8,128)(2,1)}, u32[]{:S(2)}, u32[]{:S(2)}) collective-permute-start(bf16[5,1,16,4,8,128]{5,4,3,2,0,1:T(8,128)(2,1)} %get-tuple-element.36), channel_id=1, source_target_pairs={{1,0},{2,1},{3,2},{4,3},{5,4},{6,5},{7,6},{8,7},{9,8},{10,9},{11,1... | collective-permute-start | bytes 1966088 | tf_op jit(solution)/shard_map/ppermute | solution.py:113
  60.8 0.6 pad_add_fusion.offs_ref
  61.4 1.5 collective-permute-done.10
  62.9 5.4 %collective-permute-done.11 = bf16[4,1,16,4,8,128]{5,4,3,2,0,1:T(8,128)(2,1)} collective-permute-done((bf16[4,1,16,4,8,128]{5,4,3,2,0,1:T(8,128)(2,1)}, bf16[4,1,16,4,8,128]{5,4,3,2,0,1:T(8,128)(2,1)}, u32[]{:S(2)}, u32[]{:S(2)}) %collective-permute-start.11) | collective-permute-done | bytes 524320 | tf_op jit(solution)/shard_map/ppermute | solution.py:113
  68.4 2.6 %maximum_bitcast_fusion.noise_hbm = bf16[4,16,128,128]{3,2,1,0:T(8,128)(2,1)} fusion(bf16[4,1,16,4,8,128]{5,4,3,2,0,1:T(8,128)(2,1)} %collective-permute-done.11, bf16[4,1,4,8,8,128]{5,4,3,2,0,1:T(8,128)(2,1)} %copy-done.3, bf16[4,1,8,8,8,128]{5,4,3,2,0,1:T(8,128)(2,1)S(1)} %get-tuple-element.39, bf16[4,1,4,8,8,128]{5,4,3,2,0,1:T(8,128)(2,1)} %copy-done.2, ...), kind=kLoop, calls=%fused_computation.6 | loop fusion | flops 4194304 | bytes 4194304 | tf_op jit(solution)/shard_map/reshape | solution.py:145
  71.0 3.0 %collective-permute-done.2 = bf16[5,1,16,4,8,128]{5,4,3,2,0,1:T(8,128)(2,1)S(1)} collective-permute-done((bf16[5,1,16,4,8,128]{5,4,3,2,0,1:T(8,128)(2,1)}, bf16[5,1,16,4,8,128]{5,4,3,2,0,1:T(8,128)(2,1)S(1)}, u32[]{:S(2)}, u32[]{:S(2)}) %collective-permute-start.2) | collective-permute-done | bytes 655392 | tf_op jit(solution)/shard_map/ppermute | solution.py:112
  74.0 5.3 %collective-permute-done.3 = bf16[5,1,16,4,8,128]{5,4,3,2,0,1:T(8,128)(2,1)} collective-permute-done((bf16[5,1,16,4,8,128]{5,4,3,2,0,1:T(8,128)(2,1)}, bf16[5,1,16,4,8,128]{5,4,3,2,0,1:T(8,128)(2,1)}, u32[]{:S(2)}, u32[]{:S(2)}) %collective-permute-start.3) | collective-permute-done | bytes 655392 | tf_op jit(solution)/shard_map/ppermute | solution.py:113
  79.3 1.8 %pad_maximum_fusion.7 = bf16[1,1,16,16,8,128]{5,4,3,2,0,1:T(8,128)(2,1)} fusion(bf16[5,1,16,4,8,128]{5,4,3,2,0,1:T(8,128)(2,1)} %collective-permute-done.3, bf16[5,1,16,4,8,128]{5,4,3,2,0,1:T(8,128)(2,1)S(1)} %collective-permute-done.2, bf16[5,1,4,8,8,128]{5,4,3,2,0,1:T(8,128)(2,1)S(1)} %collective-permute-done.1, ...), kind=kLoop, calls=%fused_computation.12 | loop fusion | flops 1310720 | bytes 3145728 | tf_op jit(solution)/shard_map/slice | solution.py:173
  81.1 2.6 %fusion.noise_hbm = bf16[4,16,128,128]{3,2,1,0:T(8,128)(2,1)} fusion(bf16[5,1,16,4,8,128]{5,4,3,2,0,1:T(8,128)(2,1)} %collective-permute-done.3, bf16[5,1,16,4,8,128]{5,4,3,2,0,1:T(8,128)(2,1)S(1)} %collective-permute-done.2, bf16[5,1,4,8,8,128]{5,4,3,2,0,1:T(8,128)(2,1)S(1)} %collective-permute-done.1, ...), kind=kLoop, calls=%fused_computation.1 | loop fusion | flops 5242880 | bytes 4718592 | tf_op jit(solution)/shard_map/reshape | solution.py:145
  83.6 1.4 fusion.2.lv_ref
  85.0 5.5 %shard_map.64 = (bf16[1568,128]{1,0:T(8,128)(2,1)}, bf16[512,128]{1,0:T(8,128)(2,1)}) custom-call(s32[2]{0:T(128)} %pad_add_fusion.offs_ref, f32[8]{0:T(128)} %fusion.2.lv_ref, bf16[2048,128]{1,0:T(8,128)(2,1)} %bitcast.29, bf16[4,16,128,128]{3,2,1,0:T(8,128)(2,1)} %fusion.noise_hbm, bf16[8,14,128,128]{3,2,1,0:T(8,128)(2,1)} %all-gather.2.cloned.1.call-done.w_hbm), custom_call_target="tpu_custom_call" | custom-call | flops 667942912 | bytes 2007040 | tf_op jit(solution)/shard_map/pallas_call | solution.py:81
  90.5 4.8 %shard_map.65 = (bf16[1152,128]{1,0:T(8,128)(2,1)}, bf16[512,128]{1,0:T(8,128)(2,1)}) custom-call(s32[2]{0:T(128)} %pad_add_fusion.offs_ref, f32[8]{0:T(128)} %fusion.2.lv_ref, bf16[1568,128]{1,0:T(8,128)(2,1)} %get-tuple-element.21.prior_ref, bf16[4,16,128,128]{3,2,1,0:T(8,128)(2,1)} %fusion.noise_hbm, ...), custom_call_target="tpu_custom_call" | custom-call | flops 490733568 | bytes 1654784 | tf_op jit(solution)/shard_map/pallas_call | solution.py:81
  95.3 4.3 %shard_map.66 = (bf16[800,128]{1,0:T(8,128)(2,1)}, bf16[512,128]{1,0:T(8,128)(2,1)}) custom-call(s32[2]{0:T(128)} %pad_add_fusion.offs_ref, f32[8]{0:T(128)} %fusion.2.lv_ref, bf16[1152,128]{1,0:T(8,128)(2,1)} %get-tuple-element.23.prior_ref, bf16[4,16,128,128]{3,2,1,0:T(8,128)(2,1)} %fusion.noise_hbm, ...), custom_call_target="tpu_custom_call" | custom-call | flops 340787200 | bytes 1351680 | tf_op jit(solution)/shard_map/pallas_call | solution.py:81
  99.6 3.9 %shard_map.67 = (bf16[512,128]{1,0:T(8,128)(2,1)}, bf16[512,128]{1,0:T(8,128)(2,1)}) custom-call(s32[2]{0:T(128)} %pad_add_fusion.offs_ref, f32[8]{0:T(128)} %fusion.2.lv_ref, bf16[800,128]{1,0:T(8,128)(2,1)} %get-tuple-element.25.prior_ref, bf16[4,16,128,128]{3,2,1,0:T(8,128)(2,1)} %fusion.noise_hbm, ...), custom_call_target="tpu_custom_call" | custom-call | flops 218103808 | bytes 1097728 | tf_op jit(solution)/shard_map/pallas_call | solution.py:81
  103.6 0.9 fusion.7
  104.5 3.5 %collective-permute-start.4 = (bf16[1,4,8,8,128]{4,3,2,1,0:T(8,128)(2,1)S(1)}, bf16[1,4,8,8,128]{4,3,2,1,0:T(8,128)(2,1)S(1)}, u32[]{:S(2)}, u32[]{:S(2)}) collective-permute-start(bf16[1,4,8,8,128]{4,3,2,1,0:T(8,128)(2,1)S(1)} %get-tuple-element.47), channel_id=1, source_target_pairs={{0,16},{16,32},{32,48},{1,17},{17,33},{33,49},{2,18},{18,34},{34,5... | collective-permute-start | bytes 196616 | tf_op jit(solution)/shard_map/ppermute | solution.py:112
  108.0 1.3 collective-permute-start.5
  109.4 0.5 collective-permute-done.4
  109.9 4.3 %collective-permute-done.5 = bf16[1,4,8,8,128]{4,3,2,1,0:T(8,128)(2,1)S(1)} collective-permute-done((bf16[1,4,8,8,128]{4,3,2,1,0:T(8,128)(2,1)S(1)}, bf16[1,4,8,8,128]{4,3,2,1,0:T(8,128)(2,1)S(1)}, u32[]{:S(2)}, u32[]{:S(2)}) %collective-permute-start.5) | collective-permute-done | bytes 65568 | tf_op jit(solution)/shard_map/ppermute | solution.py:113
  114.2 0.9 pad_maximum_fusion.10
  115.1 2.8 %collective-permute-start.6 = (bf16[1,16,4,8,128]{4,3,2,1,0:T(8,128)(2,1)S(1)}, bf16[1,16,4,8,128]{4,3,2,1,0:T(8,128)(2,1)S(1)}, u32[]{:S(2)}, u32[]{:S(2)}) collective-permute-start(bf16[1,16,4,8,128]{4,3,2,1,0:T(8,128)(2,1)S(1)} %get-tuple-element.45), channel_id=1, source_target_pairs={{0,1},{1,2},{2,3},{3,4},{4,5},{5,6},{6,7},{7,8},{8,9},{9,10},{10,1... | collective-permute-start | bytes 393224 | tf_op jit(solution)/shard_map/ppermute | solution.py:112
  117.9 3.2 %collective-permute-start.7 = (bf16[1,16,4,8,128]{4,3,2,1,0:T(8,128)(2,1)S(1)}, bf16[1,16,4,8,128]{4,3,2,1,0:T(8,128)(2,1)S(1)}, u32[]{:S(2)}, u32[]{:S(2)}) collective-permute-start(bf16[1,16,4,8,128]{4,3,2,1,0:T(8,128)(2,1)S(1)} %get-tuple-element.46), channel_id=1, source_target_pairs={{1,0},{2,1},{3,2},{4,3},{5,4},{6,5},{7,6},{8,7},{9,8},{10,9},{11,1... | collective-permute-start | bytes 393224 | tf_op jit(solution)/shard_map/ppermute | solution.py:113
  121.2 0.7 collective-permute-done.6
  122.0 4.0 %collective-permute-done.7 = bf16[1,16,4,8,128]{4,3,2,1,0:T(8,128)(2,1)S(1)} collective-permute-done((bf16[1,16,4,8,128]{4,3,2,1,0:T(8,128)(2,1)S(1)}, bf16[1,16,4,8,128]{4,3,2,1,0:T(8,128)(2,1)S(1)}, u32[]{:S(2)}, u32[]{:S(2)}) %collective-permute-start.7) | collective-permute-done | bytes 131104 | tf_op jit(solution)/shard_map/ppermute | solution.py:113
  126.0 0.9 pad_maximum_fusion.8
  126.9 5.4 %shard_map.68 = (bf16[1568,128]{1,0:T(8,128)(2,1)}, bf16[512,128]{1,0:T(8,128)(2,1)}) custom-call(s32[2]{0:T(128)} %pad_add_fusion.offs_ref, f32[8]{0:T(128)} %fusion.2.lv_ref, bf16[2048,128]{1,0:T(8,128)(2,1)} %bitcast.28, bf16[4,16,128,128]{3,2,1,0:T(8,128)(2,1)} %maximum_bitcast_fusion.noise_hbm, bf16[8,14,128,128]{3,2,1,0:T(8,128)(2,1)} %all-gather.2.cloned.1.call-done.w_hbm), custom_call_target="tpu_custom_call" | custom-call | flops 667942912 | bytes 2007040 | tf_op jit(solution)/shard_map/pallas_call | solution.py:81
  132.3 0.9 constant_dynamic-update-slice_fusion.3
  133.2 4.8 %shard_map.69 = (bf16[1152,128]{1,0:T(8,128)(2,1)}, bf16[512,128]{1,0:T(8,128)(2,1)}) custom-call(s32[2]{0:T(128)} %pad_add_fusion.offs_ref, f32[8]{0:T(128)} %fusion.2.lv_ref, bf16[1568,128]{1,0:T(8,128)(2,1)} %get-tuple-element.29.prior_ref, bf16[4,16,128,128]{3,2,1,0:T(8,128)(2,1)} %maximum_bitcast_fusion.noise_hbm, ...), custom_call_target="tpu_custom_call" | custom-call | flops 490733568 | bytes 1654784 | tf_op jit(solution)/shard_map/pallas_call | solution.py:81
  138.0 0.9 constant_dynamic-update-slice_fusion.2
  139.0 4.3 %shard_map.70 = (bf16[800,128]{1,0:T(8,128)(2,1)}, bf16[512,128]{1,0:T(8,128)(2,1)}) custom-call(s32[2]{0:T(128)} %pad_add_fusion.offs_ref, f32[8]{0:T(128)} %fusion.2.lv_ref, bf16[1152,128]{1,0:T(8,128)(2,1)} %get-tuple-element.31.prior_ref, bf16[4,16,128,128]{3,2,1,0:T(8,128)(2,1)} %maximum_bitcast_fusion.noise_hbm, ...), custom_call_target="tpu_custom_call" | custom-call | flops 340787200 | bytes 1351680 | tf_op jit(solution)/shard_map/pallas_call | solution.py:81
  143.3 0.9 constant_dynamic-update-slice_fusion.1
  144.2 3.9 %shard_map.71 = (bf16[512,128]{1,0:T(8,128)(2,1)}, bf16[512,128]{1,0:T(8,128)(2,1)}) custom-call(s32[2]{0:T(128)} %pad_add_fusion.offs_ref, f32[8]{0:T(128)} %fusion.2.lv_ref, bf16[800,128]{1,0:T(8,128)(2,1)} %get-tuple-element.33.prior_ref, bf16[4,16,128,128]{3,2,1,0:T(8,128)(2,1)} %maximum_bitcast_fusion.noise_hbm, ...), custom_call_target="tpu_custom_call" | custom-call | flops 218103808 | bytes 1097728 | tf_op jit(solution)/shard_map/pallas_call | solution.py:81
  148.1 0.9 constant_dynamic-update-slice_fusion
  149.0 18.5 %all_to_all.18 = bf16[8,1,8,8,8,128]{5,4,3,2,1,0:T(8,128)(2,1)S(1)} all-to-all(bf16[8,1,8,8,8,128]{5,4,3,2,1,0:T(8,128)(2,1)S(1)} %constant_dynamic-update-slice_fusion), channel_id=1, replica_groups=mesh['section'=8,'frames'=4,'space'=16] {'section'}, dimensions={0} | all-to-all | bytes 2097152 | tf_op jit(solution)/shard_map/all_to_all | solution.py:194
  167.5 1.0 copy.32
  (33 shorter events, 0.7 us)
Async XLA Ops:
  6.5 28.9 %copy-start = (bf16[8,8,8,8,128]{4,3,2,1,0:T(8,128)(2,1)S(1)}, bf16[8,8,8,8,128]{4,3,2,1,0:T(8,128)(2,1)}, u32[]{:S(2)}) copy-start(bf16[8,8,8,8,128]{4,3,2,1,0:T(8,128)(2,1)} %param.6) | copy-start | bytes 3145732
  6.5 77.1 %all-gather.2.cloned.1.call-start = ((), (), s32[]{:S(2)}) async-start(), calls=%async_computation.2 | async-start | bytes 4128768 | tf_op jit(solution)/shard_map/all_gather | solution.py:165
  30.7 10.8 %collective-permute-start.8 = (bf16[4,1,4,8,8,128]{5,4,3,2,0,1:T(8,128)(2,1)}, bf16[4,1,4,8,8,128]{5,4,3,2,0,1:T(8,128)(2,1)S(1)}, u32[]{:S(2)}, u32[]{:S(2)}) collective-permute-start(bf16[4,1,4,8,8,128]{5,4,3,2,0,1:T(8,128)(2,1)} %get-tuple-element.43), channel_id=1, source_target_pairs={{0,16},{16,32},{32,48},{1,17},{17,33},{33,49},{2,18},{18,34},{34,5... | collective-permute-start | bytes 786440 | tf_op jit(solution)/shard_map/ppermute | solution.py:112
  34.2 9.8 %collective-permute-start.9 = (bf16[4,1,4,8,8,128]{5,4,3,2,0,1:T(8,128)(2,1)}, bf16[4,1,4,8,8,128]{5,4,3,2,0,1:T(8,128)(2,1)S(1)}, u32[]{:S(2)}, u32[]{:S(2)}) collective-permute-start(bf16[4,1,4,8,8,128]{5,4,3,2,0,1:T(8,128)(2,1)} %get-tuple-element.44), channel_id=1, source_target_pairs={{16,0},{32,16},{48,32},{17,1},{33,17},{49,33},{18,2},{34,18},{50,3... | collective-permute-start | bytes 786440 | tf_op jit(solution)/shard_map/ppermute | solution.py:113
  35.6 16.6 %collective-permute-start = (bf16[5,1,4,8,8,128]{5,4,3,2,0,1:T(8,128)(2,1)S(1)}, bf16[5,1,4,8,8,128]{5,4,3,2,0,1:T(8,128)(2,1)S(1)}, u32[]{:S(2)}, u32[]{:S(2)}) collective-permute-start(bf16[5,1,4,8,8,128]{5,4,3,2,0,1:T(8,128)(2,1)S(1)} %get-tuple-element.41), channel_id=1, source_target_pairs={{0,16},{16,32},{32,48},{1,17},{17,33},{33,49},{2,18},{18,34},{34,5... | collective-permute-start | bytes 983048 | tf_op jit(solution)/shard_map/ppermute | solution.py:112
  40.2 12.1 %collective-permute-start.1 = (bf16[5,1,4,8,8,128]{5,4,3,2,0,1:T(8,128)(2,1)S(1)}, bf16[5,1,4,8,8,128]{5,4,3,2,0,1:T(8,128)(2,1)S(1)}, u32[]{:S(2)}, u32[]{:S(2)}) collective-permute-start(bf16[5,1,4,8,8,128]{5,4,3,2,0,1:T(8,128)(2,1)S(1)} %get-tuple-element.42), channel_id=1, source_target_pairs={{16,0},{32,16},{48,32},{17,1},{33,17},{49,33},{18,2},{34,18},{50,3... | collective-permute-start | bytes 983048 | tf_op jit(solution)/shard_map/ppermute | solution.py:113
  41.5 3.7 %copy-start.2 = (bf16[4,1,4,8,8,128]{5,4,3,2,0,1:T(8,128)(2,1)}, bf16[4,1,4,8,8,128]{5,4,3,2,0,1:T(8,128)(2,1)S(1)}, u32[]{:S(2)}) copy-start(bf16[4,1,4,8,8,128]{5,4,3,2,0,1:T(8,128)(2,1)S(1)} %collective-permute-done.8) | copy-start | bytes 786436
  44.0 1.2 copy-start.3
  45.2 17.7 %collective-permute-start.10 = (bf16[4,1,16,4,8,128]{5,4,3,2,0,1:T(8,128)(2,1)}, bf16[4,1,16,4,8,128]{5,4,3,2,0,1:T(8,128)(2,1)}, u32[]{:S(2)}, u32[]{:S(2)}) collective-permute-start(bf16[4,1,16,4,8,128]{5,4,3,2,0,1:T(8,128)(2,1)} %get-tuple-element.37), channel_id=1, source_target_pairs={{0,1},{1,2},{2,3},{3,4},{4,5},{5,6},{6,7},{7,8},{8,9},{9,10},{10,1... | collective-permute-start | bytes 1572872 | tf_op jit(solution)/shard_map/ppermute | solution.py:112
  50.3 18.1 %collective-permute-start.11 = (bf16[4,1,16,4,8,128]{5,4,3,2,0,1:T(8,128)(2,1)}, bf16[4,1,16,4,8,128]{5,4,3,2,0,1:T(8,128)(2,1)}, u32[]{:S(2)}, u32[]{:S(2)}) collective-permute-start(bf16[4,1,16,4,8,128]{5,4,3,2,0,1:T(8,128)(2,1)} %get-tuple-element.38), channel_id=1, source_target_pairs={{1,0},{2,1},{3,2},{4,3},{5,4},{6,5},{7,6},{8,7},{9,8},{10,9},{11,1... | collective-permute-start | bytes 1572872 | tf_op jit(solution)/shard_map/ppermute | solution.py:113
  53.7 20.2 %collective-permute-start.2 = (bf16[5,1,16,4,8,128]{5,4,3,2,0,1:T(8,128)(2,1)}, bf16[5,1,16,4,8,128]{5,4,3,2,0,1:T(8,128)(2,1)S(1)}, u32[]{:S(2)}, u32[]{:S(2)}) collective-permute-start(bf16[5,1,16,4,8,128]{5,4,3,2,0,1:T(8,128)(2,1)} %get-tuple-element.35), channel_id=1, source_target_pairs={{0,1},{1,2},{2,3},{3,4},{4,5},{5,6},{6,7},{7,8},{8,9},{9,10},{10,1... | collective-permute-start | bytes 1966088 | tf_op jit(solution)/shard_map/ppermute | solution.py:112
  58.9 20.4 %collective-permute-start.3 = (bf16[5,1,16,4,8,128]{5,4,3,2,0,1:T(8,128)(2,1)}, bf16[5,1,16,4,8,128]{5,4,3,2,0,1:T(8,128)(2,1)}, u32[]{:S(2)}, u32[]{:S(2)}) collective-permute-start(bf16[5,1,16,4,8,128]{5,4,3,2,0,1:T(8,128)(2,1)} %get-tuple-element.36), channel_id=1, source_target_pairs={{1,0},{2,1},{3,2},{4,3},{5,4},{6,5},{7,6},{8,7},{9,8},{10,9},{11,1... | collective-permute-start | bytes 1966088 | tf_op jit(solution)/shard_map/ppermute | solution.py:113
  99.6 9.7 %copy-start.6 = (bf16[512,128]{1,0:T(8,128)(2,1)S(1)}, bf16[512,128]{1,0:T(8,128)(2,1)}, u32[]{:S(2)}) copy-start(bf16[512,128]{1,0:T(8,128)(2,1)} %get-tuple-element.20) | copy-start | bytes 393220
  99.6 9.7 %copy-start.7 = (bf16[512,128]{1,0:T(8,128)(2,1)S(1)}, bf16[512,128]{1,0:T(8,128)(2,1)}, u32[]{:S(2)}) copy-start(bf16[512,128]{1,0:T(8,128)(2,1)} %get-tuple-element.22) | copy-start | bytes 393220
  99.6 21.5 %copy-start.5 = (bf16[512,128]{1,0:T(8,128)(2,1)S(1)}, bf16[512,128]{1,0:T(8,128)(2,1)}, u32[]{:S(2)}) copy-start(bf16[512,128]{1,0:T(8,128)(2,1)} %get-tuple-element.24) | copy-start | bytes 393220
  103.6 17.6 %copy-start.4 = (bf16[512,128]{1,0:T(8,128)(2,1)S(1)}, bf16[512,128]{1,0:T(8,128)(2,1)}, u32[]{:S(2)}) copy-start(bf16[512,128]{1,0:T(8,128)(2,1)} %get-tuple-element.26) | copy-start | bytes 393220
  103.6 22.4 %copy-start.1 = (bf16[512,128]{1,0:T(8,128)(2,1)S(1)}, bf16[512,128]{1,0:T(8,128)(2,1)}, u32[]{:S(2)}) copy-start(bf16[512,128]{1,0:T(8,128)(2,1)} %get-tuple-element.27) | copy-start | bytes 393220
  104.5 5.4 %collective-permute-start.4 = (bf16[1,4,8,8,128]{4,3,2,1,0:T(8,128)(2,1)S(1)}, bf16[1,4,8,8,128]{4,3,2,1,0:T(8,128)(2,1)S(1)}, u32[]{:S(2)}, u32[]{:S(2)}) collective-permute-start(bf16[1,4,8,8,128]{4,3,2,1,0:T(8,128)(2,1)S(1)} %get-tuple-element.47), channel_id=1, source_target_pairs={{0,16},{16,32},{32,48},{1,17},{17,33},{33,49},{2,18},{18,34},{34,5... | collective-permute-start | bytes 196616 | tf_op jit(solution)/shard_map/ppermute | solution.py:112
  108.0 6.2 %collective-permute-start.5 = (bf16[1,4,8,8,128]{4,3,2,1,0:T(8,128)(2,1)S(1)}, bf16[1,4,8,8,128]{4,3,2,1,0:T(8,128)(2,1)S(1)}, u32[]{:S(2)}, u32[]{:S(2)}) collective-permute-start(bf16[1,4,8,8,128]{4,3,2,1,0:T(8,128)(2,1)S(1)} %get-tuple-element.48), channel_id=1, source_target_pairs={{16,0},{32,16},{48,32},{17,1},{33,17},{49,33},{18,2},{34,18},{50,3... | collective-permute-start | bytes 196616 | tf_op jit(solution)/shard_map/ppermute | solution.py:113
  115.1 6.9 %collective-permute-start.6 = (bf16[1,16,4,8,128]{4,3,2,1,0:T(8,128)(2,1)S(1)}, bf16[1,16,4,8,128]{4,3,2,1,0:T(8,128)(2,1)S(1)}, u32[]{:S(2)}, u32[]{:S(2)}) collective-permute-start(bf16[1,16,4,8,128]{4,3,2,1,0:T(8,128)(2,1)S(1)} %get-tuple-element.45), channel_id=1, source_target_pairs={{0,1},{1,2},{2,3},{3,4},{4,5},{5,6},{6,7},{7,8},{8,9},{9,10},{10,1... | collective-permute-start | bytes 393224 | tf_op jit(solution)/shard_map/ppermute | solution.py:112
  117.9 8.1 %collective-permute-start.7 = (bf16[1,16,4,8,128]{4,3,2,1,0:T(8,128)(2,1)S(1)}, bf16[1,16,4,8,128]{4,3,2,1,0:T(8,128)(2,1)S(1)}, u32[]{:S(2)}, u32[]{:S(2)}) collective-permute-start(bf16[1,16,4,8,128]{4,3,2,1,0:T(8,128)(2,1)S(1)} %get-tuple-element.46), channel_id=1, source_target_pairs={{1,0},{2,1},{3,2},{4,3},{5,4},{6,5},{7,6},{8,7},{9,8},{10,9},{11,1... | collective-permute-start | bytes 393224 | tf_op jit(solution)/shard_map/ppermute | solution.py:113
Sparse Core Ops, SparseCore 0:
  9.5 40.9 all-gather.1

commit v9 on v3

--- a/solution.py
+++ b/solution.py
@@ -11,7 +11,8 @@
 
 def section_kernel(
     m, n, cols, inner, num_frames, num_rows, total_frames, total_rows, k,
-    offs_ref, lv_ref, prior_ref, noise_ref, w_hbm, out_ref, crop_ref, w_ref, sem, xl, xc, xr, nz,
+    offs_ref, lv_ref, prior_ref, noise_ref, w_hbm, stack_in, out_ref, stack_ref,
+    w_ref, sem, crop_buf, crop_sem, xl, xc, xr, nz,
 ):
     weight_copy = pltpu.make_async_copy(w_hbm.at[k], w_ref, sem)
     weight_copy.start()
@@ -56,10 +57,13 @@
     out_ref[...] = result.astype(out_ref.dtype)
     nz[pl.ds(0, m - 2), pl.ds(0, (n - 2) * cols), :] = result.reshape(m - 2, (n - 2) * cols, channels)
     crop = nz[pl.ds(inner, num_frames), pl.ds(inner * cols, num_rows * cols), :]
-    crop_ref[...] = crop.reshape(num_frames * num_rows * cols, channels).astype(crop_ref.dtype)
-
-
-def section_call(offs, levels, prior, noise, packed, k, m, n, cols, num_frames, num_rows, totals):
+    crop_buf[...] = crop.reshape(num_frames * num_rows * cols, channels).astype(crop_buf.dtype)
+    crop_copy = pltpu.make_async_copy(crop_buf, stack_ref.at[k], crop_sem)
+    crop_copy.start()
+    crop_copy.wait()
+
+
+def section_call(offs, levels, prior, noise, packed, stack, k, m, n, cols, num_frames, num_rows, totals):
     channels = packed.shape[-1]
     rows_in = m * n * cols
     rows_out = (m - 2) * (n - 2) * cols
@@ -77,19 +81,23 @@
         ),
         out_shape=(
             jax.ShapeDtypeStruct((rows_out, channels), jnp.bfloat16),
-            jax.ShapeDtypeStruct((rows_crop, channels), jnp.bfloat16),
-        ),
-        in_specs=[smem, smem, vmem, vmem, pl.BlockSpec(memory_space=pl.ANY)],
-        out_specs=(vmem, vmem),
+            jax.ShapeDtypeStruct(stack.shape, stack.dtype),
+        ),
+        in_specs=[smem, smem, vmem, vmem, pl.BlockSpec(memory_space=pl.ANY)] * 1
+        + [pl.BlockSpec(memory_space=pl.ANY)],
+        out_specs=(vmem, pl.BlockSpec(memory_space=pl.ANY)),
+        input_output_aliases={5: 1},
         scratch_shapes=[
             pltpu.VMEM(packed.shape[1:], packed.dtype),
+            pltpu.SemaphoreType.DMA(()),
+            pltpu.VMEM((rows_crop, channels), jnp.bfloat16),
             pltpu.SemaphoreType.DMA(()),
         ]
         + [scratch] * 4,
         cost_estimate=pl.CostEstimate(
             flops=flops, bytes_accessed=nbytes, transcendentals=rows_out * channels
         ),
-    )(offs, levels, prior, noise, packed)
+    )(offs, levels, prior, noise, packed, stack)
 
 
 def extend(block, width, frame_dim, row_dim):
@@ -104,17 +112,17 @@
     return block
 
 
-def denoise(offs, levels, previous, noise_part, packed, k, num_frames, num_rows, totals):
+def denoise(offs, levels, previous, noise_part, packed, stack, k, num_frames, num_rows, totals):
     num_videos, m, n, num_cols, channels = previous.shape
     outs = []
-    crops = []
     for v in range(num_videos):
-        out, crop = section_call(
+        out, stack = section_call(
             offs,
             levels,
             previous[v].reshape(-1, channels),
             noise_part[v].reshape(-1, channels),
             packed,
+            stack,
             k,
             m,
             n,
@@ -124,8 +132,7 @@
             totals,
         )
         outs.append(out.reshape(m - 2, n - 2, num_cols, channels))
-        crops.append(crop)
-    return jnp.stack(outs), jnp.stack(crops)
+    return jnp.stack(outs), stack
 
 
 def on_device(
@@ -155,7 +162,8 @@
     both = extend(jnp.concatenate([incoming[None], noise_t[:halo]], axis=0), halo, 2, 3)
     prior_ext = both[0]
     noise_round = both[1:]
-    results = []
+    num_cols, channels = base_frames.shape[3:]
+    stack = jnp.zeros((sections, num_frames * num_rows * num_cols, channels), jnp.bfloat16)
     for k in range(sections):
         j = k % halo
         if j == 0 and k > 0:
@@ -166,15 +174,12 @@
         noise_here = noise_round[
             j, :, cut : cut + num_frames + 2 * width, cut : cut + num_rows + 2 * width
         ]
-        prior_ext, crop = denoise(
-            offs, levels, prior_ext, noise_here, packed, k, num_frames, num_rows, totals
+        prior_ext, stack = denoise(
+            offs, levels, prior_ext, noise_here, packed, stack, k, num_frames, num_rows, totals
         )
-        results.append(crop)
         if j == 0 and k + halo < sections:
-            later, _ = lax.optimization_barrier((noise_t[k + halo : k + 2 * halo], crop))
-            noise_next = extend(later, halo, 2, 3)
-    num_cols, channels = base_frames.shape[3:]
-    stacked = jnp.stack(results).reshape(
+            noise_next = extend(noise_t[k + halo : k + 2 * halo], halo, 2, 3)
+    stacked = stack.reshape(
         (sections, per_device, num_frames, num_rows, num_cols, channels)
     )
     return lax.all_to_all(stacked, "section", 0, 1, tiled=True)

time: 171 us -> 176 us (1.029)
  waiting for transfers between devices: 27.1 us -> 20.7 us
  Pallas kernels: 32.4 us -> 37.3 us
  other arithmetic: 13.5 us -> 17.5 us
    ppermute x6, waiting for transfers between devices: 21.4 us -> 16.2 us  [extend(): lax.ppermute(lax.slice_in_dim(block, 0, width, axis=dim), axis, backward)]
    pallas_call x8, Pallas kernels: 32.4 us -> 37.3 us  [section_call(): pl.pallas_call(functools.partial(section_kernel, m, n, cols, inner, num_f...]
    slice x5, local copies, waits for them, and re-layouts: 1.32 us -> 4.22 us  [extend(): lax.slice_in_dim(block, size - width, size, axis=dim)]
    unnamed x20 -> x21, local copies, waits for them, and re-layouts: 3.84 us -> 1.01 us
    slice x6, other arithmetic: 4.65 us -> 7.2 us  [on_device(): noise_round[j, :, cut:cut + num_frames + 2 * width, cut:cut + num_rows +...]
  transfers between devices with their start and end apart: 13 -> 13, of which waited for: 9 -> 6; matrix products, arithmetic and copies ran while one was open for 6% -> 11% of each run, Pallas kernels for 0% -> 0%
where the time goes in v9:
time: 176 us; the launch traced here: 175 us
  blocking collectives  40 us (23%)
  Pallas kernels  37.3 us (21%)
  starting transfers between devices  35.4 us (20%)
  waiting for transfers between devices  20.7 us (12%)
  other arithmetic  17.5 us (10%)
  between operations  14.5 us (8%)
  local copies, waits for them, and re-layouts  9.47 us (5%)
    pallas_call x8, Pallas kernels, section_call(): pl.pallas_call(functools.partial(section_kernel, m, n, cols, inner, num_f...  37.3 us
    ppermute x6, starting transfers between devices, extend(): lax.ppermute(lax.slice_in_dim(block, size - width, size, axis=dim), axis,...  24.5 us
    all_to_all x1, blocking collectives, on_device(): noise_t = lax.all_to_all(section_noise[0], 'section', 0, 0, tiled=True)  20.4 us
    all_to_all x1, blocking collectives, on_device(): return lax.all_to_all(stacked, 'section', 0, 1, tiled=True)  19.6 us
    ppermute x6, waiting for transfers between devices, extend(): lax.ppermute(lax.slice_in_dim(block, 0, width, axis=dim), axis, backward)  16.2 us
    ppermute x6, starting transfers between devices, extend(): lax.ppermute(lax.slice_in_dim(block, 0, width, axis=dim), axis, backward)  10.9 us
    slice x6, other arithmetic, on_device(): noise_round[j, :, cut:cut + num_frames + 2 * width, cut:cut + num_rows +...  7.2 us
    concatenate x6, other arithmetic, extend(): block = jnp.concatenate([low, block, high], axis=dim)  6.26 us
  transfers between devices with their start and end apart: 13, of which 6 were waited for; matrix products, arithmetic and copies ran while one was open for 11% of the time, Pallas kernels for 0%

profile of v9, /device:TPU:96, one launch (start us, length us, event | category | flops | bytes accessed | tf_op | source)
XLA Modules:
  0.0 174.8 jit_solution(15678159064931467250)
XLA Ops:
  7.4 1.9 %maximum_maximum_fusion = bf16[1,14,128,128]{3,2,1,0:T(8,128)(2,1)} fusion(bf16[1,1,128,128]{3,2,1,0:T(8,128)(2,1)} %bitcast.42, bf16[1,3,128,128]{3,2,1,0:T(8,128)(2,1)} %param.10, bf16[1,9,128,128]{3,2,1,0:T(8,128)(2,1)} %param.9, bf16[14]{0:T(256)(128)(2,1)S(1)} %pad.31.clone), kind=kLoop, calls=%fused_computation.9 | loop fusion | flops 688128 | bytes 884764 | tf_op jit(solution)/shard_map/concatenate | solution.py:152
  9.3 20.4 %all_to_all.17 = bf16[8,8,8,8,128]{4,3,2,1,0:T(8,128)(2,1)S(1)} all-to-all(bf16[8,8,8,8,128]{4,3,2,1,0:T(8,128)(2,1)} %bitcast.39), channel_id=1, replica_groups=mesh['section'=8,'frames'=4,'space'=16] {'section'}, dimensions={0} | all-to-all | bytes 2097152 | tf_op jit(solution)/shard_map/all_to_all | solution.py:146
  29.8 0.8 fusion.5
  30.6 3.5 %collective-permute-start.8 = (bf16[4,1,4,8,8,128]{5,4,3,2,0,1:T(8,128)(2,1)}, bf16[4,1,4,8,8,128]{5,4,3,2,0,1:T(8,128)(2,1)S(1)}, u32[]{:S(2)}, u32[]{:S(2)}) collective-permute-start(bf16[4,1,4,8,8,128]{5,4,3,2,0,1:T(8,128)(2,1)} %get-tuple-element.45), channel_id=1, source_target_pairs={{0,16},{16,32},{32,48},{1,17},{17,33},{33,49},{2,18},{18,34},{34,5... | collective-permute-start | bytes 786440 | tf_op jit(solution)/shard_map/ppermute | solution.py:109
  34.1 1.3 collective-permute-start.9
  35.5 4.6 %collective-permute-start = (bf16[5,1,4,8,8,128]{5,4,3,2,0,1:T(8,128)(2,1)S(1)}, bf16[5,1,4,8,8,128]{5,4,3,2,0,1:T(8,128)(2,1)S(1)}, u32[]{:S(2)}, u32[]{:S(2)}) collective-permute-start(bf16[5,1,4,8,8,128]{5,4,3,2,0,1:T(8,128)(2,1)S(1)} %get-tuple-element.43), channel_id=1, source_target_pairs={{0,16},{16,32},{32,48},{1,17},{17,33},{33,49},{2,18},{18,34},{34,5... | collective-permute-start | bytes 983048 | tf_op jit(solution)/shard_map/ppermute | solution.py:109
  40.0 1.3 collective-permute-start.1
  41.4 2.1 %collective-permute-done.9 = bf16[4,1,4,8,8,128]{5,4,3,2,0,1:T(8,128)(2,1)S(1)} collective-permute-done((bf16[4,1,4,8,8,128]{5,4,3,2,0,1:T(8,128)(2,1)S(1)}, bf16[4,1,4,8,8,128]{5,4,3,2,0,1:T(8,128)(2,1)S(1)}, u32[]{:S(2)}, u32[]{:S(2)}) %collective-permute-start.9) | collective-permute-done | bytes 262176 | tf_op jit(solution)/shard_map/ppermute | solution.py:110
  43.6 1.1 fusion.4
  44.7 5.0 %collective-permute-start.10 = (bf16[4,1,16,4,8,128]{5,4,3,2,0,1:T(8,128)(2,1)}, bf16[4,1,16,4,8,128]{5,4,3,2,0,1:T(8,128)(2,1)}, u32[]{:S(2)}, u32[]{:S(2)}) collective-permute-start(bf16[4,1,16,4,8,128]{5,4,3,2,0,1:T(8,128)(2,1)} %get-tuple-element.39), channel_id=1, source_target_pairs={{0,1},{1,2},{2,3},{3,4},{4,5},{5,6},{6,7},{7,8},{8,9},{9,10},{10,1... | collective-permute-start | bytes 1572872 | tf_op jit(solution)/shard_map/ppermute | solution.py:109
  49.7 1.9 %collective-permute-start.11 = (bf16[4,1,16,4,8,128]{5,4,3,2,0,1:T(8,128)(2,1)}, bf16[4,1,16,4,8,128]{5,4,3,2,0,1:T(8,128)(2,1)}, u32[]{:S(2)}, u32[]{:S(2)}) collective-permute-start(bf16[4,1,16,4,8,128]{5,4,3,2,0,1:T(8,128)(2,1)} %get-tuple-element.40), channel_id=1, source_target_pairs={{1,0},{2,1},{3,2},{4,3},{5,4},{6,5},{7,6},{8,7},{9,8},{10,9},{11,1... | collective-permute-start | bytes 1572872 | tf_op jit(solution)/shard_map/ppermute | solution.py:110
  51.9 1.4 fusion.3
  53.3 5.1 %collective-permute-start.2 = (bf16[5,1,16,4,8,128]{5,4,3,2,0,1:T(8,128)(2,1)}, bf16[5,1,16,4,8,128]{5,4,3,2,0,1:T(8,128)(2,1)S(1)}, u32[]{:S(2)}, u32[]{:S(2)}) collective-permute-start(bf16[5,1,16,4,8,128]{5,4,3,2,0,1:T(8,128)(2,1)} %get-tuple-element.37), channel_id=1, source_target_pairs={{0,1},{1,2},{2,3},{3,4},{4,5},{5,6},{6,7},{7,8},{8,9},{9,10},{10,1... | collective-permute-start | bytes 1966088 | tf_op jit(solution)/shard_map/ppermute | solution.py:109
  58.5 1.9 %collective-permute-start.3 = (bf16[5,1,16,4,8,128]{5,4,3,2,0,1:T(8,128)(2,1)}, bf16[5,1,16,4,8,128]{5,4,3,2,0,1:T(8,128)(2,1)S(1)}, u32[]{:S(2)}, u32[]{:S(2)}) collective-permute-start(bf16[5,1,16,4,8,128]{5,4,3,2,0,1:T(8,128)(2,1)} %get-tuple-element.38), channel_id=1, source_target_pairs={{1,0},{2,1},{3,2},{4,3},{5,4},{6,5},{7,6},{8,7},{9,8},{10,9},{11,1... | collective-permute-start | bytes 1966088 | tf_op jit(solution)/shard_map/ppermute | solution.py:110
  60.4 0.6 pad_add_fusion.offs_ref
  61.0 1.4 collective-permute-done.10
  62.4 5.6 %collective-permute-done.11 = bf16[4,1,16,4,8,128]{5,4,3,2,0,1:T(8,128)(2,1)} collective-permute-done((bf16[4,1,16,4,8,128]{5,4,3,2,0,1:T(8,128)(2,1)}, bf16[4,1,16,4,8,128]{5,4,3,2,0,1:T(8,128)(2,1)}, u32[]{:S(2)}, u32[]{:S(2)}) %collective-permute-start.11) | collective-permute-done | bytes 524320 | tf_op jit(solution)/shard_map/ppermute | solution.py:110
  68.0 2.6 %pad_maximum_fusion.1 = bf16[4,1,16,16,8,128]{5,4,3,2,0,1:T(8,128)(2,1)} fusion(bf16[4,1,16,4,8,128]{5,4,3,2,0,1:T(8,128)(2,1)} %collective-permute-done.11, bf16[4,1,4,8,8,128]{5,4,3,2,0,1:T(8,128)(2,1)} %copy-done.7, bf16[4,1,8,8,8,128]{5,4,3,2,0,1:T(8,128)(2,1)S(1)} %get-tuple-element.41, bf16[4,1,4,8,8,128]{5,4,3,2,0,1:T(8,128)(2,1)} %copy-done.5, ...), kind=kLoop, calls=%fused_computation.1 | loop fusion | flops 4194304 | bytes 4194304 | tf_op jit(solution)/shard_map/concatenate | solution.py:111
  70.6 3.0 %collective-permute-done.2 = bf16[5,1,16,4,8,128]{5,4,3,2,0,1:T(8,128)(2,1)S(1)} collective-permute-done((bf16[5,1,16,4,8,128]{5,4,3,2,0,1:T(8,128)(2,1)}, bf16[5,1,16,4,8,128]{5,4,3,2,0,1:T(8,128)(2,1)S(1)}, u32[]{:S(2)}, u32[]{:S(2)}) %collective-permute-start.2) | collective-permute-done | bytes 655392 | tf_op jit(solution)/shard_map/ppermute | solution.py:109
  73.7 5.2 %collective-permute-done.3 = bf16[5,1,16,4,8,128]{5,4,3,2,0,1:T(8,128)(2,1)S(1)} collective-permute-done((bf16[5,1,16,4,8,128]{5,4,3,2,0,1:T(8,128)(2,1)}, bf16[5,1,16,4,8,128]{5,4,3,2,0,1:T(8,128)(2,1)S(1)}, u32[]{:S(2)}, u32[]{:S(2)}) %collective-permute-start.3) | collective-permute-done | bytes 655392 | tf_op jit(solution)/shard_map/ppermute | solution.py:110
  78.9 0.8 pad_maximum_fusion.12
  79.7 0.8 pad_maximum_fusion.9
  80.4 0.9 pad_maximum_fusion.6
  81.3 2.5 %pad_maximum_fusion = bf16[5,1,16,16,8,128]{5,4,3,2,0,1:T(8,128)(2,1)S(1)} fusion(bf16[5,1,16,4,8,128]{5,4,3,2,0,1:T(8,128)(2,1)S(1)} %collective-permute-done.3, bf16[5,1,4,8,8,128]{5,4,3,2,0,1:T(8,128)(2,1)S(1)} %copy-done.4, bf16[4,1,8,8,8,128]{5,4,3,2,0,1:T(8,128)(2,1)S(1)} %get-tuple-element.42, ...), kind=kLoop, calls=%fused_computation | loop fusion | flops 6553600 | bytes 5242880 | tf_op jit(solution)/shard_map/concatenate | solution.py:111
  83.8 1.0 fusion.2
  84.8 1.4 fusion.1.lv_ref
  86.2 1.1 broadcast_in_dim.20.stack_in
  87.3 5.3 %shard_map.64 = (bf16[1568,128]{1,0:T(8,128)(2,1)}, bf16[8,512,128]{2,1,0:T(8,128)(2,1)}) custom-call(s32[2]{0:T(128)} %pad_add_fusion.offs_ref, f32[8]{0:T(128)} %fusion.1.lv_ref, bf16[2048,128]{1,0:T(8,128)(2,1)} %bitcast.31, bf16[2048,128]{1,0:T(8,128)(2,1)} %bitcast.30, ...), custom_call_target="tpu_custom_call", output_to_operand_aliasing={{1}: (5, {})} | custom-call | flops 667942912 | bytes 2007040 | tf_op jit(solution)/shard_map/pallas_call | solution.py:78
  92.6 4.8 %shard_map.65 = (bf16[1152,128]{1,0:T(8,128)(2,1)}, bf16[8,512,128]{2,1,0:T(8,128)(2,1)}) custom-call(s32[2]{0:T(128)} %pad_add_fusion.offs_ref, f32[8]{0:T(128)} %fusion.1.lv_ref, bf16[1568,128]{1,0:T(8,128)(2,1)} %get-tuple-element.20.prior_ref, bf16[1568,128]{1,0:T(8,128)(2,1)} %bitcast.33, ...), custom_call_target="tpu_custom_call", output_to_operand_aliasing={{1}: (5, {})} | custom-call | flops 490733568 | bytes 1654784 | tf_op jit(solution)/shard_map/pallas_call | solution.py:78
  97.5 4.4 %shard_map.66 = (bf16[800,128]{1,0:T(8,128)(2,1)}, bf16[8,512,128]{2,1,0:T(8,128)(2,1)}) custom-call(s32[2]{0:T(128)} %pad_add_fusion.offs_ref, f32[8]{0:T(128)} %fusion.1.lv_ref, bf16[1152,128]{1,0:T(8,128)(2,1)} %get-tuple-element.22.prior_ref, bf16[1152,128]{1,0:T(8,128)(2,1)} %bitcast.35, ...), custom_call_target="tpu_custom_call", output_to_operand_aliasing={{1}: (5, {})} | custom-call | flops 340787200 | bytes 1351680 | tf_op jit(solution)/shard_map/pallas_call | solution.py:78
  101.9 4.2 %shard_map.67 = (bf16[512,128]{1,0:T(8,128)(2,1)}, bf16[8,512,128]{2,1,0:T(8,128)(2,1)}) custom-call(s32[2]{0:T(128)} %pad_add_fusion.offs_ref, f32[8]{0:T(128)} %fusion.1.lv_ref, bf16[800,128]{1,0:T(8,128)(2,1)} %get-tuple-element.24.prior_ref, bf16[800,128]{1,0:T(8,128)(2,1)} %bitcast.41, ...), custom_call_target="tpu_custom_call", output_to_operand_aliasing={{1}: (5, {})} | custom-call | flops 218103808 | bytes 1097728 | tf_op jit(solution)/shard_map/pallas_call | solution.py:78
  106.1 0.9 fusion.7
  107.0 3.5 %collective-permute-start.4 = (bf16[1,4,8,8,128]{4,3,2,1,0:T(8,128)(2,1)S(1)}, bf16[1,4,8,8,128]{4,3,2,1,0:T(8,128)(2,1)S(1)}, u32[]{:S(2)}, u32[]{:S(2)}) collective-permute-start(bf16[1,4,8,8,128]{4,3,2,1,0:T(8,128)(2,1)S(1)} %get-tuple-element.49), channel_id=1, source_target_pairs={{0,16},{16,32},{32,48},{1,17},{17,33},{33,49},{2,18},{18,34},{34,5... | collective-permute-start | bytes 196616 | tf_op jit(solution)/shard_map/ppermute | solution.py:109
  110.5 1.3 collective-permute-start.5
  111.8 1.6 pad_maximum_fusion.8
  113.4 3.2 %collective-permute-done.5 = bf16[1,4,8,8,128]{4,3,2,1,0:T(8,128)(2,1)S(1)} collective-permute-done((bf16[1,4,8,8,128]{4,3,2,1,0:T(8,128)(2,1)S(1)}, bf16[1,4,8,8,128]{4,3,2,1,0:T(8,128)(2,1)S(1)}, u32[]{:S(2)}, u32[]{:S(2)}) %collective-permute-start.5) | collective-permute-done | bytes 65568 | tf_op jit(solution)/shard_map/ppermute | solution.py:110
  116.7 2.8 %collective-permute-start.6 = (bf16[1,16,4,8,128]{4,3,2,1,0:T(8,128)(2,1)S(1)}, bf16[1,16,4,8,128]{4,3,2,1,0:T(8,128)(2,1)S(1)}, u32[]{:S(2)}, u32[]{:S(2)}) collective-permute-start(bf16[1,16,4,8,128]{4,3,2,1,0:T(8,128)(2,1)S(1)} %get-tuple-element.47), channel_id=1, source_target_pairs={{0,1},{1,2},{2,3},{3,4},{4,5},{5,6},{6,7},{7,8},{8,9},{9,10},{10,1... | collective-permute-start | bytes 393224 | tf_op jit(solution)/shard_map/ppermute | solution.py:109
  119.5 3.2 %collective-permute-start.7 = (bf16[1,16,4,8,128]{4,3,2,1,0:T(8,128)(2,1)S(1)}, bf16[1,16,4,8,128]{4,3,2,1,0:T(8,128)(2,1)S(1)}, u32[]{:S(2)}, u32[]{:S(2)}) collective-permute-start(bf16[1,16,4,8,128]{4,3,2,1,0:T(8,128)(2,1)S(1)} %get-tuple-element.48), channel_id=1, source_target_pairs={{1,0},{2,1},{3,2},{4,3},{5,4},{6,5},{7,6},{8,7},{9,8},{10,9},{11,1... | collective-permute-start | bytes 393224 | tf_op jit(solution)/shard_map/ppermute | solution.py:110
  122.8 1.5 pad_maximum_fusion.11
  124.2 1.9 %slice.126 = bf16[1,1,16,16,8,128]{5,4,3,2,0,1:T(8,128)(2,1)} slice(bf16[4,1,16,16,8,128]{5,4,3,2,0,1:T(8,128)(2,1)} %pad_maximum_fusion.1), slice={[0:1], [0:1], [0:16], [0:16], [0:8], [0:128]} | slice | bytes 1048576 | tf_op jit(solution)/shard_map/slice | solution.py:174
  126.2 1.8 %pad_maximum_fusion.5 = bf16[1,1,14,14,8,128]{5,4,3,2,0,1:T(8,128)(2,1)} fusion(bf16[4,1,16,4,8,128]{5,4,3,2,0,1:T(8,128)(2,1)} %collective-permute-done.11, bf16[4,1,16,4,8,128]{5,4,3,2,0,1:T(8,128)(2,1)} %collective-permute-done.10, bf16[4,1,4,8,8,128]{5,4,3,2,0,1:T(8,128)(2,1)S(1)} %copy-done.8, bf16[4,1,8,8,8,128]{5,4,3,2,0,1:T(8,128)(2,1)S(1)} %get-tuple-element.41, ...), kind=kLoop, calls=%fused_computation.10 | loop fusion | flops 802816 | bytes 2498560 | tf_op jit(solution)/shard_map/slice | solution.py:174
  127.9 0.9 pad_maximum_fusion.4
  128.8 5.3 %shard_map.68 = (bf16[1568,128]{1,0:T(8,128)(2,1)}, bf16[8,512,128]{2,1,0:T(8,128)(2,1)}) custom-call(s32[2]{0:T(128)} %pad_add_fusion.offs_ref, f32[8]{0:T(128)} %fusion.1.lv_ref, bf16[2048,128]{1,0:T(8,128)(2,1)} %bitcast.29, bf16[2048,128]{1,0:T(8,128)(2,1)} %bitcast.28, ...), custom_call_target="tpu_custom_call", output_to_operand_aliasing={{1}: (5, {})} | custom-call | flops 667942912 | bytes 2007040 | tf_op jit(solution)/shard_map/pallas_call | solution.py:78
  134.1 4.8 %shard_map.69 = (bf16[1152,128]{1,0:T(8,128)(2,1)}, bf16[8,512,128]{2,1,0:T(8,128)(2,1)}) custom-call(s32[2]{0:T(128)} %pad_add_fusion.offs_ref, f32[8]{0:T(128)} %fusion.1.lv_ref, bf16[1568,128]{1,0:T(8,128)(2,1)} %get-tuple-element.28.prior_ref, bf16[1568,128]{1,0:T(8,128)(2,1)} %bitcast.32, ...), custom_call_target="tpu_custom_call", output_to_operand_aliasing={{1}: (5, {})} | custom-call | flops 490733568 | bytes 1654784 | tf_op jit(solution)/shard_map/pallas_call | solution.py:78
  138.9 4.4 %shard_map.70 = (bf16[800,128]{1,0:T(8,128)(2,1)}, bf16[8,512,128]{2,1,0:T(8,128)(2,1)}) custom-call(s32[2]{0:T(128)} %pad_add_fusion.offs_ref, f32[8]{0:T(128)} %fusion.1.lv_ref, bf16[1152,128]{1,0:T(8,128)(2,1)} %get-tuple-element.30.prior_ref, bf16[1152,128]{1,0:T(8,128)(2,1)} %bitcast.34, ...), custom_call_target="tpu_custom_call", output_to_operand_aliasing={{1}: (5, {})} | custom-call | flops 340787200 | bytes 1351680 | tf_op jit(solution)/shard_map/pallas_call | solution.py:78
  143.3 4.1 %shard_map.71 = (bf16[512,128]{1,0:T(8,128)(2,1)}, bf16[8,512,128]{2,1,0:T(8,128)(2,1)}) custom-call(s32[2]{0:T(128)} %pad_add_fusion.offs_ref, f32[8]{0:T(128)} %fusion.1.lv_ref, bf16[800,128]{1,0:T(8,128)(2,1)} %get-tuple-element.32.prior_ref, bf16[800,128]{1,0:T(8,128)(2,1)} %bitcast.40, ...), custom_call_target="tpu_custom_call", output_to_operand_aliasing={{1}: (5, {})} | custom-call | flops 218103808 | bytes 1097728 | tf_op jit(solution)/shard_map/pallas_call | solution.py:78
  147.4 19.6 %all_to_all.18 = bf16[8,1,8,8,8,128]{5,4,3,2,1,0:T(8,128)(2,1)S(1)} all-to-all(bf16[8,1,8,8,8,128]{5,4,3,2,1,0:T(8,128)(2,1)} %bitcast.26), channel_id=1, replica_groups=mesh['section'=8,'frames'=4,'space'=16] {'section'}, dimensions={0} | all-to-all | bytes 2097152 | tf_op jit(solution)/shard_map/all_to_all | solution.py:185
  167.0 1.0 copy.26
  (37 shorter events, 0.6 us)
Async XLA Ops:
  6.5 28.8 %copy-start = (bf16[8,8,8,8,128]{4,3,2,1,0:T(8,128)(2,1)S(1)}, bf16[8,8,8,8,128]{4,3,2,1,0:T(8,128)(2,1)}, u32[]{:S(2)}) copy-start(bf16[8,8,8,8,128]{4,3,2,1,0:T(8,128)(2,1)} %param.6) | copy-start | bytes 3145732
  6.5 78.2 %all-gather.2.cloned.1.call-start = ((), (), s32[]{:S(2)}) async-start(), calls=%async_computation.2 | async-start | bytes 4128768 | tf_op jit(solution)/shard_map/all_gather | solution.py:155
  30.6 10.8 %collective-permute-start.8 = (bf16[4,1,4,8,8,128]{5,4,3,2,0,1:T(8,128)(2,1)}, bf16[4,1,4,8,8,128]{5,4,3,2,0,1:T(8,128)(2,1)S(1)}, u32[]{:S(2)}, u32[]{:S(2)}) collective-permute-start(bf16[4,1,4,8,8,128]{5,4,3,2,0,1:T(8,128)(2,1)} %get-tuple-element.45), channel_id=1, source_target_pairs={{0,16},{16,32},{32,48},{1,17},{17,33},{33,49},{2,18},{18,34},{34,5... | collective-permute-start | bytes 786440 | tf_op jit(solution)/shard_map/ppermute | solution.py:109
  34.1 9.4 %collective-permute-start.9 = (bf16[4,1,4,8,8,128]{5,4,3,2,0,1:T(8,128)(2,1)S(1)}, bf16[4,1,4,8,8,128]{5,4,3,2,0,1:T(8,128)(2,1)S(1)}, u32[]{:S(2)}, u32[]{:S(2)}) collective-permute-start(bf16[4,1,4,8,8,128]{5,4,3,2,0,1:T(8,128)(2,1)S(1)} %get-tuple-element.46), channel_id=1, source_target_pairs={{16,0},{32,16},{48,32},{17,1},{33,17},{49,33},{18,2},{34,18},{50,3... | collective-permute-start | bytes 786440 | tf_op jit(solution)/shard_map/ppermute | solution.py:110
  35.5 16.2 %collective-permute-start = (bf16[5,1,4,8,8,128]{5,4,3,2,0,1:T(8,128)(2,1)S(1)}, bf16[5,1,4,8,8,128]{5,4,3,2,0,1:T(8,128)(2,1)S(1)}, u32[]{:S(2)}, u32[]{:S(2)}) collective-permute-start(bf16[5,1,4,8,8,128]{5,4,3,2,0,1:T(8,128)(2,1)S(1)} %get-tuple-element.43), channel_id=1, source_target_pairs={{0,16},{16,32},{32,48},{1,17},{17,33},{33,49},{2,18},{18,34},{34,5... | collective-permute-start | bytes 983048 | tf_op jit(solution)/shard_map/ppermute | solution.py:109
  40.0 11.7 %collective-permute-start.1 = (bf16[5,1,4,8,8,128]{5,4,3,2,0,1:T(8,128)(2,1)S(1)}, bf16[5,1,4,8,8,128]{5,4,3,2,0,1:T(8,128)(2,1)S(1)}, u32[]{:S(2)}, u32[]{:S(2)}) collective-permute-start(bf16[5,1,4,8,8,128]{5,4,3,2,0,1:T(8,128)(2,1)S(1)} %get-tuple-element.44), channel_id=1, source_target_pairs={{16,0},{32,16},{48,32},{17,1},{33,17},{49,33},{18,2},{34,18},{50,3... | collective-permute-start | bytes 983048 | tf_op jit(solution)/shard_map/ppermute | solution.py:110
  41.4 3.4 %copy-start.5 = (bf16[4,1,4,8,8,128]{5,4,3,2,0,1:T(8,128)(2,1)}, bf16[4,1,4,8,8,128]{5,4,3,2,0,1:T(8,128)(2,1)S(1)}, u32[]{:S(2)}) copy-start(bf16[4,1,4,8,8,128]{5,4,3,2,0,1:T(8,128)(2,1)S(1)} %collective-permute-done.8) | copy-start | bytes 786436
  43.5 1.2 copy-start.7
  44.7 17.7 %collective-permute-start.10 = (bf16[4,1,16,4,8,128]{5,4,3,2,0,1:T(8,128)(2,1)}, bf16[4,1,16,4,8,128]{5,4,3,2,0,1:T(8,128)(2,1)}, u32[]{:S(2)}, u32[]{:S(2)}) collective-permute-start(bf16[4,1,16,4,8,128]{5,4,3,2,0,1:T(8,128)(2,1)} %get-tuple-element.39), channel_id=1, source_target_pairs={{0,1},{1,2},{2,3},{3,4},{4,5},{5,6},{6,7},{7,8},{8,9},{9,10},{10,1... | collective-permute-start | bytes 1572872 | tf_op jit(solution)/shard_map/ppermute | solution.py:109
  49.7 18.3 %collective-permute-start.11 = (bf16[4,1,16,4,8,128]{5,4,3,2,0,1:T(8,128)(2,1)}, bf16[4,1,16,4,8,128]{5,4,3,2,0,1:T(8,128)(2,1)}, u32[]{:S(2)}, u32[]{:S(2)}) collective-permute-start(bf16[4,1,16,4,8,128]{5,4,3,2,0,1:T(8,128)(2,1)} %get-tuple-element.40), channel_id=1, source_target_pairs={{1,0},{2,1},{3,2},{4,3},{5,4},{6,5},{7,6},{8,7},{9,8},{10,9},{11,1... | collective-permute-start | bytes 1572872 | tf_op jit(solution)/shard_map/ppermute | solution.py:110
  51.7 1.6 copy-start.1
  51.7 1.6 copy-start.3
  53.3 20.3 %collective-permute-start.2 = (bf16[5,1,16,4,8,128]{5,4,3,2,0,1:T(8,128)(2,1)}, bf16[5,1,16,4,8,128]{5,4,3,2,0,1:T(8,128)(2,1)S(1)}, u32[]{:S(2)}, u32[]{:S(2)}) collective-permute-start(bf16[5,1,16,4,8,128]{5,4,3,2,0,1:T(8,128)(2,1)} %get-tuple-element.37), channel_id=1, source_target_pairs={{0,1},{1,2},{2,3},{3,4},{4,5},{5,6},{6,7},{7,8},{8,9},{9,10},{10,1... | collective-permute-start | bytes 1966088 | tf_op jit(solution)/shard_map/ppermute | solution.py:109
  58.5 20.4 %collective-permute-start.3 = (bf16[5,1,16,4,8,128]{5,4,3,2,0,1:T(8,128)(2,1)}, bf16[5,1,16,4,8,128]{5,4,3,2,0,1:T(8,128)(2,1)S(1)}, u32[]{:S(2)}, u32[]{:S(2)}) collective-permute-start(bf16[5,1,16,4,8,128]{5,4,3,2,0,1:T(8,128)(2,1)} %get-tuple-element.38), channel_id=1, source_target_pairs={{1,0},{2,1},{3,2},{4,3},{5,4},{6,5},{7,6},{8,7},{9,8},{10,9},{11,1... | collective-permute-start | bytes 1966088 | tf_op jit(solution)/shard_map/ppermute | solution.py:110
  61.0 17.9 %copy-start.2 = (bf16[5,1,4,8,8,128]{5,4,3,2,0,1:T(8,128)(2,1)S(1)}, bf16[5,1,4,8,8,128]{5,4,3,2,0,1:T(8,128)(2,1)}, u32[]{:S(2)}) copy-start(bf16[5,1,4,8,8,128]{5,4,3,2,0,1:T(8,128)(2,1)} %copy-done.1) | copy-start | bytes 983044
  61.0 17.9 %copy-start.4 = (bf16[5,1,4,8,8,128]{5,4,3,2,0,1:T(8,128)(2,1)S(1)}, bf16[5,1,4,8,8,128]{5,4,3,2,0,1:T(8,128)(2,1)}, u32[]{:S(2)}) copy-start(bf16[5,1,4,8,8,128]{5,4,3,2,0,1:T(8,128)(2,1)} %copy-done.3) | copy-start | bytes 983044
  101.9 9.9 %copy-start.6 = (bf16[4,1,4,8,8,128]{5,4,3,2,0,1:T(8,128)(2,1)S(1)}, bf16[4,1,4,8,8,128]{5,4,3,2,0,1:T(8,128)(2,1)}, u32[]{:S(2)}) copy-start(bf16[4,1,4,8,8,128]{5,4,3,2,0,1:T(8,128)(2,1)} %copy-done.5) | copy-start | bytes 786436
  101.9 9.9 %copy-start.8 = (bf16[4,1,4,8,8,128]{5,4,3,2,0,1:T(8,128)(2,1)S(1)}, bf16[4,1,4,8,8,128]{5,4,3,2,0,1:T(8,128)(2,1)}, u32[]{:S(2)}) copy-start(bf16[4,1,4,8,8,128]{5,4,3,2,0,1:T(8,128)(2,1)} %copy-done.7) | copy-start | bytes 786436
  106.1 10.6 %copy-start.9 = (bf16[512,128]{1,0:T(8,128)(2,1)S(1)}, bf16[512,128]{1,0:T(8,128)(2,1)}, u32[]{:S(2)}) copy-start(bf16[512,128]{1,0:T(8,128)(2,1)} %get-tuple-element.26) | copy-start | bytes 393220
  107.0 6.4 %collective-permute-start.4 = (bf16[1,4,8,8,128]{4,3,2,1,0:T(8,128)(2,1)S(1)}, bf16[1,4,8,8,128]{4,3,2,1,0:T(8,128)(2,1)S(1)}, u32[]{:S(2)}, u32[]{:S(2)}) collective-permute-start(bf16[1,4,8,8,128]{4,3,2,1,0:T(8,128)(2,1)S(1)} %get-tuple-element.49), channel_id=1, source_target_pairs={{0,16},{16,32},{32,48},{1,17},{17,33},{33,49},{2,18},{18,34},{34,5... | collective-permute-start | bytes 196616 | tf_op jit(solution)/shard_map/ppermute | solution.py:109
  110.5 6.2 %collective-permute-start.5 = (bf16[1,4,8,8,128]{4,3,2,1,0:T(8,128)(2,1)S(1)}, bf16[1,4,8,8,128]{4,3,2,1,0:T(8,128)(2,1)S(1)}, u32[]{:S(2)}, u32[]{:S(2)}) collective-permute-start(bf16[1,4,8,8,128]{4,3,2,1,0:T(8,128)(2,1)S(1)} %get-tuple-element.50), channel_id=1, source_target_pairs={{16,0},{32,16},{48,32},{17,1},{33,17},{49,33},{18,2},{34,18},{50,3... | collective-permute-start | bytes 196616 | tf_op jit(solution)/shard_map/ppermute | solution.py:110
  116.7 11.2 %collective-permute-start.6 = (bf16[1,16,4,8,128]{4,3,2,1,0:T(8,128)(2,1)S(1)}, bf16[1,16,4,8,128]{4,3,2,1,0:T(8,128)(2,1)S(1)}, u32[]{:S(2)}, u32[]{:S(2)}) collective-permute-start(bf16[1,16,4,8,128]{4,3,2,1,0:T(8,128)(2,1)S(1)} %get-tuple-element.47), channel_id=1, source_target_pairs={{0,1},{1,2},{2,3},{3,4},{4,5},{5,6},{6,7},{7,8},{8,9},{9,10},{10,1... | collective-permute-start | bytes 393224 | tf_op jit(solution)/shard_map/ppermute | solution.py:109
  119.5 8.4 %collective-permute-start.7 = (bf16[1,16,4,8,128]{4,3,2,1,0:T(8,128)(2,1)S(1)}, bf16[1,16,4,8,128]{4,3,2,1,0:T(8,128)(2,1)S(1)}, u32[]{:S(2)}, u32[]{:S(2)}) collective-permute-start(bf16[1,16,4,8,128]{4,3,2,1,0:T(8,128)(2,1)S(1)} %get-tuple-element.48), channel_id=1, source_target_pairs={{1,0},{2,1},{3,2},{4,3},{5,4},{6,5},{7,6},{8,7},{9,8},{10,9},{11,1... | collective-permute-start | bytes 393224 | tf_op jit(solution)/shard_map/ppermute | solution.py:110
Sparse Core Ops, SparseCore 0:
  9.5 40.9 all-gather.1

commit v10 on v3

--- a/solution.py
+++ b/solution.py
@@ -159,8 +159,8 @@
     for k in range(sections):
         j = k % halo
         if j == 0 and k > 0:
+            noise_round, prior_ext = lax.optimization_barrier((noise_next, prior_ext))
             prior_ext = extend(prior_ext, halo, 1, 2)
-            noise_round = noise_next
         width = halo - j
         cut = halo - width
         noise_here = noise_round[

time: 171 us -> 175 us (1.023)
  local copies, waits for them, and re-layouts: 8.14 us -> 18.6 us
  waiting for transfers between devices: 27.1 us -> 20.5 us
    unnamed x20 -> x34, local copies, waits for them, and re-layouts: 3.84 us -> 9.36 us
    ppermute x6, waiting for transfers between devices: 21.4 us -> 15.9 us  [extend(): lax.ppermute(lax.slice_in_dim(block, 0, width, axis=dim), axis, backward)]
    slice x6 -> x3, other arithmetic: 4.65 us -> 2.34 us  [on_device(): noise_round[j, :, cut:cut + num_frames + 2 * width, cut:cut + num_rows +...]
    slice x2 -> x5, local copies, waits for them, and re-layouts: 1.89 us -> 4.11 us  [on_device(): noise_round[j, :, cut:cut + num_frames + 2 * width, cut:cut + num_rows +...]
    concatenate x6 -> x5, other arithmetic: 4.85 us -> 6.21 us  [extend(): block = jnp.concatenate([low, block, high], axis=dim)]
  transfers between devices with their start and end apart: 13 -> 13, of which waited for: 9 -> 7; matrix products, arithmetic and copies ran while one was open for 6% -> 11% of each run, Pallas kernels for 0% -> 0%
where the time goes in v10:
time: 175 us; the launch traced here: 174 us
  blocking collectives  40 us (23%)
  starting transfers between devices  35.4 us (20%)
  Pallas kernels  32.5 us (19%)
  waiting for transfers between devices  20.5 us (12%)
  local copies, waits for them, and re-layouts  18.6 us (11%)
  between operations  14.5 us (8%)
  other arithmetic  12.6 us (7%)
    pallas_call x8, Pallas kernels, section_call(): pl.pallas_call(functools.partial(section_kernel, m, n, cols, inner, num_f...  32.5 us
    ppermute x6, starting transfers between devices, extend(): lax.ppermute(lax.slice_in_dim(block, size - width, size, axis=dim), axis,...  24.5 us
    all_to_all x1, blocking collectives, on_device(): noise_t = lax.all_to_all(section_noise[0], 'section', 0, 0, tiled=True)  20.4 us
    all_to_all x1, blocking collectives, on_device(): return lax.all_to_all(stacked, 'section', 0, 1, tiled=True)  19.6 us
    ppermute x6, waiting for transfers between devices, extend(): lax.ppermute(lax.slice_in_dim(block, 0, width, axis=dim), axis, backward)  15.9 us
    ppermute x6, starting transfers between devices, extend(): lax.ppermute(lax.slice_in_dim(block, 0, width, axis=dim), axis, backward)  10.9 us
    unnamed x34, local copies, waits for them, and re-layouts  9.36 us
    concatenate x5, other arithmetic, extend(): block = jnp.concatenate([low, block, high], axis=dim)  6.21 us
  transfers between devices with their start and end apart: 13, of which 7 were waited for; matrix products, arithmetic and copies ran while one was open for 11% of the time, Pallas kernels for 0%

profile of v10, /device:TPU:96, one launch (start us, length us, event | category | flops | bytes accessed | tf_op | source)
XLA Modules:
  0.0 174.0 jit_solution(3895493862986802414)
XLA Ops:
  7.4 1.9 %maximum_maximum_fusion = bf16[1,14,128,128]{3,2,1,0:T(8,128)(2,1)} fusion(bf16[1,1,128,128]{3,2,1,0:T(8,128)(2,1)} %bitcast.53, bf16[1,3,128,128]{3,2,1,0:T(8,128)(2,1)} %param.10, bf16[1,9,128,128]{3,2,1,0:T(8,128)(2,1)} %param.9, bf16[14]{0:T(256)(128)(2,1)S(1)} %pad.26.clone), kind=kLoop, calls=%fused_computation.9 | loop fusion | flops 688128 | bytes 884764 | tf_op jit(solution)/shard_map/concatenate | solution.py:145
  9.3 20.4 %all_to_all.17 = bf16[8,8,8,8,128]{4,3,2,1,0:T(8,128)(2,1)S(1)} all-to-all(bf16[8,8,8,8,128]{4,3,2,1,0:T(8,128)(2,1)} %bitcast.40), channel_id=1, replica_groups=mesh['section'=8,'frames'=4,'space'=16] {'section'}, dimensions={0} | all-to-all | bytes 2097152 | tf_op jit(solution)/shard_map/all_to_all | solution.py:139
  29.9 3.5 %collective-permute-start.4 = (bf16[4,1,4,8,8,128]{5,4,3,2,0,1:T(8,128)(2,1)S(1)}, bf16[4,1,4,8,8,128]{5,4,3,2,0,1:T(8,128)(2,1)S(1)}, u32[]{:S(2)}, u32[]{:S(2)}) collective-permute-start(bf16[4,1,4,8,8,128]{5,4,3,2,0,1:T(8,128)(2,1)S(1)} %get-tuple-element.49), channel_id=1, source_target_pairs={{0,16},{16,32},{32,48},{1,17},{17,33},{33,49},{2,18},{18,34},{34,5... | collective-permute-start | bytes 786440 | tf_op jit(solution)/shard_map/ppermute | solution.py:101
  33.4 1.3 collective-permute-start.5
  34.8 4.6 %collective-permute-start = (bf16[5,1,4,8,8,128]{5,4,3,2,0,1:T(8,128)(2,1)S(1)}, bf16[5,1,4,8,8,128]{5,4,3,2,0,1:T(8,128)(2,1)S(1)}, u32[]{:S(2)}, u32[]{:S(2)}) collective-permute-start(bf16[5,1,4,8,8,128]{5,4,3,2,0,1:T(8,128)(2,1)S(1)} %get-tuple-element.47), channel_id=1, source_target_pairs={{0,16},{16,32},{32,48},{1,17},{17,33},{33,49},{2,18},{18,34},{34,5... | collective-permute-start | bytes 983048 | tf_op jit(solution)/shard_map/ppermute | solution.py:101
  39.3 1.3 collective-permute-start.1
  40.7 2.1 %collective-permute-done.5 = bf16[4,1,4,8,8,128]{5,4,3,2,0,1:T(8,128)(2,1)S(1)} collective-permute-done((bf16[4,1,4,8,8,128]{5,4,3,2,0,1:T(8,128)(2,1)S(1)}, bf16[4,1,4,8,8,128]{5,4,3,2,0,1:T(8,128)(2,1)S(1)}, u32[]{:S(2)}, u32[]{:S(2)}) %collective-permute-start.5) | collective-permute-done | bytes 262176 | tf_op jit(solution)/shard_map/ppermute | solution.py:102
  42.9 1.1 fusion.4
  44.0 5.0 %collective-permute-start.6 = (bf16[4,1,16,4,8,128]{5,4,3,2,0,1:T(8,128)(2,1)}, bf16[4,1,16,4,8,128]{5,4,3,2,0,1:T(8,128)(2,1)}, u32[]{:S(2)}, u32[]{:S(2)}) collective-permute-start(bf16[4,1,16,4,8,128]{5,4,3,2,0,1:T(8,128)(2,1)} %get-tuple-element.43), channel_id=1, source_target_pairs={{0,1},{1,2},{2,3},{3,4},{4,5},{5,6},{6,7},{7,8},{8,9},{9,10},{10,1... | collective-permute-start | bytes 1572872 | tf_op jit(solution)/shard_map/ppermute | solution.py:101
  49.0 1.9 %collective-permute-start.7 = (bf16[4,1,16,4,8,128]{5,4,3,2,0,1:T(8,128)(2,1)}, bf16[4,1,16,4,8,128]{5,4,3,2,0,1:T(8,128)(2,1)}, u32[]{:S(2)}, u32[]{:S(2)}) collective-permute-start(bf16[4,1,16,4,8,128]{5,4,3,2,0,1:T(8,128)(2,1)} %get-tuple-element.44), channel_id=1, source_target_pairs={{1,0},{2,1},{3,2},{4,3},{5,4},{6,5},{7,6},{8,7},{9,8},{10,9},{11,1... | collective-permute-start | bytes 1572872 | tf_op jit(solution)/shard_map/ppermute | solution.py:102
  51.2 1.4 fusion.3
  52.5 5.1 %collective-permute-start.2 = (bf16[5,1,16,4,8,128]{5,4,3,2,0,1:T(8,128)(2,1)}, bf16[5,1,16,4,8,128]{5,4,3,2,0,1:T(8,128)(2,1)S(1)}, u32[]{:S(2)}, u32[]{:S(2)}) collective-permute-start(bf16[5,1,16,4,8,128]{5,4,3,2,0,1:T(8,128)(2,1)} %get-tuple-element.41), channel_id=1, source_target_pairs={{0,1},{1,2},{2,3},{3,4},{4,5},{5,6},{6,7},{7,8},{8,9},{9,10},{10,1... | collective-permute-start | bytes 1966088 | tf_op jit(solution)/shard_map/ppermute | solution.py:101
  57.6 1.9 %collective-permute-start.3 = (bf16[5,1,16,4,8,128]{5,4,3,2,0,1:T(8,128)(2,1)}, bf16[5,1,16,4,8,128]{5,4,3,2,0,1:T(8,128)(2,1)S(1)}, u32[]{:S(2)}, u32[]{:S(2)}) collective-permute-start(bf16[5,1,16,4,8,128]{5,4,3,2,0,1:T(8,128)(2,1)} %get-tuple-element.42), channel_id=1, source_target_pairs={{1,0},{2,1},{3,2},{4,3},{5,4},{6,5},{7,6},{8,7},{9,8},{10,9},{11,1... | collective-permute-start | bytes 1966088 | tf_op jit(solution)/shard_map/ppermute | solution.py:102
  60.2 1.5 collective-permute-done.6
  61.7 5.6 %collective-permute-done.7 = bf16[4,1,16,4,8,128]{5,4,3,2,0,1:T(8,128)(2,1)} collective-permute-done((bf16[4,1,16,4,8,128]{5,4,3,2,0,1:T(8,128)(2,1)}, bf16[4,1,16,4,8,128]{5,4,3,2,0,1:T(8,128)(2,1)}, u32[]{:S(2)}, u32[]{:S(2)}) %collective-permute-start.7) | collective-permute-done | bytes 524320 | tf_op jit(solution)/shard_map/ppermute | solution.py:102
  67.3 2.6 %pad_maximum_fusion.1 = bf16[4,1,16,16,8,128]{5,4,3,2,0,1:T(8,128)(2,1)} fusion(bf16[4,1,16,4,8,128]{5,4,3,2,0,1:T(8,128)(2,1)} %collective-permute-done.7, bf16[4,1,4,8,8,128]{5,4,3,2,0,1:T(8,128)(2,1)} %copy-done.7, bf16[4,1,8,8,8,128]{5,4,3,2,0,1:T(8,128)(2,1)S(1)} %get-tuple-element.45, bf16[4,1,4,8,8,128]{5,4,3,2,0,1:T(8,128)(2,1)} %copy-done.6, ...), kind=kLoop, calls=%fused_computation.1 | loop fusion | flops 4194304 | bytes 4194304 | tf_op jit(solution)/shard_map/concatenate | solution.py:103
  69.9 3.0 %collective-permute-done.2 = bf16[5,1,16,4,8,128]{5,4,3,2,0,1:T(8,128)(2,1)S(1)} collective-permute-done((bf16[5,1,16,4,8,128]{5,4,3,2,0,1:T(8,128)(2,1)}, bf16[5,1,16,4,8,128]{5,4,3,2,0,1:T(8,128)(2,1)S(1)}, u32[]{:S(2)}, u32[]{:S(2)}) %collective-permute-start.2) | collective-permute-done | bytes 655392 | tf_op jit(solution)/shard_map/ppermute | solution.py:101
  72.9 5.2 %collective-permute-done.3 = bf16[5,1,16,4,8,128]{5,4,3,2,0,1:T(8,128)(2,1)S(1)} collective-permute-done((bf16[5,1,16,4,8,128]{5,4,3,2,0,1:T(8,128)(2,1)}, bf16[5,1,16,4,8,128]{5,4,3,2,0,1:T(8,128)(2,1)S(1)}, u32[]{:S(2)}, u32[]{:S(2)}) %collective-permute-start.3) | collective-permute-done | bytes 655392 | tf_op jit(solution)/shard_map/ppermute | solution.py:102
  78.2 0.7 pad_maximum_fusion.8
  78.9 0.8 pad_maximum_fusion.7
  79.7 0.8 pad_maximum_fusion.5
  80.5 2.5 %pad_maximum_fusion = bf16[5,1,16,16,8,128]{5,4,3,2,0,1:T(8,128)(2,1)S(1)} fusion(bf16[5,1,16,4,8,128]{5,4,3,2,0,1:T(8,128)(2,1)S(1)} %collective-permute-done.3, bf16[5,1,4,8,8,128]{5,4,3,2,0,1:T(8,128)(2,1)S(1)} %copy-done.4, bf16[4,1,8,8,8,128]{5,4,3,2,0,1:T(8,128)(2,1)S(1)} %get-tuple-element.46, ...), kind=kLoop, calls=%fused_computation | loop fusion | flops 6553600 | bytes 5242880 | tf_op jit(solution)/shard_map/concatenate | solution.py:103
  83.0 1.1 fusion.2
  84.0 1.4 fusion.1.lv_ref
  85.5 4.6 %shard_map.64 = (bf16[1568,128]{1,0:T(8,128)(2,1)}, bf16[512,128]{1,0:T(8,128)(2,1)}) custom-call(s32[2]{0:T(128)} %pad_add_fusion.offs_ref, f32[8]{0:T(128)} %fusion.1.lv_ref, bf16[2048,128]{1,0:T(8,128)(2,1)} %bitcast.35, bf16[2048,128]{1,0:T(8,128)(2,1)} %bitcast.34, bf16[8,14,128,128]{3,2,1,0:T(8,128)(2,1)} %all-gather.2.cloned.1.call-done.w_hbm), custom_call_target="tpu_custom_call" | custom-call | flops 667942912 | bytes 2007040 | tf_op jit(solution)/shard_map/pallas_call | solution.py:74
  90.1 4.2 %shard_map.65 = (bf16[1152,128]{1,0:T(8,128)(2,1)}, bf16[512,128]{1,0:T(8,128)(2,1)}) custom-call(s32[2]{0:T(128)} %pad_add_fusion.offs_ref, f32[8]{0:T(128)} %fusion.1.lv_ref, bf16[1568,128]{1,0:T(8,128)(2,1)} %get-tuple-element.23.prior_ref, bf16[1568,128]{1,0:T(8,128)(2,1)} %bitcast.37, bf16[8,14,128,128]{3,2,1,0:T(8,128)(2,1)} %all-gather.2.cloned.1.call-done.w_hbm), custom_call_target="tpu_custom_call" | custom-call | flops 490733568 | bytes 1654784 | tf_op jit(solution)/shard_map/pallas_call | solution.py:74
  94.3 3.8 %shard_map.66 = (bf16[800,128]{1,0:T(8,128)(2,1)}, bf16[512,128]{1,0:T(8,128)(2,1)}) custom-call(s32[2]{0:T(128)} %pad_add_fusion.offs_ref, f32[8]{0:T(128)} %fusion.1.lv_ref, bf16[1152,128]{1,0:T(8,128)(2,1)} %get-tuple-element.25.prior_ref, bf16[1152,128]{1,0:T(8,128)(2,1)} %bitcast.39, bf16[8,14,128,128]{3,2,1,0:T(8,128)(2,1)} %all-gather.2.cloned.1.call-done.w_hbm), custom_call_target="tpu_custom_call" | custom-call | flops 340787200 | bytes 1351680 | tf_op jit(solution)/shard_map/pallas_call | solution.py:74
  98.2 3.7 %shard_map.67 = (bf16[512,128]{1,0:T(8,128)(2,1)}, bf16[512,128]{1,0:T(8,128)(2,1)}) custom-call(s32[2]{0:T(128)} %pad_add_fusion.offs_ref, f32[8]{0:T(128)} %fusion.1.lv_ref, bf16[800,128]{1,0:T(8,128)(2,1)} %get-tuple-element.27.prior_ref, bf16[800,128]{1,0:T(8,128)(2,1)} %bitcast.42, bf16[8,14,128,128]{3,2,1,0:T(8,128)(2,1)} %all-gather.2.cloned.1.call-done.w_hbm), custom_call_target="tpu_custom_call" | custom-call | flops 218103808 | bytes 1097728 | tf_op jit(solution)/shard_map/pallas_call | solution.py:74
  101.8 0.9 fusion.7
  102.7 3.5 %collective-permute-start.8 = (bf16[1,4,8,8,128]{4,3,2,1,0:T(8,128)(2,1)S(1)}, bf16[1,4,8,8,128]{4,3,2,1,0:T(8,128)(2,1)S(1)}, u32[]{:S(2)}, u32[]{:S(2)}) collective-permute-start(bf16[1,4,8,8,128]{4,3,2,1,0:T(8,128)(2,1)S(1)} %get-tuple-element.54), channel_id=1, source_target_pairs={{0,16},{16,32},{32,48},{1,17},{17,33},{33,49},{2,18},{18,34},{34,5... | collective-permute-start | bytes 196616 | tf_op jit(solution)/shard_map/ppermute | solution.py:101
  106.2 1.3 collective-permute-start.9
  108.9 1.0 constant_dynamic-update-slice_fusion.1
  109.8 2.5 %collective-permute-done.9 = bf16[1,4,8,8,128]{4,3,2,1,0:T(8,128)(2,1)S(1)} collective-permute-done((bf16[1,4,8,8,128]{4,3,2,1,0:T(8,128)(2,1)S(1)}, bf16[1,4,8,8,128]{4,3,2,1,0:T(8,128)(2,1)S(1)}, u32[]{:S(2)}, u32[]{:S(2)}) %collective-permute-start.9) | collective-permute-done | bytes 65568 | tf_op jit(solution)/shard_map/ppermute | solution.py:102
  112.4 2.8 %collective-permute-start.10 = (bf16[1,16,4,8,128]{4,3,2,1,0:T(8,128)(2,1)S(1)}, bf16[1,16,4,8,128]{4,3,2,1,0:T(8,128)(2,1)S(1)}, u32[]{:S(2)}, u32[]{:S(2)}) collective-permute-start(bf16[1,16,4,8,128]{4,3,2,1,0:T(8,128)(2,1)S(1)} %get-tuple-element.51), channel_id=1, source_target_pairs={{0,1},{1,2},{2,3},{3,4},{4,5},{5,6},{6,7},{7,8},{8,9},{9,10},{10,1... | collective-permute-start | bytes 393224 | tf_op jit(solution)/shard_map/ppermute | solution.py:101
  115.2 3.2 %collective-permute-start.11 = (bf16[1,16,4,8,128]{4,3,2,1,0:T(8,128)(2,1)S(1)}, bf16[1,16,4,8,128]{4,3,2,1,0:T(8,128)(2,1)S(1)}, u32[]{:S(2)}, u32[]{:S(2)}) collective-permute-start(bf16[1,16,4,8,128]{4,3,2,1,0:T(8,128)(2,1)S(1)} %get-tuple-element.52), channel_id=1, source_target_pairs={{1,0},{2,1},{3,2},{4,3},{5,4},{6,5},{7,6},{8,7},{9,8},{10,9},{11,1... | collective-permute-start | bytes 393224 | tf_op jit(solution)/shard_map/ppermute | solution.py:102
  119.1 0.8 slice.105
  120.0 0.8 slice.106
  123.3 0.9 pad_maximum_fusion.4
  124.1 4.7 %shard_map.68 = (bf16[1568,128]{1,0:T(8,128)(2,1)}, bf16[512,128]{1,0:T(8,128)(2,1)}) custom-call(s32[2]{0:T(128)} %pad_add_fusion.offs_ref, f32[8]{0:T(128)} %fusion.1.lv_ref, bf16[2048,128]{1,0:T(8,128)(2,1)} %bitcast.33, bf16[2048,128]{1,0:T(8,128)(2,1)} %bitcast.32, bf16[8,14,128,128]{3,2,1,0:T(8,128)(2,1)} %all-gather.2.cloned.1.call-done.w_hbm), custom_call_target="tpu_custom_call" | custom-call | flops 667942912 | bytes 2007040 | tf_op jit(solution)/shard_map/pallas_call | solution.py:74
  128.8 1.6 constant_dynamic-update-slice_fusion.6
  130.4 4.2 %shard_map.69 = (bf16[1152,128]{1,0:T(8,128)(2,1)}, bf16[512,128]{1,0:T(8,128)(2,1)}) custom-call(s32[2]{0:T(128)} %pad_add_fusion.offs_ref, f32[8]{0:T(128)} %fusion.1.lv_ref, bf16[1568,128]{1,0:T(8,128)(2,1)} %get-tuple-element.33.prior_ref, bf16[1568,128]{1,0:T(8,128)(2,1)} %bitcast.36, bf16[8,14,128,128]{3,2,1,0:T(8,128)(2,1)} %all-gather.2.cloned.1.call-done.w_hbm), custom_call_target="tpu_custom_call" | custom-call | flops 490733568 | bytes 1654784 | tf_op jit(solution)/shard_map/pallas_call | solution.py:74
  134.6 1.6 constant_dynamic-update-slice_fusion.5
  136.1 3.8 %shard_map.70 = (bf16[800,128]{1,0:T(8,128)(2,1)}, bf16[512,128]{1,0:T(8,128)(2,1)}) custom-call(s32[2]{0:T(128)} %pad_add_fusion.offs_ref, f32[8]{0:T(128)} %fusion.1.lv_ref, bf16[1152,128]{1,0:T(8,128)(2,1)} %get-tuple-element.35.prior_ref, bf16[1152,128]{1,0:T(8,128)(2,1)} %bitcast.38, bf16[8,14,128,128]{3,2,1,0:T(8,128)(2,1)} %all-gather.2.cloned.1.call-done.w_hbm), custom_call_target="tpu_custom_call" | custom-call | flops 340787200 | bytes 1351680 | tf_op jit(solution)/shard_map/pallas_call | solution.py:74
  140.0 1.6 constant_dynamic-update-slice_fusion.4
  141.5 3.5 %shard_map.71 = (bf16[512,128]{1,0:T(8,128)(2,1)}, bf16[512,128]{1,0:T(8,128)(2,1)}) custom-call(s32[2]{0:T(128)} %pad_add_fusion.offs_ref, f32[8]{0:T(128)} %fusion.1.lv_ref, bf16[800,128]{1,0:T(8,128)(2,1)} %get-tuple-element.37.prior_ref, bf16[800,128]{1,0:T(8,128)(2,1)} %bitcast.41, bf16[8,14,128,128]{3,2,1,0:T(8,128)(2,1)} %all-gather.2.cloned.1.call-done.w_hbm), custom_call_target="tpu_custom_call" | custom-call | flops 218103808 | bytes 1097728 | tf_op jit(solution)/shard_map/pallas_call | solution.py:74
  145.0 1.6 constant_dynamic-update-slice_fusion.3
  146.6 19.6 %all_to_all.18 = bf16[8,1,8,8,8,128]{5,4,3,2,1,0:T(8,128)(2,1)S(1)} all-to-all(bf16[8,1,8,8,8,128]{5,4,3,2,1,0:T(8,128)(2,1)} %constant_dynamic-update-slice_fusion.3), channel_id=1, replica_groups=mesh['section'=8,'frames'=4,'space'=16] {'section'}, dimensions={0} | all-to-all | bytes 2097152 | tf_op jit(solution)/shard_map/all_to_all | solution.py:180
  166.2 1.0 copy.34
  (50 shorter events, 5.8 us)
Async XLA Ops:
  6.5 28.1 %copy-start = (bf16[8,8,8,8,128]{4,3,2,1,0:T(8,128)(2,1)S(1)}, bf16[8,8,8,8,128]{4,3,2,1,0:T(8,128)(2,1)}, u32[]{:S(2)}) copy-start(bf16[8,8,8,8,128]{4,3,2,1,0:T(8,128)(2,1)} %param.6) | copy-start | bytes 3145732
  6.5 77.5 %all-gather.2.cloned.1.call-start = ((), (), s32[]{:S(2)}) async-start(), calls=%async_computation.2 | async-start | bytes 4128768 | tf_op jit(solution)/shard_map/all_gather | solution.py:148
  29.9 10.8 %collective-permute-start.4 = (bf16[4,1,4,8,8,128]{5,4,3,2,0,1:T(8,128)(2,1)S(1)}, bf16[4,1,4,8,8,128]{5,4,3,2,0,1:T(8,128)(2,1)S(1)}, u32[]{:S(2)}, u32[]{:S(2)}) collective-permute-start(bf16[4,1,4,8,8,128]{5,4,3,2,0,1:T(8,128)(2,1)S(1)} %get-tuple-element.49), channel_id=1, source_target_pairs={{0,16},{16,32},{32,48},{1,17},{17,33},{33,49},{2,18},{18,34},{34,5... | collective-permute-start | bytes 786440 | tf_op jit(solution)/shard_map/ppermute | solution.py:101
  33.4 9.4 %collective-permute-start.5 = (bf16[4,1,4,8,8,128]{5,4,3,2,0,1:T(8,128)(2,1)S(1)}, bf16[4,1,4,8,8,128]{5,4,3,2,0,1:T(8,128)(2,1)S(1)}, u32[]{:S(2)}, u32[]{:S(2)}) collective-permute-start(bf16[4,1,4,8,8,128]{5,4,3,2,0,1:T(8,128)(2,1)S(1)} %get-tuple-element.50), channel_id=1, source_target_pairs={{16,0},{32,16},{48,32},{17,1},{33,17},{49,33},{18,2},{34,18},{50,3... | collective-permute-start | bytes 786440 | tf_op jit(solution)/shard_map/ppermute | solution.py:102
  34.8 16.2 %collective-permute-start = (bf16[5,1,4,8,8,128]{5,4,3,2,0,1:T(8,128)(2,1)S(1)}, bf16[5,1,4,8,8,128]{5,4,3,2,0,1:T(8,128)(2,1)S(1)}, u32[]{:S(2)}, u32[]{:S(2)}) collective-permute-start(bf16[5,1,4,8,8,128]{5,4,3,2,0,1:T(8,128)(2,1)S(1)} %get-tuple-element.47), channel_id=1, source_target_pairs={{0,16},{16,32},{32,48},{1,17},{17,33},{33,49},{2,18},{18,34},{34,5... | collective-permute-start | bytes 983048 | tf_op jit(solution)/shard_map/ppermute | solution.py:101
  39.3 11.6 %collective-permute-start.1 = (bf16[5,1,4,8,8,128]{5,4,3,2,0,1:T(8,128)(2,1)S(1)}, bf16[5,1,4,8,8,128]{5,4,3,2,0,1:T(8,128)(2,1)S(1)}, u32[]{:S(2)}, u32[]{:S(2)}) collective-permute-start(bf16[5,1,4,8,8,128]{5,4,3,2,0,1:T(8,128)(2,1)S(1)} %get-tuple-element.48), channel_id=1, source_target_pairs={{16,0},{32,16},{48,32},{17,1},{33,17},{49,33},{18,2},{34,18},{50,3... | collective-permute-start | bytes 983048 | tf_op jit(solution)/shard_map/ppermute | solution.py:102
  40.7 3.3 %copy-start.6 = (bf16[4,1,4,8,8,128]{5,4,3,2,0,1:T(8,128)(2,1)}, bf16[4,1,4,8,8,128]{5,4,3,2,0,1:T(8,128)(2,1)S(1)}, u32[]{:S(2)}) copy-start(bf16[4,1,4,8,8,128]{5,4,3,2,0,1:T(8,128)(2,1)S(1)} %collective-permute-done.4) | copy-start | bytes 786436
  42.8 1.2 copy-start.7
  44.0 17.7 %collective-permute-start.6 = (bf16[4,1,16,4,8,128]{5,4,3,2,0,1:T(8,128)(2,1)}, bf16[4,1,16,4,8,128]{5,4,3,2,0,1:T(8,128)(2,1)}, u32[]{:S(2)}, u32[]{:S(2)}) collective-permute-start(bf16[4,1,16,4,8,128]{5,4,3,2,0,1:T(8,128)(2,1)} %get-tuple-element.43), channel_id=1, source_target_pairs={{0,1},{1,2},{2,3},{3,4},{4,5},{5,6},{6,7},{7,8},{8,9},{9,10},{10,1... | collective-permute-start | bytes 1572872 | tf_op jit(solution)/shard_map/ppermute | solution.py:101
  49.0 18.3 %collective-permute-start.7 = (bf16[4,1,16,4,8,128]{5,4,3,2,0,1:T(8,128)(2,1)}, bf16[4,1,16,4,8,128]{5,4,3,2,0,1:T(8,128)(2,1)}, u32[]{:S(2)}, u32[]{:S(2)}) collective-permute-start(bf16[4,1,16,4,8,128]{5,4,3,2,0,1:T(8,128)(2,1)} %get-tuple-element.44), channel_id=1, source_target_pairs={{1,0},{2,1},{3,2},{4,3},{5,4},{6,5},{7,6},{8,7},{9,8},{10,9},{11,1... | collective-permute-start | bytes 1572872 | tf_op jit(solution)/shard_map/ppermute | solution.py:102
  51.0 1.6 copy-start.1
  51.0 1.5 copy-start.3
  52.5 20.4 %collective-permute-start.2 = (bf16[5,1,16,4,8,128]{5,4,3,2,0,1:T(8,128)(2,1)}, bf16[5,1,16,4,8,128]{5,4,3,2,0,1:T(8,128)(2,1)S(1)}, u32[]{:S(2)}, u32[]{:S(2)}) collective-permute-start(bf16[5,1,16,4,8,128]{5,4,3,2,0,1:T(8,128)(2,1)} %get-tuple-element.41), channel_id=1, source_target_pairs={{0,1},{1,2},{2,3},{3,4},{4,5},{5,6},{6,7},{7,8},{8,9},{9,10},{10,1... | collective-permute-start | bytes 1966088 | tf_op jit(solution)/shard_map/ppermute | solution.py:101
  57.6 20.5 %collective-permute-start.3 = (bf16[5,1,16,4,8,128]{5,4,3,2,0,1:T(8,128)(2,1)}, bf16[5,1,16,4,8,128]{5,4,3,2,0,1:T(8,128)(2,1)S(1)}, u32[]{:S(2)}, u32[]{:S(2)}) collective-permute-start(bf16[5,1,16,4,8,128]{5,4,3,2,0,1:T(8,128)(2,1)} %get-tuple-element.42), channel_id=1, source_target_pairs={{1,0},{2,1},{3,2},{4,3},{5,4},{6,5},{7,6},{8,7},{9,8},{10,9},{11,1... | collective-permute-start | bytes 1966088 | tf_op jit(solution)/shard_map/ppermute | solution.py:102
  60.2 18.0 %copy-start.2 = (bf16[5,1,4,8,8,128]{5,4,3,2,0,1:T(8,128)(2,1)S(1)}, bf16[5,1,4,8,8,128]{5,4,3,2,0,1:T(8,128)(2,1)}, u32[]{:S(2)}) copy-start(bf16[5,1,4,8,8,128]{5,4,3,2,0,1:T(8,128)(2,1)} %copy-done.1) | copy-start | bytes 983044
  60.2 18.0 %copy-start.4 = (bf16[5,1,4,8,8,128]{5,4,3,2,0,1:T(8,128)(2,1)S(1)}, bf16[5,1,4,8,8,128]{5,4,3,2,0,1:T(8,128)(2,1)}, u32[]{:S(2)}) copy-start(bf16[5,1,4,8,8,128]{5,4,3,2,0,1:T(8,128)(2,1)} %copy-done.3) | copy-start | bytes 983044
  98.1 9.4 %copy-start.10 = (bf16[512,128]{1,0:T(8,128)(2,1)S(1)}, bf16[512,128]{1,0:T(8,128)(2,1)}, u32[]{:S(2)}) copy-start(bf16[512,128]{1,0:T(8,128)(2,1)} %get-tuple-element.22) | copy-start | bytes 393220
  98.1 10.1 %copy-start.11 = (bf16[512,128]{1,0:T(8,128)(2,1)S(1)}, bf16[512,128]{1,0:T(8,128)(2,1)}, u32[]{:S(2)}) copy-start(bf16[512,128]{1,0:T(8,128)(2,1)} %get-tuple-element.24) | copy-start | bytes 393220
  98.1 20.3 %copy-start.9 = (bf16[512,128]{1,0:T(8,128)(2,1)S(1)}, bf16[512,128]{1,0:T(8,128)(2,1)}, u32[]{:S(2)}) copy-start(bf16[512,128]{1,0:T(8,128)(2,1)} %get-tuple-element.26) | copy-start | bytes 393220
  98.1 21.0 %copy-start.5 = (bf16[4,1,16,16,8,128]{5,4,3,2,0,1:T(8,128)(2,1)S(1)}, bf16[4,1,16,16,8,128]{5,4,3,2,0,1:T(8,128)(2,1)}, u32[]{:S(2)}) copy-start(bf16[4,1,16,16,8,128]{5,4,3,2,0,1:T(8,128)(2,1)} %pad_maximum_fusion.1) | copy-start | bytes 6291460
  102.7 6.1 %collective-permute-start.8 = (bf16[1,4,8,8,128]{4,3,2,1,0:T(8,128)(2,1)S(1)}, bf16[1,4,8,8,128]{4,3,2,1,0:T(8,128)(2,1)S(1)}, u32[]{:S(2)}, u32[]{:S(2)}) collective-permute-start(bf16[1,4,8,8,128]{4,3,2,1,0:T(8,128)(2,1)S(1)} %get-tuple-element.54), channel_id=1, source_target_pairs={{0,16},{16,32},{32,48},{1,17},{17,33},{33,49},{2,18},{18,34},{34,5... | collective-permute-start | bytes 196616 | tf_op jit(solution)/shard_map/ppermute | solution.py:101
  106.2 6.2 %collective-permute-start.9 = (bf16[1,4,8,8,128]{4,3,2,1,0:T(8,128)(2,1)S(1)}, bf16[1,4,8,8,128]{4,3,2,1,0:T(8,128)(2,1)S(1)}, u32[]{:S(2)}, u32[]{:S(2)}) collective-permute-start(bf16[1,4,8,8,128]{4,3,2,1,0:T(8,128)(2,1)S(1)} %get-tuple-element.53), channel_id=1, source_target_pairs={{16,0},{32,16},{48,32},{17,1},{33,17},{49,33},{18,2},{34,18},{50,3... | collective-permute-start | bytes 196616 | tf_op jit(solution)/shard_map/ppermute | solution.py:102
  108.9 13.3 %copy-start.8 = (bf16[512,128]{1,0:T(8,128)(2,1)S(1)}, bf16[512,128]{1,0:T(8,128)(2,1)}, u32[]{:S(2)}) copy-start(bf16[512,128]{1,0:T(8,128)(2,1)} %get-tuple-element.28) | copy-start | bytes 393220
  112.4 10.4 %collective-permute-start.10 = (bf16[1,16,4,8,128]{4,3,2,1,0:T(8,128)(2,1)S(1)}, bf16[1,16,4,8,128]{4,3,2,1,0:T(8,128)(2,1)S(1)}, u32[]{:S(2)}, u32[]{:S(2)}) collective-permute-start(bf16[1,16,4,8,128]{4,3,2,1,0:T(8,128)(2,1)S(1)} %get-tuple-element.51), channel_id=1, source_target_pairs={{0,1},{1,2},{2,3},{3,4},{4,5},{5,6},{6,7},{7,8},{8,9},{9,10},{10,1... | collective-permute-start | bytes 393224 | tf_op jit(solution)/shard_map/ppermute | solution.py:101
  115.2 8.1 %collective-permute-start.11 = (bf16[1,16,4,8,128]{4,3,2,1,0:T(8,128)(2,1)S(1)}, bf16[1,16,4,8,128]{4,3,2,1,0:T(8,128)(2,1)S(1)}, u32[]{:S(2)}, u32[]{:S(2)}) collective-permute-start(bf16[1,16,4,8,128]{4,3,2,1,0:T(8,128)(2,1)S(1)} %get-tuple-element.52), channel_id=1, source_target_pairs={{1,0},{2,1},{3,2},{4,3},{5,4},{6,5},{7,6},{8,7},{9,8},{10,9},{11,1... | collective-permute-start | bytes 393224 | tf_op jit(solution)/shard_map/ppermute | solution.py:102
Sparse Core Ops, SparseCore 0:
  9.5 40.9 all-gather.1

commit v11 on v3

--- a/solution.py
+++ b/solution.py
@@ -11,7 +11,7 @@
 
 def section_kernel(
     m, n, cols, inner, num_frames, num_rows, total_frames, total_rows, k,
-    offs_ref, lv_ref, prior_ref, noise_ref, w_hbm, out_ref, crop_ref, w_ref, sem, xl, xc, xr, nz,
+    offs_ref, prior_ref, noise_ref, w_hbm, out_ref, crop_ref, w_ref, sem, xl, xc, xr, nz,
 ):
     weight_copy = pltpu.make_async_copy(w_hbm.at[k], w_ref, sem)
     weight_copy.start()
@@ -19,8 +19,11 @@
     rows_in = m * n * cols
     rows_out = (m - 2) * (n - 2) * cols
     width = (m - num_frames) // 2
-    level = lv_ref[k]
-    noisy = prior_ref[...].astype(jnp.float32) + level * noise_ref[...].astype(jnp.float32)
+    prior = prior_ref[...].astype(jnp.float32)
+    noise = noise_ref[...].astype(jnp.float32)
+    weight_copy.wait()
+    level = w_ref[13][0:1, :].astype(jnp.float32)
+    noisy = prior + level * noise
     mean_sq = jnp.mean(noisy * noisy, axis=-1, keepdims=True)
     normalized = (noisy * lax.rsqrt(mean_sq + 1e-05)).astype(jnp.bfloat16).astype(jnp.float32)
     shape4 = (m, n, cols, channels)
@@ -37,7 +40,6 @@
     xc[...] = normalized.reshape(m, n * cols, channels)
     xr[...] = right.reshape(m, n * cols, channels)
     nz[...] = noisy.reshape(m, n * cols, channels)
-    weight_copy.wait()
     views = (xl, xc, xr)
     acc = jnp.zeros((rows_out, channels), jnp.float32)
     for tap in range(9):
@@ -59,7 +61,7 @@
     crop_ref[...] = crop.reshape(num_frames * num_rows * cols, channels).astype(crop_ref.dtype)
 
 
-def section_call(offs, levels, prior, noise, packed, k, m, n, cols, num_frames, num_rows, totals):
+def section_call(offs, prior, noise, packed, k, m, n, cols, num_frames, num_rows, totals):
     channels = packed.shape[-1]
     rows_in = m * n * cols
     rows_out = (m - 2) * (n - 2) * cols
@@ -79,7 +81,7 @@
             jax.ShapeDtypeStruct((rows_out, channels), jnp.bfloat16),
             jax.ShapeDtypeStruct((rows_crop, channels), jnp.bfloat16),
         ),
-        in_specs=[smem, smem, vmem, vmem, pl.BlockSpec(memory_space=pl.ANY)],
+        in_specs=[smem, vmem, vmem, pl.BlockSpec(memory_space=pl.ANY)],
         out_specs=(vmem, vmem),
         scratch_shapes=[
             pltpu.VMEM(packed.shape[1:], packed.dtype),
@@ -89,7 +91,7 @@
         cost_estimate=pl.CostEstimate(
             flops=flops, bytes_accessed=nbytes, transcendentals=rows_out * channels
         ),
-    )(offs, levels, prior, noise, packed)
+    )(offs, prior, noise, packed)
 
 
 def extend(block, width, frame_dim, row_dim):
@@ -104,14 +106,13 @@
     return block
 
 
-def denoise(offs, levels, previous, noise_part, packed, k, num_frames, num_rows, totals):
+def denoise(offs, previous, noise_part, packed, k, num_frames, num_rows, totals):
     num_videos, m, n, num_cols, channels = previous.shape
     outs = []
     crops = []
     for v in range(num_videos):
         out, crop = section_call(
             offs,
-            levels,
             previous[v].reshape(-1, channels),
             noise_part[v].reshape(-1, channels),
             packed,
@@ -147,7 +148,6 @@
     )
     packed = lax.all_gather(packed, "section", tiled=True)
     incoming = lax.dynamic_slice_in_dim(base_frames, place * per_device, per_device, 0)
-    levels = packed[:, 13, 0, 0].astype(jnp.float32)
     offs = jnp.stack(
         [lax.axis_index("frames") * num_frames, lax.axis_index("space") * num_rows]
     ).astype(jnp.int32)
@@ -167,7 +167,7 @@
             j, :, cut : cut + num_frames + 2 * width, cut : cut + num_rows + 2 * width
         ]
         prior_ext, crop = denoise(
-            offs, levels, prior_ext, noise_here, packed, k, num_frames, num_rows, totals
+            offs, prior_ext, noise_here, packed, k, num_frames, num_rows, totals
         )
         results.append(crop)
         if j == 0 and k + halo < sections:

time: 171 us -> 172 us (level)
  Pallas kernels: 32.4 us -> 34.6 us
    pallas_call x8, Pallas kernels: 32.4 us -> 34.6 us  [section_call(): pl.pallas_call(functools.partial(section_kernel, m, n, cols, inner, num_f...]
where the time goes in v11:
time: 172 us; the launch traced here: 171 us
  blocking collectives  38.9 us (23%)
  starting transfers between devices  35.4 us (21%)
  Pallas kernels  34.6 us (20%)
  waiting for transfers between devices  27.1 us (16%)
  between operations  14.5 us (8%)
  other arithmetic  12.1 us (7%)
  local copies, waits for them, and re-layouts  8.16 us (5%)
    pallas_call x8, Pallas kernels, section_call(): pl.pallas_call(functools.partial(section_kernel, m, n, cols, inner, num_f...  34.6 us
    ppermute x6, starting transfers between devices, extend(): lax.ppermute(lax.slice_in_dim(block, size - width, size, axis=dim), axis,...  24.5 us
    ppermute x6, waiting for transfers between devices, extend(): lax.ppermute(lax.slice_in_dim(block, 0, width, axis=dim), axis, backward)  21.4 us
    all_to_all x1, blocking collectives, on_device(): noise_t = lax.all_to_all(section_noise[0], 'section', 0, 0, tiled=True)  20.4 us
    all_to_all x1, blocking collectives, on_device(): return lax.all_to_all(stacked, 'section', 0, 1, tiled=True)  18.5 us
    ppermute x6, starting transfers between devices, extend(): lax.ppermute(lax.slice_in_dim(block, 0, width, axis=dim), axis, backward)  10.9 us
    ppermute x6, waiting for transfers between devices, extend(): lax.ppermute(lax.slice_in_dim(block, size - width, size, axis=dim), axis,...  5.68 us
    concatenate x6, other arithmetic, extend(): block = jnp.concatenate([low, block, high], axis=dim)  4.85 us
  transfers between devices with their start and end apart: 13, of which 9 were waited for; matrix products, arithmetic and copies ran while one was open for 6% of the time, Pallas kernels for 0%

profile of v11, /device:TPU:96, one launch (start us, length us, event | category | flops | bytes accessed | tf_op | source)
XLA Modules:
  0.0 170.8 jit_solution(12274533541518885100)
XLA Ops:
  7.4 1.9 %maximum_maximum_fusion = bf16[1,14,128,128]{3,2,1,0:T(8,128)(2,1)} fusion(bf16[1,1,128,128]{3,2,1,0:T(8,128)(2,1)} %bitcast.54, bf16[1,3,128,128]{3,2,1,0:T(8,128)(2,1)} %param.10, bf16[1,9,128,128]{3,2,1,0:T(8,128)(2,1)} %param.9, bf16[14]{0:T(256)(128)(2,1)S(1)} %pad.19.clone), kind=kLoop, calls=%fused_computation.9 | loop fusion | flops 688128 | bytes 884764 | tf_op jit(solution)/shard_map/concatenate | solution.py:146
  9.3 20.4 %all_to_all.17 = bf16[8,8,8,8,128]{4,3,2,1,0:T(8,128)(2,1)S(1)} all-to-all(bf16[8,8,8,8,128]{4,3,2,1,0:T(8,128)(2,1)} %bitcast.43), channel_id=1, replica_groups=mesh['section'=8,'frames'=4,'space'=16] {'section'}, dimensions={0} | all-to-all | bytes 2097152 | tf_op jit(solution)/shard_map/all_to_all | solution.py:140
  29.8 3.5 %collective-permute-start.8 = (bf16[4,1,4,8,8,128]{5,4,3,2,0,1:T(8,128)(2,1)S(1)}, bf16[4,1,4,8,8,128]{5,4,3,2,0,1:T(8,128)(2,1)S(1)}, u32[]{:S(2)}, u32[]{:S(2)}) collective-permute-start(bf16[4,1,4,8,8,128]{5,4,3,2,0,1:T(8,128)(2,1)S(1)} %get-tuple-element.45), channel_id=1, source_target_pairs={{0,16},{16,32},{32,48},{1,17},{17,33},{33,49},{2,18},{18,34},{34,5... | collective-permute-start | bytes 786440 | tf_op jit(solution)/shard_map/ppermute | solution.py:103
  33.3 1.3 collective-permute-start.9
  34.7 4.6 %collective-permute-start = (bf16[5,1,4,8,8,128]{5,4,3,2,0,1:T(8,128)(2,1)S(1)}, bf16[5,1,4,8,8,128]{5,4,3,2,0,1:T(8,128)(2,1)S(1)}, u32[]{:S(2)}, u32[]{:S(2)}) collective-permute-start(bf16[5,1,4,8,8,128]{5,4,3,2,0,1:T(8,128)(2,1)S(1)} %get-tuple-element.43), channel_id=1, source_target_pairs={{0,16},{16,32},{32,48},{1,17},{17,33},{33,49},{2,18},{18,34},{34,5... | collective-permute-start | bytes 983048 | tf_op jit(solution)/shard_map/ppermute | solution.py:103
  39.3 1.3 collective-permute-start.1
  40.6 2.1 %collective-permute-done.9 = bf16[4,1,4,8,8,128]{5,4,3,2,0,1:T(8,128)(2,1)S(1)} collective-permute-done((bf16[4,1,4,8,8,128]{5,4,3,2,0,1:T(8,128)(2,1)S(1)}, bf16[4,1,4,8,8,128]{5,4,3,2,0,1:T(8,128)(2,1)S(1)}, u32[]{:S(2)}, u32[]{:S(2)}) %collective-permute-start.9) | collective-permute-done | bytes 262176 | tf_op jit(solution)/shard_map/ppermute | solution.py:104
  42.9 5.0 %collective-permute-start.10 = (bf16[4,1,16,4,8,128]{5,4,3,2,0,1:T(8,128)(2,1)S(1)}, bf16[4,1,16,4,8,128]{5,4,3,2,0,1:T(8,128)(2,1)S(1)}, u32[]{:S(2)}, u32[]{:S(2)}) collective-permute-start(bf16[4,1,16,4,8,128]{5,4,3,2,0,1:T(8,128)(2,1)S(1)} %get-tuple-element.39), channel_id=1, source_target_pairs={{0,1},{1,2},{2,3},{3,4},{4,5},{5,6},{6,7},{7,8},{8,9},{9,10},{10,1... | collective-permute-start | bytes 1572872 | tf_op jit(solution)/shard_map/ppermute | solution.py:103
  48.0 1.9 %collective-permute-start.11 = (bf16[4,1,16,4,8,128]{5,4,3,2,0,1:T(8,128)(2,1)S(1)}, bf16[4,1,16,4,8,128]{5,4,3,2,0,1:T(8,128)(2,1)S(1)}, u32[]{:S(2)}, u32[]{:S(2)}) collective-permute-start(bf16[4,1,16,4,8,128]{5,4,3,2,0,1:T(8,128)(2,1)S(1)} %get-tuple-element.40), channel_id=1, source_target_pairs={{1,0},{2,1},{3,2},{4,3},{5,4},{6,5},{7,6},{8,7},{9,8},{10,9},{11,1... | collective-permute-start | bytes 1572872 | tf_op jit(solution)/shard_map/ppermute | solution.py:104
  50.4 5.1 %collective-permute-start.2 = (bf16[5,1,16,4,8,128]{5,4,3,2,0,1:T(8,128)(2,1)S(1)}, bf16[5,1,16,4,8,128]{5,4,3,2,0,1:T(8,128)(2,1)S(1)}, u32[]{:S(2)}, u32[]{:S(2)}) collective-permute-start(bf16[5,1,16,4,8,128]{5,4,3,2,0,1:T(8,128)(2,1)S(1)} %get-tuple-element.37), channel_id=1, source_target_pairs={{0,1},{1,2},{2,3},{3,4},{4,5},{5,6},{6,7},{7,8},{8,9},{9,10},{10,1... | collective-permute-start | bytes 1966088 | tf_op jit(solution)/shard_map/ppermute | solution.py:103
  55.5 1.9 %collective-permute-start.3 = (bf16[5,1,16,4,8,128]{5,4,3,2,0,1:T(8,128)(2,1)S(1)}, bf16[5,1,16,4,8,128]{5,4,3,2,0,1:T(8,128)(2,1)S(1)}, u32[]{:S(2)}, u32[]{:S(2)}) collective-permute-start(bf16[5,1,16,4,8,128]{5,4,3,2,0,1:T(8,128)(2,1)S(1)} %get-tuple-element.38), channel_id=1, source_target_pairs={{1,0},{2,1},{3,2},{4,3},{5,4},{6,5},{7,6},{8,7},{9,8},{10,9},{11,1... | collective-permute-start | bytes 1966088 | tf_op jit(solution)/shard_map/ppermute | solution.py:104
  58.1 2.3 %collective-permute-done.10 = bf16[4,1,16,4,8,128]{5,4,3,2,0,1:T(8,128)(2,1)S(1)} collective-permute-done((bf16[4,1,16,4,8,128]{5,4,3,2,0,1:T(8,128)(2,1)S(1)}, bf16[4,1,16,4,8,128]{5,4,3,2,0,1:T(8,128)(2,1)S(1)}, u32[]{:S(2)}, u32[]{:S(2)}) %collective-permute-start.10) | collective-permute-done | bytes 524320 | tf_op jit(solution)/shard_map/ppermute | solution.py:103
  60.4 5.6 %collective-permute-done.11 = bf16[4,1,16,4,8,128]{5,4,3,2,0,1:T(8,128)(2,1)S(1)} collective-permute-done((bf16[4,1,16,4,8,128]{5,4,3,2,0,1:T(8,128)(2,1)S(1)}, bf16[4,1,16,4,8,128]{5,4,3,2,0,1:T(8,128)(2,1)S(1)}, u32[]{:S(2)}, u32[]{:S(2)}) %collective-permute-start.11) | collective-permute-done | bytes 524320 | tf_op jit(solution)/shard_map/ppermute | solution.py:104
  66.3 0.9 slice.121
  67.1 0.7 pad_maximum_fusion.11
  67.9 0.8 pad_maximum_fusion.8
  68.6 0.8 pad_maximum_fusion.5
  69.5 2.1 %collective-permute-done.2 = bf16[5,1,16,4,8,128]{5,4,3,2,0,1:T(8,128)(2,1)S(1)} collective-permute-done((bf16[5,1,16,4,8,128]{5,4,3,2,0,1:T(8,128)(2,1)S(1)}, bf16[5,1,16,4,8,128]{5,4,3,2,0,1:T(8,128)(2,1)S(1)}, u32[]{:S(2)}, u32[]{:S(2)}) %collective-permute-start.2) | collective-permute-done | bytes 655392 | tf_op jit(solution)/shard_map/ppermute | solution.py:103
  71.6 5.3 %collective-permute-done.3 = bf16[5,1,16,4,8,128]{5,4,3,2,0,1:T(8,128)(2,1)S(1)} collective-permute-done((bf16[5,1,16,4,8,128]{5,4,3,2,0,1:T(8,128)(2,1)S(1)}, bf16[5,1,16,4,8,128]{5,4,3,2,0,1:T(8,128)(2,1)S(1)}, u32[]{:S(2)}, u32[]{:S(2)}) %collective-permute-start.3) | collective-permute-done | bytes 655392 | tf_op jit(solution)/shard_map/ppermute | solution.py:104
  76.9 0.7 pad_maximum_fusion.12
  77.7 0.8 pad_maximum_fusion.9
  78.4 0.8 pad_maximum_fusion.6
  79.2 2.5 %pad_maximum_fusion = bf16[5,1,16,16,8,128]{5,4,3,2,0,1:T(8,128)(2,1)S(1)} fusion(bf16[5,1,16,4,8,128]{5,4,3,2,0,1:T(8,128)(2,1)S(1)} %collective-permute-done.3, bf16[5,1,4,8,8,128]{5,4,3,2,0,1:T(8,128)(2,1)S(1)} %collective-permute-done.1, bf16[4,1,8,8,8,128]{5,4,3,2,0,1:T(8,128)(2,1)S(1)} %get-tuple-element.42, ...), kind=kLoop, calls=%fused_computation | loop fusion | flops 6553600 | bytes 5242880 | tf_op jit(solution)/shard_map/concatenate | solution.py:105
  81.7 1.1 fusion.1
  82.8 5.1 %shard_map.64 = (bf16[1568,128]{1,0:T(8,128)(2,1)}, bf16[512,128]{1,0:T(8,128)(2,1)}) custom-call(s32[2]{0:T(128)} %pad_add_fusion.offs_ref, bf16[2048,128]{1,0:T(8,128)(2,1)} %bitcast.35, bf16[2048,128]{1,0:T(8,128)(2,1)} %bitcast.34, bf16[8,14,128,128]{3,2,1,0:T(8,128)(2,1)} %all-gather.2.cloned.1.call-done.w_hbm), custom_call_target="tpu_custom_call" | custom-call | flops 667942912 | bytes 2007040 | tf_op jit(solution)/shard_map/pallas_call | solution.py:76
  87.9 4.5 %shard_map.65 = (bf16[1152,128]{1,0:T(8,128)(2,1)}, bf16[512,128]{1,0:T(8,128)(2,1)}) custom-call(s32[2]{0:T(128)} %pad_add_fusion.offs_ref, bf16[1568,128]{1,0:T(8,128)(2,1)} %get-tuple-element.21.prior_ref, bf16[1568,128]{1,0:T(8,128)(2,1)} %bitcast.37, bf16[8,14,128,128]{3,2,1,0:T(8,128)(2,1)} %all-gather.2.cloned.1.call-done.w_hbm), custom_call_target="tpu_custom_call" | custom-call | flops 490733568 | bytes 1654784 | tf_op jit(solution)/shard_map/pallas_call | solution.py:76
  92.4 4.0 %shard_map.66 = (bf16[800,128]{1,0:T(8,128)(2,1)}, bf16[512,128]{1,0:T(8,128)(2,1)}) custom-call(s32[2]{0:T(128)} %pad_add_fusion.offs_ref, bf16[1152,128]{1,0:T(8,128)(2,1)} %get-tuple-element.23.prior_ref, bf16[1152,128]{1,0:T(8,128)(2,1)} %bitcast.39, bf16[8,14,128,128]{3,2,1,0:T(8,128)(2,1)} %all-gather.2.cloned.1.call-done.w_hbm), custom_call_target="tpu_custom_call" | custom-call | flops 340787200 | bytes 1351680 | tf_op jit(solution)/shard_map/pallas_call | solution.py:76
  96.4 3.7 %shard_map.67 = (bf16[512,128]{1,0:T(8,128)(2,1)}, bf16[512,128]{1,0:T(8,128)(2,1)}) custom-call(s32[2]{0:T(128)} %pad_add_fusion.offs_ref, bf16[800,128]{1,0:T(8,128)(2,1)} %get-tuple-element.25.prior_ref, bf16[800,128]{1,0:T(8,128)(2,1)} %bitcast.45, bf16[8,14,128,128]{3,2,1,0:T(8,128)(2,1)} %all-gather.2.cloned.1.call-done.w_hbm), custom_call_target="tpu_custom_call" | custom-call | flops 218103808 | bytes 1097728 | tf_op jit(solution)/shard_map/pallas_call | solution.py:76
  100.1 0.9 fusion.6
  101.1 3.5 %collective-permute-start.4 = (bf16[1,4,8,8,128]{4,3,2,1,0:T(8,128)(2,1)S(1)}, bf16[1,4,8,8,128]{4,3,2,1,0:T(8,128)(2,1)S(1)}, u32[]{:S(2)}, u32[]{:S(2)}) collective-permute-start(bf16[1,4,8,8,128]{4,3,2,1,0:T(8,128)(2,1)S(1)} %get-tuple-element.49), channel_id=1, source_target_pairs={{0,16},{16,32},{32,48},{1,17},{17,33},{33,49},{2,18},{18,34},{34,5... | collective-permute-start | bytes 196616 | tf_op jit(solution)/shard_map/ppermute | solution.py:103
  104.5 1.3 collective-permute-start.5
  106.4 4.3 %collective-permute-done.5 = bf16[1,4,8,8,128]{4,3,2,1,0:T(8,128)(2,1)S(1)} collective-permute-done((bf16[1,4,8,8,128]{4,3,2,1,0:T(8,128)(2,1)S(1)}, bf16[1,4,8,8,128]{4,3,2,1,0:T(8,128)(2,1)S(1)}, u32[]{:S(2)}, u32[]{:S(2)}) %collective-permute-start.5) | collective-permute-done | bytes 65568 | tf_op jit(solution)/shard_map/ppermute | solution.py:104
  110.7 0.9 pad_maximum_fusion.10
  111.7 2.8 %collective-permute-start.6 = (bf16[1,16,4,8,128]{4,3,2,1,0:T(8,128)(2,1)S(1)}, bf16[1,16,4,8,128]{4,3,2,1,0:T(8,128)(2,1)S(1)}, u32[]{:S(2)}, u32[]{:S(2)}) collective-permute-start(bf16[1,16,4,8,128]{4,3,2,1,0:T(8,128)(2,1)S(1)} %get-tuple-element.47), channel_id=1, source_target_pairs={{0,1},{1,2},{2,3},{3,4},{4,5},{5,6},{6,7},{7,8},{8,9},{9,10},{10,1... | collective-permute-start | bytes 393224 | tf_op jit(solution)/shard_map/ppermute | solution.py:103
  114.5 3.2 %collective-permute-start.7 = (bf16[1,16,4,8,128]{4,3,2,1,0:T(8,128)(2,1)S(1)}, bf16[1,16,4,8,128]{4,3,2,1,0:T(8,128)(2,1)S(1)}, u32[]{:S(2)}, u32[]{:S(2)}) collective-permute-start(bf16[1,16,4,8,128]{4,3,2,1,0:T(8,128)(2,1)S(1)} %get-tuple-element.48), channel_id=1, source_target_pairs={{1,0},{2,1},{3,2},{4,3},{5,4},{6,5},{7,6},{8,7},{9,8},{10,9},{11,1... | collective-permute-start | bytes 393224 | tf_op jit(solution)/shard_map/ppermute | solution.py:104
  117.8 0.7 collective-permute-done.6
  118.5 4.0 %collective-permute-done.7 = bf16[1,16,4,8,128]{4,3,2,1,0:T(8,128)(2,1)S(1)} collective-permute-done((bf16[1,16,4,8,128]{4,3,2,1,0:T(8,128)(2,1)S(1)}, bf16[1,16,4,8,128]{4,3,2,1,0:T(8,128)(2,1)S(1)}, u32[]{:S(2)}, u32[]{:S(2)}) %collective-permute-start.7) | collective-permute-done | bytes 131104 | tf_op jit(solution)/shard_map/ppermute | solution.py:104
  122.5 0.9 pad_maximum_fusion.4
  123.4 5.1 %shard_map.68 = (bf16[1568,128]{1,0:T(8,128)(2,1)}, bf16[512,128]{1,0:T(8,128)(2,1)}) custom-call(s32[2]{0:T(128)} %pad_add_fusion.offs_ref, bf16[2048,128]{1,0:T(8,128)(2,1)} %bitcast.33, bf16[2048,128]{1,0:T(8,128)(2,1)} %bitcast.32, bf16[8,14,128,128]{3,2,1,0:T(8,128)(2,1)} %all-gather.2.cloned.1.call-done.w_hbm), custom_call_target="tpu_custom_call" | custom-call | flops 667942912 | bytes 2007040 | tf_op jit(solution)/shard_map/pallas_call | solution.py:76
  128.5 0.9 constant_dynamic-update-slice_fusion.3
  129.4 4.5 %shard_map.69 = (bf16[1152,128]{1,0:T(8,128)(2,1)}, bf16[512,128]{1,0:T(8,128)(2,1)}) custom-call(s32[2]{0:T(128)} %pad_add_fusion.offs_ref, bf16[1568,128]{1,0:T(8,128)(2,1)} %get-tuple-element.29.prior_ref, bf16[1568,128]{1,0:T(8,128)(2,1)} %bitcast.36, bf16[8,14,128,128]{3,2,1,0:T(8,128)(2,1)} %all-gather.2.cloned.1.call-done.w_hbm), custom_call_target="tpu_custom_call" | custom-call | flops 490733568 | bytes 1654784 | tf_op jit(solution)/shard_map/pallas_call | solution.py:76
  133.9 0.9 constant_dynamic-update-slice_fusion.2
  134.9 4.0 %shard_map.70 = (bf16[800,128]{1,0:T(8,128)(2,1)}, bf16[512,128]{1,0:T(8,128)(2,1)}) custom-call(s32[2]{0:T(128)} %pad_add_fusion.offs_ref, bf16[1152,128]{1,0:T(8,128)(2,1)} %get-tuple-element.31.prior_ref, bf16[1152,128]{1,0:T(8,128)(2,1)} %bitcast.38, bf16[8,14,128,128]{3,2,1,0:T(8,128)(2,1)} %all-gather.2.cloned.1.call-done.w_hbm), custom_call_target="tpu_custom_call" | custom-call | flops 340787200 | bytes 1351680 | tf_op jit(solution)/shard_map/pallas_call | solution.py:76
  138.9 0.9 constant_dynamic-update-slice_fusion.1
  139.9 3.6 %shard_map.71 = (bf16[512,128]{1,0:T(8,128)(2,1)}, bf16[512,128]{1,0:T(8,128)(2,1)}) custom-call(s32[2]{0:T(128)} %pad_add_fusion.offs_ref, bf16[800,128]{1,0:T(8,128)(2,1)} %get-tuple-element.33.prior_ref, bf16[800,128]{1,0:T(8,128)(2,1)} %bitcast.44, bf16[8,14,128,128]{3,2,1,0:T(8,128)(2,1)} %all-gather.2.cloned.1.call-done.w_hbm), custom_call_target="tpu_custom_call" | custom-call | flops 218103808 | bytes 1097728 | tf_op jit(solution)/shard_map/pallas_call | solution.py:76
  143.5 0.9 constant_dynamic-update-slice_fusion
  144.4 18.5 %all_to_all.18 = bf16[8,1,8,8,8,128]{5,4,3,2,1,0:T(8,128)(2,1)S(1)} all-to-all(bf16[8,1,8,8,8,128]{5,4,3,2,1,0:T(8,128)(2,1)S(1)} %constant_dynamic-update-slice_fusion), channel_id=1, replica_groups=mesh['section'=8,'frames'=4,'space'=16] {'section'}, dimensions={0} | all-to-all | bytes 2097152 | tf_op jit(solution)/shard_map/all_to_all | solution.py:180
  163.0 1.0 copy.24
  (35 shorter events, 2.5 us)
Async XLA Ops:
  6.5 28.1 %copy-start = (bf16[8,8,8,8,128]{4,3,2,1,0:T(8,128)(2,1)S(1)}, bf16[8,8,8,8,128]{4,3,2,1,0:T(8,128)(2,1)}, u32[]{:S(2)}) copy-start(bf16[8,8,8,8,128]{4,3,2,1,0:T(8,128)(2,1)} %param.6) | copy-start | bytes 3145732
  6.5 76.2 %all-gather.2.cloned.1.call-start = ((), (), s32[]{:S(2)}) async-start(), calls=%async_computation.2 | async-start | bytes 4128768 | tf_op jit(solution)/shard_map/all_gather | solution.py:149
  29.8 10.8 %collective-permute-start.8 = (bf16[4,1,4,8,8,128]{5,4,3,2,0,1:T(8,128)(2,1)S(1)}, bf16[4,1,4,8,8,128]{5,4,3,2,0,1:T(8,128)(2,1)S(1)}, u32[]{:S(2)}, u32[]{:S(2)}) collective-permute-start(bf16[4,1,4,8,8,128]{5,4,3,2,0,1:T(8,128)(2,1)S(1)} %get-tuple-element.45), channel_id=1, source_target_pairs={{0,16},{16,32},{32,48},{1,17},{17,33},{33,49},{2,18},{18,34},{34,5... | collective-permute-start | bytes 786440 | tf_op jit(solution)/shard_map/ppermute | solution.py:103
  33.3 9.4 %collective-permute-start.9 = (bf16[4,1,4,8,8,128]{5,4,3,2,0,1:T(8,128)(2,1)S(1)}, bf16[4,1,4,8,8,128]{5,4,3,2,0,1:T(8,128)(2,1)S(1)}, u32[]{:S(2)}, u32[]{:S(2)}) collective-permute-start(bf16[4,1,4,8,8,128]{5,4,3,2,0,1:T(8,128)(2,1)S(1)} %get-tuple-element.46), channel_id=1, source_target_pairs={{16,0},{32,16},{48,32},{17,1},{33,17},{49,33},{18,2},{34,18},{50,3... | collective-permute-start | bytes 786440 | tf_op jit(solution)/shard_map/ppermute | solution.py:104
  34.7 15.2 %collective-permute-start = (bf16[5,1,4,8,8,128]{5,4,3,2,0,1:T(8,128)(2,1)S(1)}, bf16[5,1,4,8,8,128]{5,4,3,2,0,1:T(8,128)(2,1)S(1)}, u32[]{:S(2)}, u32[]{:S(2)}) collective-permute-start(bf16[5,1,4,8,8,128]{5,4,3,2,0,1:T(8,128)(2,1)S(1)} %get-tuple-element.43), channel_id=1, source_target_pairs={{0,16},{16,32},{32,48},{1,17},{17,33},{33,49},{2,18},{18,34},{34,5... | collective-permute-start | bytes 983048 | tf_op jit(solution)/shard_map/ppermute | solution.py:103
  39.3 10.6 %collective-permute-start.1 = (bf16[5,1,4,8,8,128]{5,4,3,2,0,1:T(8,128)(2,1)S(1)}, bf16[5,1,4,8,8,128]{5,4,3,2,0,1:T(8,128)(2,1)S(1)}, u32[]{:S(2)}, u32[]{:S(2)}) collective-permute-start(bf16[5,1,4,8,8,128]{5,4,3,2,0,1:T(8,128)(2,1)S(1)} %get-tuple-element.44), channel_id=1, source_target_pairs={{16,0},{32,16},{48,32},{17,1},{33,17},{49,33},{18,2},{34,18},{50,3... | collective-permute-start | bytes 983048 | tf_op jit(solution)/shard_map/ppermute | solution.py:104
  42.9 17.4 %collective-permute-start.10 = (bf16[4,1,16,4,8,128]{5,4,3,2,0,1:T(8,128)(2,1)S(1)}, bf16[4,1,16,4,8,128]{5,4,3,2,0,1:T(8,128)(2,1)S(1)}, u32[]{:S(2)}, u32[]{:S(2)}) collective-permute-start(bf16[4,1,16,4,8,128]{5,4,3,2,0,1:T(8,128)(2,1)S(1)} %get-tuple-element.39), channel_id=1, source_target_pairs={{0,1},{1,2},{2,3},{3,4},{4,5},{5,6},{6,7},{7,8},{8,9},{9,10},{10,1... | collective-permute-start | bytes 1572872 | tf_op jit(solution)/shard_map/ppermute | solution.py:103
  48.0 18.0 %collective-permute-start.11 = (bf16[4,1,16,4,8,128]{5,4,3,2,0,1:T(8,128)(2,1)S(1)}, bf16[4,1,16,4,8,128]{5,4,3,2,0,1:T(8,128)(2,1)S(1)}, u32[]{:S(2)}, u32[]{:S(2)}) collective-permute-start(bf16[4,1,16,4,8,128]{5,4,3,2,0,1:T(8,128)(2,1)S(1)} %get-tuple-element.40), channel_id=1, source_target_pairs={{1,0},{2,1},{3,2},{4,3},{5,4},{6,5},{7,6},{8,7},{9,8},{10,9},{11,1... | collective-permute-start | bytes 1572872 | tf_op jit(solution)/shard_map/ppermute | solution.py:104
  50.4 21.2 %collective-permute-start.2 = (bf16[5,1,16,4,8,128]{5,4,3,2,0,1:T(8,128)(2,1)S(1)}, bf16[5,1,16,4,8,128]{5,4,3,2,0,1:T(8,128)(2,1)S(1)}, u32[]{:S(2)}, u32[]{:S(2)}) collective-permute-start(bf16[5,1,16,4,8,128]{5,4,3,2,0,1:T(8,128)(2,1)S(1)} %get-tuple-element.37), channel_id=1, source_target_pairs={{0,1},{1,2},{2,3},{3,4},{4,5},{5,6},{6,7},{7,8},{8,9},{9,10},{10,1... | collective-permute-start | bytes 1966088 | tf_op jit(solution)/shard_map/ppermute | solution.py:103
  55.5 21.4 %collective-permute-start.3 = (bf16[5,1,16,4,8,128]{5,4,3,2,0,1:T(8,128)(2,1)S(1)}, bf16[5,1,16,4,8,128]{5,4,3,2,0,1:T(8,128)(2,1)S(1)}, u32[]{:S(2)}, u32[]{:S(2)}) collective-permute-start(bf16[5,1,16,4,8,128]{5,4,3,2,0,1:T(8,128)(2,1)S(1)} %get-tuple-element.38), channel_id=1, source_target_pairs={{1,0},{2,1},{3,2},{4,3},{5,4},{6,5},{7,6},{8,7},{9,8},{10,9},{11,1... | collective-permute-start | bytes 1966088 | tf_op jit(solution)/shard_map/ppermute | solution.py:104
  96.4 9.5 %copy-start.4 = (bf16[512,128]{1,0:T(8,128)(2,1)S(1)}, bf16[512,128]{1,0:T(8,128)(2,1)}, u32[]{:S(2)}) copy-start(bf16[512,128]{1,0:T(8,128)(2,1)} %get-tuple-element.20) | copy-start | bytes 393220
  96.4 9.5 %copy-start.5 = (bf16[512,128]{1,0:T(8,128)(2,1)S(1)}, bf16[512,128]{1,0:T(8,128)(2,1)}, u32[]{:S(2)}) copy-start(bf16[512,128]{1,0:T(8,128)(2,1)} %get-tuple-element.22) | copy-start | bytes 393220
  96.4 21.3 %copy-start.2 = (bf16[512,128]{1,0:T(8,128)(2,1)S(1)}, bf16[512,128]{1,0:T(8,128)(2,1)}, u32[]{:S(2)}) copy-start(bf16[512,128]{1,0:T(8,128)(2,1)} %get-tuple-element.24) | copy-start | bytes 393220
  100.1 17.6 %copy-start.3 = (bf16[512,128]{1,0:T(8,128)(2,1)S(1)}, bf16[512,128]{1,0:T(8,128)(2,1)}, u32[]{:S(2)}) copy-start(bf16[512,128]{1,0:T(8,128)(2,1)} %get-tuple-element.26) | copy-start | bytes 393220
  100.1 22.4 %copy-start.1 = (bf16[512,128]{1,0:T(8,128)(2,1)S(1)}, bf16[512,128]{1,0:T(8,128)(2,1)}, u32[]{:S(2)}) copy-start(bf16[512,128]{1,0:T(8,128)(2,1)} %get-tuple-element.27) | copy-start | bytes 393220
  101.1 5.4 %collective-permute-start.4 = (bf16[1,4,8,8,128]{4,3,2,1,0:T(8,128)(2,1)S(1)}, bf16[1,4,8,8,128]{4,3,2,1,0:T(8,128)(2,1)S(1)}, u32[]{:S(2)}, u32[]{:S(2)}) collective-permute-start(bf16[1,4,8,8,128]{4,3,2,1,0:T(8,128)(2,1)S(1)} %get-tuple-element.49), channel_id=1, source_target_pairs={{0,16},{16,32},{32,48},{1,17},{17,33},{33,49},{2,18},{18,34},{34,5... | collective-permute-start | bytes 196616 | tf_op jit(solution)/shard_map/ppermute | solution.py:103
  104.5 6.2 %collective-permute-start.5 = (bf16[1,4,8,8,128]{4,3,2,1,0:T(8,128)(2,1)S(1)}, bf16[1,4,8,8,128]{4,3,2,1,0:T(8,128)(2,1)S(1)}, u32[]{:S(2)}, u32[]{:S(2)}) collective-permute-start(bf16[1,4,8,8,128]{4,3,2,1,0:T(8,128)(2,1)S(1)} %get-tuple-element.50), channel_id=1, source_target_pairs={{16,0},{32,16},{48,32},{17,1},{33,17},{49,33},{18,2},{34,18},{50,3... | collective-permute-start | bytes 196616 | tf_op jit(solution)/shard_map/ppermute | solution.py:104
  111.7 6.9 %collective-permute-start.6 = (bf16[1,16,4,8,128]{4,3,2,1,0:T(8,128)(2,1)S(1)}, bf16[1,16,4,8,128]{4,3,2,1,0:T(8,128)(2,1)S(1)}, u32[]{:S(2)}, u32[]{:S(2)}) collective-permute-start(bf16[1,16,4,8,128]{4,3,2,1,0:T(8,128)(2,1)S(1)} %get-tuple-element.47), channel_id=1, source_target_pairs={{0,1},{1,2},{2,3},{3,4},{4,5},{5,6},{6,7},{7,8},{8,9},{9,10},{10,1... | collective-permute-start | bytes 393224 | tf_op jit(solution)/shard_map/ppermute | solution.py:103
  114.5 8.1 %collective-permute-start.7 = (bf16[1,16,4,8,128]{4,3,2,1,0:T(8,128)(2,1)S(1)}, bf16[1,16,4,8,128]{4,3,2,1,0:T(8,128)(2,1)S(1)}, u32[]{:S(2)}, u32[]{:S(2)}) collective-permute-start(bf16[1,16,4,8,128]{4,3,2,1,0:T(8,128)(2,1)S(1)} %get-tuple-element.48), channel_id=1, source_target_pairs={{1,0},{2,1},{3,2},{4,3},{5,4},{6,5},{7,6},{8,7},{9,8},{10,9},{11,1... | collective-permute-start | bytes 393224 | tf_op jit(solution)/shard_map/ppermute | solution.py:104
Sparse Core Ops, SparseCore 0:
  9.5 40.9 all-gather.1

commit v12 on v3

--- a/solution.py
+++ b/solution.py
@@ -139,6 +139,9 @@
     noise_t = lax.all_to_all(section_noise[0], "section", 0, 0, tiled=True)
     noise_t = noise_t.reshape((sections, per_device) + noise_t.shape[1:])
     channels = spatial_kernel.shape[-1]
+    noise_t, spatial_kernel, temporal_kernel, output_weight, noise_levels = lax.optimization_barrier(
+        (noise_t, spatial_kernel, temporal_kernel, output_weight, noise_levels)
+    )
     level_slab = jnp.broadcast_to(
         noise_levels.reshape(1, 1, 1, 1), (1, 1, channels, channels)
     ).astype(spatial_kernel.dtype)

time: 171 us -> 170 us (level)
  blocking collectives: 38.9 us -> 18.5 us
  waiting for transfers between devices: 27.1 us -> 42.4 us
  starting transfers between devices: 35.4 us -> 39.9 us
    all_to_all x1 -> x0, blocking collectives: 20.4 us -> none  [on_device(): noise_t = lax.all_to_all(section_noise[0], 'section', 0, 0, tiled=True)]
    all_to_all x0 -> x1, waiting for transfers between devices: none -> 15.2 us  [on_device(): noise_t = lax.all_to_all(section_noise[0], 'section', 0, 0, tiled=True)]
    all_to_all x0 -> x1, starting transfers between devices: none -> 4.44 us  [on_device(): noise_t = lax.all_to_all(section_noise[0], 'section', 0, 0, tiled=True)]
    unnamed x20 -> x26, local copies, waits for them, and re-layouts: 3.84 us -> 3.85 us
  transfers between devices with their start and end apart: 13 -> 14, of which waited for: 9 -> 10; matrix products, arithmetic and copies ran while one was open for 6% -> 7% of each run, Pallas kernels for 0% -> 0%
where the time goes in v12:
time: 170 us; the launch traced here: 168 us
  waiting for transfers between devices  42.4 us (25%)
  starting transfers between devices  39.9 us (23%)
  Pallas kernels  32.3 us (19%)
  blocking collectives  18.5 us (11%)
  between operations  14.5 us (9%)
  other arithmetic  12.5 us (7%)
  local copies, waits for them, and re-layouts  8.14 us (5%)
    pallas_call x8, Pallas kernels, section_call(): pl.pallas_call(functools.partial(section_kernel, m, n, cols, inner, num_f...  32.3 us
    ppermute x6, starting transfers between devices, extend(): lax.ppermute(lax.slice_in_dim(block, size - width, size, axis=dim), axis,...  24.5 us
    ppermute x6, waiting for transfers between devices, extend(): lax.ppermute(lax.slice_in_dim(block, 0, width, axis=dim), axis, backward)  21.5 us
    all_to_all x1, blocking collectives, on_device(): return lax.all_to_all(stacked, 'section', 0, 1, tiled=True)  18.5 us
    all_to_all x1, waiting for transfers between devices, on_device(): noise_t = lax.all_to_all(section_noise[0], 'section', 0, 0, tiled=True)  15.2 us
    ppermute x6, starting transfers between devices, extend(): lax.ppermute(lax.slice_in_dim(block, 0, width, axis=dim), axis, backward)  10.9 us
    ppermute x6, waiting for transfers between devices, extend(): lax.ppermute(lax.slice_in_dim(block, size - width, size, axis=dim), axis,...  5.7 us
    concatenate x6, other arithmetic, extend(): block = jnp.concatenate([low, block, high], axis=dim)  4.85 us
  transfers between devices with their start and end apart: 14, of which 10 were waited for; matrix products, arithmetic and copies ran while one was open for 7% of the time, Pallas kernels for 0%

profile of v12, /device:TPU:96, one launch (start us, length us, event | category | flops | bytes accessed | tf_op | source)
XLA Modules:
  0.0 168.4 jit_solution(9127207290180407140)
XLA Ops:
  6.5 4.4 %all-to-all-start = ((bf16[8,8,8,8,128]{4,3,2,1,0:T(8,128)(2,1)}), bf16[8,8,8,8,128]{4,3,2,1,0:T(8,128)(2,1)S(1)}, u32[]{:S(2)}, u32[]{:S(2)}) async-start(bf16[8,8,8,8,128]{4,3,2,1,0:T(8,128)(2,1)} %bitcast.41), calls=%async_computation | async-start | bytes 2097152 | tf_op jit(solution)/shard_map/all_to_all | solution.py:139
  11.8 15.2 %all-to-all-done = bf16[8,8,8,8,128]{4,3,2,1,0:T(8,128)(2,1)S(1)} async-done(((bf16[8,8,8,8,128]{4,3,2,1,0:T(8,128)(2,1)}), bf16[8,8,8,8,128]{4,3,2,1,0:T(8,128)(2,1)S(1)}, u32[]{:S(2)}, u32[]{:S(2)}) %all-to-all-start) | async-done | bytes 1048608 | tf_op jit(solution)/shard_map/all_to_all | solution.py:139
  27.0 0.9 maximum_maximum_fusion
  28.0 3.5 %collective-permute-start.8 = (bf16[4,1,4,8,8,128]{5,4,3,2,0,1:T(8,128)(2,1)S(1)}, bf16[4,1,4,8,8,128]{5,4,3,2,0,1:T(8,128)(2,1)S(1)}, u32[]{:S(2)}, u32[]{:S(2)}) collective-permute-start(bf16[4,1,4,8,8,128]{5,4,3,2,0,1:T(8,128)(2,1)S(1)} %get-tuple-element.55), channel_id=1, source_target_pairs={{0,16},{16,32},{32,48},{1,17},{17,33},{33,49},{2,18},{18,34},{34,5... | collective-permute-start | bytes 786440 | tf_op jit(solution)/shard_map/ppermute | solution.py:101
  31.5 1.3 collective-permute-start.9
  32.9 4.6 %collective-permute-start = (bf16[5,1,4,8,8,128]{5,4,3,2,0,1:T(8,128)(2,1)S(1)}, bf16[5,1,4,8,8,128]{5,4,3,2,0,1:T(8,128)(2,1)S(1)}, u32[]{:S(2)}, u32[]{:S(2)}) collective-permute-start(bf16[5,1,4,8,8,128]{5,4,3,2,0,1:T(8,128)(2,1)S(1)} %get-tuple-element.53), channel_id=1, source_target_pairs={{0,16},{16,32},{32,48},{1,17},{17,33},{33,49},{2,18},{18,34},{34,5... | collective-permute-start | bytes 983048 | tf_op jit(solution)/shard_map/ppermute | solution.py:101
  37.5 1.3 collective-permute-start.1
  38.8 2.3 %collective-permute-done.9 = bf16[4,1,4,8,8,128]{5,4,3,2,0,1:T(8,128)(2,1)S(1)} collective-permute-done((bf16[4,1,4,8,8,128]{5,4,3,2,0,1:T(8,128)(2,1)S(1)}, bf16[4,1,4,8,8,128]{5,4,3,2,0,1:T(8,128)(2,1)S(1)}, u32[]{:S(2)}, u32[]{:S(2)}) %collective-permute-start.9) | collective-permute-done | bytes 262176 | tf_op jit(solution)/shard_map/ppermute | solution.py:102
  41.3 5.0 %collective-permute-start.10 = (bf16[4,1,16,4,8,128]{5,4,3,2,0,1:T(8,128)(2,1)S(1)}, bf16[4,1,16,4,8,128]{5,4,3,2,0,1:T(8,128)(2,1)S(1)}, u32[]{:S(2)}, u32[]{:S(2)}) collective-permute-start(bf16[4,1,16,4,8,128]{5,4,3,2,0,1:T(8,128)(2,1)S(1)} %get-tuple-element.49), channel_id=1, source_target_pairs={{0,1},{1,2},{2,3},{3,4},{4,5},{5,6},{6,7},{7,8},{8,9},{9,10},{10,1... | collective-permute-start | bytes 1572872 | tf_op jit(solution)/shard_map/ppermute | solution.py:101
  46.3 1.9 %collective-permute-start.11 = (bf16[4,1,16,4,8,128]{5,4,3,2,0,1:T(8,128)(2,1)S(1)}, bf16[4,1,16,4,8,128]{5,4,3,2,0,1:T(8,128)(2,1)S(1)}, u32[]{:S(2)}, u32[]{:S(2)}) collective-permute-start(bf16[4,1,16,4,8,128]{5,4,3,2,0,1:T(8,128)(2,1)S(1)} %get-tuple-element.50), channel_id=1, source_target_pairs={{1,0},{2,1},{3,2},{4,3},{5,4},{6,5},{7,6},{8,7},{9,8},{10,9},{11,1... | collective-permute-start | bytes 1572872 | tf_op jit(solution)/shard_map/ppermute | solution.py:102
  48.8 5.1 %collective-permute-start.2 = (bf16[5,1,16,4,8,128]{5,4,3,2,0,1:T(8,128)(2,1)S(1)}, bf16[5,1,16,4,8,128]{5,4,3,2,0,1:T(8,128)(2,1)S(1)}, u32[]{:S(2)}, u32[]{:S(2)}) collective-permute-start(bf16[5,1,16,4,8,128]{5,4,3,2,0,1:T(8,128)(2,1)S(1)} %get-tuple-element.47), channel_id=1, source_target_pairs={{0,1},{1,2},{2,3},{3,4},{4,5},{5,6},{6,7},{7,8},{8,9},{9,10},{10,1... | collective-permute-start | bytes 1966088 | tf_op jit(solution)/shard_map/ppermute | solution.py:101
  53.9 1.9 %collective-permute-start.3 = (bf16[5,1,16,4,8,128]{5,4,3,2,0,1:T(8,128)(2,1)S(1)}, bf16[5,1,16,4,8,128]{5,4,3,2,0,1:T(8,128)(2,1)S(1)}, u32[]{:S(2)}, u32[]{:S(2)}) collective-permute-start(bf16[5,1,16,4,8,128]{5,4,3,2,0,1:T(8,128)(2,1)S(1)} %get-tuple-element.48), channel_id=1, source_target_pairs={{1,0},{2,1},{3,2},{4,3},{5,4},{6,5},{7,6},{8,7},{9,8},{10,9},{11,1... | collective-permute-start | bytes 1966088 | tf_op jit(solution)/shard_map/ppermute | solution.py:102
  56.5 2.2 %collective-permute-done.10 = bf16[4,1,16,4,8,128]{5,4,3,2,0,1:T(8,128)(2,1)S(1)} collective-permute-done((bf16[4,1,16,4,8,128]{5,4,3,2,0,1:T(8,128)(2,1)S(1)}, bf16[4,1,16,4,8,128]{5,4,3,2,0,1:T(8,128)(2,1)S(1)}, u32[]{:S(2)}, u32[]{:S(2)}) %collective-permute-start.10) | collective-permute-done | bytes 524320 | tf_op jit(solution)/shard_map/ppermute | solution.py:101
  58.7 5.6 %collective-permute-done.11 = bf16[4,1,16,4,8,128]{5,4,3,2,0,1:T(8,128)(2,1)S(1)} collective-permute-done((bf16[4,1,16,4,8,128]{5,4,3,2,0,1:T(8,128)(2,1)S(1)}, bf16[4,1,16,4,8,128]{5,4,3,2,0,1:T(8,128)(2,1)S(1)}, u32[]{:S(2)}, u32[]{:S(2)}) %collective-permute-start.11) | collective-permute-done | bytes 524320 | tf_op jit(solution)/shard_map/ppermute | solution.py:102
  64.6 0.8 slice.116
  66.2 0.8 pad_maximum_fusion.8
  67.0 0.8 pad_maximum_fusion.5
  67.8 2.2 %collective-permute-done.2 = bf16[5,1,16,4,8,128]{5,4,3,2,0,1:T(8,128)(2,1)S(1)} collective-permute-done((bf16[5,1,16,4,8,128]{5,4,3,2,0,1:T(8,128)(2,1)S(1)}, bf16[5,1,16,4,8,128]{5,4,3,2,0,1:T(8,128)(2,1)S(1)}, u32[]{:S(2)}, u32[]{:S(2)}) %collective-permute-start.2) | collective-permute-done | bytes 655392 | tf_op jit(solution)/shard_map/ppermute | solution.py:101
  70.0 5.3 %collective-permute-done.3 = bf16[5,1,16,4,8,128]{5,4,3,2,0,1:T(8,128)(2,1)S(1)} collective-permute-done((bf16[5,1,16,4,8,128]{5,4,3,2,0,1:T(8,128)(2,1)S(1)}, bf16[5,1,16,4,8,128]{5,4,3,2,0,1:T(8,128)(2,1)S(1)}, u32[]{:S(2)}, u32[]{:S(2)}) %collective-permute-start.3) | collective-permute-done | bytes 655392 | tf_op jit(solution)/shard_map/ppermute | solution.py:102
  76.1 0.8 pad_maximum_fusion.9
  76.9 0.8 pad_maximum_fusion.6
  77.7 2.5 %pad_maximum_fusion = bf16[5,1,16,16,8,128]{5,4,3,2,0,1:T(8,128)(2,1)S(1)} fusion(bf16[5,1,16,4,8,128]{5,4,3,2,0,1:T(8,128)(2,1)S(1)} %collective-permute-done.3, bf16[5,1,4,8,8,128]{5,4,3,2,0,1:T(8,128)(2,1)S(1)} %collective-permute-done.1, bf16[4,1,8,8,8,128]{5,4,3,2,0,1:T(8,128)(2,1)S(1)} %get-tuple-element.52, ...), kind=kLoop, calls=%fused_computation | loop fusion | flops 6553600 | bytes 5242880 | tf_op jit(solution)/shard_map/concatenate | solution.py:103
  80.2 1.0 fusion.2
  81.2 1.4 fusion.1.lv_ref
  82.6 4.7 %shard_map.64 = (bf16[1568,128]{1,0:T(8,128)(2,1)}, bf16[512,128]{1,0:T(8,128)(2,1)}) custom-call(s32[2]{0:T(128)} %pad_add_fusion.offs_ref, f32[8]{0:T(128)} %fusion.1.lv_ref, bf16[2048,128]{1,0:T(8,128)(2,1)} %bitcast.33, bf16[2048,128]{1,0:T(8,128)(2,1)} %bitcast.32, bf16[8,14,128,128]{3,2,1,0:T(8,128)(2,1)} %all-gather.2.cloned.1.call-done.w_hbm), custom_call_target="tpu_custom_call" | custom-call | flops 667942912 | bytes 2007040 | tf_op jit(solution)/shard_map/pallas_call | solution.py:74
  87.3 4.2 %shard_map.65 = (bf16[1152,128]{1,0:T(8,128)(2,1)}, bf16[512,128]{1,0:T(8,128)(2,1)}) custom-call(s32[2]{0:T(128)} %pad_add_fusion.offs_ref, f32[8]{0:T(128)} %fusion.1.lv_ref, bf16[1568,128]{1,0:T(8,128)(2,1)} %get-tuple-element.31.prior_ref, bf16[1568,128]{1,0:T(8,128)(2,1)} %bitcast.35, bf16[8,14,128,128]{3,2,1,0:T(8,128)(2,1)} %all-gather.2.cloned.1.call-done.w_hbm), custom_call_target="tpu_custom_call" | custom-call | flops 490733568 | bytes 1654784 | tf_op jit(solution)/shard_map/pallas_call | solution.py:74
  91.5 3.8 %shard_map.66 = (bf16[800,128]{1,0:T(8,128)(2,1)}, bf16[512,128]{1,0:T(8,128)(2,1)}) custom-call(s32[2]{0:T(128)} %pad_add_fusion.offs_ref, f32[8]{0:T(128)} %fusion.1.lv_ref, bf16[1152,128]{1,0:T(8,128)(2,1)} %get-tuple-element.33.prior_ref, bf16[1152,128]{1,0:T(8,128)(2,1)} %bitcast.37, bf16[8,14,128,128]{3,2,1,0:T(8,128)(2,1)} %all-gather.2.cloned.1.call-done.w_hbm), custom_call_target="tpu_custom_call" | custom-call | flops 340787200 | bytes 1351680 | tf_op jit(solution)/shard_map/pallas_call | solution.py:74
  95.3 3.5 %shard_map.67 = (bf16[512,128]{1,0:T(8,128)(2,1)}, bf16[512,128]{1,0:T(8,128)(2,1)}) custom-call(s32[2]{0:T(128)} %pad_add_fusion.offs_ref, f32[8]{0:T(128)} %fusion.1.lv_ref, bf16[800,128]{1,0:T(8,128)(2,1)} %get-tuple-element.35.prior_ref, bf16[800,128]{1,0:T(8,128)(2,1)} %bitcast.43, bf16[8,14,128,128]{3,2,1,0:T(8,128)(2,1)} %all-gather.2.cloned.1.call-done.w_hbm), custom_call_target="tpu_custom_call" | custom-call | flops 218103808 | bytes 1097728 | tf_op jit(solution)/shard_map/pallas_call | solution.py:74
  98.9 0.9 fusion.8
  99.8 3.5 %collective-permute-start.4 = (bf16[1,4,8,8,128]{4,3,2,1,0:T(8,128)(2,1)S(1)}, bf16[1,4,8,8,128]{4,3,2,1,0:T(8,128)(2,1)S(1)}, u32[]{:S(2)}, u32[]{:S(2)}) collective-permute-start(bf16[1,4,8,8,128]{4,3,2,1,0:T(8,128)(2,1)S(1)} %get-tuple-element.59), channel_id=1, source_target_pairs={{0,16},{16,32},{32,48},{1,17},{17,33},{33,49},{2,18},{18,34},{34,5... | collective-permute-start | bytes 196616 | tf_op jit(solution)/shard_map/ppermute | solution.py:101
  103.3 1.3 collective-permute-start.5
  105.2 4.3 %collective-permute-done.5 = bf16[1,4,8,8,128]{4,3,2,1,0:T(8,128)(2,1)S(1)} collective-permute-done((bf16[1,4,8,8,128]{4,3,2,1,0:T(8,128)(2,1)S(1)}, bf16[1,4,8,8,128]{4,3,2,1,0:T(8,128)(2,1)S(1)}, u32[]{:S(2)}, u32[]{:S(2)}) %collective-permute-start.5) | collective-permute-done | bytes 65568 | tf_op jit(solution)/shard_map/ppermute | solution.py:102
  109.4 0.9 pad_maximum_fusion.10
  110.4 2.8 %collective-permute-start.6 = (bf16[1,16,4,8,128]{4,3,2,1,0:T(8,128)(2,1)S(1)}, bf16[1,16,4,8,128]{4,3,2,1,0:T(8,128)(2,1)S(1)}, u32[]{:S(2)}, u32[]{:S(2)}) collective-permute-start(bf16[1,16,4,8,128]{4,3,2,1,0:T(8,128)(2,1)S(1)} %get-tuple-element.57), channel_id=1, source_target_pairs={{0,1},{1,2},{2,3},{3,4},{4,5},{5,6},{6,7},{7,8},{8,9},{9,10},{10,1... | collective-permute-start | bytes 393224 | tf_op jit(solution)/shard_map/ppermute | solution.py:101
  113.2 3.2 %collective-permute-start.7 = (bf16[1,16,4,8,128]{4,3,2,1,0:T(8,128)(2,1)S(1)}, bf16[1,16,4,8,128]{4,3,2,1,0:T(8,128)(2,1)S(1)}, u32[]{:S(2)}, u32[]{:S(2)}) collective-permute-start(bf16[1,16,4,8,128]{4,3,2,1,0:T(8,128)(2,1)S(1)} %get-tuple-element.58), channel_id=1, source_target_pairs={{1,0},{2,1},{3,2},{4,3},{5,4},{6,5},{7,6},{8,7},{9,8},{10,9},{11,1... | collective-permute-start | bytes 393224 | tf_op jit(solution)/shard_map/ppermute | solution.py:102
  116.5 0.7 collective-permute-done.6
  117.3 4.0 %collective-permute-done.7 = bf16[1,16,4,8,128]{4,3,2,1,0:T(8,128)(2,1)S(1)} collective-permute-done((bf16[1,16,4,8,128]{4,3,2,1,0:T(8,128)(2,1)S(1)}, bf16[1,16,4,8,128]{4,3,2,1,0:T(8,128)(2,1)S(1)}, u32[]{:S(2)}, u32[]{:S(2)}) %collective-permute-start.7) | collective-permute-done | bytes 131104 | tf_op jit(solution)/shard_map/ppermute | solution.py:102
  121.3 0.9 pad_maximum_fusion.4
  122.2 4.7 %shard_map.68 = (bf16[1568,128]{1,0:T(8,128)(2,1)}, bf16[512,128]{1,0:T(8,128)(2,1)}) custom-call(s32[2]{0:T(128)} %pad_add_fusion.offs_ref, f32[8]{0:T(128)} %fusion.1.lv_ref, bf16[2048,128]{1,0:T(8,128)(2,1)} %bitcast.31, bf16[2048,128]{1,0:T(8,128)(2,1)} %bitcast.30, bf16[8,14,128,128]{3,2,1,0:T(8,128)(2,1)} %all-gather.2.cloned.1.call-done.w_hbm), custom_call_target="tpu_custom_call" | custom-call | flops 667942912 | bytes 2007040 | tf_op jit(solution)/shard_map/pallas_call | solution.py:74
  126.8 0.9 constant_dynamic-update-slice_fusion.3
  127.8 4.2 %shard_map.69 = (bf16[1152,128]{1,0:T(8,128)(2,1)}, bf16[512,128]{1,0:T(8,128)(2,1)}) custom-call(s32[2]{0:T(128)} %pad_add_fusion.offs_ref, f32[8]{0:T(128)} %fusion.1.lv_ref, bf16[1568,128]{1,0:T(8,128)(2,1)} %get-tuple-element.39.prior_ref, bf16[1568,128]{1,0:T(8,128)(2,1)} %bitcast.34, bf16[8,14,128,128]{3,2,1,0:T(8,128)(2,1)} %all-gather.2.cloned.1.call-done.w_hbm), custom_call_target="tpu_custom_call" | custom-call | flops 490733568 | bytes 1654784 | tf_op jit(solution)/shard_map/pallas_call | solution.py:74
  132.0 0.9 constant_dynamic-update-slice_fusion.2
  132.9 3.8 %shard_map.70 = (bf16[800,128]{1,0:T(8,128)(2,1)}, bf16[512,128]{1,0:T(8,128)(2,1)}) custom-call(s32[2]{0:T(128)} %pad_add_fusion.offs_ref, f32[8]{0:T(128)} %fusion.1.lv_ref, bf16[1152,128]{1,0:T(8,128)(2,1)} %get-tuple-element.41.prior_ref, bf16[1152,128]{1,0:T(8,128)(2,1)} %bitcast.36, bf16[8,14,128,128]{3,2,1,0:T(8,128)(2,1)} %all-gather.2.cloned.1.call-done.w_hbm), custom_call_target="tpu_custom_call" | custom-call | flops 340787200 | bytes 1351680 | tf_op jit(solution)/shard_map/pallas_call | solution.py:74
  136.7 0.9 constant_dynamic-update-slice_fusion.1
  137.6 3.5 %shard_map.71 = (bf16[512,128]{1,0:T(8,128)(2,1)}, bf16[512,128]{1,0:T(8,128)(2,1)}) custom-call(s32[2]{0:T(128)} %pad_add_fusion.offs_ref, f32[8]{0:T(128)} %fusion.1.lv_ref, bf16[800,128]{1,0:T(8,128)(2,1)} %get-tuple-element.43.prior_ref, bf16[800,128]{1,0:T(8,128)(2,1)} %bitcast.42, bf16[8,14,128,128]{3,2,1,0:T(8,128)(2,1)} %all-gather.2.cloned.1.call-done.w_hbm), custom_call_target="tpu_custom_call" | custom-call | flops 218103808 | bytes 1097728 | tf_op jit(solution)/shard_map/pallas_call | solution.py:74
  141.1 0.9 constant_dynamic-update-slice_fusion
  142.0 18.5 %all_to_all.17 = bf16[8,1,8,8,8,128]{5,4,3,2,1,0:T(8,128)(2,1)S(1)} all-to-all(bf16[8,1,8,8,8,128]{5,4,3,2,1,0:T(8,128)(2,1)S(1)} %constant_dynamic-update-slice_fusion), channel_id=1, replica_groups=mesh['section'=8,'frames'=4,'space'=16] {'section'}, dimensions={0} | all-to-all | bytes 2097152 | tf_op jit(solution)/shard_map/all_to_all | solution.py:183
  160.6 1.0 copy.32
  (43 shorter events, 4.0 us)
Async XLA Ops:
  6.5 26.3 %copy-start = (bf16[8,8,8,8,128]{4,3,2,1,0:T(8,128)(2,1)S(1)}, bf16[8,8,8,8,128]{4,3,2,1,0:T(8,128)(2,1)}, u32[]{:S(2)}) copy-start(bf16[8,8,8,8,128]{4,3,2,1,0:T(8,128)(2,1)} %param.6) | copy-start | bytes 3145732
  6.5 20.4 %copy-start.7 = (bf16[1,3,128,128]{3,2,1,0:T(8,128)(2,1)S(1)}, bf16[1,3,128,128]{3,2,1,0:T(8,128)(2,1)}, u32[]{:S(2)}) copy-start(bf16[1,3,128,128]{3,2,1,0:T(8,128)(2,1)} %param.10) | copy-start | bytes 294916
  6.5 20.4 %copy-start.8 = (bf16[1,128,128]{2,1,0:T(8,128)(2,1)S(1)}, bf16[1,128,128]{2,1,0:T(8,128)(2,1)}, u32[]{:S(2)}) copy-start(bf16[1,128,128]{2,1,0:T(8,128)(2,1)} %param.11) | copy-start | bytes 98308
  6.5 20.4 %copy-start.2 = (bf16[1,9,128,128]{3,2,1,0:T(8,128)(2,1)S(1)}, bf16[1,9,128,128]{3,2,1,0:T(8,128)(2,1)}, u32[]{:S(2)}) copy-start(bf16[1,9,128,128]{3,2,1,0:T(8,128)(2,1)} %param.9) | copy-start | bytes 884740
  6.5 20.4 %all-to-all-start = ((bf16[8,8,8,8,128]{4,3,2,1,0:T(8,128)(2,1)}), bf16[8,8,8,8,128]{4,3,2,1,0:T(8,128)(2,1)S(1)}, u32[]{:S(2)}, u32[]{:S(2)}) async-start(bf16[8,8,8,8,128]{4,3,2,1,0:T(8,128)(2,1)} %bitcast.41), calls=%async_computation | async-start | bytes 2097152 | tf_op jit(solution)/shard_map/all_to_all | solution.py:139
  11.0 70.2 %all-gather.2.cloned.1.call-start = ((), (), s32[]{:S(2)}) async-start(), calls=%async_computation.2 | async-start | bytes 4128768 | tf_op jit(solution)/shard_map/all_gather | solution.py:151
  28.0 10.8 %collective-permute-start.8 = (bf16[4,1,4,8,8,128]{5,4,3,2,0,1:T(8,128)(2,1)S(1)}, bf16[4,1,4,8,8,128]{5,4,3,2,0,1:T(8,128)(2,1)S(1)}, u32[]{:S(2)}, u32[]{:S(2)}) collective-permute-start(bf16[4,1,4,8,8,128]{5,4,3,2,0,1:T(8,128)(2,1)S(1)} %get-tuple-element.55), channel_id=1, source_target_pairs={{0,16},{16,32},{32,48},{1,17},{17,33},{33,49},{2,18},{18,34},{34,5... | collective-permute-start | bytes 786440 | tf_op jit(solution)/shard_map/ppermute | solution.py:101
  31.5 9.6 %collective-permute-start.9 = (bf16[4,1,4,8,8,128]{5,4,3,2,0,1:T(8,128)(2,1)S(1)}, bf16[4,1,4,8,8,128]{5,4,3,2,0,1:T(8,128)(2,1)S(1)}, u32[]{:S(2)}, u32[]{:S(2)}) collective-permute-start(bf16[4,1,4,8,8,128]{5,4,3,2,0,1:T(8,128)(2,1)S(1)} %get-tuple-element.56), channel_id=1, source_target_pairs={{16,0},{32,16},{48,32},{17,1},{33,17},{49,33},{18,2},{34,18},{50,3... | collective-permute-start | bytes 786440 | tf_op jit(solution)/shard_map/ppermute | solution.py:102
  32.9 15.4 %collective-permute-start = (bf16[5,1,4,8,8,128]{5,4,3,2,0,1:T(8,128)(2,1)S(1)}, bf16[5,1,4,8,8,128]{5,4,3,2,0,1:T(8,128)(2,1)S(1)}, u32[]{:S(2)}, u32[]{:S(2)}) collective-permute-start(bf16[5,1,4,8,8,128]{5,4,3,2,0,1:T(8,128)(2,1)S(1)} %get-tuple-element.53), channel_id=1, source_target_pairs={{0,16},{16,32},{32,48},{1,17},{17,33},{33,49},{2,18},{18,34},{34,5... | collective-permute-start | bytes 983048 | tf_op jit(solution)/shard_map/ppermute | solution.py:101
  37.5 10.8 %collective-permute-start.1 = (bf16[5,1,4,8,8,128]{5,4,3,2,0,1:T(8,128)(2,1)S(1)}, bf16[5,1,4,8,8,128]{5,4,3,2,0,1:T(8,128)(2,1)S(1)}, u32[]{:S(2)}, u32[]{:S(2)}) collective-permute-start(bf16[5,1,4,8,8,128]{5,4,3,2,0,1:T(8,128)(2,1)S(1)} %get-tuple-element.54), channel_id=1, source_target_pairs={{16,0},{32,16},{48,32},{17,1},{33,17},{49,33},{18,2},{34,18},{50,3... | collective-permute-start | bytes 983048 | tf_op jit(solution)/shard_map/ppermute | solution.py:102
  41.3 17.4 %collective-permute-start.10 = (bf16[4,1,16,4,8,128]{5,4,3,2,0,1:T(8,128)(2,1)S(1)}, bf16[4,1,16,4,8,128]{5,4,3,2,0,1:T(8,128)(2,1)S(1)}, u32[]{:S(2)}, u32[]{:S(2)}) collective-permute-start(bf16[4,1,16,4,8,128]{5,4,3,2,0,1:T(8,128)(2,1)S(1)} %get-tuple-element.49), channel_id=1, source_target_pairs={{0,1},{1,2},{2,3},{3,4},{4,5},{5,6},{6,7},{7,8},{8,9},{9,10},{10,1... | collective-permute-start | bytes 1572872 | tf_op jit(solution)/shard_map/ppermute | solution.py:101
  46.3 18.0 %collective-permute-start.11 = (bf16[4,1,16,4,8,128]{5,4,3,2,0,1:T(8,128)(2,1)S(1)}, bf16[4,1,16,4,8,128]{5,4,3,2,0,1:T(8,128)(2,1)S(1)}, u32[]{:S(2)}, u32[]{:S(2)}) collective-permute-start(bf16[4,1,16,4,8,128]{5,4,3,2,0,1:T(8,128)(2,1)S(1)} %get-tuple-element.50), channel_id=1, source_target_pairs={{1,0},{2,1},{3,2},{4,3},{5,4},{6,5},{7,6},{8,7},{9,8},{10,9},{11,1... | collective-permute-start | bytes 1572872 | tf_op jit(solution)/shard_map/ppermute | solution.py:102
  48.8 21.3 %collective-permute-start.2 = (bf16[5,1,16,4,8,128]{5,4,3,2,0,1:T(8,128)(2,1)S(1)}, bf16[5,1,16,4,8,128]{5,4,3,2,0,1:T(8,128)(2,1)S(1)}, u32[]{:S(2)}, u32[]{:S(2)}) collective-permute-start(bf16[5,1,16,4,8,128]{5,4,3,2,0,1:T(8,128)(2,1)S(1)} %get-tuple-element.47), channel_id=1, source_target_pairs={{0,1},{1,2},{2,3},{3,4},{4,5},{5,6},{6,7},{7,8},{8,9},{9,10},{10,1... | collective-permute-start | bytes 1966088 | tf_op jit(solution)/shard_map/ppermute | solution.py:101
  53.9 21.5 %collective-permute-start.3 = (bf16[5,1,16,4,8,128]{5,4,3,2,0,1:T(8,128)(2,1)S(1)}, bf16[5,1,16,4,8,128]{5,4,3,2,0,1:T(8,128)(2,1)S(1)}, u32[]{:S(2)}, u32[]{:S(2)}) collective-permute-start(bf16[5,1,16,4,8,128]{5,4,3,2,0,1:T(8,128)(2,1)S(1)} %get-tuple-element.48), channel_id=1, source_target_pairs={{1,0},{2,1},{3,2},{4,3},{5,4},{6,5},{7,6},{8,7},{9,8},{10,9},{11,1... | collective-permute-start | bytes 1966088 | tf_op jit(solution)/shard_map/ppermute | solution.py:102
  95.3 9.3 %copy-start.5 = (bf16[512,128]{1,0:T(8,128)(2,1)S(1)}, bf16[512,128]{1,0:T(8,128)(2,1)}, u32[]{:S(2)}) copy-start(bf16[512,128]{1,0:T(8,128)(2,1)} %get-tuple-element.30) | copy-start | bytes 393220
  95.3 9.3 %copy-start.6 = (bf16[512,128]{1,0:T(8,128)(2,1)S(1)}, bf16[512,128]{1,0:T(8,128)(2,1)}, u32[]{:S(2)}) copy-start(bf16[512,128]{1,0:T(8,128)(2,1)} %get-tuple-element.32) | copy-start | bytes 393220
  95.3 21.2 %copy-start.3 = (bf16[512,128]{1,0:T(8,128)(2,1)S(1)}, bf16[512,128]{1,0:T(8,128)(2,1)}, u32[]{:S(2)}) copy-start(bf16[512,128]{1,0:T(8,128)(2,1)} %get-tuple-element.34) | copy-start | bytes 393220
  98.8 17.6 %copy-start.4 = (bf16[512,128]{1,0:T(8,128)(2,1)S(1)}, bf16[512,128]{1,0:T(8,128)(2,1)}, u32[]{:S(2)}) copy-start(bf16[512,128]{1,0:T(8,128)(2,1)} %get-tuple-element.36) | copy-start | bytes 393220
  98.9 22.4 %copy-start.1 = (bf16[512,128]{1,0:T(8,128)(2,1)S(1)}, bf16[512,128]{1,0:T(8,128)(2,1)}, u32[]{:S(2)}) copy-start(bf16[512,128]{1,0:T(8,128)(2,1)} %get-tuple-element.37) | copy-start | bytes 393220
  99.8 5.4 %collective-permute-start.4 = (bf16[1,4,8,8,128]{4,3,2,1,0:T(8,128)(2,1)S(1)}, bf16[1,4,8,8,128]{4,3,2,1,0:T(8,128)(2,1)S(1)}, u32[]{:S(2)}, u32[]{:S(2)}) collective-permute-start(bf16[1,4,8,8,128]{4,3,2,1,0:T(8,128)(2,1)S(1)} %get-tuple-element.59), channel_id=1, source_target_pairs={{0,16},{16,32},{32,48},{1,17},{17,33},{33,49},{2,18},{18,34},{34,5... | collective-permute-start | bytes 196616 | tf_op jit(solution)/shard_map/ppermute | solution.py:101
  103.3 6.2 %collective-permute-start.5 = (bf16[1,4,8,8,128]{4,3,2,1,0:T(8,128)(2,1)S(1)}, bf16[1,4,8,8,128]{4,3,2,1,0:T(8,128)(2,1)S(1)}, u32[]{:S(2)}, u32[]{:S(2)}) collective-permute-start(bf16[1,4,8,8,128]{4,3,2,1,0:T(8,128)(2,1)S(1)} %get-tuple-element.60), channel_id=1, source_target_pairs={{16,0},{32,16},{48,32},{17,1},{33,17},{49,33},{18,2},{34,18},{50,3... | collective-permute-start | bytes 196616 | tf_op jit(solution)/shard_map/ppermute | solution.py:102
  110.4 6.9 %collective-permute-start.6 = (bf16[1,16,4,8,128]{4,3,2,1,0:T(8,128)(2,1)S(1)}, bf16[1,16,4,8,128]{4,3,2,1,0:T(8,128)(2,1)S(1)}, u32[]{:S(2)}, u32[]{:S(2)}) collective-permute-start(bf16[1,16,4,8,128]{4,3,2,1,0:T(8,128)(2,1)S(1)} %get-tuple-element.57), channel_id=1, source_target_pairs={{0,1},{1,2},{2,3},{3,4},{4,5},{5,6},{6,7},{7,8},{8,9},{9,10},{10,1... | collective-permute-start | bytes 393224 | tf_op jit(solution)/shard_map/ppermute | solution.py:101
  113.2 8.1 %collective-permute-start.7 = (bf16[1,16,4,8,128]{4,3,2,1,0:T(8,128)(2,1)S(1)}, bf16[1,16,4,8,128]{4,3,2,1,0:T(8,128)(2,1)S(1)}, u32[]{:S(2)}, u32[]{:S(2)}) collective-permute-start(bf16[1,16,4,8,128]{4,3,2,1,0:T(8,128)(2,1)S(1)} %get-tuple-element.58), channel_id=1, source_target_pairs={{1,0},{2,1},{3,2},{4,3},{5,4},{6,5},{7,6},{8,7},{9,8},{10,9},{11,1... | collective-permute-start | bytes 393224 | tf_op jit(solution)/shard_map/ppermute | solution.py:102
Sparse Core Ops, SparseCore 0:
  28.0 39.0 all-gather.1

commit v13 on v11

--- a/solution.py
+++ b/solution.py
@@ -140,6 +140,9 @@
     noise_t = lax.all_to_all(section_noise[0], "section", 0, 0, tiled=True)
     noise_t = noise_t.reshape((sections, per_device) + noise_t.shape[1:])
     channels = spatial_kernel.shape[-1]
+    noise_t, spatial_kernel, temporal_kernel, output_weight, noise_levels = lax.optimization_barrier(
+        (noise_t, spatial_kernel, temporal_kernel, output_weight, noise_levels)
+    )
     level_slab = jnp.broadcast_to(
         noise_levels.reshape(1, 1, 1, 1), (1, 1, channels, channels)
     ).astype(spatial_kernel.dtype)

time: 172 us -> 170 us (0.988)
  blocking collectives: 38.9 us -> 18.5 us
  waiting for transfers between devices: 27.1 us -> 42.5 us
  starting transfers between devices: 35.4 us -> 39.9 us
    all_to_all x1 -> x0, blocking collectives: 20.4 us -> none  [on_device(): noise_t = lax.all_to_all(section_noise[0], 'section', 0, 0, tiled=True)]
    all_to_all x0 -> x1, waiting for transfers between devices: none -> 15.2 us  [on_device(): noise_t = lax.all_to_all(section_noise[0], 'section', 0, 0, tiled=True)]
    all_to_all x0 -> x1, starting transfers between devices: none -> 4.44 us  [on_device(): noise_t = lax.all_to_all(section_noise[0], 'section', 0, 0, tiled=True)]
    unnamed x20 -> x26, local copies, waits for them, and re-layouts: 3.84 us -> 3.85 us
  transfers between devices with their start and end apart: 13 -> 14, of which waited for: 9 -> 10; matrix products, arithmetic and copies ran while one was open for 6% -> 6% of each run, Pallas kernels for 0% -> 0%
where the time goes in v13:
time: 170 us; the launch traced here: 169 us
  waiting for transfers between devices  42.5 us (25%)
  starting transfers between devices  39.9 us (23%)
  Pallas kernels  34.5 us (20%)
  blocking collectives  18.5 us (11%)
  between operations  14.5 us (9%)
  other arithmetic  11.1 us (7%)
  local copies, waits for them, and re-layouts  8.15 us (5%)
    pallas_call x8, Pallas kernels, section_call(): pl.pallas_call(functools.partial(section_kernel, m, n, cols, inner, num_f...  34.5 us
    ppermute x6, starting transfers between devices, extend(): lax.ppermute(lax.slice_in_dim(block, size - width, size, axis=dim), axis,...  24.5 us
    ppermute x6, waiting for transfers between devices, extend(): lax.ppermute(lax.slice_in_dim(block, 0, width, axis=dim), axis, backward)  21.5 us
    all_to_all x1, blocking collectives, on_device(): return lax.all_to_all(stacked, 'section', 0, 1, tiled=True)  18.5 us
    all_to_all x1, waiting for transfers between devices, on_device(): noise_t = lax.all_to_all(section_noise[0], 'section', 0, 0, tiled=True)  15.2 us
    ppermute x6, starting transfers between devices, extend(): lax.ppermute(lax.slice_in_dim(block, 0, width, axis=dim), axis, backward)  10.9 us
    ppermute x6, waiting for transfers between devices, extend(): lax.ppermute(lax.slice_in_dim(block, size - width, size, axis=dim), axis,...  5.76 us
    concatenate x6, other arithmetic, extend(): block = jnp.concatenate([low, block, high], axis=dim)  4.85 us
  transfers between devices with their start and end apart: 14, of which 10 were waited for; matrix products, arithmetic and copies ran while one was open for 6% of the time, Pallas kernels for 0%

profile of v13, /device:TPU:96, one launch (start us, length us, event | category | flops | bytes accessed | tf_op | source)
XLA Modules:
  0.0 169.2 jit_solution(6711397538495898986)
XLA Ops:
  6.5 4.4 %all-to-all-start = ((bf16[8,8,8,8,128]{4,3,2,1,0:T(8,128)(2,1)}), bf16[8,8,8,8,128]{4,3,2,1,0:T(8,128)(2,1)S(1)}, u32[]{:S(2)}, u32[]{:S(2)}) async-start(bf16[8,8,8,8,128]{4,3,2,1,0:T(8,128)(2,1)} %bitcast.41), calls=%async_computation | async-start | bytes 2097152 | tf_op jit(solution)/shard_map/all_to_all | solution.py:140
  11.8 15.2 %all-to-all-done = bf16[8,8,8,8,128]{4,3,2,1,0:T(8,128)(2,1)S(1)} async-done(((bf16[8,8,8,8,128]{4,3,2,1,0:T(8,128)(2,1)}), bf16[8,8,8,8,128]{4,3,2,1,0:T(8,128)(2,1)S(1)}, u32[]{:S(2)}, u32[]{:S(2)}) %all-to-all-start) | async-done | bytes 1048608 | tf_op jit(solution)/shard_map/all_to_all | solution.py:140
  27.0 0.9 maximum_maximum_fusion
  28.0 3.5 %collective-permute-start.8 = (bf16[4,1,4,8,8,128]{5,4,3,2,0,1:T(8,128)(2,1)S(1)}, bf16[4,1,4,8,8,128]{5,4,3,2,0,1:T(8,128)(2,1)S(1)}, u32[]{:S(2)}, u32[]{:S(2)}) collective-permute-start(bf16[4,1,4,8,8,128]{5,4,3,2,0,1:T(8,128)(2,1)S(1)} %get-tuple-element.55), channel_id=1, source_target_pairs={{0,16},{16,32},{32,48},{1,17},{17,33},{33,49},{2,18},{18,34},{34,5... | collective-permute-start | bytes 786440 | tf_op jit(solution)/shard_map/ppermute | solution.py:103
  31.5 1.3 collective-permute-start.9
  32.9 4.6 %collective-permute-start = (bf16[5,1,4,8,8,128]{5,4,3,2,0,1:T(8,128)(2,1)S(1)}, bf16[5,1,4,8,8,128]{5,4,3,2,0,1:T(8,128)(2,1)S(1)}, u32[]{:S(2)}, u32[]{:S(2)}) collective-permute-start(bf16[5,1,4,8,8,128]{5,4,3,2,0,1:T(8,128)(2,1)S(1)} %get-tuple-element.53), channel_id=1, source_target_pairs={{0,16},{16,32},{32,48},{1,17},{17,33},{33,49},{2,18},{18,34},{34,5... | collective-permute-start | bytes 983048 | tf_op jit(solution)/shard_map/ppermute | solution.py:103
  37.5 1.3 collective-permute-start.1
  38.8 2.3 %collective-permute-done.9 = bf16[4,1,4,8,8,128]{5,4,3,2,0,1:T(8,128)(2,1)S(1)} collective-permute-done((bf16[4,1,4,8,8,128]{5,4,3,2,0,1:T(8,128)(2,1)S(1)}, bf16[4,1,4,8,8,128]{5,4,3,2,0,1:T(8,128)(2,1)S(1)}, u32[]{:S(2)}, u32[]{:S(2)}) %collective-permute-start.9) | collective-permute-done | bytes 262176 | tf_op jit(solution)/shard_map/ppermute | solution.py:104
  41.3 5.0 %collective-permute-start.10 = (bf16[4,1,16,4,8,128]{5,4,3,2,0,1:T(8,128)(2,1)S(1)}, bf16[4,1,16,4,8,128]{5,4,3,2,0,1:T(8,128)(2,1)S(1)}, u32[]{:S(2)}, u32[]{:S(2)}) collective-permute-start(bf16[4,1,16,4,8,128]{5,4,3,2,0,1:T(8,128)(2,1)S(1)} %get-tuple-element.49), channel_id=1, source_target_pairs={{0,1},{1,2},{2,3},{3,4},{4,5},{5,6},{6,7},{7,8},{8,9},{9,10},{10,1... | collective-permute-start | bytes 1572872 | tf_op jit(solution)/shard_map/ppermute | solution.py:103
  46.3 1.9 %collective-permute-start.11 = (bf16[4,1,16,4,8,128]{5,4,3,2,0,1:T(8,128)(2,1)S(1)}, bf16[4,1,16,4,8,128]{5,4,3,2,0,1:T(8,128)(2,1)S(1)}, u32[]{:S(2)}, u32[]{:S(2)}) collective-permute-start(bf16[4,1,16,4,8,128]{5,4,3,2,0,1:T(8,128)(2,1)S(1)} %get-tuple-element.50), channel_id=1, source_target_pairs={{1,0},{2,1},{3,2},{4,3},{5,4},{6,5},{7,6},{8,7},{9,8},{10,9},{11,1... | collective-permute-start | bytes 1572872 | tf_op jit(solution)/shard_map/ppermute | solution.py:104
  48.7 5.1 %collective-permute-start.2 = (bf16[5,1,16,4,8,128]{5,4,3,2,0,1:T(8,128)(2,1)S(1)}, bf16[5,1,16,4,8,128]{5,4,3,2,0,1:T(8,128)(2,1)S(1)}, u32[]{:S(2)}, u32[]{:S(2)}) collective-permute-start(bf16[5,1,16,4,8,128]{5,4,3,2,0,1:T(8,128)(2,1)S(1)} %get-tuple-element.47), channel_id=1, source_target_pairs={{0,1},{1,2},{2,3},{3,4},{4,5},{5,6},{6,7},{7,8},{8,9},{9,10},{10,1... | collective-permute-start | bytes 1966088 | tf_op jit(solution)/shard_map/ppermute | solution.py:103
  53.9 1.9 %collective-permute-start.3 = (bf16[5,1,16,4,8,128]{5,4,3,2,0,1:T(8,128)(2,1)S(1)}, bf16[5,1,16,4,8,128]{5,4,3,2,0,1:T(8,128)(2,1)S(1)}, u32[]{:S(2)}, u32[]{:S(2)}) collective-permute-start(bf16[5,1,16,4,8,128]{5,4,3,2,0,1:T(8,128)(2,1)S(1)} %get-tuple-element.48), channel_id=1, source_target_pairs={{1,0},{2,1},{3,2},{4,3},{5,4},{6,5},{7,6},{8,7},{9,8},{10,9},{11,1... | collective-permute-start | bytes 1966088 | tf_op jit(solution)/shard_map/ppermute | solution.py:104
  56.4 2.3 %collective-permute-done.10 = bf16[4,1,16,4,8,128]{5,4,3,2,0,1:T(8,128)(2,1)S(1)} collective-permute-done((bf16[4,1,16,4,8,128]{5,4,3,2,0,1:T(8,128)(2,1)S(1)}, bf16[4,1,16,4,8,128]{5,4,3,2,0,1:T(8,128)(2,1)S(1)}, u32[]{:S(2)}, u32[]{:S(2)}) %collective-permute-start.10) | collective-permute-done | bytes 524320 | tf_op jit(solution)/shard_map/ppermute | solution.py:103
  58.7 5.6 %collective-permute-done.11 = bf16[4,1,16,4,8,128]{5,4,3,2,0,1:T(8,128)(2,1)S(1)} collective-permute-done((bf16[4,1,16,4,8,128]{5,4,3,2,0,1:T(8,128)(2,1)S(1)}, bf16[4,1,16,4,8,128]{5,4,3,2,0,1:T(8,128)(2,1)S(1)}, u32[]{:S(2)}, u32[]{:S(2)}) %collective-permute-start.11) | collective-permute-done | bytes 524320 | tf_op jit(solution)/shard_map/ppermute | solution.py:104
  64.6 0.8 slice.111
  66.2 0.8 pad_maximum_fusion.8
  67.0 0.8 pad_maximum_fusion.5
  67.8 2.2 %collective-permute-done.2 = bf16[5,1,16,4,8,128]{5,4,3,2,0,1:T(8,128)(2,1)S(1)} collective-permute-done((bf16[5,1,16,4,8,128]{5,4,3,2,0,1:T(8,128)(2,1)S(1)}, bf16[5,1,16,4,8,128]{5,4,3,2,0,1:T(8,128)(2,1)S(1)}, u32[]{:S(2)}, u32[]{:S(2)}) %collective-permute-start.2) | collective-permute-done | bytes 655392 | tf_op jit(solution)/shard_map/ppermute | solution.py:103
  70.0 5.3 %collective-permute-done.3 = bf16[5,1,16,4,8,128]{5,4,3,2,0,1:T(8,128)(2,1)S(1)} collective-permute-done((bf16[5,1,16,4,8,128]{5,4,3,2,0,1:T(8,128)(2,1)S(1)}, bf16[5,1,16,4,8,128]{5,4,3,2,0,1:T(8,128)(2,1)S(1)}, u32[]{:S(2)}, u32[]{:S(2)}) %collective-permute-start.3) | collective-permute-done | bytes 655392 | tf_op jit(solution)/shard_map/ppermute | solution.py:104
  75.3 0.7 pad_maximum_fusion.12
  76.1 0.8 pad_maximum_fusion.9
  76.9 0.8 pad_maximum_fusion.6
  77.7 2.5 %pad_maximum_fusion = bf16[5,1,16,16,8,128]{5,4,3,2,0,1:T(8,128)(2,1)S(1)} fusion(bf16[5,1,16,4,8,128]{5,4,3,2,0,1:T(8,128)(2,1)S(1)} %collective-permute-done.3, bf16[5,1,4,8,8,128]{5,4,3,2,0,1:T(8,128)(2,1)S(1)} %collective-permute-done.1, bf16[4,1,8,8,8,128]{5,4,3,2,0,1:T(8,128)(2,1)S(1)} %get-tuple-element.52, ...), kind=kLoop, calls=%fused_computation | loop fusion | flops 6553600 | bytes 5242880 | tf_op jit(solution)/shard_map/concatenate | solution.py:105
  80.1 1.0 fusion.1
  81.2 5.1 %shard_map.64 = (bf16[1568,128]{1,0:T(8,128)(2,1)}, bf16[512,128]{1,0:T(8,128)(2,1)}) custom-call(s32[2]{0:T(128)} %pad_add_fusion.offs_ref, bf16[2048,128]{1,0:T(8,128)(2,1)} %bitcast.33, bf16[2048,128]{1,0:T(8,128)(2,1)} %bitcast.32, bf16[8,14,128,128]{3,2,1,0:T(8,128)(2,1)} %all-gather.2.cloned.1.call-done.w_hbm), custom_call_target="tpu_custom_call" | custom-call | flops 667942912 | bytes 2007040 | tf_op jit(solution)/shard_map/pallas_call | solution.py:76
  86.3 4.5 %shard_map.65 = (bf16[1152,128]{1,0:T(8,128)(2,1)}, bf16[512,128]{1,0:T(8,128)(2,1)}) custom-call(s32[2]{0:T(128)} %pad_add_fusion.offs_ref, bf16[1568,128]{1,0:T(8,128)(2,1)} %get-tuple-element.31.prior_ref, bf16[1568,128]{1,0:T(8,128)(2,1)} %bitcast.35, bf16[8,14,128,128]{3,2,1,0:T(8,128)(2,1)} %all-gather.2.cloned.1.call-done.w_hbm), custom_call_target="tpu_custom_call" | custom-call | flops 490733568 | bytes 1654784 | tf_op jit(solution)/shard_map/pallas_call | solution.py:76
  90.8 4.0 %shard_map.66 = (bf16[800,128]{1,0:T(8,128)(2,1)}, bf16[512,128]{1,0:T(8,128)(2,1)}) custom-call(s32[2]{0:T(128)} %pad_add_fusion.offs_ref, bf16[1152,128]{1,0:T(8,128)(2,1)} %get-tuple-element.33.prior_ref, bf16[1152,128]{1,0:T(8,128)(2,1)} %bitcast.37, bf16[8,14,128,128]{3,2,1,0:T(8,128)(2,1)} %all-gather.2.cloned.1.call-done.w_hbm), custom_call_target="tpu_custom_call" | custom-call | flops 340787200 | bytes 1351680 | tf_op jit(solution)/shard_map/pallas_call | solution.py:76
  94.8 3.7 %shard_map.67 = (bf16[512,128]{1,0:T(8,128)(2,1)}, bf16[512,128]{1,0:T(8,128)(2,1)}) custom-call(s32[2]{0:T(128)} %pad_add_fusion.offs_ref, bf16[800,128]{1,0:T(8,128)(2,1)} %get-tuple-element.35.prior_ref, bf16[800,128]{1,0:T(8,128)(2,1)} %bitcast.43, bf16[8,14,128,128]{3,2,1,0:T(8,128)(2,1)} %all-gather.2.cloned.1.call-done.w_hbm), custom_call_target="tpu_custom_call" | custom-call | flops 218103808 | bytes 1097728 | tf_op jit(solution)/shard_map/pallas_call | solution.py:76
  98.6 0.9 fusion.7
  99.5 3.5 %collective-permute-start.4 = (bf16[1,4,8,8,128]{4,3,2,1,0:T(8,128)(2,1)S(1)}, bf16[1,4,8,8,128]{4,3,2,1,0:T(8,128)(2,1)S(1)}, u32[]{:S(2)}, u32[]{:S(2)}) collective-permute-start(bf16[1,4,8,8,128]{4,3,2,1,0:T(8,128)(2,1)S(1)} %get-tuple-element.59), channel_id=1, source_target_pairs={{0,16},{16,32},{32,48},{1,17},{17,33},{33,49},{2,18},{18,34},{34,5... | collective-permute-start | bytes 196616 | tf_op jit(solution)/shard_map/ppermute | solution.py:103
  103.0 1.3 collective-permute-start.5
  104.9 4.3 %collective-permute-done.5 = bf16[1,4,8,8,128]{4,3,2,1,0:T(8,128)(2,1)S(1)} collective-permute-done((bf16[1,4,8,8,128]{4,3,2,1,0:T(8,128)(2,1)S(1)}, bf16[1,4,8,8,128]{4,3,2,1,0:T(8,128)(2,1)S(1)}, u32[]{:S(2)}, u32[]{:S(2)}) %collective-permute-start.5) | collective-permute-done | bytes 65568 | tf_op jit(solution)/shard_map/ppermute | solution.py:104
  109.1 0.9 pad_maximum_fusion.10
  110.1 2.8 %collective-permute-start.6 = (bf16[1,16,4,8,128]{4,3,2,1,0:T(8,128)(2,1)S(1)}, bf16[1,16,4,8,128]{4,3,2,1,0:T(8,128)(2,1)S(1)}, u32[]{:S(2)}, u32[]{:S(2)}) collective-permute-start(bf16[1,16,4,8,128]{4,3,2,1,0:T(8,128)(2,1)S(1)} %get-tuple-element.57), channel_id=1, source_target_pairs={{0,1},{1,2},{2,3},{3,4},{4,5},{5,6},{6,7},{7,8},{8,9},{9,10},{10,1... | collective-permute-start | bytes 393224 | tf_op jit(solution)/shard_map/ppermute | solution.py:103
  112.9 3.2 %collective-permute-start.7 = (bf16[1,16,4,8,128]{4,3,2,1,0:T(8,128)(2,1)S(1)}, bf16[1,16,4,8,128]{4,3,2,1,0:T(8,128)(2,1)S(1)}, u32[]{:S(2)}, u32[]{:S(2)}) collective-permute-start(bf16[1,16,4,8,128]{4,3,2,1,0:T(8,128)(2,1)S(1)} %get-tuple-element.58), channel_id=1, source_target_pairs={{1,0},{2,1},{3,2},{4,3},{5,4},{6,5},{7,6},{8,7},{9,8},{10,9},{11,1... | collective-permute-start | bytes 393224 | tf_op jit(solution)/shard_map/ppermute | solution.py:104
  116.2 0.7 collective-permute-done.6
  117.0 4.0 %collective-permute-done.7 = bf16[1,16,4,8,128]{4,3,2,1,0:T(8,128)(2,1)S(1)} collective-permute-done((bf16[1,16,4,8,128]{4,3,2,1,0:T(8,128)(2,1)S(1)}, bf16[1,16,4,8,128]{4,3,2,1,0:T(8,128)(2,1)S(1)}, u32[]{:S(2)}, u32[]{:S(2)}) %collective-permute-start.7) | collective-permute-done | bytes 131104 | tf_op jit(solution)/shard_map/ppermute | solution.py:104
  121.0 0.9 pad_maximum_fusion.4
  121.8 5.1 %shard_map.68 = (bf16[1568,128]{1,0:T(8,128)(2,1)}, bf16[512,128]{1,0:T(8,128)(2,1)}) custom-call(s32[2]{0:T(128)} %pad_add_fusion.offs_ref, bf16[2048,128]{1,0:T(8,128)(2,1)} %bitcast.31, bf16[2048,128]{1,0:T(8,128)(2,1)} %bitcast.30, bf16[8,14,128,128]{3,2,1,0:T(8,128)(2,1)} %all-gather.2.cloned.1.call-done.w_hbm), custom_call_target="tpu_custom_call" | custom-call | flops 667942912 | bytes 2007040 | tf_op jit(solution)/shard_map/pallas_call | solution.py:76
  127.0 0.9 constant_dynamic-update-slice_fusion.3
  127.9 4.5 %shard_map.69 = (bf16[1152,128]{1,0:T(8,128)(2,1)}, bf16[512,128]{1,0:T(8,128)(2,1)}) custom-call(s32[2]{0:T(128)} %pad_add_fusion.offs_ref, bf16[1568,128]{1,0:T(8,128)(2,1)} %get-tuple-element.39.prior_ref, bf16[1568,128]{1,0:T(8,128)(2,1)} %bitcast.34, bf16[8,14,128,128]{3,2,1,0:T(8,128)(2,1)} %all-gather.2.cloned.1.call-done.w_hbm), custom_call_target="tpu_custom_call" | custom-call | flops 490733568 | bytes 1654784 | tf_op jit(solution)/shard_map/pallas_call | solution.py:76
  132.4 0.9 constant_dynamic-update-slice_fusion.2
  133.3 4.0 %shard_map.70 = (bf16[800,128]{1,0:T(8,128)(2,1)}, bf16[512,128]{1,0:T(8,128)(2,1)}) custom-call(s32[2]{0:T(128)} %pad_add_fusion.offs_ref, bf16[1152,128]{1,0:T(8,128)(2,1)} %get-tuple-element.41.prior_ref, bf16[1152,128]{1,0:T(8,128)(2,1)} %bitcast.36, bf16[8,14,128,128]{3,2,1,0:T(8,128)(2,1)} %all-gather.2.cloned.1.call-done.w_hbm), custom_call_target="tpu_custom_call" | custom-call | flops 340787200 | bytes 1351680 | tf_op jit(solution)/shard_map/pallas_call | solution.py:76
  137.3 0.9 constant_dynamic-update-slice_fusion.1
  138.2 3.6 %shard_map.71 = (bf16[512,128]{1,0:T(8,128)(2,1)}, bf16[512,128]{1,0:T(8,128)(2,1)}) custom-call(s32[2]{0:T(128)} %pad_add_fusion.offs_ref, bf16[800,128]{1,0:T(8,128)(2,1)} %get-tuple-element.43.prior_ref, bf16[800,128]{1,0:T(8,128)(2,1)} %bitcast.42, bf16[8,14,128,128]{3,2,1,0:T(8,128)(2,1)} %all-gather.2.cloned.1.call-done.w_hbm), custom_call_target="tpu_custom_call" | custom-call | flops 218103808 | bytes 1097728 | tf_op jit(solution)/shard_map/pallas_call | solution.py:76
  141.9 0.9 constant_dynamic-update-slice_fusion
  142.8 18.5 %all_to_all.17 = bf16[8,1,8,8,8,128]{5,4,3,2,1,0:T(8,128)(2,1)S(1)} all-to-all(bf16[8,1,8,8,8,128]{5,4,3,2,1,0:T(8,128)(2,1)S(1)} %constant_dynamic-update-slice_fusion), channel_id=1, replica_groups=mesh['section'=8,'frames'=4,'space'=16] {'section'}, dimensions={0} | all-to-all | bytes 2097152 | tf_op jit(solution)/shard_map/all_to_all | solution.py:183
  161.3 1.0 copy.24
  (42 shorter events, 3.3 us)
Async XLA Ops:
  6.5 26.3 %copy-start = (bf16[8,8,8,8,128]{4,3,2,1,0:T(8,128)(2,1)S(1)}, bf16[8,8,8,8,128]{4,3,2,1,0:T(8,128)(2,1)}, u32[]{:S(2)}) copy-start(bf16[8,8,8,8,128]{4,3,2,1,0:T(8,128)(2,1)} %param.6) | copy-start | bytes 3145732
  6.5 20.4 %copy-start.7 = (bf16[1,3,128,128]{3,2,1,0:T(8,128)(2,1)S(1)}, bf16[1,3,128,128]{3,2,1,0:T(8,128)(2,1)}, u32[]{:S(2)}) copy-start(bf16[1,3,128,128]{3,2,1,0:T(8,128)(2,1)} %param.10) | copy-start | bytes 294916
  6.5 20.4 %copy-start.8 = (bf16[1,128,128]{2,1,0:T(8,128)(2,1)S(1)}, bf16[1,128,128]{2,1,0:T(8,128)(2,1)}, u32[]{:S(2)}) copy-start(bf16[1,128,128]{2,1,0:T(8,128)(2,1)} %param.11) | copy-start | bytes 98308
  6.5 20.4 %copy-start.2 = (bf16[1,9,128,128]{3,2,1,0:T(8,128)(2,1)S(1)}, bf16[1,9,128,128]{3,2,1,0:T(8,128)(2,1)}, u32[]{:S(2)}) copy-start(bf16[1,9,128,128]{3,2,1,0:T(8,128)(2,1)} %param.9) | copy-start | bytes 884740
  6.5 20.4 %all-to-all-start = ((bf16[8,8,8,8,128]{4,3,2,1,0:T(8,128)(2,1)}), bf16[8,8,8,8,128]{4,3,2,1,0:T(8,128)(2,1)S(1)}, u32[]{:S(2)}, u32[]{:S(2)}) async-start(bf16[8,8,8,8,128]{4,3,2,1,0:T(8,128)(2,1)} %bitcast.41), calls=%async_computation | async-start | bytes 2097152 | tf_op jit(solution)/shard_map/all_to_all | solution.py:140
  11.0 70.2 %all-gather.2.cloned.1.call-start = ((), (), s32[]{:S(2)}) async-start(), calls=%async_computation.2 | async-start | bytes 4128768 | tf_op jit(solution)/shard_map/all_gather | solution.py:152
  28.0 10.8 %collective-permute-start.8 = (bf16[4,1,4,8,8,128]{5,4,3,2,0,1:T(8,128)(2,1)S(1)}, bf16[4,1,4,8,8,128]{5,4,3,2,0,1:T(8,128)(2,1)S(1)}, u32[]{:S(2)}, u32[]{:S(2)}) collective-permute-start(bf16[4,1,4,8,8,128]{5,4,3,2,0,1:T(8,128)(2,1)S(1)} %get-tuple-element.55), channel_id=1, source_target_pairs={{0,16},{16,32},{32,48},{1,17},{17,33},{33,49},{2,18},{18,34},{34,5... | collective-permute-start | bytes 786440 | tf_op jit(solution)/shard_map/ppermute | solution.py:103
  31.5 9.6 %collective-permute-start.9 = (bf16[4,1,4,8,8,128]{5,4,3,2,0,1:T(8,128)(2,1)S(1)}, bf16[4,1,4,8,8,128]{5,4,3,2,0,1:T(8,128)(2,1)S(1)}, u32[]{:S(2)}, u32[]{:S(2)}) collective-permute-start(bf16[4,1,4,8,8,128]{5,4,3,2,0,1:T(8,128)(2,1)S(1)} %get-tuple-element.56), channel_id=1, source_target_pairs={{16,0},{32,16},{48,32},{17,1},{33,17},{49,33},{18,2},{34,18},{50,3... | collective-permute-start | bytes 786440 | tf_op jit(solution)/shard_map/ppermute | solution.py:104
  32.9 15.4 %collective-permute-start = (bf16[5,1,4,8,8,128]{5,4,3,2,0,1:T(8,128)(2,1)S(1)}, bf16[5,1,4,8,8,128]{5,4,3,2,0,1:T(8,128)(2,1)S(1)}, u32[]{:S(2)}, u32[]{:S(2)}) collective-permute-start(bf16[5,1,4,8,8,128]{5,4,3,2,0,1:T(8,128)(2,1)S(1)} %get-tuple-element.53), channel_id=1, source_target_pairs={{0,16},{16,32},{32,48},{1,17},{17,33},{33,49},{2,18},{18,34},{34,5... | collective-permute-start | bytes 983048 | tf_op jit(solution)/shard_map/ppermute | solution.py:103
  37.5 10.8 %collective-permute-start.1 = (bf16[5,1,4,8,8,128]{5,4,3,2,0,1:T(8,128)(2,1)S(1)}, bf16[5,1,4,8,8,128]{5,4,3,2,0,1:T(8,128)(2,1)S(1)}, u32[]{:S(2)}, u32[]{:S(2)}) collective-permute-start(bf16[5,1,4,8,8,128]{5,4,3,2,0,1:T(8,128)(2,1)S(1)} %get-tuple-element.54), channel_id=1, source_target_pairs={{16,0},{32,16},{48,32},{17,1},{33,17},{49,33},{18,2},{34,18},{50,3... | collective-permute-start | bytes 983048 | tf_op jit(solution)/shard_map/ppermute | solution.py:104
  41.3 17.4 %collective-permute-start.10 = (bf16[4,1,16,4,8,128]{5,4,3,2,0,1:T(8,128)(2,1)S(1)}, bf16[4,1,16,4,8,128]{5,4,3,2,0,1:T(8,128)(2,1)S(1)}, u32[]{:S(2)}, u32[]{:S(2)}) collective-permute-start(bf16[4,1,16,4,8,128]{5,4,3,2,0,1:T(8,128)(2,1)S(1)} %get-tuple-element.49), channel_id=1, source_target_pairs={{0,1},{1,2},{2,3},{3,4},{4,5},{5,6},{6,7},{7,8},{8,9},{9,10},{10,1... | collective-permute-start | bytes 1572872 | tf_op jit(solution)/shard_map/ppermute | solution.py:103
  46.3 18.0 %collective-permute-start.11 = (bf16[4,1,16,4,8,128]{5,4,3,2,0,1:T(8,128)(2,1)S(1)}, bf16[4,1,16,4,8,128]{5,4,3,2,0,1:T(8,128)(2,1)S(1)}, u32[]{:S(2)}, u32[]{:S(2)}) collective-permute-start(bf16[4,1,16,4,8,128]{5,4,3,2,0,1:T(8,128)(2,1)S(1)} %get-tuple-element.50), channel_id=1, source_target_pairs={{1,0},{2,1},{3,2},{4,3},{5,4},{6,5},{7,6},{8,7},{9,8},{10,9},{11,1... | collective-permute-start | bytes 1572872 | tf_op jit(solution)/shard_map/ppermute | solution.py:104
  48.7 21.3 %collective-permute-start.2 = (bf16[5,1,16,4,8,128]{5,4,3,2,0,1:T(8,128)(2,1)S(1)}, bf16[5,1,16,4,8,128]{5,4,3,2,0,1:T(8,128)(2,1)S(1)}, u32[]{:S(2)}, u32[]{:S(2)}) collective-permute-start(bf16[5,1,16,4,8,128]{5,4,3,2,0,1:T(8,128)(2,1)S(1)} %get-tuple-element.47), channel_id=1, source_target_pairs={{0,1},{1,2},{2,3},{3,4},{4,5},{5,6},{6,7},{7,8},{8,9},{9,10},{10,1... | collective-permute-start | bytes 1966088 | tf_op jit(solution)/shard_map/ppermute | solution.py:103
  53.9 21.5 %collective-permute-start.3 = (bf16[5,1,16,4,8,128]{5,4,3,2,0,1:T(8,128)(2,1)S(1)}, bf16[5,1,16,4,8,128]{5,4,3,2,0,1:T(8,128)(2,1)S(1)}, u32[]{:S(2)}, u32[]{:S(2)}) collective-permute-start(bf16[5,1,16,4,8,128]{5,4,3,2,0,1:T(8,128)(2,1)S(1)} %get-tuple-element.48), channel_id=1, source_target_pairs={{1,0},{2,1},{3,2},{4,3},{5,4},{6,5},{7,6},{8,7},{9,8},{10,9},{11,1... | collective-permute-start | bytes 1966088 | tf_op jit(solution)/shard_map/ppermute | solution.py:104
  94.8 9.5 %copy-start.5 = (bf16[512,128]{1,0:T(8,128)(2,1)S(1)}, bf16[512,128]{1,0:T(8,128)(2,1)}, u32[]{:S(2)}) copy-start(bf16[512,128]{1,0:T(8,128)(2,1)} %get-tuple-element.30) | copy-start | bytes 393220
  94.8 9.5 %copy-start.6 = (bf16[512,128]{1,0:T(8,128)(2,1)S(1)}, bf16[512,128]{1,0:T(8,128)(2,1)}, u32[]{:S(2)}) copy-start(bf16[512,128]{1,0:T(8,128)(2,1)} %get-tuple-element.32) | copy-start | bytes 393220
  94.8 21.3 %copy-start.3 = (bf16[512,128]{1,0:T(8,128)(2,1)S(1)}, bf16[512,128]{1,0:T(8,128)(2,1)}, u32[]{:S(2)}) copy-start(bf16[512,128]{1,0:T(8,128)(2,1)} %get-tuple-element.34) | copy-start | bytes 393220
  98.5 17.6 %copy-start.4 = (bf16[512,128]{1,0:T(8,128)(2,1)S(1)}, bf16[512,128]{1,0:T(8,128)(2,1)}, u32[]{:S(2)}) copy-start(bf16[512,128]{1,0:T(8,128)(2,1)} %get-tuple-element.36) | copy-start | bytes 393220
  98.6 22.4 %copy-start.1 = (bf16[512,128]{1,0:T(8,128)(2,1)S(1)}, bf16[512,128]{1,0:T(8,128)(2,1)}, u32[]{:S(2)}) copy-start(bf16[512,128]{1,0:T(8,128)(2,1)} %get-tuple-element.37) | copy-start | bytes 393220
  99.5 5.4 %collective-permute-start.4 = (bf16[1,4,8,8,128]{4,3,2,1,0:T(8,128)(2,1)S(1)}, bf16[1,4,8,8,128]{4,3,2,1,0:T(8,128)(2,1)S(1)}, u32[]{:S(2)}, u32[]{:S(2)}) collective-permute-start(bf16[1,4,8,8,128]{4,3,2,1,0:T(8,128)(2,1)S(1)} %get-tuple-element.59), channel_id=1, source_target_pairs={{0,16},{16,32},{32,48},{1,17},{17,33},{33,49},{2,18},{18,34},{34,5... | collective-permute-start | bytes 196616 | tf_op jit(solution)/shard_map/ppermute | solution.py:103
  103.0 6.2 %collective-permute-start.5 = (bf16[1,4,8,8,128]{4,3,2,1,0:T(8,128)(2,1)S(1)}, bf16[1,4,8,8,128]{4,3,2,1,0:T(8,128)(2,1)S(1)}, u32[]{:S(2)}, u32[]{:S(2)}) collective-permute-start(bf16[1,4,8,8,128]{4,3,2,1,0:T(8,128)(2,1)S(1)} %get-tuple-element.60), channel_id=1, source_target_pairs={{16,0},{32,16},{48,32},{17,1},{33,17},{49,33},{18,2},{34,18},{50,3... | collective-permute-start | bytes 196616 | tf_op jit(solution)/shard_map/ppermute | solution.py:104
  110.1 6.9 %collective-permute-start.6 = (bf16[1,16,4,8,128]{4,3,2,1,0:T(8,128)(2,1)S(1)}, bf16[1,16,4,8,128]{4,3,2,1,0:T(8,128)(2,1)S(1)}, u32[]{:S(2)}, u32[]{:S(2)}) collective-permute-start(bf16[1,16,4,8,128]{4,3,2,1,0:T(8,128)(2,1)S(1)} %get-tuple-element.57), channel_id=1, source_target_pairs={{0,1},{1,2},{2,3},{3,4},{4,5},{5,6},{6,7},{7,8},{8,9},{9,10},{10,1... | collective-permute-start | bytes 393224 | tf_op jit(solution)/shard_map/ppermute | solution.py:103
  112.9 8.1 %collective-permute-start.7 = (bf16[1,16,4,8,128]{4,3,2,1,0:T(8,128)(2,1)S(1)}, bf16[1,16,4,8,128]{4,3,2,1,0:T(8,128)(2,1)S(1)}, u32[]{:S(2)}, u32[]{:S(2)}) collective-permute-start(bf16[1,16,4,8,128]{4,3,2,1,0:T(8,128)(2,1)S(1)} %get-tuple-element.58), channel_id=1, source_target_pairs={{1,0},{2,1},{3,2},{4,3},{5,4},{6,5},{7,6},{8,7},{9,8},{10,9},{11,1... | collective-permute-start | bytes 393224 | tf_op jit(solution)/shard_map/ppermute | solution.py:104
Sparse Core Ops, SparseCore 0:
  28.0 39.1 all-gather.1

commit v14 on v12

--- a/solution.py
+++ b/solution.py
@@ -156,6 +156,7 @@
     ).astype(jnp.int32)
     totals = (num_frames * lax.axis_size("frames"), num_rows * lax.axis_size("space"))
     both = extend(jnp.concatenate([incoming[None], noise_t[:halo]], axis=0), halo, 2, 3)
+    later_noise, both = lax.optimization_barrier((noise_t[halo:], both))
     prior_ext = both[0]
     noise_round = both[1:]
     results = []
@@ -174,7 +175,7 @@
         )
         results.append(crop)
         if j == 0 and k + halo < sections:
-            later, _ = lax.optimization_barrier((noise_t[k + halo : k + 2 * halo], crop))
+            later = later_noise[k : k + halo]
             noise_next = extend(later, halo, 2, 3)
     num_cols, channels = base_frames.shape[3:]
     stacked = jnp.stack(results).reshape(

time: 170 us -> 193 us (1.14)
  waiting for transfers between devices: 42.4 us -> 59.3 us
  local copies, waits for them, and re-layouts: 8.14 us -> 16.5 us
  starting transfers between devices: 39.9 us -> 37.8 us
    ppermute x6, waiting for transfers between devices: 5.7 us -> 19.2 us  [extend(): lax.ppermute(lax.slice_in_dim(block, size - width, size, axis=dim), axis,...]
    slice x2 -> x5, local copies, waits for them, and re-layouts: 1.88 us -> 8.27 us  [on_device(): noise_round[j, :, cut:cut + num_frames + 2 * width, cut:cut + num_rows +...]
    ppermute x6, waiting for transfers between devices: 21.5 us -> 24.9 us  [extend(): lax.ppermute(lax.slice_in_dim(block, 0, width, axis=dim), axis, backward)]
    slice x6 -> x3, other arithmetic: 4.7 us -> 2.27 us  [on_device(): noise_round[j, :, cut:cut + num_frames + 2 * width, cut:cut + num_rows +...]
    ppermute x6, starting transfers between devices: 24.5 us -> 22.4 us  [extend(): lax.ppermute(lax.slice_in_dim(block, size - width, size, axis=dim), axis,...]
    concatenate x6 -> x5, other arithmetic: 4.85 us -> 6.65 us  [extend(): block = jnp.concatenate([low, block, high], axis=dim)]
    unnamed x26 -> x18, local copies, waits for them, and re-layouts: 3.85 us -> 4.82 us
  transfers between devices with their start and end apart: 14 -> 14, of which waited for: 10 -> 11; matrix products, arithmetic and copies ran while one was open for 7% -> 9% of each run, Pallas kernels for 0% -> 0%
where the time goes in v14:
time: 193 us; the launch traced here: 192 us
  waiting for transfers between devices  59.3 us (31%)
  starting transfers between devices  37.8 us (20%)
  Pallas kernels  32.3 us (17%)
  blocking collectives  18.5 us (10%)
  local copies, waits for them, and re-layouts  16.5 us (9%)
  between operations  14.4 us (7%)
  other arithmetic  13 us (7%)
    pallas_call x8, Pallas kernels, section_call(): pl.pallas_call(functools.partial(section_kernel, m, n, cols, inner, num_f...  32.3 us
    ppermute x6, waiting for transfers between devices, extend(): lax.ppermute(lax.slice_in_dim(block, 0, width, axis=dim), axis, backward)  24.9 us
    ppermute x6, starting transfers between devices, extend(): lax.ppermute(lax.slice_in_dim(block, size - width, size, axis=dim), axis,...  22.4 us
    ppermute x6, waiting for transfers between devices, extend(): lax.ppermute(lax.slice_in_dim(block, size - width, size, axis=dim), axis,...  19.2 us
    all_to_all x1, blocking collectives, on_device(): return lax.all_to_all(stacked, 'section', 0, 1, tiled=True)  18.5 us
    all_to_all x1, waiting for transfers between devices, on_device(): noise_t = lax.all_to_all(section_noise[0], 'section', 0, 0, tiled=True)  15.2 us
    ppermute x6, starting transfers between devices, extend(): lax.ppermute(lax.slice_in_dim(block, 0, width, axis=dim), axis, backward)  10.9 us
    slice x5, local copies, waits for them, and re-layouts, on_device(): noise_round[j, :, cut:cut + num_frames + 2 * width, cut:cut + num_rows +...  8.27 us
  transfers between devices with their start and end apart: 14, of which 11 were waited for; matrix products, arithmetic and copies ran while one was open for 9% of the time, Pallas kernels for 0%

profile of v14, /device:TPU:96, one launch (start us, length us, event | category | flops | bytes accessed | tf_op | source)
XLA Modules:
  0.0 191.8 jit_solution(4404057820013346822)
XLA Ops:
  6.5 4.4 %all-to-all-start = ((bf16[8,8,8,8,128]{4,3,2,1,0:T(8,128)(2,1)}), bf16[8,8,8,8,128]{4,3,2,1,0:T(8,128)(2,1)S(1)}, u32[]{:S(2)}, u32[]{:S(2)}) async-start(bf16[8,8,8,8,128]{4,3,2,1,0:T(8,128)(2,1)} %bitcast.41), calls=%async_computation | async-start | bytes 2097152 | tf_op jit(solution)/shard_map/all_to_all | solution.py:139
  11.7 15.2 %all-to-all-done = bf16[8,8,8,8,128]{4,3,2,1,0:T(8,128)(2,1)S(1)} async-done(((bf16[8,8,8,8,128]{4,3,2,1,0:T(8,128)(2,1)}), bf16[8,8,8,8,128]{4,3,2,1,0:T(8,128)(2,1)S(1)}, u32[]{:S(2)}, u32[]{:S(2)}) %all-to-all-start) | async-done | bytes 1048608 | tf_op jit(solution)/shard_map/all_to_all | solution.py:139
  26.9 2.0 %maximum_maximum_fusion = bf16[1,14,128,128]{3,2,1,0:T(8,128)(2,1)} fusion(bf16[1,1,128,128]{3,2,1,0:T(8,128)(2,1)} %bitcast.52, bf16[1,3,128,128]{3,2,1,0:T(8,128)(2,1)} %param.10, bf16[1,9,128,128]{3,2,1,0:T(8,128)(2,1)} %param.9, bf16[14]{0:T(256)(128)(2,1)S(1)} %pad.26.clone), kind=kLoop, calls=%fused_computation.6 | loop fusion | flops 688128 | bytes 884764 | tf_op jit(solution)/shard_map/concatenate | solution.py:148
  29.1 3.5 %collective-permute-start = (bf16[5,1,4,8,8,128]{5,4,3,2,0,1:T(8,128)(2,1)S(1)}, bf16[5,1,4,8,8,128]{5,4,3,2,0,1:T(8,128)(2,1)S(1)}, u32[]{:S(2)}, u32[]{:S(2)}) collective-permute-start(bf16[5,1,4,8,8,128]{5,4,3,2,0,1:T(8,128)(2,1)S(1)} %get-tuple-element.57), channel_id=1, source_target_pairs={{0,16},{16,32},{32,48},{1,17},{17,33},{33,49},{2,18},{18,34},{34,5... | collective-permute-start | bytes 983048 | tf_op jit(solution)/shard_map/ppermute | solution.py:101
  32.6 1.3 collective-permute-start.1
  33.9 5.4 %collective-permute-done = bf16[5,1,4,8,8,128]{5,4,3,2,0,1:T(8,128)(2,1)S(1)} collective-permute-done((bf16[5,1,4,8,8,128]{5,4,3,2,0,1:T(8,128)(2,1)S(1)}, bf16[5,1,4,8,8,128]{5,4,3,2,0,1:T(8,128)(2,1)S(1)}, u32[]{:S(2)}, u32[]{:S(2)}) %collective-permute-start) | collective-permute-done | bytes 327712 | tf_op jit(solution)/shard_map/ppermute | solution.py:101
  39.3 4.1 %collective-permute-done.1 = bf16[5,1,4,8,8,128]{5,4,3,2,0,1:T(8,128)(2,1)S(1)} collective-permute-done((bf16[5,1,4,8,8,128]{5,4,3,2,0,1:T(8,128)(2,1)S(1)}, bf16[5,1,4,8,8,128]{5,4,3,2,0,1:T(8,128)(2,1)S(1)}, u32[]{:S(2)}, u32[]{:S(2)}) %collective-permute-start.1) | collective-permute-done | bytes 327712 | tf_op jit(solution)/shard_map/ppermute | solution.py:102
  43.9 5.0 %collective-permute-start.2 = (bf16[5,1,16,4,8,128]{5,4,3,2,0,1:T(8,128)(2,1)S(1)}, bf16[5,1,16,4,8,128]{5,4,3,2,0,1:T(8,128)(2,1)S(1)}, u32[]{:S(2)}, u32[]{:S(2)}) collective-permute-start(bf16[5,1,16,4,8,128]{5,4,3,2,0,1:T(8,128)(2,1)S(1)} %get-tuple-element.51), channel_id=1, source_target_pairs={{0,1},{1,2},{2,3},{3,4},{4,5},{5,6},{6,7},{7,8},{8,9},{9,10},{10,1... | collective-permute-start | bytes 1966088 | tf_op jit(solution)/shard_map/ppermute | solution.py:101
  49.0 1.9 %collective-permute-start.3 = (bf16[5,1,16,4,8,128]{5,4,3,2,0,1:T(8,128)(2,1)S(1)}, bf16[5,1,16,4,8,128]{5,4,3,2,0,1:T(8,128)(2,1)S(1)}, u32[]{:S(2)}, u32[]{:S(2)}) collective-permute-start(bf16[5,1,16,4,8,128]{5,4,3,2,0,1:T(8,128)(2,1)S(1)} %get-tuple-element.52), channel_id=1, source_target_pairs={{1,0},{2,1},{3,2},{4,3},{5,4},{6,5},{7,6},{8,7},{9,8},{10,9},{11,1... | collective-permute-start | bytes 1966088 | tf_op jit(solution)/shard_map/ppermute | solution.py:102
  50.9 10.6 %collective-permute-done.2 = bf16[5,1,16,4,8,128]{5,4,3,2,0,1:T(8,128)(2,1)S(1)} collective-permute-done((bf16[5,1,16,4,8,128]{5,4,3,2,0,1:T(8,128)(2,1)S(1)}, bf16[5,1,16,4,8,128]{5,4,3,2,0,1:T(8,128)(2,1)S(1)}, u32[]{:S(2)}, u32[]{:S(2)}) %collective-permute-start.2) | collective-permute-done | bytes 655392 | tf_op jit(solution)/shard_map/ppermute | solution.py:101
  61.6 5.3 %collective-permute-done.3 = bf16[5,1,16,4,8,128]{5,4,3,2,0,1:T(8,128)(2,1)S(1)} collective-permute-done((bf16[5,1,16,4,8,128]{5,4,3,2,0,1:T(8,128)(2,1)S(1)}, bf16[5,1,16,4,8,128]{5,4,3,2,0,1:T(8,128)(2,1)S(1)}, u32[]{:S(2)}, u32[]{:S(2)}) %collective-permute-start.3) | collective-permute-done | bytes 655392 | tf_op jit(solution)/shard_map/ppermute | solution.py:102
  66.9 3.5 %pad_maximum_fusion = bf16[5,1,16,16,8,128]{5,4,3,2,0,1:T(8,128)(2,1)} fusion(bf16[5,1,16,4,8,128]{5,4,3,2,0,1:T(8,128)(2,1)S(1)} %collective-permute-done.3, bf16[5,1,4,8,8,128]{5,4,3,2,0,1:T(8,128)(2,1)S(1)} %collective-permute-done.1, bf16[4,1,8,8,8,128]{5,4,3,2,0,1:T(8,128)(2,1)S(1)} %get-tuple-element.55, ...), kind=kLoop, calls=%fused_computation | loop fusion | flops 6553600 | bytes 5242880 | tf_op jit(solution)/shard_map/concatenate | solution.py:103
  70.5 3.5 %collective-permute-start.8 = (bf16[4,1,4,8,8,128]{5,4,3,2,0,1:T(8,128)(2,1)S(1)}, bf16[4,1,4,8,8,128]{5,4,3,2,0,1:T(8,128)(2,1)S(1)}, u32[]{:S(2)}, u32[]{:S(2)}) collective-permute-start(bf16[4,1,4,8,8,128]{5,4,3,2,0,1:T(8,128)(2,1)S(1)} %get-tuple-element.60), channel_id=1, source_target_pairs={{0,16},{16,32},{32,48},{1,17},{17,33},{33,49},{2,18},{18,34},{34,5... | collective-permute-start | bytes 786440 | tf_op jit(solution)/shard_map/ppermute | solution.py:101
  74.0 1.3 collective-permute-start.9
  75.3 2.6 %collective-permute-done.8 = bf16[4,1,4,8,8,128]{5,4,3,2,0,1:T(8,128)(2,1)S(1)} collective-permute-done((bf16[4,1,4,8,8,128]{5,4,3,2,0,1:T(8,128)(2,1)S(1)}, bf16[4,1,4,8,8,128]{5,4,3,2,0,1:T(8,128)(2,1)S(1)}, u32[]{:S(2)}, u32[]{:S(2)}) %collective-permute-start.8) | collective-permute-done | bytes 262176 | tf_op jit(solution)/shard_map/ppermute | solution.py:101
  77.9 4.3 %collective-permute-done.9 = bf16[4,1,4,8,8,128]{5,4,3,2,0,1:T(8,128)(2,1)S(1)} collective-permute-done((bf16[4,1,4,8,8,128]{5,4,3,2,0,1:T(8,128)(2,1)S(1)}, bf16[4,1,4,8,8,128]{5,4,3,2,0,1:T(8,128)(2,1)S(1)}, u32[]{:S(2)}, u32[]{:S(2)}) %collective-permute-start.9) | collective-permute-done | bytes 262176 | tf_op jit(solution)/shard_map/ppermute | solution.py:102
  82.3 1.1 fusion.4
  83.4 2.8 %collective-permute-start.10 = (bf16[4,1,16,4,8,128]{5,4,3,2,0,1:T(8,128)(2,1)}, bf16[4,1,16,4,8,128]{5,4,3,2,0,1:T(8,128)(2,1)S(1)}, u32[]{:S(2)}, u32[]{:S(2)}) collective-permute-start(bf16[4,1,16,4,8,128]{5,4,3,2,0,1:T(8,128)(2,1)} %get-tuple-element.53), channel_id=1, source_target_pairs={{0,1},{1,2},{2,3},{3,4},{4,5},{5,6},{6,7},{7,8},{8,9},{9,10},{10,1... | collective-permute-start | bytes 1572872 | tf_op jit(solution)/shard_map/ppermute | solution.py:101
  86.2 3.0 %collective-permute-start.11 = (bf16[4,1,16,4,8,128]{5,4,3,2,0,1:T(8,128)(2,1)}, bf16[4,1,16,4,8,128]{5,4,3,2,0,1:T(8,128)(2,1)S(1)}, u32[]{:S(2)}, u32[]{:S(2)}) collective-permute-start(bf16[4,1,16,4,8,128]{5,4,3,2,0,1:T(8,128)(2,1)} %get-tuple-element.54), channel_id=1, source_target_pairs={{1,0},{2,1},{3,2},{4,3},{5,4},{6,5},{7,6},{8,7},{9,8},{10,9},{11,1... | collective-permute-start | bytes 1572872 | tf_op jit(solution)/shard_map/ppermute | solution.py:102
  89.8 1.8 slice.86
  91.6 1.7 slice.87
  93.3 1.6 slice.88
  95.0 2.3 %fusion.2 = (bf16[1,1,16,16,8,128]{5,4,3,2,0,1:T(8,128)(2,1)}, bf16[1,1,16,16,8,128]{5,4,3,2,0,1:T(8,128)(2,1)}) fusion(bf16[5,1,16,16,8,128]{5,4,3,2,0,1:T(8,128)(2,1)} %pad_maximum_fusion), kind=kLoop, calls=%fused_computation.28 | loop fusion | bytes 2097152 | tf_op jit(solution)/shard_map/slice | solution.py:170
  97.3 1.9 collective-permute-done.11
  102.5 1.4 fusion.1.lv_ref
  103.9 4.7 %shard_map.64 = (bf16[1568,128]{1,0:T(8,128)(2,1)}, bf16[512,128]{1,0:T(8,128)(2,1)}) custom-call(s32[2]{0:T(128)} %pad_add_fusion.offs_ref, f32[8]{0:T(128)} %fusion.1.lv_ref, bf16[2048,128]{1,0:T(8,128)(2,1)} %bitcast.33, bf16[2048,128]{1,0:T(8,128)(2,1)} %bitcast.32, bf16[8,14,128,128]{3,2,1,0:T(8,128)(2,1)} %all-gather.2.cloned.1.call-done.w_hbm), custom_call_target="tpu_custom_call" | custom-call | flops 667942912 | bytes 2007040 | tf_op jit(solution)/shard_map/pallas_call | solution.py:74
  108.6 4.2 %shard_map.65 = (bf16[1152,128]{1,0:T(8,128)(2,1)}, bf16[512,128]{1,0:T(8,128)(2,1)}) custom-call(s32[2]{0:T(128)} %pad_add_fusion.offs_ref, f32[8]{0:T(128)} %fusion.1.lv_ref, bf16[1568,128]{1,0:T(8,128)(2,1)} %get-tuple-element.34.prior_ref, bf16[1568,128]{1,0:T(8,128)(2,1)} %bitcast.35, bf16[8,14,128,128]{3,2,1,0:T(8,128)(2,1)} %all-gather.2.cloned.1.call-done.w_hbm), custom_call_target="tpu_custom_call" | custom-call | flops 490733568 | bytes 1654784 | tf_op jit(solution)/shard_map/pallas_call | solution.py:74
  112.7 3.8 %shard_map.66 = (bf16[800,128]{1,0:T(8,128)(2,1)}, bf16[512,128]{1,0:T(8,128)(2,1)}) custom-call(s32[2]{0:T(128)} %pad_add_fusion.offs_ref, f32[8]{0:T(128)} %fusion.1.lv_ref, bf16[1152,128]{1,0:T(8,128)(2,1)} %get-tuple-element.36.prior_ref, bf16[1152,128]{1,0:T(8,128)(2,1)} %bitcast.37, bf16[8,14,128,128]{3,2,1,0:T(8,128)(2,1)} %all-gather.2.cloned.1.call-done.w_hbm), custom_call_target="tpu_custom_call" | custom-call | flops 340787200 | bytes 1351680 | tf_op jit(solution)/shard_map/pallas_call | solution.py:74
  116.6 3.5 %shard_map.67 = (bf16[512,128]{1,0:T(8,128)(2,1)}, bf16[512,128]{1,0:T(8,128)(2,1)}) custom-call(s32[2]{0:T(128)} %pad_add_fusion.offs_ref, f32[8]{0:T(128)} %fusion.1.lv_ref, bf16[800,128]{1,0:T(8,128)(2,1)} %get-tuple-element.38.prior_ref, bf16[800,128]{1,0:T(8,128)(2,1)} %bitcast.43, bf16[8,14,128,128]{3,2,1,0:T(8,128)(2,1)} %all-gather.2.cloned.1.call-done.w_hbm), custom_call_target="tpu_custom_call" | custom-call | flops 218103808 | bytes 1097728 | tf_op jit(solution)/shard_map/pallas_call | solution.py:74
  121.0 3.5 %collective-permute-start.4 = (bf16[1,4,8,8,128]{4,3,2,1,0:T(8,128)(2,1)S(1)}, bf16[1,4,8,8,128]{4,3,2,1,0:T(8,128)(2,1)S(1)}, u32[]{:S(2)}, u32[]{:S(2)}) collective-permute-start(bf16[1,4,8,8,128]{4,3,2,1,0:T(8,128)(2,1)S(1)} %get-tuple-element.63), channel_id=1, source_target_pairs={{0,16},{16,32},{32,48},{1,17},{17,33},{33,49},{2,18},{18,34},{34,5... | collective-permute-start | bytes 196616 | tf_op jit(solution)/shard_map/ppermute | solution.py:101
  124.5 1.3 collective-permute-start.5
  126.4 4.3 %collective-permute-done.5 = bf16[1,4,8,8,128]{4,3,2,1,0:T(8,128)(2,1)S(1)} collective-permute-done((bf16[1,4,8,8,128]{4,3,2,1,0:T(8,128)(2,1)S(1)}, bf16[1,4,8,8,128]{4,3,2,1,0:T(8,128)(2,1)S(1)}, u32[]{:S(2)}, u32[]{:S(2)}) %collective-permute-start.5) | collective-permute-done | bytes 65568 | tf_op jit(solution)/shard_map/ppermute | solution.py:102
  130.7 0.9 pad_maximum_fusion.7
  131.6 4.1 %collective-permute-start.6 = (bf16[1,16,4,8,128]{4,3,2,1,0:T(8,128)(2,1)S(1)}, bf16[1,16,4,8,128]{4,3,2,1,0:T(8,128)(2,1)S(1)}, u32[]{:S(2)}, u32[]{:S(2)}) collective-permute-start(bf16[1,16,4,8,128]{4,3,2,1,0:T(8,128)(2,1)S(1)} %get-tuple-element.61), channel_id=1, source_target_pairs={{0,1},{1,2},{2,3},{3,4},{4,5},{5,6},{6,7},{7,8},{8,9},{9,10},{10,1... | collective-permute-start | bytes 393224 | tf_op jit(solution)/shard_map/ppermute | solution.py:101
  135.7 2.1 %collective-permute-start.7 = (bf16[1,16,4,8,128]{4,3,2,1,0:T(8,128)(2,1)S(1)}, bf16[1,16,4,8,128]{4,3,2,1,0:T(8,128)(2,1)S(1)}, u32[]{:S(2)}, u32[]{:S(2)}) collective-permute-start(bf16[1,16,4,8,128]{4,3,2,1,0:T(8,128)(2,1)S(1)} %get-tuple-element.62), channel_id=1, source_target_pairs={{1,0},{2,1},{3,2},{4,3},{5,4},{6,5},{7,6},{8,7},{9,8},{10,9},{11,1... | collective-permute-start | bytes 393224 | tf_op jit(solution)/shard_map/ppermute | solution.py:102
  137.9 0.9 constant_dynamic-update-slice_fusion.7
  138.8 5.0 %collective-permute-done.7 = bf16[1,16,4,8,128]{4,3,2,1,0:T(8,128)(2,1)S(1)} collective-permute-done((bf16[1,16,4,8,128]{4,3,2,1,0:T(8,128)(2,1)S(1)}, bf16[1,16,4,8,128]{4,3,2,1,0:T(8,128)(2,1)S(1)}, u32[]{:S(2)}, u32[]{:S(2)}) %collective-permute-start.7) | collective-permute-done | bytes 131104 | tf_op jit(solution)/shard_map/ppermute | solution.py:102
  143.8 1.8 pad_maximum_fusion.3
  145.6 4.7 %shard_map.68 = (bf16[1568,128]{1,0:T(8,128)(2,1)}, bf16[512,128]{1,0:T(8,128)(2,1)}) custom-call(s32[2]{0:T(128)} %pad_add_fusion.offs_ref, f32[8]{0:T(128)} %fusion.1.lv_ref, bf16[2048,128]{1,0:T(8,128)(2,1)} %bitcast.31, bf16[2048,128]{1,0:T(8,128)(2,1)} %bitcast.30, bf16[8,14,128,128]{3,2,1,0:T(8,128)(2,1)} %all-gather.2.cloned.1.call-done.w_hbm), custom_call_target="tpu_custom_call" | custom-call | flops 667942912 | bytes 2007040 | tf_op jit(solution)/shard_map/pallas_call | solution.py:74
  150.3 0.9 constant_dynamic-update-slice_fusion.6
  151.2 4.2 %shard_map.69 = (bf16[1152,128]{1,0:T(8,128)(2,1)}, bf16[512,128]{1,0:T(8,128)(2,1)}) custom-call(s32[2]{0:T(128)} %pad_add_fusion.offs_ref, f32[8]{0:T(128)} %fusion.1.lv_ref, bf16[1568,128]{1,0:T(8,128)(2,1)} %get-tuple-element.43.prior_ref, bf16[1568,128]{1,0:T(8,128)(2,1)} %bitcast.34, bf16[8,14,128,128]{3,2,1,0:T(8,128)(2,1)} %all-gather.2.cloned.1.call-done.w_hbm), custom_call_target="tpu_custom_call" | custom-call | flops 490733568 | bytes 1654784 | tf_op jit(solution)/shard_map/pallas_call | solution.py:74
  155.4 0.9 constant_dynamic-update-slice_fusion.5
  156.3 3.8 %shard_map.70 = (bf16[800,128]{1,0:T(8,128)(2,1)}, bf16[512,128]{1,0:T(8,128)(2,1)}) custom-call(s32[2]{0:T(128)} %pad_add_fusion.offs_ref, f32[8]{0:T(128)} %fusion.1.lv_ref, bf16[1152,128]{1,0:T(8,128)(2,1)} %get-tuple-element.45.prior_ref, bf16[1152,128]{1,0:T(8,128)(2,1)} %bitcast.36, bf16[8,14,128,128]{3,2,1,0:T(8,128)(2,1)} %all-gather.2.cloned.1.call-done.w_hbm), custom_call_target="tpu_custom_call" | custom-call | flops 340787200 | bytes 1351680 | tf_op jit(solution)/shard_map/pallas_call | solution.py:74
  160.1 0.9 constant_dynamic-update-slice_fusion.4
  161.0 3.5 %shard_map.71 = (bf16[512,128]{1,0:T(8,128)(2,1)}, bf16[512,128]{1,0:T(8,128)(2,1)}) custom-call(s32[2]{0:T(128)} %pad_add_fusion.offs_ref, f32[8]{0:T(128)} %fusion.1.lv_ref, bf16[800,128]{1,0:T(8,128)(2,1)} %get-tuple-element.47.prior_ref, bf16[800,128]{1,0:T(8,128)(2,1)} %bitcast.42, bf16[8,14,128,128]{3,2,1,0:T(8,128)(2,1)} %all-gather.2.cloned.1.call-done.w_hbm), custom_call_target="tpu_custom_call" | custom-call | flops 218103808 | bytes 1097728 | tf_op jit(solution)/shard_map/pallas_call | solution.py:74
  164.5 0.9 constant_dynamic-update-slice_fusion.3
  165.5 18.5 %all_to_all.17 = bf16[8,1,8,8,8,128]{5,4,3,2,1,0:T(8,128)(2,1)S(1)} all-to-all(bf16[8,1,8,8,8,128]{5,4,3,2,1,0:T(8,128)(2,1)S(1)} %constant_dynamic-update-slice_fusion.3), channel_id=1, replica_groups=mesh['section'=8,'frames'=4,'space'=16] {'section'}, dimensions={0} | all-to-all | bytes 2097152 | tf_op jit(solution)/shard_map/all_to_all | solution.py:184
  184.0 1.0 copy.34
  (35 shorter events, 6.3 us)
Async XLA Ops:
  6.5 22.4 %copy-start = (bf16[8,8,8,8,128]{4,3,2,1,0:T(8,128)(2,1)S(1)}, bf16[8,8,8,8,128]{4,3,2,1,0:T(8,128)(2,1)}, u32[]{:S(2)}) copy-start(bf16[8,8,8,8,128]{4,3,2,1,0:T(8,128)(2,1)} %param.6) | copy-start | bytes 3145732
  6.5 20.4 %all-to-all-start = ((bf16[8,8,8,8,128]{4,3,2,1,0:T(8,128)(2,1)}), bf16[8,8,8,8,128]{4,3,2,1,0:T(8,128)(2,1)S(1)}, u32[]{:S(2)}, u32[]{:S(2)}) async-start(bf16[8,8,8,8,128]{4,3,2,1,0:T(8,128)(2,1)} %bitcast.41), calls=%async_computation | async-start | bytes 2097152 | tf_op jit(solution)/shard_map/all_to_all | solution.py:139
  11.0 91.5 %all-gather.2.cloned.1.call-start = ((), (), s32[]{:S(2)}) async-start(), calls=%async_computation.2 | async-start | bytes 4128768 | tf_op jit(solution)/shard_map/all_gather | solution.py:151
  29.1 10.2 %collective-permute-start = (bf16[5,1,4,8,8,128]{5,4,3,2,0,1:T(8,128)(2,1)S(1)}, bf16[5,1,4,8,8,128]{5,4,3,2,0,1:T(8,128)(2,1)S(1)}, u32[]{:S(2)}, u32[]{:S(2)}) collective-permute-start(bf16[5,1,4,8,8,128]{5,4,3,2,0,1:T(8,128)(2,1)S(1)} %get-tuple-element.57), channel_id=1, source_target_pairs={{0,16},{16,32},{32,48},{1,17},{17,33},{33,49},{2,18},{18,34},{34,5... | collective-permute-start | bytes 983048 | tf_op jit(solution)/shard_map/ppermute | solution.py:101
  32.6 10.9 %collective-permute-start.1 = (bf16[5,1,4,8,8,128]{5,4,3,2,0,1:T(8,128)(2,1)S(1)}, bf16[5,1,4,8,8,128]{5,4,3,2,0,1:T(8,128)(2,1)S(1)}, u32[]{:S(2)}, u32[]{:S(2)}) collective-permute-start(bf16[5,1,4,8,8,128]{5,4,3,2,0,1:T(8,128)(2,1)S(1)} %get-tuple-element.58), channel_id=1, source_target_pairs={{16,0},{32,16},{48,32},{17,1},{33,17},{49,33},{18,2},{34,18},{50,3... | collective-permute-start | bytes 983048 | tf_op jit(solution)/shard_map/ppermute | solution.py:102
  43.9 17.6 %collective-permute-start.2 = (bf16[5,1,16,4,8,128]{5,4,3,2,0,1:T(8,128)(2,1)S(1)}, bf16[5,1,16,4,8,128]{5,4,3,2,0,1:T(8,128)(2,1)S(1)}, u32[]{:S(2)}, u32[]{:S(2)}) collective-permute-start(bf16[5,1,16,4,8,128]{5,4,3,2,0,1:T(8,128)(2,1)S(1)} %get-tuple-element.51), channel_id=1, source_target_pairs={{0,1},{1,2},{2,3},{3,4},{4,5},{5,6},{6,7},{7,8},{8,9},{9,10},{10,1... | collective-permute-start | bytes 1966088 | tf_op jit(solution)/shard_map/ppermute | solution.py:101
  49.0 17.9 %collective-permute-start.3 = (bf16[5,1,16,4,8,128]{5,4,3,2,0,1:T(8,128)(2,1)S(1)}, bf16[5,1,16,4,8,128]{5,4,3,2,0,1:T(8,128)(2,1)S(1)}, u32[]{:S(2)}, u32[]{:S(2)}) collective-permute-start(bf16[5,1,16,4,8,128]{5,4,3,2,0,1:T(8,128)(2,1)S(1)} %get-tuple-element.52), channel_id=1, source_target_pairs={{1,0},{2,1},{3,2},{4,3},{5,4},{6,5},{7,6},{8,7},{9,8},{10,9},{11,1... | collective-permute-start | bytes 1966088 | tf_op jit(solution)/shard_map/ppermute | solution.py:102
  70.5 7.3 %collective-permute-start.8 = (bf16[4,1,4,8,8,128]{5,4,3,2,0,1:T(8,128)(2,1)S(1)}, bf16[4,1,4,8,8,128]{5,4,3,2,0,1:T(8,128)(2,1)S(1)}, u32[]{:S(2)}, u32[]{:S(2)}) collective-permute-start(bf16[4,1,4,8,8,128]{5,4,3,2,0,1:T(8,128)(2,1)S(1)} %get-tuple-element.60), channel_id=1, source_target_pairs={{0,16},{16,32},{32,48},{1,17},{17,33},{33,49},{2,18},{18,34},{34,5... | collective-permute-start | bytes 786440 | tf_op jit(solution)/shard_map/ppermute | solution.py:101
  74.0 8.3 %collective-permute-start.9 = (bf16[4,1,4,8,8,128]{5,4,3,2,0,1:T(8,128)(2,1)S(1)}, bf16[4,1,4,8,8,128]{5,4,3,2,0,1:T(8,128)(2,1)S(1)}, u32[]{:S(2)}, u32[]{:S(2)}) collective-permute-start(bf16[4,1,4,8,8,128]{5,4,3,2,0,1:T(8,128)(2,1)S(1)} %get-tuple-element.59), channel_id=1, source_target_pairs={{16,0},{32,16},{48,32},{17,1},{33,17},{49,33},{18,2},{34,18},{50,3... | collective-permute-start | bytes 786440 | tf_op jit(solution)/shard_map/ppermute | solution.py:102
  83.4 13.9 %collective-permute-start.10 = (bf16[4,1,16,4,8,128]{5,4,3,2,0,1:T(8,128)(2,1)}, bf16[4,1,16,4,8,128]{5,4,3,2,0,1:T(8,128)(2,1)S(1)}, u32[]{:S(2)}, u32[]{:S(2)}) collective-permute-start(bf16[4,1,16,4,8,128]{5,4,3,2,0,1:T(8,128)(2,1)} %get-tuple-element.53), channel_id=1, source_target_pairs={{0,1},{1,2},{2,3},{3,4},{4,5},{5,6},{6,7},{7,8},{8,9},{9,10},{10,1... | collective-permute-start | bytes 1572872 | tf_op jit(solution)/shard_map/ppermute | solution.py:101
  86.2 13.0 %collective-permute-start.11 = (bf16[4,1,16,4,8,128]{5,4,3,2,0,1:T(8,128)(2,1)}, bf16[4,1,16,4,8,128]{5,4,3,2,0,1:T(8,128)(2,1)S(1)}, u32[]{:S(2)}, u32[]{:S(2)}) collective-permute-start(bf16[4,1,16,4,8,128]{5,4,3,2,0,1:T(8,128)(2,1)} %get-tuple-element.54), channel_id=1, source_target_pairs={{1,0},{2,1},{3,2},{4,3},{5,4},{6,5},{7,6},{8,7},{9,8},{10,9},{11,1... | collective-permute-start | bytes 1572872 | tf_op jit(solution)/shard_map/ppermute | solution.py:102
  116.5 9.3 %copy-start.2 = (bf16[512,128]{1,0:T(8,128)(2,1)S(1)}, bf16[512,128]{1,0:T(8,128)(2,1)}, u32[]{:S(2)}) copy-start(bf16[512,128]{1,0:T(8,128)(2,1)} %get-tuple-element.33) | copy-start | bytes 393220
  116.6 9.3 %copy-start.3 = (bf16[512,128]{1,0:T(8,128)(2,1)S(1)}, bf16[512,128]{1,0:T(8,128)(2,1)}, u32[]{:S(2)}) copy-start(bf16[512,128]{1,0:T(8,128)(2,1)} %get-tuple-element.35) | copy-start | bytes 393220
  116.6 21.3 %copy-start.1 = (bf16[512,128]{1,0:T(8,128)(2,1)S(1)}, bf16[512,128]{1,0:T(8,128)(2,1)}, u32[]{:S(2)}) copy-start(bf16[512,128]{1,0:T(8,128)(2,1)} %get-tuple-element.37) | copy-start | bytes 393220
  121.0 5.4 %collective-permute-start.4 = (bf16[1,4,8,8,128]{4,3,2,1,0:T(8,128)(2,1)S(1)}, bf16[1,4,8,8,128]{4,3,2,1,0:T(8,128)(2,1)S(1)}, u32[]{:S(2)}, u32[]{:S(2)}) collective-permute-start(bf16[1,4,8,8,128]{4,3,2,1,0:T(8,128)(2,1)S(1)} %get-tuple-element.63), channel_id=1, source_target_pairs={{0,16},{16,32},{32,48},{1,17},{17,33},{33,49},{2,18},{18,34},{34,5... | collective-permute-start | bytes 196616 | tf_op jit(solution)/shard_map/ppermute | solution.py:101
  124.5 6.2 %collective-permute-start.5 = (bf16[1,4,8,8,128]{4,3,2,1,0:T(8,128)(2,1)S(1)}, bf16[1,4,8,8,128]{4,3,2,1,0:T(8,128)(2,1)S(1)}, u32[]{:S(2)}, u32[]{:S(2)}) collective-permute-start(bf16[1,4,8,8,128]{4,3,2,1,0:T(8,128)(2,1)S(1)} %get-tuple-element.64), channel_id=1, source_target_pairs={{16,0},{32,16},{48,32},{17,1},{33,17},{49,33},{18,2},{34,18},{50,3... | collective-permute-start | bytes 196616 | tf_op jit(solution)/shard_map/ppermute | solution.py:102
  131.6 7.2 %collective-permute-start.6 = (bf16[1,16,4,8,128]{4,3,2,1,0:T(8,128)(2,1)S(1)}, bf16[1,16,4,8,128]{4,3,2,1,0:T(8,128)(2,1)S(1)}, u32[]{:S(2)}, u32[]{:S(2)}) collective-permute-start(bf16[1,16,4,8,128]{4,3,2,1,0:T(8,128)(2,1)S(1)} %get-tuple-element.61), channel_id=1, source_target_pairs={{0,1},{1,2},{2,3},{3,4},{4,5},{5,6},{6,7},{7,8},{8,9},{9,10},{10,1... | collective-permute-start | bytes 393224 | tf_op jit(solution)/shard_map/ppermute | solution.py:101
  135.7 8.1 %collective-permute-start.7 = (bf16[1,16,4,8,128]{4,3,2,1,0:T(8,128)(2,1)S(1)}, bf16[1,16,4,8,128]{4,3,2,1,0:T(8,128)(2,1)S(1)}, u32[]{:S(2)}, u32[]{:S(2)}) collective-permute-start(bf16[1,16,4,8,128]{4,3,2,1,0:T(8,128)(2,1)S(1)} %get-tuple-element.62), channel_id=1, source_target_pairs={{1,0},{2,1},{3,2},{4,3},{5,4},{6,5},{7,6},{8,7},{9,8},{10,9},{11,1... | collective-permute-start | bytes 393224 | tf_op jit(solution)/shard_map/ppermute | solution.py:102
Sparse Core Ops, SparseCore 0:
  29.0 39.0 all-gather.1
